TPU v7x, 128 devices: a whole 4x4x4 slice. The times are simulated.
128 devices in a mesh: row: 8 (over z, core), col: 16 (over x, y).
Axes of the slice: x: 4, y: 4, z: 4, core: 2. Of those that a mesh axis runs over, the one named last changes fastest.
Arguments:
- snapshots: float32 [512, 196608], P(('row', 'col')), may hold values from -6 to 6
- panels: float32 [8, 6, 32768, 256], P(None, None, ('row', 'col')), may hold values from -0.1875 to 0.1875
- diag_inverse: float32 [8, 256, 256], replicated, may hold values from -0.6 to 1.5, as said below
Outputs:
- whitened: float32 [6, 32768, 512], P(None, ('row', 'col'))
Inputs may be any that keep to these rules, and one draw needn't show every extreme that they name: Each block of diag_inverse is lower triangular with a diagonal of 0.5 to 1.5.
All inputs are finite; a program needn't handle non-finite values.
Results may differ from a plain program's by a relative error of at most 0.0001.
Values sent between devices are 32-bit elements; how exact they have to be, the bound alone decides.
No kernel may reach another device: no remote copies, remote signals or barrier semaphores. Data moves between devices by JAX's collectives and lax.ppermute only.
A program may use at most 128 MiB of HBM per device.

v0:
```python
import jax
import jax.numpy as jnp
from jax import lax
from jax.sharding import PartitionSpec as P

AXES = ("row", "col")
HI = lax.Precision.HIGHEST


def mm(a, b):
    return jnp.dot(a, b, precision=HI, preferred_element_type=jnp.float32)


def transpose_in(pieces, devices):
    local_count, blocks, _, width_block = pieces.shape
    arrived = lax.all_to_all(pieces, AXES, split_axis=2, concat_axis=0, tiled=True)
    return jnp.transpose(arrived.reshape(devices * local_count, blocks, width_block), (1, 2, 0))


def per_device(snapshots, panels, diag_inverse):
    local_count, order_size = snapshots.shape
    sections, blocks, width_block, _ = panels.shape
    devices = lax.axis_size(AXES)
    cols = lax.axis_size("col")
    pieces = snapshots.reshape(local_count, blocks, devices, width_block)
    lead = transpose_in(pieces[:, :1], devices)[0]
    rest = transpose_in(pieces[:, 1:], devices)
    device = lax.axis_index(AXES)
    row = lax.axis_index("row")
    col = lax.axis_index("col")
    low = panels[:, 0]

    after = [[None] * 3 for _ in range(sections)]
    first_hop = [None] * sections
    own = jnp.zeros_like(lead)
    settled = lead
    for section in range(sections):
        chain = settled
        if section >= 1:
            chain = chain - mm(low[section - 1], first_hop[section - 1])
        for back in (2, 3):
            if section - back >= 0:
                chain = chain - mm(low[section - back], after[section - back][1])
        solved = mm(diag_inverse[section], chain)
        here = device == section
        own = jnp.where(here, solved, own)
        buf = jnp.where(here, solved, jnp.zeros_like(solved))
        for level in range(3):
            step = 2**level
            pairs = [
                (section + q, section + q + step)
                for q in range(step)
                if section + q + step < sections
            ]
            if pairs:
                got = lax.ppermute(buf, AXES, pairs)
                if level == 0:
                    first_hop[section] = got
                buf = buf + got
            after[section][level] = buf
        if section - 3 >= 0:
            settled = settled - mm(low[section - 3], after[section - 3][2])

    moved = lax.ppermute(own, AXES, [(k, k * cols + k) for k in range(1, sections)])
    spread = jnp.where(device == 0, own, moved)
    level = 1
    while level < cols:
        pairs = [
            (r * cols + (r + q) % cols, r * cols + (r + q + level) % cols)
            for r in range(sections)
            for q in range(level)
        ]
        spread = spread + lax.ppermute(spread, AXES, pairs)
        level *= 2
    whole = lax.all_gather(spread, "row", tiled=True)

    update = jnp.concatenate([lead[None], rest], axis=0)
    for section in range(sections):
        update = update - jnp.einsum(
            "jrc,cs->jrs",
            panels[section],
            whole[section * width_block:(section + 1) * width_block],
            precision=HI,
            preferred_element_type=jnp.float32,
        )
    first = jnp.where(device < sections, own, update[0])
    return jnp.concatenate([first[None], update[1:]], axis=0)


def solution(mesh):
    in_specs = (P(AXES, None), P(None, None, AXES, None), P())
    out_specs = P(None, AXES, None)
    return jax.shard_map(
        per_device, mesh=mesh, in_specs=in_specs, out_specs=out_specs, check_vma=False
    )
```

profile of v0, /device:TPU:1, one launch (start us, length us, event | category | flops | bytes accessed | tf_op | source)
XLA Modules:
  0.0 340.4 jit_solution(10384800668024695137)
XLA Ops:
  6.5 2.5 copy.208
  9.0 1.7 copy-done
  10.7 1.1 copy.115
  11.9 11.5 %all-to-all-start = ((f32[4,1,128,256]{3,0,1,2:T(4,128)}), f32[4,1,128,256]{3,0,1,2:T(4,128)S(1)}, u32[]{:S(2)}, u32[]{:S(2)}) async-start(f32[4,1,128,256]{3,0,1,2:T(4,128)} %copy.115), calls=%async_computation | async-start | bytes 1048576 | tf_op jit(solution)/shard_map/all_to_all | solution.py:16
  23.4 13.3 %all-to-all-done = f32[4,1,128,256]{3,0,1,2:T(4,128)S(1)} async-done(((f32[4,1,128,256]{3,0,1,2:T(4,128)}), f32[4,1,128,256]{3,0,1,2:T(4,128)S(1)}, u32[]{:S(2)}, u32[]{:S(2)}) %all-to-all-start) | async-done | bytes 524320 | tf_op jit(solution)/shard_map/all_to_all | solution.py:16
  38.0 1.6 convolution_select_fusion
  39.6 0.7 collective-permute-start
  40.3 1.6 fusion.32
  41.9 2.4 broadcast_select_fusion.5
  45.1 1.5 collective-permute-start.1
  46.6 1.1 add.67
  47.7 1.5 collective-permute-start.4
  49.2 1.1 add.65
  50.3 1.6 convolution_bitcast_fusion.18
  51.9 1.6 fusion.35
  53.5 2.4 broadcast_select_fusion.4
  56.0 1.5 collective-permute-start.6
  58.1 1.1 add.68
  59.3 0.8 collective-permute-start.5
  60.1 1.6 convolution_bitcast_fusion.14
  61.7 1.1 add.70
  63.5 1.8 fusion.39
  65.3 1.4 broadcast_select_fusion.3
  67.5 1.6 fusion.31
  69.2 12.5 %collective-permute-start.8 = (f32[256,512]{1,0:T(8,128)S(1)}, f32[256,512]{1,0:T(8,128)S(1)}, u32[]{:S(2)}, u32[]{:S(2)}) collective-permute-start(f32[256,512]{1,0:T(8,128)S(1)} %add.71), channel_id=1, source_target_pairs={{2,6},{3,7}} | collective-permute-start | bytes 1572872 | tf_op jit(solution)/shard_map/ppermute | solution.py:56
  81.7 1.6 convolution_bitcast_fusion.10
  83.4 0.7 collective-permute-start.10
  84.1 1.6 fusion.46
  85.7 1.4 broadcast_select_fusion.2
  87.8 1.6 fusion.33
  89.6 1.6 convolution_bitcast_fusion.7
  92.0 1.6 fusion.49
  93.6 1.4 broadcast_select_fusion.1
  95.7 1.6 fusion.36
  97.4 1.6 convolution_bitcast_fusion.4
  99.0 1.6 fusion.52
  100.6 1.6 broadcast_select_fusion
  102.2 1.5 collective-permute-start.15
  103.8 1.5 collective-permute-start.16
  106.0 1.8 convolution_bitcast_fusion.2
  107.8 1.9 convolution_bitcast_fusion.1
  109.7 1.7 fusion.43
  111.4 1.7 fusion.30
  116.3 1.3 collective-permute-start.21
  117.6 59.7 %collective-permute-done.21 = f32[256,512]{1,0:T(8,128)S(1)} collective-permute-done((f32[256,512]{1,0:T(8,128)S(1)}, f32[256,512]{1,0:T(8,128)S(1)}, u32[]{:S(2)}, u32[]{:S(2)}) %collective-permute-start.21) | collective-permute-done | bytes 524320 | tf_op jit(solution)/shard_map/ppermute | solution.py:73
  177.3 0.9 add.83
  178.3 1.9 slice.171
  180.2 3.2 copy.141
  183.4 60.6 %all-to-all-start.1 = ((f32[4,5,128,256]{3,0,1,2:T(4,128)}), f32[4,5,128,256]{3,0,1,2:T(4,128)S(1)}, u32[]{:S(2)}, u32[]{:S(2)}) async-start(f32[4,5,128,256]{3,0,1,2:T(4,128)} %copy.141), calls=%async_computation.1 | async-start | bytes 5242880 | tf_op jit(solution)/shard_map/all_to_all | solution.py:16
  244.0 35.4 %all-to-all-done.1 = f32[4,5,128,256]{3,0,1,2:T(4,128)S(1)} async-done(((f32[4,5,128,256]{3,0,1,2:T(4,128)}), f32[4,5,128,256]{3,0,1,2:T(4,128)S(1)}, u32[]{:S(2)}, u32[]{:S(2)}) %all-to-all-start.1) | async-done | bytes 2621472 | tf_op jit(solution)/shard_map/all_to_all | solution.py:16
  279.4 1.9 copy.142
  281.4 2.9 reshape.27
  284.3 2.5 copy.143
  286.8 4.8 %all-gather.2.cloned.1.call-done = f32[2048,512]{1,0:T(8,128)} async-done(((f32[256,512]{1,0:T(8,128)}), f32[2048,512]{1,0:T(8,128)}) %all-gather.2.cloned.1.call-update) | async-done | bytes 4194320 | tf_op jit(solution)/shard_map/all_gather | solution.py:75
  291.6 4.4 %fusion.8 = f32[512,6,256]{0,2,1:T(8,128)S(1)} fusion(f32[8,6,256,256]{3,2,1,0:T(8,128)} %param.4, f32[2048,512]{1,0:T(8,128)} %all-gather.2.cloned.1.call-done), kind=kOutput, calls=%fused_computation.10 | convolution fusion | flops 2415919104 | bytes 5242880 | tf_op jit(solution)/shard_map/jrc,cs->jrs/dot_general | solution.py:79
  296.1 4.1 %fusion.10 = f32[512,6,256]{0,2,1:T(8,128)S(1)} fusion(f32[8,6,256,256]{3,2,1,0:T(8,128)} %param.4, f32[2048,512]{1,0:T(8,128)S(1)} %copy-done.3), kind=kOutput, calls=%fused_computation.12 | convolution fusion | flops 2415919104 | bytes 5242880 | tf_op jit(solution)/shard_map/jrc,cs->jrs/dot_general | solution.py:79
  300.2 4.1 %fusion.12 = f32[512,6,256]{0,2,1:T(8,128)S(1)} fusion(f32[8,6,256,256]{3,2,1,0:T(8,128)} %param.4, f32[2048,512]{1,0:T(8,128)S(1)} %copy-done.3), kind=kOutput, calls=%fused_computation.14 | convolution fusion | flops 2415919104 | bytes 5242880 | tf_op jit(solution)/shard_map/jrc,cs->jrs/dot_general | solution.py:79
  304.3 4.1 %fusion.14 = f32[512,6,256]{0,2,1:T(8,128)S(1)} fusion(f32[8,6,256,256]{3,2,1,0:T(8,128)} %param.4, f32[2048,512]{1,0:T(8,128)S(1)} %copy-done.3), kind=kOutput, calls=%fused_computation.16 | convolution fusion | flops 2415919104 | bytes 5242880 | tf_op jit(solution)/shard_map/jrc,cs->jrs/dot_general | solution.py:79
  308.5 4.3 %fusion.16 = f32[512,6,256]{0,2,1:T(8,128)S(1)} fusion(f32[8,6,256,256]{3,2,1,0:T(8,128)} %param.4, f32[2048,512]{1,0:T(8,128)S(1)} %copy-done.3), kind=kOutput, calls=%fused_computation.18 | convolution fusion | flops 2415919104 | bytes 5242880 | tf_op jit(solution)/shard_map/jrc,cs->jrs/dot_general | solution.py:79
  312.8 4.1 %fusion.18 = f32[512,6,256]{0,2,1:T(8,128)S(1)} fusion(f32[8,6,256,256]{3,2,1,0:T(8,128)} %param.4, f32[2048,512]{1,0:T(8,128)S(1)} %copy-done.3), kind=kOutput, calls=%fused_computation.20 | convolution fusion | flops 2415919104 | bytes 5242880 | tf_op jit(solution)/shard_map/jrc,cs->jrs/dot_general | solution.py:79
  316.9 5.7 %fusion.20 = f32[512,6,256]{0,2,1:T(8,128)} fusion(f32[8,6,256,256]{3,2,1,0:T(8,128)} %param.4, f32[2048,512]{1,0:T(8,128)S(1)} %copy-done.3), kind=kOutput, calls=%fused_computation.22 | convolution fusion | flops 2415919104 | bytes 5242880 | tf_op jit(solution)/shard_map/jrc,cs->jrs/dot_general | solution.py:79
  322.7 7.6 %fusion.6 = f32[6,256,512]{2,1,0:T(8,128)S(1)} fusion(f32[5,256,512]{2,1,0:T(8,128)} %bitcast.288, f32[1,256,512]{2,1,0:T(8,128)S(1)} %bitcast.284, f32[512,6,256]{0,2,1:T(8,128)S(1)} %fusion.8, f32[512,6,256]{0,2,1:T(8,128)S(1)} %fusion.10, f32[512,6,256]{0,2,1:T(8,128)S(1)} %fusion.12, f32[512,6,256]{0,2,1:T(8,128)S(1)} %fusion.14, ...), kind=kOutput, calls=%fused_computation.7 | convolution fusion | flops 2422996992 | bytes 30408704 | tf_op jit(solution)/shard_map/jrc,cs->jrs/dot_general | solution.py:79
  330.5 0.8 copy-done.2
  331.3 2.0 pad_maximum_fusion
  (72 shorter events, 10.9 us)
Async XLA Ops:
  9.0 1.7 copy-start
  11.9 24.8 %all-to-all-start = ((f32[4,1,128,256]{3,0,1,2:T(4,128)}), f32[4,1,128,256]{3,0,1,2:T(4,128)S(1)}, u32[]{:S(2)}, u32[]{:S(2)}) async-start(f32[4,1,128,256]{3,0,1,2:T(4,128)} %copy.115), calls=%async_computation | async-start | bytes 1048576 | tf_op jit(solution)/shard_map/all_to_all | solution.py:16
  23.4 268.2 %all-gather.2.cloned.1.call-start = ((), (), s32[]{:S(2)}) async-start(), calls=%async_computation.2 | async-start | bytes 4718592 | tf_op jit(solution)/shard_map/all_gather | solution.py:75
  39.6 0.7 collective-permute-start
  44.3 2.3 copy-start.4
  44.3 2.3 collective-permute-start.3
  45.1 4.1 %collective-permute-start.1 = (f32[256,512]{1,0:T(8,128)S(1)}, f32[256,512]{1,0:T(8,128)}, u32[]{:S(2)}, u32[]{:S(2)}) collective-permute-start(f32[256,512]{1,0:T(8,128)S(1)} %add.64), channel_id=1, source_target_pairs={{0,2},{1,3}} | collective-permute-start | bytes 1572872 | tf_op jit(solution)/shard_map/ppermute | solution.py:56
  47.7 10.4 %collective-permute-start.4 = (f32[256,512]{1,0:T(8,128)S(1)}, f32[256,512]{1,0:T(8,128)}, u32[]{:S(2)}, u32[]{:S(2)}) collective-permute-start(f32[256,512]{1,0:T(8,128)S(1)} %add.67), channel_id=1, source_target_pairs={{1,3},{2,4}} | collective-permute-start | bytes 1572872 | tf_op jit(solution)/shard_map/ppermute | solution.py:56
  56.0 5.7 %collective-permute-start.6 = (f32[256,512]{1,0:T(8,128)S(1)}, f32[256,512]{1,0:T(8,128)}, u32[]{:S(2)}, u32[]{:S(2)}) collective-permute-start(f32[256,512]{1,0:T(8,128)S(1)} %get-tuple-element.7), channel_id=1, source_target_pairs={{2,3}} | collective-permute-start | bytes 1572872 | tf_op jit(solution)/shard_map/ppermute | solution.py:56
  57.4 10.0 %collective-permute-start.2 = (f32[256,512]{1,0:T(8,128)S(1)}, f32[256,512]{1,0:T(8,128)S(1)}, u32[]{:S(2)}, u32[]{:S(2)}) collective-permute-start(f32[256,512]{1,0:T(8,128)S(1)} %add.65), channel_id=1, source_target_pairs={{0,4},{1,5},{2,6},{3,7}} | collective-permute-start | bytes 1572872 | tf_op jit(solution)/shard_map/ppermute | solution.py:56
  59.2 6.1 %copy-start.5 = (f32[8,256,256]{2,1,0:T(8,128)S(1)}, f32[8,256,256]{2,1,0:T(8,128)}, u32[]{:S(2)}) copy-start(f32[8,256,256]{2,1,0:T(8,128)} %param.5) | copy-start | bytes 6291460
  59.3 28.6 %collective-permute-start.5 = (f32[256,512]{1,0:T(8,128)S(1)}, f32[256,512]{1,0:T(8,128)S(1)}, u32[]{:S(2)}, u32[]{:S(2)}) collective-permute-start(f32[256,512]{1,0:T(8,128)S(1)} %add.68), channel_id=1, source_target_pairs={{1,5},{2,6},{3,7}} | collective-permute-start | bytes 1572872 | tf_op jit(solution)/shard_map/ppermute | solution.py:56
  62.8 6.3 %collective-permute-start.7 = (f32[256,512]{1,0:T(8,128)S(1)}, f32[256,512]{1,0:T(8,128)S(1)}, u32[]{:S(2)}, u32[]{:S(2)}) collective-permute-start(f32[256,512]{1,0:T(8,128)S(1)} %add.70), channel_id=1, source_target_pairs={{2,4},{3,5}} | collective-permute-start | bytes 1572872 | tf_op jit(solution)/shard_map/ppermute | solution.py:56
  66.8 16.5 %collective-permute-start.9 = (f32[256,512]{1,0:T(8,128)S(1)}, f32[256,512]{1,0:T(8,128)S(1)}, u32[]{:S(2)}, u32[]{:S(2)}) collective-permute-start(f32[256,512]{1,0:T(8,128)S(1)} %get-tuple-element.9), channel_id=1, source_target_pairs={{3,4}} | collective-permute-start | bytes 1572872 | tf_op jit(solution)/shard_map/ppermute | solution.py:56
  69.2 26.5 %collective-permute-start.8 = (f32[256,512]{1,0:T(8,128)S(1)}, f32[256,512]{1,0:T(8,128)S(1)}, u32[]{:S(2)}, u32[]{:S(2)}) collective-permute-start(f32[256,512]{1,0:T(8,128)S(1)} %add.71), channel_id=1, source_target_pairs={{2,6},{3,7}} | collective-permute-start | bytes 1572872 | tf_op jit(solution)/shard_map/ppermute | solution.py:56
  83.4 6.1 %collective-permute-start.10 = (f32[256,512]{1,0:T(8,128)S(1)}, f32[256,512]{1,0:T(8,128)S(1)}, u32[]{:S(2)}, u32[]{:S(2)}) collective-permute-start(f32[256,512]{1,0:T(8,128)S(1)} %add.73), channel_id=1, source_target_pairs={{3,5},{4,6}} | collective-permute-start | bytes 1572872 | tf_op jit(solution)/shard_map/ppermute | solution.py:56
  87.1 4.0 %collective-permute-start.12 = (f32[256,512]{1,0:T(8,128)S(1)}, f32[256,512]{1,0:T(8,128)S(1)}, u32[]{:S(2)}, u32[]{:S(2)}) collective-permute-start(f32[256,512]{1,0:T(8,128)S(1)} %get-tuple-element.11), channel_id=1, source_target_pairs={{4,5}} | collective-permute-start | bytes 1572872 | tf_op jit(solution)/shard_map/ppermute | solution.py:56
  91.3 6.1 %collective-permute-start.14 = (f32[256,512]{1,0:T(8,128)S(1)}, f32[256,512]{1,0:T(8,128)S(1)}, u32[]{:S(2)}, u32[]{:S(2)}) collective-permute-start(f32[256,512]{1,0:T(8,128)S(1)} %add.76), channel_id=1, source_target_pairs={{4,6},{5,7}} | collective-permute-start | bytes 1572872 | tf_op jit(solution)/shard_map/ppermute | solution.py:56
  95.0 4.0 %collective-permute-start.13 = (f32[256,512]{1,0:T(8,128)S(1)}, f32[256,512]{1,0:T(8,128)S(1)}, u32[]{:S(2)}, u32[]{:S(2)}) collective-permute-start(f32[256,512]{1,0:T(8,128)S(1)} %get-tuple-element.13), channel_id=1, source_target_pairs={{5,6}} | collective-permute-start | bytes 1572872 | tf_op jit(solution)/shard_map/ppermute | solution.py:56
  102.2 3.7 %collective-permute-start.15 = (f32[256,512]{1,0:T(8,128)}, f32[256,512]{1,0:T(8,128)}, u32[]{:S(2)}, u32[]{:S(2)}) collective-permute-start(f32[256,512]{1,0:T(8,128)} %get-tuple-element.15), channel_id=1, source_target_pairs={{6,7}} | collective-permute-start | bytes 1572872 | tf_op jit(solution)/shard_map/ppermute | solution.py:56
  103.8 4.0 %collective-permute-start.16 = (f32[256,512]{1,0:T(8,128)S(1)}, f32[256,512]{1,0:T(8,128)}, u32[]{:S(2)}, u32[]{:S(2)}) collective-permute-start(f32[256,512]{1,0:T(8,128)S(1)} %add.78), channel_id=1, source_target_pairs={{5,7}} | collective-permute-start | bytes 1572872 | tf_op jit(solution)/shard_map/ppermute | solution.py:56
  105.3 4.5 %collective-permute-start.11 = (f32[256,512]{1,0:T(8,128)S(1)}, f32[256,512]{1,0:T(8,128)S(1)}, u32[]{:S(2)}, u32[]{:S(2)}) collective-permute-start(f32[256,512]{1,0:T(8,128)S(1)} %add.74), channel_id=1, source_target_pairs={{3,7}} | collective-permute-start | bytes 1572872 | tf_op jit(solution)/shard_map/ppermute | solution.py:56
  107.7 3.7 %copy-start.6 = (f32[256,512]{1,0:T(8,128)S(1)}, f32[256,512]{1,0:T(8,128)}, u32[]{:S(2)}) copy-start(f32[256,512]{1,0:T(8,128)} %get-tuple-element.6) | copy-start | bytes 1572868
  107.7 3.7 %copy-start.7 = (f32[256,512]{1,0:T(8,128)S(1)}, f32[256,512]{1,0:T(8,128)}, u32[]{:S(2)}) copy-start(f32[256,512]{1,0:T(8,128)} %get-tuple-element.8) | copy-start | bytes 1572868
  107.7 3.7 %copy-start.8 = (f32[256,512]{1,0:T(8,128)S(1)}, f32[256,512]{1,0:T(8,128)}, u32[]{:S(2)}) copy-start(f32[256,512]{1,0:T(8,128)} %get-tuple-element.10) | copy-start | bytes 1572868
  107.7 3.7 %copy-start.9 = (f32[256,512]{1,0:T(8,128)S(1)}, f32[256,512]{1,0:T(8,128)}, u32[]{:S(2)}) copy-start(f32[256,512]{1,0:T(8,128)} %get-tuple-element.12) | copy-start | bytes 1572868
  107.8 3.7 %copy-start.10 = (f32[256,512]{1,0:T(8,128)S(1)}, f32[256,512]{1,0:T(8,128)}, u32[]{:S(2)}) copy-start(f32[256,512]{1,0:T(8,128)} %get-tuple-element.14) | copy-start | bytes 1572868
  107.8 3.7 %copy-start.11 = (f32[256,512]{1,0:T(8,128)S(1)}, f32[256,512]{1,0:T(8,128)}, u32[]{:S(2)}) copy-start(f32[256,512]{1,0:T(8,128)} %get-tuple-element.16) | copy-start | bytes 1572868
  113.1 3.2 copy-start.1
  113.1 0.7 collective-permute-start.17
  113.9 0.7 collective-permute-start.18
  114.7 0.7 collective-permute-start.19
  115.5 0.7 collective-permute-start.20
  116.3 61.0 %collective-permute-start.21 = (f32[256,512]{1,0:T(8,128)S(1)}, f32[256,512]{1,0:T(8,128)S(1)}, u32[]{:S(2)}, u32[]{:S(2)}) collective-permute-start(f32[256,512]{1,0:T(8,128)S(1)} %add.82), channel_id=1, source_target_pairs={{0,8},{1,9},{2,10},{3,11},{4,12},{5,13},{6,14},{7,15},{17,25},{18,... | collective-permute-start | bytes 1572872 | tf_op jit(solution)/shard_map/ppermute | solution.py:73
  183.4 96.1 %all-to-all-start.1 = ((f32[4,5,128,256]{3,0,1,2:T(4,128)}), f32[4,5,128,256]{3,0,1,2:T(4,128)S(1)}, u32[]{:S(2)}, u32[]{:S(2)}) async-start(f32[4,5,128,256]{3,0,1,2:T(4,128)} %copy.141), calls=%async_computation.1 | async-start | bytes 5242880 | tf_op jit(solution)/shard_map/all_to_all | solution.py:16
  291.6 4.4 %copy-start.3 = (f32[2048,512]{1,0:T(8,128)S(1)}, f32[2048,512]{1,0:T(8,128)}, u32[]{:S(2)}) copy-start(f32[2048,512]{1,0:T(8,128)} %all-gather.2.cloned.1.call-done) | copy-start | bytes 12582916
  330.2 1.0 copy-start.2
Sparse Core Ops, SparseCore 0:
  178.4 113.1 all-gather.1
where the time goes:
time: 344 us; the launch traced here: 340 us
  waiting for transfers between devices  113 us (33%)
  starting transfers between devices  104 us (30%)
  matrix products  80.5 us (23%)
  local copies, waits for them, and re-layouts  20.2 us (6%)
  between operations  14.4 us (4%)
  other arithmetic  8.31 us (2%)
    all_to_all x2, starting transfers between devices, transpose_in(): lax.all_to_all(pieces, AXES, split_axis=2, concat_axis=0, tiled=True)  72.1 us
    ppermute x4, waiting for transfers between devices, per_device(): spread = spread + lax.ppermute(spread, AXES, pairs)  59.7 us
    all_to_all x2, waiting for transfers between devices, transpose_in(): lax.all_to_all(pieces, AXES, split_axis=2, concat_axis=0, tiled=True)  48.7 us
    dot_general x25, matrix products, mm(): return jnp.dot(a, b, precision=HI, preferred_element_type=jnp.float32)  42 us
    dot_general x8, matrix products, per_device(): jnp.einsum('jrc,cs->jrs', panels[section], whole[section * width_block:(s...  38.6 us
    ppermute x17, starting transfers between devices, per_device(): got = lax.ppermute(buf, AXES, pairs)  27.5 us
  transfers between devices with their start and end apart: 25, of which 4 were waited for; matrix products, arithmetic and copies ran while one was open for 14% of the time, Pallas kernels for 0%

commit v1 on v0

--- a/solution.py
+++ b/solution.py
@@ -61,18 +61,27 @@
         if section - 3 >= 0:
             settled = settled - mm(low[section - 3], after[section - 3][2])
 
-    moved = lax.ppermute(own, AXES, [(k, k * cols + k) for k in range(1, sections)])
-    spread = jnp.where(device == 0, own, moved)
-    level = 1
-    while level < cols:
+    rows = lax.axis_size("row")
+    halves = cols // sections
+    cut = width_block // rows
+    down = lax.all_to_all(own.reshape(rows, cut, -1), "row", 0, 0, tiled=True)[0]
+    part = cut // halves
+    pieces_out = down.reshape(halves, part, -1)
+    mine = pieces_out[0]
+    for h in range(1, halves):
         pairs = [
-            (r * cols + (r + q) % cols, r * cols + (r + q + level) % cols)
-            for r in range(sections)
-            for q in range(level)
+            (r * cols + k, r * cols + k + h * sections)
+            for r in range(rows)
+            for k in range(sections)
         ]
-        spread = spread + lax.ppermute(spread, AXES, pairs)
-        level *= 2
-    whole = lax.all_gather(spread, "row", tiled=True)
+        got = lax.ppermute(pieces_out[h], AXES, pairs)
+        mine = jnp.where(col // sections == h, got, mine)
+    gathered = lax.all_gather(mine, AXES, tiled=True)
+    whole = (
+        gathered.reshape(rows, halves, sections, part, -1)
+        .transpose(2, 0, 1, 3, 4)
+        .reshape(sections * width_block, -1)
+    )
 
     update = jnp.concatenate([lead[None], rest], axis=0)
     for section in range(sections):

time: 344 us -> 328 us (0.953)
  waiting for transfers between devices: 113 us -> 76.3 us
  blocking collectives: 0 us -> 26.2 us
  starting transfers between devices: 104 us -> 92.1 us
  local copies, waits for them, and re-layouts: 20.2 us -> 25.3 us
    ppermute x5 -> x1, waiting for transfers between devices: 59.7 us -> 0.99 us  [per_device(): got = lax.ppermute(pieces_out[h], AXES, pairs)]
    all_to_all x0 -> x1, blocking collectives: none -> 26.2 us  [per_device(): lax.all_to_all(own.reshape(rows, cut, -1), 'row', 0, 0, tiled=True)[0]]
    all_gather x1, waiting for transfers between devices: 4.78 us -> 26.3 us  [per_device(): gathered = lax.all_gather(mine, AXES, tiled=True)]
    all_to_all x2, starting transfers between devices: 72.1 us -> 63.8 us  [transpose_in(): lax.all_to_all(pieces, AXES, split_axis=2, concat_axis=0, tiled=True)]
    unnamed x25 -> x31, local copies, waits for them, and re-layouts: 4.99 us -> 6.93 us
  transfers between devices with their start and end apart: 25 -> 21, of which waited for: 4 -> 4; matrix products, arithmetic and copies ran while one was open for 14% -> 15% of each run, Pallas kernels for 0% -> 0%
where the time goes in v1:
time: 328 us; the launch traced here: 324 us
  starting transfers between devices  92.1 us (28%)
  matrix products  81.8 us (25%)
  waiting for transfers between devices  76.3 us (23%)
  blocking collectives  26.2 us (8%)
  local copies, waits for them, and re-layouts  25.3 us (8%)
  between operations  14.3 us (4%)
  other arithmetic  7.74 us (2%)
    all_to_all x2, starting transfers between devices, transpose_in(): lax.all_to_all(pieces, AXES, split_axis=2, concat_axis=0, tiled=True)  63.8 us
    all_to_all x2, waiting for transfers between devices, transpose_in(): lax.all_to_all(pieces, AXES, split_axis=2, concat_axis=0, tiled=True)  48.9 us
    dot_general x25, matrix products, mm(): return jnp.dot(a, b, precision=HI, preferred_element_type=jnp.float32)  42 us
    dot_general x8, matrix products, per_device(): jnp.einsum('jrc,cs->jrs', panels[section], whole[section * width_block:(s...  39.8 us
    ppermute x17, starting transfers between devices, per_device(): got = lax.ppermute(buf, AXES, pairs)  27 us
    all_gather x1, waiting for transfers between devices, per_device(): gathered = lax.all_gather(mine, AXES, tiled=True)  26.3 us
    all_to_all x1, blocking collectives, per_device(): lax.all_to_all(own.reshape(rows, cut, -1), 'row', 0, 0, tiled=True)[0]  26.2 us
    unnamed x31, local copies, waits for them, and re-layouts  6.93 us
  transfers between devices with their start and end apart: 21, of which 4 were waited for; matrix products, arithmetic and copies ran while one was open for 15% of the time, Pallas kernels for 0%

profile of v1, /device:TPU:1, one launch (start us, length us, event | category | flops | bytes accessed | tf_op | source)
XLA Modules:
  0.0 323.7 jit_solution(3016711907551453104)
XLA Ops:
  6.5 2.5 copy.203
  9.0 1.7 copy-done.1
  10.7 1.1 copy.124
  11.9 11.5 %all-to-all-start = ((f32[4,1,128,256]{3,0,1,2:T(4,128)}), f32[4,1,128,256]{3,0,1,2:T(4,128)S(1)}, u32[]{:S(2)}, u32[]{:S(2)}) async-start(f32[4,1,128,256]{3,0,1,2:T(4,128)} %copy.124), calls=%async_computation | async-start | bytes 1048576 | tf_op jit(solution)/shard_map/all_to_all | solution.py:16
  23.4 13.3 %all-to-all-done = f32[4,1,128,256]{3,0,1,2:T(4,128)S(1)} async-done(((f32[4,1,128,256]{3,0,1,2:T(4,128)}), f32[4,1,128,256]{3,0,1,2:T(4,128)S(1)}, u32[]{:S(2)}, u32[]{:S(2)}) %all-to-all-start) | async-done | bytes 524320 | tf_op jit(solution)/shard_map/all_to_all | solution.py:16
  38.0 1.6 convolution_select_fusion
  40.3 1.6 fusion.32
  41.9 2.4 broadcast_select_fusion.5
  45.1 1.5 collective-permute-start.1
  46.6 1.1 add.56
  47.7 1.5 collective-permute-start.4
  49.2 1.1 add.54
  50.3 1.6 convolution_bitcast_fusion.18
  51.9 1.6 fusion.35
  53.5 2.4 broadcast_select_fusion.4
  56.0 1.5 collective-permute-start.6
  58.1 1.1 add.57
  59.3 0.8 collective-permute-start.5
  60.1 1.6 convolution_bitcast_fusion.14
  61.7 1.1 add.59
  63.5 1.8 fusion.39
  65.3 1.5 broadcast_select_fusion.3
  67.5 1.6 fusion.31
  69.2 12.0 %collective-permute-start.8 = (f32[256,512]{1,0:T(8,128)S(1)}, f32[256,512]{1,0:T(8,128)S(1)}, u32[]{:S(2)}, u32[]{:S(2)}) collective-permute-start(f32[256,512]{1,0:T(8,128)S(1)} %add.60), channel_id=1, source_target_pairs={{2,6},{3,7}} | collective-permute-start | bytes 1572872 | tf_op jit(solution)/shard_map/ppermute | solution.py:56
  81.2 1.6 convolution_bitcast_fusion.10
  83.6 1.6 fusion.46
  85.2 1.4 broadcast_select_fusion.2
  87.3 1.6 fusion.33
  89.1 1.6 convolution_bitcast_fusion.7
  91.5 1.6 fusion.49
  93.1 1.4 broadcast_select_fusion.1
  95.2 1.6 fusion.36
  96.8 1.6 convolution_bitcast_fusion.4
  98.5 1.6 fusion.52
  100.1 1.6 broadcast_select_fusion
  101.7 1.5 collective-permute-start.15
  103.3 1.5 collective-permute-start.16
  105.4 1.8 convolution_bitcast_fusion.2
  107.3 1.9 convolution_bitcast_fusion.1
  109.2 1.7 fusion.43
  110.9 1.7 fusion.30
  112.6 0.8 copy-done.2
  113.4 26.2 %all_to_all.35 = f32[8,32,512]{2,1,0:T(8,128)S(1)} all-to-all(f32[8,32,512]{2,1,0:T(8,128)S(1)} %bitcast.309), channel_id=1, replica_groups=mesh['row'=8,'col'=16] {'row'}, dimensions={0} | all-to-all | bytes 1048576 | tf_op jit(solution)/shard_map/all_to_all | solution.py:67
  139.6 1.3 collective-permute-start.17
  140.9 1.0 collective-permute-done.17
  142.5 1.9 slice.216
  144.5 3.2 copy.143
  147.6 52.3 %all-to-all-start.1 = ((f32[4,5,128,256]{3,0,1,2:T(4,128)}), f32[4,5,128,256]{3,0,1,2:T(4,128)S(1)}, u32[]{:S(2)}, u32[]{:S(2)}) async-start(f32[4,5,128,256]{3,0,1,2:T(4,128)} %copy.143), calls=%async_computation.1 | async-start | bytes 5242880 | tf_op jit(solution)/shard_map/all_to_all | solution.py:16
  199.9 35.7 %all-to-all-done.1 = f32[4,5,128,256]{3,0,1,2:T(4,128)S(1)} async-done(((f32[4,5,128,256]{3,0,1,2:T(4,128)}), f32[4,5,128,256]{3,0,1,2:T(4,128)S(1)}, u32[]{:S(2)}, u32[]{:S(2)}) %all-to-all-start.1) | async-done | bytes 2621472 | tf_op jit(solution)/shard_map/all_to_all | solution.py:16
  235.6 1.9 copy.144
  237.5 2.8 reshape.46
  240.4 2.5 copy.145
  242.9 26.3 %all-gather.2.cloned.1.call-done = f32[2048,512]{1,0:T(8,128)} async-done(((f32[16,512]{1,0:T(8,128)}), f32[2048,512]{1,0:T(8,128)}) %all-gather.2.cloned.1.call-update) | async-done | bytes 4194320 | tf_op jit(solution)/shard_map/all_gather | solution.py:79
  269.2 2.8 fusion.113
  272.0 4.9 %fusion.8 = f32[512,6,256]{0,2,1:T(8,128)S(1)} fusion(f32[256,512,1]{1,0,2:T(8,128)S(1)} %bitcast.318, f32[8,6,256,256]{3,2,1,0:T(8,128)} %param.4), kind=kOutput, calls=%fused_computation.10 | convolution fusion | flops 2415919104 | bytes 5242880 | tf_op jit(solution)/shard_map/jrc,cs->jrs/dot_general | solution.py:88
  276.9 4.3 %fusion.10 = f32[512,6,256]{0,2,1:T(8,128)S(1)} fusion(f32[256,512,1]{1,0,2:T(8,128)S(1)} %bitcast.317, f32[8,6,256,256]{3,2,1,0:T(8,128)} %param.4), kind=kOutput, calls=%fused_computation.12 | convolution fusion | flops 2415919104 | bytes 5242880 | tf_op jit(solution)/shard_map/jrc,cs->jrs/dot_general | solution.py:88
  281.2 4.1 %fusion.12 = f32[512,6,256]{0,2,1:T(8,128)S(1)} fusion(f32[256,512,1]{1,0,2:T(8,128)S(1)} %bitcast.316, f32[8,6,256,256]{3,2,1,0:T(8,128)} %param.4), kind=kOutput, calls=%fused_computation.14 | convolution fusion | flops 2415919104 | bytes 5242880 | tf_op jit(solution)/shard_map/jrc,cs->jrs/dot_general | solution.py:88
  285.3 4.4 %fusion.14 = f32[512,6,256]{0,2,1:T(8,128)} fusion(f32[256,512,1]{1,0,2:T(8,128)S(1)} %bitcast.315, f32[8,6,256,256]{3,2,1,0:T(8,128)S(1)} %bitcast.304), kind=kOutput, calls=%fused_computation.16 | convolution fusion | flops 2415919104 | bytes 5242880 | tf_op jit(solution)/shard_map/jrc,cs->jrs/dot_general | solution.py:88
  289.7 4.5 %fusion.16 = f32[512,6,256]{0,2,1:T(8,128)} fusion(f32[256,512,1]{1,0,2:T(8,128)S(1)} %bitcast.314, f32[8,6,256,256]{3,2,1,0:T(8,128)S(1)} %bitcast.304), kind=kOutput, calls=%fused_computation.18 | convolution fusion | flops 2415919104 | bytes 5242880 | tf_op jit(solution)/shard_map/jrc,cs->jrs/dot_general | solution.py:88
  294.2 4.4 %fusion.18 = f32[512,6,256]{0,2,1:T(8,128)} fusion(f32[256,512,1]{1,0,2:T(8,128)S(1)} %bitcast.313, f32[8,6,256,256]{3,2,1,0:T(8,128)S(1)} %bitcast.304), kind=kOutput, calls=%fused_computation.20 | convolution fusion | flops 2415919104 | bytes 5242880 | tf_op jit(solution)/shard_map/jrc,cs->jrs/dot_general | solution.py:88
  298.6 4.4 %fusion.20 = f32[512,6,256]{0,2,1:T(8,128)} fusion(f32[256,512,1]{1,0,2:T(8,128)S(1)} %bitcast.312, f32[8,6,256,256]{3,2,1,0:T(8,128)S(1)} %bitcast.304), kind=kOutput, calls=%fused_computation.22 | convolution fusion | flops 2415919104 | bytes 5242880 | tf_op jit(solution)/shard_map/jrc,cs->jrs/dot_general | solution.py:88
  303.0 8.9 %fusion.6 = f32[6,256,512]{2,1,0:T(8,128)} fusion(f32[5,256,512]{2,1,0:T(8,128)} %bitcast.308, f32[1,256,512]{2,1,0:T(8,128)S(1)} %bitcast.302, f32[512,6,256]{0,2,1:T(8,128)S(1)} %fusion.8, f32[512,6,256]{0,2,1:T(8,128)S(1)} %fusion.10, f32[512,6,256]{0,2,1:T(8,128)S(1)} %fusion.12, f32[512,6,256]{0,2,1:T(8,128)} %fusion.14, f32[512,6,256]{0,2,1:T(8,128)} %fusion.16, ...), kind=kOutput, calls=%fused_computation.7 | convolution fusion | flops 2422996992 | bytes 30408704 | tf_op jit(solution)/shard_map/jrc,cs->jrs/dot_general | solution.py:88
  311.9 1.9 copy-done
  314.6 2.1 pad_maximum_fusion
  (71 shorter events, 10.3 us)
Async XLA Ops:
  9.0 1.7 copy-start.1
  11.9 24.8 %all-to-all-start = ((f32[4,1,128,256]{3,0,1,2:T(4,128)}), f32[4,1,128,256]{3,0,1,2:T(4,128)S(1)}, u32[]{:S(2)}, u32[]{:S(2)}) async-start(f32[4,1,128,256]{3,0,1,2:T(4,128)} %copy.124), calls=%async_computation | async-start | bytes 1048576 | tf_op jit(solution)/shard_map/all_to_all | solution.py:16
  23.4 245.8 %all-gather.2.cloned.1.call-start = ((), (), s32[]{:S(2)}) async-start(), calls=%async_computation.3 | async-start | bytes 4227072 | tf_op jit(solution)/shard_map/all_gather | solution.py:79
  39.6 0.7 collective-permute-start
  44.3 2.3 copy-start.4
  44.3 2.3 collective-permute-start.3
  45.1 4.1 %collective-permute-start.1 = (f32[256,512]{1,0:T(8,128)S(1)}, f32[256,512]{1,0:T(8,128)}, u32[]{:S(2)}, u32[]{:S(2)}) collective-permute-start(f32[256,512]{1,0:T(8,128)S(1)} %add.53), channel_id=1, source_target_pairs={{0,2},{1,3}} | collective-permute-start | bytes 1572872 | tf_op jit(solution)/shard_map/ppermute | solution.py:56
  47.7 10.4 %collective-permute-start.4 = (f32[256,512]{1,0:T(8,128)S(1)}, f32[256,512]{1,0:T(8,128)}, u32[]{:S(2)}, u32[]{:S(2)}) collective-permute-start(f32[256,512]{1,0:T(8,128)S(1)} %add.56), channel_id=1, source_target_pairs={{1,3},{2,4}} | collective-permute-start | bytes 1572872 | tf_op jit(solution)/shard_map/ppermute | solution.py:56
  56.0 5.7 %collective-permute-start.6 = (f32[256,512]{1,0:T(8,128)S(1)}, f32[256,512]{1,0:T(8,128)}, u32[]{:S(2)}, u32[]{:S(2)}) collective-permute-start(f32[256,512]{1,0:T(8,128)S(1)} %get-tuple-element.15), channel_id=1, source_target_pairs={{2,3}} | collective-permute-start | bytes 1572872 | tf_op jit(solution)/shard_map/ppermute | solution.py:56
  57.4 10.1 %collective-permute-start.2 = (f32[256,512]{1,0:T(8,128)S(1)}, f32[256,512]{1,0:T(8,128)S(1)}, u32[]{:S(2)}, u32[]{:S(2)}) collective-permute-start(f32[256,512]{1,0:T(8,128)S(1)} %add.54), channel_id=1, source_target_pairs={{0,4},{1,5},{2,6},{3,7}} | collective-permute-start | bytes 1572872 | tf_op jit(solution)/shard_map/ppermute | solution.py:56
  59.2 6.1 %copy-start.5 = (f32[8,256,256]{2,1,0:T(8,128)S(1)}, f32[8,256,256]{2,1,0:T(8,128)}, u32[]{:S(2)}) copy-start(f32[8,256,256]{2,1,0:T(8,128)} %param.5) | copy-start | bytes 6291460
  59.3 28.1 %collective-permute-start.5 = (f32[256,512]{1,0:T(8,128)S(1)}, f32[256,512]{1,0:T(8,128)S(1)}, u32[]{:S(2)}, u32[]{:S(2)}) collective-permute-start(f32[256,512]{1,0:T(8,128)S(1)} %add.57), channel_id=1, source_target_pairs={{1,5},{2,6},{3,7}} | collective-permute-start | bytes 1572872 | tf_op jit(solution)/shard_map/ppermute | solution.py:56
  62.8 6.3 %collective-permute-start.7 = (f32[256,512]{1,0:T(8,128)S(1)}, f32[256,512]{1,0:T(8,128)S(1)}, u32[]{:S(2)}, u32[]{:S(2)}) collective-permute-start(f32[256,512]{1,0:T(8,128)S(1)} %add.59), channel_id=1, source_target_pairs={{2,4},{3,5}} | collective-permute-start | bytes 1572872 | tf_op jit(solution)/shard_map/ppermute | solution.py:56
  66.8 16.0 %collective-permute-start.9 = (f32[256,512]{1,0:T(8,128)S(1)}, f32[256,512]{1,0:T(8,128)S(1)}, u32[]{:S(2)}, u32[]{:S(2)}) collective-permute-start(f32[256,512]{1,0:T(8,128)S(1)} %get-tuple-element.17), channel_id=1, source_target_pairs={{3,4}} | collective-permute-start | bytes 1572872 | tf_op jit(solution)/shard_map/ppermute | solution.py:56
  69.2 26.0 %collective-permute-start.8 = (f32[256,512]{1,0:T(8,128)S(1)}, f32[256,512]{1,0:T(8,128)S(1)}, u32[]{:S(2)}, u32[]{:S(2)}) collective-permute-start(f32[256,512]{1,0:T(8,128)S(1)} %add.60), channel_id=1, source_target_pairs={{2,6},{3,7}} | collective-permute-start | bytes 1572872 | tf_op jit(solution)/shard_map/ppermute | solution.py:56
  82.9 6.1 %collective-permute-start.10 = (f32[256,512]{1,0:T(8,128)S(1)}, f32[256,512]{1,0:T(8,128)S(1)}, u32[]{:S(2)}, u32[]{:S(2)}) collective-permute-start(f32[256,512]{1,0:T(8,128)S(1)} %add.62), channel_id=1, source_target_pairs={{3,5},{4,6}} | collective-permute-start | bytes 1572872 | tf_op jit(solution)/shard_map/ppermute | solution.py:56
  86.6 4.0 %collective-permute-start.12 = (f32[256,512]{1,0:T(8,128)S(1)}, f32[256,512]{1,0:T(8,128)S(1)}, u32[]{:S(2)}, u32[]{:S(2)}) collective-permute-start(f32[256,512]{1,0:T(8,128)S(1)} %get-tuple-element.19), channel_id=1, source_target_pairs={{4,5}} | collective-permute-start | bytes 1572872 | tf_op jit(solution)/shard_map/ppermute | solution.py:56
  90.8 6.1 %collective-permute-start.14 = (f32[256,512]{1,0:T(8,128)S(1)}, f32[256,512]{1,0:T(8,128)S(1)}, u32[]{:S(2)}, u32[]{:S(2)}) collective-permute-start(f32[256,512]{1,0:T(8,128)S(1)} %add.65), channel_id=1, source_target_pairs={{4,6},{5,7}} | collective-permute-start | bytes 1572872 | tf_op jit(solution)/shard_map/ppermute | solution.py:56
  94.5 4.0 %collective-permute-start.13 = (f32[256,512]{1,0:T(8,128)S(1)}, f32[256,512]{1,0:T(8,128)S(1)}, u32[]{:S(2)}, u32[]{:S(2)}) collective-permute-start(f32[256,512]{1,0:T(8,128)S(1)} %get-tuple-element.21), channel_id=1, source_target_pairs={{5,6}} | collective-permute-start | bytes 1572872 | tf_op jit(solution)/shard_map/ppermute | solution.py:56
  101.7 3.7 %collective-permute-start.15 = (f32[256,512]{1,0:T(8,128)}, f32[256,512]{1,0:T(8,128)}, u32[]{:S(2)}, u32[]{:S(2)}) collective-permute-start(f32[256,512]{1,0:T(8,128)} %get-tuple-element.23), channel_id=1, source_target_pairs={{6,7}} | collective-permute-start | bytes 1572872 | tf_op jit(solution)/shard_map/ppermute | solution.py:56
  103.3 4.0 %collective-permute-start.16 = (f32[256,512]{1,0:T(8,128)S(1)}, f32[256,512]{1,0:T(8,128)}, u32[]{:S(2)}, u32[]{:S(2)}) collective-permute-start(f32[256,512]{1,0:T(8,128)S(1)} %add.67), channel_id=1, source_target_pairs={{5,7}} | collective-permute-start | bytes 1572872 | tf_op jit(solution)/shard_map/ppermute | solution.py:56
  104.7 4.5 %collective-permute-start.11 = (f32[256,512]{1,0:T(8,128)S(1)}, f32[256,512]{1,0:T(8,128)S(1)}, u32[]{:S(2)}, u32[]{:S(2)}) collective-permute-start(f32[256,512]{1,0:T(8,128)S(1)} %add.63), channel_id=1, source_target_pairs={{3,7}} | collective-permute-start | bytes 1572872 | tf_op jit(solution)/shard_map/ppermute | solution.py:56
  107.2 3.7 %copy-start.6 = (f32[256,512]{1,0:T(8,128)S(1)}, f32[256,512]{1,0:T(8,128)}, u32[]{:S(2)}) copy-start(f32[256,512]{1,0:T(8,128)} %get-tuple-element.14) | copy-start | bytes 1572868
  107.2 3.7 %copy-start.7 = (f32[256,512]{1,0:T(8,128)S(1)}, f32[256,512]{1,0:T(8,128)}, u32[]{:S(2)}) copy-start(f32[256,512]{1,0:T(8,128)} %get-tuple-element.16) | copy-start | bytes 1572868
  107.2 3.7 %copy-start.8 = (f32[256,512]{1,0:T(8,128)S(1)}, f32[256,512]{1,0:T(8,128)}, u32[]{:S(2)}) copy-start(f32[256,512]{1,0:T(8,128)} %get-tuple-element.18) | copy-start | bytes 1572868
  107.2 3.7 %copy-start.9 = (f32[256,512]{1,0:T(8,128)S(1)}, f32[256,512]{1,0:T(8,128)}, u32[]{:S(2)}) copy-start(f32[256,512]{1,0:T(8,128)} %get-tuple-element.20) | copy-start | bytes 1572868
  107.2 3.7 %copy-start.10 = (f32[256,512]{1,0:T(8,128)S(1)}, f32[256,512]{1,0:T(8,128)}, u32[]{:S(2)}) copy-start(f32[256,512]{1,0:T(8,128)} %get-tuple-element.22) | copy-start | bytes 1572868
  107.2 3.7 %copy-start.11 = (f32[256,512]{1,0:T(8,128)S(1)}, f32[256,512]{1,0:T(8,128)}, u32[]{:S(2)}) copy-start(f32[256,512]{1,0:T(8,128)} %get-tuple-element.24) | copy-start | bytes 1572868
  112.6 0.8 copy-start.2
  139.6 2.3 collective-permute-start.17
  147.6 87.9 %all-to-all-start.1 = ((f32[4,5,128,256]{3,0,1,2:T(4,128)}), f32[4,5,128,256]{3,0,1,2:T(4,128)S(1)}, u32[]{:S(2)}, u32[]{:S(2)}) async-start(f32[4,5,128,256]{3,0,1,2:T(4,128)} %copy.143), calls=%async_computation.1 | async-start | bytes 5242880 | tf_op jit(solution)/shard_map/all_to_all | solution.py:16
  269.2 16.1 %slice-start = ((s8[12582912]{0:T(1024)(128)(4,1)}), s8[4194304]{0:T(1024)(128)(4,1)S(1)}, s32[]{:S(2)}) async-start(s8[12582912]{0:T(1024)(128)(4,1)} %bitcast.303), calls=%async_computation.4 | async-start | bytes 8388608
  269.2 16.1 %slice-start.1 = ((s8[12582912]{0:T(1024)(128)(4,1)}), s8[4194304]{0:T(1024)(128)(4,1)S(1)}, s32[]{:S(2)}) async-start(s8[12582912]{0:T(1024)(128)(4,1)} %bitcast.303), calls=%async_computation.5 | async-start | bytes 8388608
  276.9 8.5 %slice-start.2 = ((s8[12582912]{0:T(1024)(128)(4,1)}), s8[4194304]{0:T(1024)(128)(4,1)S(1)}, s32[]{:S(2)}) async-start(s8[12582912]{0:T(1024)(128)(4,1)} %bitcast.303), calls=%async_computation.6 | async-start | bytes 8388608
  303.0 8.9 %copy-start.3 = (f32[256,512]{1,0:T(8,128)S(1)}, f32[256,512]{1,0:T(8,128)}, u32[]{:S(2)}) copy-start(f32[256,512]{1,0:T(8,128)} %copy-done.2) | copy-start | bytes 1572868
  311.9 1.9 copy-start
  311.9 2.7 slice-start.3
Sparse Core Ops, SparseCore 0:
  142.7 126.4 all-gather.1

commit v2 on v1

--- a/solution.py
+++ b/solution.py
@@ -23,8 +23,8 @@
     devices = lax.axis_size(AXES)
     cols = lax.axis_size("col")
     pieces = snapshots.reshape(local_count, blocks, devices, width_block)
-    lead = transpose_in(pieces[:, :1], devices)[0]
-    rest = transpose_in(pieces[:, 1:], devices)
+    remaining = transpose_in(pieces, devices)
+    lead = remaining[0]
     device = lax.axis_index(AXES)
     row = lax.axis_index("row")
     col = lax.axis_index("col")
@@ -76,14 +76,14 @@
         ]
         got = lax.ppermute(pieces_out[h], AXES, pairs)
         mine = jnp.where(col // sections == h, got, mine)
-    gathered = lax.all_gather(mine, AXES, tiled=True)
+    gathered = lax.all_gather(lax.all_gather(mine, "col", tiled=True), "row", tiled=True)
     whole = (
         gathered.reshape(rows, halves, sections, part, -1)
         .transpose(2, 0, 1, 3, 4)
         .reshape(sections * width_block, -1)
     )
 
-    update = jnp.concatenate([lead[None], rest], axis=0)
+    update = remaining
     for section in range(sections):
         update = update - jnp.einsum(
             "jrc,cs->jrs",

time: 328 us -> 347 us (1.058)
  blocking collectives: 26.2 us -> 95.5 us
  starting transfers between devices: 92.1 us -> 30.5 us
  other arithmetic: 7.74 us -> 12.1 us
  matrix products: 81.8 us -> 85.6 us
    all_gather x0 -> x1, blocking collectives: none -> 70.7 us  [per_device(): lax.all_gather(mine, 'col', tiled=True)]
    all_to_all x2 -> x1, starting transfers between devices: 63.8 us -> 11.5 us  [transpose_in(): lax.all_to_all(pieces, AXES, split_axis=2, concat_axis=0, tiled=True)]
    all_gather x1, waiting for transfers between devices: 26.3 us -> 36.7 us  [per_device(): lax.all_gather(lax.all_gather(mine, 'col', tiled=True), 'row', tiled=True)]
    ppermute x17, starting transfers between devices: 27 us -> 17.7 us  [per_device(): got = lax.ppermute(buf, AXES, pairs)]
    all_to_all x2 -> x1, waiting for transfers between devices: 48.9 us -> 41 us  [transpose_in(): lax.all_to_all(pieces, AXES, split_axis=2, concat_axis=0, tiled=True)]
    slice x4 -> x0, local copies, waits for them, and re-layouts: 6.27 us -> none  [the longest x2 5.1 us: per_device(): rest = transpose_in(pieces[:, 1:], devices)]
    add x10, other arithmetic: 4.97 us -> 9.25 us  [per_device(): buf = buf + got]
    reshape x0 -> x1, local copies, waits for them, and re-layouts: none -> 3.69 us  [per_device(): pieces = snapshots.reshape(local_count, blocks, devices, width_block)]
  transfers between devices with their start and end apart: 21 -> 20, of which waited for: 4 -> 3; matrix products, arithmetic and copies ran while one was open for 15% -> 12% of each run, Pallas kernels for 0% -> 0%
where the time goes in v2:
time: 347 us; the launch traced here: 342 us
  blocking collectives  95.5 us (28%)
  matrix products  85.6 us (25%)
  waiting for transfers between devices  78.8 us (23%)
  starting transfers between devices  30.5 us (9%)
  local copies, waits for them, and re-layouts  25.1 us (7%)
  between operations  14.3 us (4%)
  other arithmetic  12.1 us (3%)
    all_gather x1, blocking collectives, per_device(): lax.all_gather(mine, 'col', tiled=True)  70.7 us
    dot_general x25, matrix products, mm(): return jnp.dot(a, b, precision=HI, preferred_element_type=jnp.float32)  44.1 us
    dot_general x8, matrix products, per_device(): jnp.einsum('jrc,cs->jrs', panels[section], whole[section * width_block:(s...  41.5 us
    all_to_all x1, waiting for transfers between devices, transpose_in(): lax.all_to_all(pieces, AXES, split_axis=2, concat_axis=0, tiled=True)  41 us
    all_gather x1, waiting for transfers between devices, per_device(): lax.all_gather(lax.all_gather(mine, 'col', tiled=True), 'row', tiled=True)  36.7 us
    all_to_all x1, blocking collectives, per_device(): lax.all_to_all(own.reshape(rows, cut, -1), 'row', 0, 0, tiled=True)[0]  24.9 us
    ppermute x17, starting transfers between devices, per_device(): got = lax.ppermute(buf, AXES, pairs)  17.7 us
    all_to_all x1, starting transfers between devices, transpose_in(): lax.all_to_all(pieces, AXES, split_axis=2, concat_axis=0, tiled=True)  11.5 us
  transfers between devices with their start and end apart: 20, of which 3 were waited for; matrix products, arithmetic and copies ran while one was open for 12% of the time, Pallas kernels for 0%

profile of v2, /device:TPU:1, one launch (start us, length us, event | category | flops | bytes accessed | tf_op | source)
XLA Modules:
  0.0 342.0 jit_solution(2412296179662480369)
XLA Ops:
  6.5 2.5 copy.195
  9.0 3.7 %copy.118 = f32[4,6,128,256]{3,0,1,2:T(4,128)} copy(f32[4,6,128,256]{3,2,1,0:T(8,128)S(1)} %bitcast.322) | data formatting | bytes 6291456 | tf_op jit(solution)/shard_map/reshape | solution.py:25
  12.7 11.5 %all-to-all-start = ((f32[4,6,128,256]{3,0,1,2:T(4,128)}), f32[4,6,128,256]{3,0,1,2:T(4,128)S(1)}, u32[]{:S(2)}, u32[]{:S(2)}) async-start(f32[4,6,128,256]{3,0,1,2:T(4,128)} %copy.118), calls=%async_computation | async-start | bytes 6291456 | tf_op jit(solution)/shard_map/all_to_all | solution.py:16
  24.3 41.0 %all-to-all-done = f32[4,6,128,256]{3,0,1,2:T(4,128)S(1)} async-done(((f32[4,6,128,256]{3,0,1,2:T(4,128)}), f32[4,6,128,256]{3,0,1,2:T(4,128)S(1)}, u32[]{:S(2)}, u32[]{:S(2)}) %all-to-all-start) | async-done | bytes 3145760 | tf_op jit(solution)/shard_map/all_to_all | solution.py:16
  65.3 2.2 copy.119
  67.5 4.9 %reshape.41 = f32[512,6,256]{2,0,1:T(8,128)} reshape(f32[128,4,6,1,256]{4,1,0,2,3:T(4,128)} %copy.119) | data formatting | bytes 6291456 | tf_op jit(solution)/shard_map/reshape | solution.py:17
  72.4 2.4 copy.120
  74.8 2.4 convolution_select_fusion
  77.1 1.5 collective-permute-start
  78.6 1.8 fusion.25
  80.3 2.6 broadcast_select_fusion.5
  82.9 1.5 collective-permute-start.3
  84.4 2.1 add.53
  86.5 1.4 collective-permute-start.1
  87.9 2.1 add.56
  90.0 1.5 collective-permute-start.4
  91.4 1.3 add.54
  93.5 1.6 convolution_bitcast_fusion.18
  95.9 1.8 fusion.28
  97.7 2.6 broadcast_select_fusion.4
  100.3 1.5 collective-permute-start.6
  101.7 0.8 collective-permute-start.2
  102.6 1.3 add.57
  103.9 0.8 collective-permute-start.5
  104.7 1.6 convolution_bitcast_fusion.14
  106.3 1.3 add.59
  107.7 1.0 collective-permute-start.7
  108.6 1.8 fusion.32
  110.4 1.4 broadcast_select_fusion.3
  112.6 1.6 fusion.24
  115.0 1.6 convolution_bitcast_fusion.10
  117.4 1.6 fusion.39
  119.0 1.4 broadcast_select_fusion.2
  121.2 1.6 fusion.26
  123.7 1.6 convolution_bitcast_fusion.7
  126.1 1.6 fusion.42
  127.7 1.4 broadcast_select_fusion.1
  129.9 1.6 fusion.29
  131.5 1.8 convolution_bitcast_fusion.4
  133.3 1.8 fusion.45
  135.1 1.6 broadcast_select_fusion
  136.8 1.5 collective-permute-start.15
  138.2 0.9 add.67
  139.1 1.5 collective-permute-start.16
  141.4 1.8 convolution_bitcast_fusion.2
  143.2 2.1 convolution_bitcast_fusion.1
  145.3 1.7 fusion.36
  147.1 1.8 fusion.23
  149.7 24.9 %all_to_all.20 = f32[8,32,512]{2,1,0:T(8,128)S(1)} all-to-all(f32[8,32,512]{2,1,0:T(8,128)S(1)} %bitcast.323), channel_id=1, replica_groups=mesh['row'=8,'col'=16] {'row'}, dimensions={0} | all-to-all | bytes 1048576 | tf_op jit(solution)/shard_map/all_to_all | solution.py:67
  175.4 1.3 collective-permute-start.17
  176.7 1.0 collective-permute-done.17
  178.4 70.7 %all_gather.6 = f32[256,512]{1,0:T(8,128)} all-gather(f32[16,512]{1,0:T(8,128)S(1)} %fusion.104), channel_id=1, replica_groups=mesh['row'=8,'col'=16] {'col'}, dimensions={0}, use_global_device_ids=true | all-gather | bytes 557056 | tf_op jit(solution)/shard_map/all_gather | solution.py:79
  249.1 36.7 %all-gather.2.cloned.1.call-done = f32[2048,512]{1,0:T(8,128)} async-done(((f32[256,512]{1,0:T(8,128)}), f32[2048,512]{1,0:T(8,128)}) %all-gather.2.cloned.1.call-update) | async-done | bytes 4194320 | tf_op jit(solution)/shard_map/all_gather | solution.py:79
  285.9 2.8 fusion.105
  288.7 4.9 %fusion.1 = f32[512,6,256]{0,2,1:T(8,128)S(1)} fusion(f32[256,512,1]{1,0,2:T(8,128)S(1)} %bitcast.332, f32[8,6,256,256]{3,2,1,0:T(8,128)} %param.4), kind=kOutput, calls=%fused_computation.10 | convolution fusion | flops 2415919104 | bytes 5242880 | tf_op jit(solution)/shard_map/jrc,cs->jrs/dot_general | solution.py:88
  293.6 4.3 %fusion.3 = f32[512,6,256]{0,2,1:T(8,128)S(1)} fusion(f32[256,512,1]{1,0,2:T(8,128)S(1)} %bitcast.331, f32[8,6,256,256]{3,2,1,0:T(8,128)} %param.4), kind=kOutput, calls=%fused_computation.12 | convolution fusion | flops 2415919104 | bytes 5242880 | tf_op jit(solution)/shard_map/jrc,cs->jrs/dot_general | solution.py:88
  297.8 5.7 %fusion.5 = f32[512,6,256]{0,2,1:T(8,128)} fusion(f32[256,512,1]{1,0,2:T(8,128)S(1)} %bitcast.330, f32[8,6,256,256]{3,2,1,0:T(8,128)} %param.4), kind=kOutput, calls=%fused_computation.14 | convolution fusion | flops 2415919104 | bytes 5242880 | tf_op jit(solution)/shard_map/jrc,cs->jrs/dot_general | solution.py:88
  303.6 4.3 %fusion.7 = f32[512,6,256]{0,2,1:T(8,128)} fusion(f32[256,512,1]{1,0,2:T(8,128)S(1)} %bitcast.329, f32[8,6,256,256]{3,2,1,0:T(8,128)S(1)} %bitcast.320), kind=kOutput, calls=%fused_computation.16 | convolution fusion | flops 2415919104 | bytes 5242880 | tf_op jit(solution)/shard_map/jrc,cs->jrs/dot_general | solution.py:88
  307.9 4.6 %fusion.9 = f32[512,6,256]{0,2,1:T(8,128)} fusion(f32[256,512,1]{1,0,2:T(8,128)S(1)} %bitcast.328, f32[8,6,256,256]{3,2,1,0:T(8,128)S(1)} %bitcast.320), kind=kOutput, calls=%fused_computation.18 | convolution fusion | flops 2415919104 | bytes 5242880 | tf_op jit(solution)/shard_map/jrc,cs->jrs/dot_general | solution.py:88
  312.5 4.4 %fusion.11 = f32[512,6,256]{0,2,1:T(8,128)} fusion(f32[256,512,1]{1,0,2:T(8,128)S(1)} %bitcast.327, f32[8,6,256,256]{3,2,1,0:T(8,128)S(1)} %bitcast.320), kind=kOutput, calls=%fused_computation.20 | convolution fusion | flops 2415919104 | bytes 5242880 | tf_op jit(solution)/shard_map/jrc,cs->jrs/dot_general | solution.py:88
  316.9 4.4 %fusion.13 = f32[512,6,256]{0,2,1:T(8,128)} fusion(f32[256,512,1]{1,0,2:T(8,128)S(1)} %bitcast.326, f32[8,6,256,256]{3,2,1,0:T(8,128)S(1)} %bitcast.320), kind=kOutput, calls=%fused_computation.22 | convolution fusion | flops 2415919104 | bytes 5242880 | tf_op jit(solution)/shard_map/jrc,cs->jrs/dot_general | solution.py:88
  321.4 8.9 %bitcast_subtract_fusion = f32[6,256,512]{2,1,0:T(8,128)} fusion(f32[512,6,256]{0,2,1:T(8,128)S(1)} %fusion.1, f32[512,6,256]{0,2,1:T(8,128)S(1)} %fusion.3, f32[512,6,256]{0,2,1:T(8,128)} %fusion.5, f32[512,6,256]{0,2,1:T(8,128)} %fusion.7, f32[512,6,256]{0,2,1:T(8,128)} %fusion.9, f32[512,6,256]{0,2,1:T(8,128)} %fusion.11, f32[512,6,256]{0,2,1:T(8,128)} %fusion.13, ...), kind=kOutput, calls=%fused_computation.1 | convolution fusion | flops 2422210560 | bytes 30408704 | tf_op jit(solution)/shard_map/jrc,cs->jrs/dot_general | solution.py:88
  330.2 1.9 copy-done
  332.9 2.0 pad_maximum_fusion
  (83 shorter events, 11.0 us)
Async XLA Ops:
  12.7 52.5 %all-to-all-start = ((f32[4,6,128,256]{3,0,1,2:T(4,128)}), f32[4,6,128,256]{3,0,1,2:T(4,128)S(1)}, u32[]{:S(2)}, u32[]{:S(2)}) async-start(f32[4,6,128,256]{3,0,1,2:T(4,128)} %copy.118), calls=%async_computation | async-start | bytes 6291456 | tf_op jit(solution)/shard_map/all_to_all | solution.py:16
  24.2 261.6 %all-gather.2.cloned.1.call-start = ((), (), s32[]{:S(2)}) async-start(), calls=%async_computation.2 | async-start | bytes 4718592 | tf_op jit(solution)/shard_map/all_gather | solution.py:79
  77.1 1.5 collective-permute-start
  82.9 5.0 %collective-permute-start.3 = (f32[256,512]{1,0:T(8,128)}, f32[256,512]{1,0:T(8,128)}, u32[]{:S(2)}, u32[]{:S(2)}) collective-permute-start(f32[256,512]{1,0:T(8,128)} %get-tuple-element.13), channel_id=1, source_target_pairs={{1,2}} | collective-permute-start | bytes 1572872 | tf_op jit(solution)/shard_map/ppermute | solution.py:56
  86.5 5.0 %collective-permute-start.1 = (f32[256,512]{1,0:T(8,128)}, f32[256,512]{1,0:T(8,128)}, u32[]{:S(2)}, u32[]{:S(2)}) collective-permute-start(f32[256,512]{1,0:T(8,128)} %add.53), channel_id=1, source_target_pairs={{0,2},{1,3}} | collective-permute-start | bytes 1572872 | tf_op jit(solution)/shard_map/ppermute | solution.py:56
  90.0 12.6 %collective-permute-start.4 = (f32[256,512]{1,0:T(8,128)}, f32[256,512]{1,0:T(8,128)}, u32[]{:S(2)}, u32[]{:S(2)}) collective-permute-start(f32[256,512]{1,0:T(8,128)} %add.56), channel_id=1, source_target_pairs={{1,3},{2,4}} | collective-permute-start | bytes 1572872 | tf_op jit(solution)/shard_map/ppermute | solution.py:56
  92.7 0.8 copy-start.5
  95.1 0.8 copy-start.9
  100.3 6.0 %collective-permute-start.6 = (f32[256,512]{1,0:T(8,128)}, f32[256,512]{1,0:T(8,128)}, u32[]{:S(2)}, u32[]{:S(2)}) collective-permute-start(f32[256,512]{1,0:T(8,128)} %get-tuple-element.15), channel_id=1, source_target_pairs={{2,3}} | collective-permute-start | bytes 1572872 | tf_op jit(solution)/shard_map/ppermute | solution.py:56
  101.7 6.9 %copy-start.10 = (f32[256,512]{1,0:T(8,128)S(1)}, f32[256,512]{1,0:T(8,128)}, u32[]{:S(2)}) copy-start(f32[256,512]{1,0:T(8,128)} %copy-done.9) | copy-start | bytes 1572868
  101.7 10.8 %collective-permute-start.2 = (f32[256,512]{1,0:T(8,128)}, f32[256,512]{1,0:T(8,128)S(1)}, u32[]{:S(2)}, u32[]{:S(2)}) collective-permute-start(f32[256,512]{1,0:T(8,128)} %copy-done.5), channel_id=1, source_target_pairs={{0,4},{1,5},{2,6},{3,7}} | collective-permute-start | bytes 1572872 | tf_op jit(solution)/shard_map/ppermute | solution.py:56
  103.9 6.6 %copy-start.13 = (f32[8,256,256]{2,1,0:T(8,128)S(1)}, f32[8,256,256]{2,1,0:T(8,128)}, u32[]{:S(2)}) copy-start(f32[8,256,256]{2,1,0:T(8,128)} %param.5) | copy-start | bytes 6291460
  103.9 17.3 %collective-permute-start.5 = (f32[256,512]{1,0:T(8,128)S(1)}, f32[256,512]{1,0:T(8,128)S(1)}, u32[]{:S(2)}, u32[]{:S(2)}) collective-permute-start(f32[256,512]{1,0:T(8,128)S(1)} %add.57), channel_id=1, source_target_pairs={{1,5},{2,6},{3,7}} | collective-permute-start | bytes 1572872 | tf_op jit(solution)/shard_map/ppermute | solution.py:56
  106.3 6.3 %copy-start.6 = (f32[256,512]{1,0:T(8,128)S(1)}, f32[256,512]{1,0:T(8,128)}, u32[]{:S(2)}) copy-start(f32[256,512]{1,0:T(8,128)} %copy-done.5) | copy-start | bytes 1572868
  107.7 6.5 %collective-permute-start.7 = (f32[256,512]{1,0:T(8,128)S(1)}, f32[256,512]{1,0:T(8,128)S(1)}, u32[]{:S(2)}, u32[]{:S(2)}) collective-permute-start(f32[256,512]{1,0:T(8,128)S(1)} %add.59), channel_id=1, source_target_pairs={{2,4},{3,5}} | collective-permute-start | bytes 1572872 | tf_op jit(solution)/shard_map/ppermute | solution.py:56
  111.9 4.7 %collective-permute-start.9 = (f32[256,512]{1,0:T(8,128)S(1)}, f32[256,512]{1,0:T(8,128)S(1)}, u32[]{:S(2)}, u32[]{:S(2)}) collective-permute-start(f32[256,512]{1,0:T(8,128)S(1)} %get-tuple-element.17), channel_id=1, source_target_pairs={{3,4}} | collective-permute-start | bytes 1572872 | tf_op jit(solution)/shard_map/ppermute | solution.py:56
  114.3 15.5 %collective-permute-start.8 = (f32[256,512]{1,0:T(8,128)S(1)}, f32[256,512]{1,0:T(8,128)S(1)}, u32[]{:S(2)}, u32[]{:S(2)}) collective-permute-start(f32[256,512]{1,0:T(8,128)S(1)} %add.60), channel_id=1, source_target_pairs={{2,6},{3,7}} | collective-permute-start | bytes 1572872 | tf_op jit(solution)/shard_map/ppermute | solution.py:56
  116.7 6.1 %collective-permute-start.10 = (f32[256,512]{1,0:T(8,128)S(1)}, f32[256,512]{1,0:T(8,128)S(1)}, u32[]{:S(2)}, u32[]{:S(2)}) collective-permute-start(f32[256,512]{1,0:T(8,128)S(1)} %add.62), channel_id=1, source_target_pairs={{3,5},{4,6}} | collective-permute-start | bytes 1572872 | tf_op jit(solution)/shard_map/ppermute | solution.py:56
  120.5 4.8 %collective-permute-start.12 = (f32[256,512]{1,0:T(8,128)S(1)}, f32[256,512]{1,0:T(8,128)S(1)}, u32[]{:S(2)}, u32[]{:S(2)}) collective-permute-start(f32[256,512]{1,0:T(8,128)S(1)} %get-tuple-element.19), channel_id=1, source_target_pairs={{4,5}} | collective-permute-start | bytes 1572872 | tf_op jit(solution)/shard_map/ppermute | solution.py:56
  122.9 0.8 copy-start.1
  125.4 6.1 %collective-permute-start.14 = (f32[256,512]{1,0:T(8,128)S(1)}, f32[256,512]{1,0:T(8,128)S(1)}, u32[]{:S(2)}, u32[]{:S(2)}) collective-permute-start(f32[256,512]{1,0:T(8,128)S(1)} %add.65), channel_id=1, source_target_pairs={{4,6},{5,7}} | collective-permute-start | bytes 1572872 | tf_op jit(solution)/shard_map/ppermute | solution.py:56
  129.2 4.2 %collective-permute-start.13 = (f32[256,512]{1,0:T(8,128)S(1)}, f32[256,512]{1,0:T(8,128)S(1)}, u32[]{:S(2)}, u32[]{:S(2)}) collective-permute-start(f32[256,512]{1,0:T(8,128)S(1)} %get-tuple-element.21), channel_id=1, source_target_pairs={{5,6}} | collective-permute-start | bytes 1572872 | tf_op jit(solution)/shard_map/ppermute | solution.py:56
  131.5 5.3 %copy-start.7 = (f32[256,512]{1,0:T(8,128)}, f32[256,512]{1,0:T(8,128)S(1)}, u32[]{:S(2)}) copy-start(f32[256,512]{1,0:T(8,128)S(1)} %fusion.29) | copy-start | bytes 1572868
  133.3 5.8 %copy-start.3 = (f32[256,512]{1,0:T(8,128)}, f32[256,512]{1,0:T(8,128)S(1)}, u32[]{:S(2)}) copy-start(f32[256,512]{1,0:T(8,128)S(1)} %convolution_bitcast_fusion.4) | copy-start | bytes 1572868
  136.8 4.6 %collective-permute-start.15 = (f32[256,512]{1,0:T(8,128)}, f32[256,512]{1,0:T(8,128)}, u32[]{:S(2)}, u32[]{:S(2)}) collective-permute-start(f32[256,512]{1,0:T(8,128)} %get-tuple-element.23), channel_id=1, source_target_pairs={{6,7}} | collective-permute-start | bytes 1572872 | tf_op jit(solution)/shard_map/ppermute | solution.py:56
  139.1 4.1 %collective-permute-start.16 = (f32[256,512]{1,0:T(8,128)}, f32[256,512]{1,0:T(8,128)}, u32[]{:S(2)}, u32[]{:S(2)}) collective-permute-start(f32[256,512]{1,0:T(8,128)} %add.67), channel_id=1, source_target_pairs={{5,7}} | collective-permute-start | bytes 1572872 | tf_op jit(solution)/shard_map/ppermute | solution.py:56
  140.6 4.8 %copy-start.2 = (f32[256,512]{1,0:T(8,128)S(1)}, f32[256,512]{1,0:T(8,128)}, u32[]{:S(2)}) copy-start(f32[256,512]{1,0:T(8,128)} %copy-done.1) | copy-start | bytes 1572868
  140.6 4.8 %copy-start.4 = (f32[256,512]{1,0:T(8,128)S(1)}, f32[256,512]{1,0:T(8,128)}, u32[]{:S(2)}) copy-start(f32[256,512]{1,0:T(8,128)} %copy-done.3) | copy-start | bytes 1572868
  140.6 4.8 %copy-start.8 = (f32[256,512]{1,0:T(8,128)S(1)}, f32[256,512]{1,0:T(8,128)}, u32[]{:S(2)}) copy-start(f32[256,512]{1,0:T(8,128)} %copy-done.7) | copy-start | bytes 1572868
  140.6 4.7 %collective-permute-start.11 = (f32[256,512]{1,0:T(8,128)}, f32[256,512]{1,0:T(8,128)S(1)}, u32[]{:S(2)}, u32[]{:S(2)}) collective-permute-start(f32[256,512]{1,0:T(8,128)} %copy-done.1), channel_id=1, source_target_pairs={{3,7}} | collective-permute-start | bytes 1572872 | tf_op jit(solution)/shard_map/ppermute | solution.py:56
  143.2 3.9 %copy-start.14 = (f32[256,512]{1,0:T(8,128)S(1)}, f32[256,512]{1,0:T(8,128)}, u32[]{:S(2)}) copy-start(f32[256,512]{1,0:T(8,128)} %get-tuple-element.14) | copy-start | bytes 1572868
  143.2 3.9 %copy-start.15 = (f32[256,512]{1,0:T(8,128)S(1)}, f32[256,512]{1,0:T(8,128)}, u32[]{:S(2)}) copy-start(f32[256,512]{1,0:T(8,128)} %get-tuple-element.16) | copy-start | bytes 1572868
  143.2 3.9 %copy-start.16 = (f32[256,512]{1,0:T(8,128)S(1)}, f32[256,512]{1,0:T(8,128)}, u32[]{:S(2)}) copy-start(f32[256,512]{1,0:T(8,128)} %get-tuple-element.18) | copy-start | bytes 1572868
  143.2 3.9 %copy-start.17 = (f32[256,512]{1,0:T(8,128)S(1)}, f32[256,512]{1,0:T(8,128)}, u32[]{:S(2)}) copy-start(f32[256,512]{1,0:T(8,128)} %get-tuple-element.20) | copy-start | bytes 1572868
  143.2 3.9 %copy-start.18 = (f32[256,512]{1,0:T(8,128)S(1)}, f32[256,512]{1,0:T(8,128)}, u32[]{:S(2)}) copy-start(f32[256,512]{1,0:T(8,128)} %get-tuple-element.22) | copy-start | bytes 1572868
  143.2 3.9 %copy-start.19 = (f32[256,512]{1,0:T(8,128)S(1)}, f32[256,512]{1,0:T(8,128)}, u32[]{:S(2)}) copy-start(f32[256,512]{1,0:T(8,128)} %get-tuple-element.24) | copy-start | bytes 1572868
  148.9 0.8 copy-start.11
  174.6 0.8 copy-start.20
  175.4 2.3 collective-permute-start.17
  285.9 17.7 %slice-start = ((s8[12582912]{0:T(1024)(128)(4,1)}), s8[4194304]{0:T(1024)(128)(4,1)S(1)}, s32[]{:S(2)}) async-start(s8[12582912]{0:T(1024)(128)(4,1)} %bitcast.319), calls=%async_computation.3 | async-start | bytes 8388608
  285.9 17.7 %slice-start.1 = ((s8[12582912]{0:T(1024)(128)(4,1)}), s8[4194304]{0:T(1024)(128)(4,1)S(1)}, s32[]{:S(2)}) async-start(s8[12582912]{0:T(1024)(128)(4,1)} %bitcast.319), calls=%async_computation.4 | async-start | bytes 8388608
  293.5 10.1 %slice-start.2 = ((s8[12582912]{0:T(1024)(128)(4,1)}), s8[4194304]{0:T(1024)(128)(4,1)S(1)}, s32[]{:S(2)}) async-start(s8[12582912]{0:T(1024)(128)(4,1)} %bitcast.319), calls=%async_computation.5 | async-start | bytes 8388608
  321.4 8.9 %copy-start.12 = (f32[256,512]{1,0:T(8,128)S(1)}, f32[256,512]{1,0:T(8,128)}, u32[]{:S(2)}) copy-start(f32[256,512]{1,0:T(8,128)} %copy-done.11) | copy-start | bytes 1572868
  330.2 1.9 copy-start
  330.2 2.7 slice-start.3
Sparse Core Ops, SparseCore 0:
  249.3 36.5 all-gather.1

commit v3 on v1

--- a/solution.py
+++ b/solution.py
@@ -28,12 +28,15 @@
     device = lax.axis_index(AXES)
     row = lax.axis_index("row")
     col = lax.axis_index("col")
-    low = panels[:, 0]
+    inverse = lax.dynamic_index_in_dim(
+        diag_inverse, jnp.minimum(device, sections - 1), 0, keepdims=False
+    )
+    low = jnp.stack([mm(inverse, panels[k, 0]) for k in range(sections - 1)])
 
     after = [[None] * 3 for _ in range(sections)]
     first_hop = [None] * sections
     own = jnp.zeros_like(lead)
-    settled = lead
+    settled = mm(inverse, lead)
     for section in range(sections):
         chain = settled
         if section >= 1:
@@ -41,7 +44,7 @@
         for back in (2, 3):
             if section - back >= 0:
                 chain = chain - mm(low[section - back], after[section - back][1])
-        solved = mm(diag_inverse[section], chain)
+        solved = chain
         here = device == section
         own = jnp.where(here, solved, own)
         buf = jnp.where(here, solved, jnp.zeros_like(solved))
@@ -89,7 +92,7 @@
             "jrc,cs->jrs",
             panels[section],
             whole[section * width_block:(section + 1) * width_block],
-            precision=HI,
+            precision=lax.Precision.HIGH,
             preferred_element_type=jnp.float32,
         )
     first = jnp.where(device < sections, own, update[0])

time: 328 us -> 305 us (0.930)
  starting transfers between devices: 92.1 us -> 73.1 us
  matrix products: 81.8 us -> 68.5 us
  other arithmetic: 7.74 us -> 18.5 us
  local copies, waits for them, and re-layouts: 25.3 us -> 35.6 us
  blocking collectives: 26.2 us -> 21.3 us
  waiting for transfers between devices: 76.3 us -> 72.3 us
    all_to_all x2, starting transfers between devices: 63.8 us -> 49.6 us  [transpose_in(): lax.all_to_all(pieces, AXES, split_axis=2, concat_axis=0, tiled=True)]
    add x10, other arithmetic: 4.97 us -> 15.8 us  [per_device(): buf = buf + got]
    dot_general x8, matrix products: 39.8 us -> 29.4 us  [per_device(): jnp.einsum('jrc,cs->jrs', panels[section], whole[section * width_block:(s...]
    unnamed x31 -> x79, local copies, waits for them, and re-layouts: 6.93 us -> 11.8 us
    all_to_all x1, blocking collectives: 26.2 us -> 21.3 us  [per_device(): lax.all_to_all(own.reshape(rows, cut, -1), 'row', 0, 0, tiled=True)[0]]
    ppermute x17, starting transfers between devices: 27 us -> 22.2 us  [per_device(): got = lax.ppermute(buf, AXES, pairs)]
    all_gather x1, waiting for transfers between devices: 26.3 us -> 22.6 us  [per_device(): gathered = lax.all_gather(mine, AXES, tiled=True)]
  transfers between devices with their start and end apart: 21 -> 21, of which waited for: 4 -> 4; matrix products, arithmetic and copies ran while one was open for 15% -> 21% of each run, Pallas kernels for 0% -> 0%
where the time goes in v3:
time: 305 us; the launch traced here: 303 us
  starting transfers between devices  73.1 us (24%)
  waiting for transfers between devices  72.3 us (24%)
  matrix products  68.5 us (22%)
  local copies, waits for them, and re-layouts  35.6 us (12%)
  blocking collectives  21.3 us (7%)
  other arithmetic  18.5 us (6%)
  between operations  14.2 us (5%)
    all_to_all x2, starting transfers between devices, transpose_in(): lax.all_to_all(pieces, AXES, split_axis=2, concat_axis=0, tiled=True)  49.6 us
    all_to_all x2, waiting for transfers between devices, transpose_in(): lax.all_to_all(pieces, AXES, split_axis=2, concat_axis=0, tiled=True)  48.6 us
    dot_general x25, matrix products, mm(): return jnp.dot(a, b, precision=HI, preferred_element_type=jnp.float32)  39.1 us
    dot_general x8, matrix products, per_device(): jnp.einsum('jrc,cs->jrs', panels[section], whole[section * width_block:(s...  29.4 us
    all_gather x1, waiting for transfers between devices, per_device(): gathered = lax.all_gather(mine, AXES, tiled=True)  22.6 us
    ppermute x17, starting transfers between devices, per_device(): got = lax.ppermute(buf, AXES, pairs)  22.2 us
    all_to_all x1, blocking collectives, per_device(): lax.all_to_all(own.reshape(rows, cut, -1), 'row', 0, 0, tiled=True)[0]  21.3 us
    add x10, other arithmetic, per_device(): buf = buf + got  15.8 us
  transfers between devices with their start and end apart: 21, of which 4 were waited for; matrix products, arithmetic and copies ran while one was open for 21% of the time, Pallas kernels for 0%

profile of v3, /device:TPU:1, one launch (start us, length us, event | category | flops | bytes accessed | tf_op | source)
XLA Modules:
  0.0 303.5 jit_solution(5397678636490039913)
XLA Ops:
  6.5 2.6 copy.119
  9.2 1.7 copy-done.3
  12.0 11.5 %all-to-all-start = ((f32[4,1,128,256]{3,0,1,2:T(4,128)}), f32[4,1,128,256]{3,0,1,2:T(4,128)S(1)}, u32[]{:S(2)}, u32[]{:S(2)}) async-start(f32[4,1,128,256]{3,0,1,2:T(4,128)} %copy.74), calls=%async_computation | async-start | bytes 1048576 | tf_op jit(solution)/shard_map/all_to_all | solution.py:16
  23.6 13.3 %all-to-all-done = f32[4,1,128,256]{3,0,1,2:T(4,128)S(1)} async-done(((f32[4,1,128,256]{3,0,1,2:T(4,128)}), f32[4,1,128,256]{3,0,1,2:T(4,128)S(1)}, u32[]{:S(2)}, u32[]{:S(2)}) %all-to-all-start) | async-done | bytes 524320 | tf_op jit(solution)/shard_map/all_to_all | solution.py:16
  37.5 1.4 copy.75
  38.9 1.7 broadcast_select_fusion.6
  40.5 1.5 collective-permute-start
  42.0 1.3 fusion.67
  44.1 2.7 broadcast_select_fusion.5
  46.7 1.5 collective-permute-start.3
  48.2 1.9 add.58
  50.1 1.4 collective-permute-start.1
  51.6 1.4 fusion.65
  53.0 2.2 add.61
  55.2 1.5 collective-permute-start.4
  56.6 1.3 add.59
  60.2 2.7 broadcast_select_fusion.4
  62.8 1.5 collective-permute-start.6
  64.3 1.4 fusion.63
  65.7 1.5 collective-permute-start.2
  70.7 2.7 broadcast_select_fusion.3
  73.4 1.5 collective-permute-start.9
  74.9 2.1 add.64
  76.9 1.5 collective-permute-start.7
  78.4 1.4 fusion.61
  79.8 1.6 collective-permute-start.5
  81.4 1.9 convolution_subtract_fusion.9
  83.4 2.3 add.67
  85.6 1.5 collective-permute-start.10
  89.9 2.9 broadcast_select_fusion.2
  92.7 1.5 collective-permute-start.12
  94.2 2.1 fusion.55
  96.2 1.3 fusion.57
  98.5 1.9 convolution_subtract_fusion.7
  100.4 1.3 add.70
  102.5 1.3 add.68
  104.5 2.5 broadcast_select_fusion.1
  109.8 1.6 broadcast_select_fusion
  111.4 1.4 collective-permute-start.15
  113.8 1.5 collective-permute-start.16
  115.3 1.5 fusion.59
  117.5 1.7 fusion.106
  119.2 1.9 fusion.47
  122.2 21.3 %all_to_all.35 = f32[8,32,512]{2,1,0:T(8,128)S(1)} all-to-all(f32[8,32,512]{2,1,0:T(8,128)S(1)} %bitcast.184), channel_id=1, replica_groups=mesh['row'=8,'col'=16] {'row'}, dimensions={0} | all-to-all | bytes 1048576 | tf_op jit(solution)/shard_map/all_to_all | solution.py:70
  143.5 1.3 collective-permute-start.17
  146.4 1.9 slice.154
  148.3 3.2 %copy.76 = f32[4,5,128,256]{3,0,1,2:T(4,128)} copy(f32[4,5,128,256]{3,2,1,0:T(8,128)S(1)} %slice.154) | data formatting | bytes 5242880 | tf_op jit(solution)/shard_map/slice | solution.py:27
  151.5 38.1 %all-to-all-start.1 = ((f32[4,5,128,256]{3,0,1,2:T(4,128)}), f32[4,5,128,256]{3,0,1,2:T(4,128)}, u32[]{:S(2)}, u32[]{:S(2)}) async-start(f32[4,5,128,256]{3,0,1,2:T(4,128)} %copy.76), calls=%async_computation.1 | async-start | bytes 5242880 | tf_op jit(solution)/shard_map/all_to_all | solution.py:16
  189.6 35.4 %all-to-all-done.1 = f32[4,5,128,256]{3,0,1,2:T(4,128)} async-done(((f32[4,5,128,256]{3,0,1,2:T(4,128)}), f32[4,5,128,256]{3,0,1,2:T(4,128)}, u32[]{:S(2)}, u32[]{:S(2)}) %all-to-all-start.1) | async-done | bytes 2621472 | tf_op jit(solution)/shard_map/all_to_all | solution.py:16
  225.0 3.7 %copy.77 = f32[128,4,5,1,256]{4,1,0,2,3:T(4,128)} copy(f32[128,4,5,1,256]{4,1,2,0,3:T(4,128)} %bitcast.13) | data formatting | bytes 5242880 | tf_op jit(solution)/shard_map/all_to_all | solution.py:16
  228.7 4.0 %reshape.32 = f32[512,5,256]{2,0,1:T(8,128)} reshape(f32[128,4,5,1,256]{4,1,0,2,3:T(4,128)} %copy.77) | data formatting | bytes 5242880 | tf_op jit(solution)/shard_map/reshape | solution.py:17
  232.7 3.3 %copy.78 = f32[512,5,256]{0,2,1:T(8,128)} copy(f32[512,5,256]{2,0,1:T(8,128)} %reshape.32) | data formatting | bytes 5242880 | tf_op jit(solution)/shard_map/reshape | solution.py:17
  236.0 22.6 %all-gather.2.cloned.1.call-done = f32[2048,512]{1,0:T(8,128)} async-done(((f32[16,512]{1,0:T(8,128)}), f32[2048,512]{1,0:T(8,128)}) %all-gather.2.cloned.1.call-update) | async-done | bytes 4194320 | tf_op jit(solution)/shard_map/all_gather | solution.py:82
  258.6 3.8 %fusion.101 = (f32[1,8,2,16,512]{4,3,0,2,1:T(8,128)}, f32[1,8,2,16,512]{4,3,0,2,1:T(8,128)S(1)}, f32[1,8,2,16,512]{4,3,0,2,1:T(8,128)S(1)}, f32[1,8,2,16,512]{4,...) fusion(f32[8,8,2,16,512]{4,3,0,2,1:T(8,128)} %bitcast.186), kind=kLoop, calls=%fused_computation.123 | loop fusion | bytes 8388608 | tf_op jit(solution)/shard_map/slice | solution.py:94
  262.4 3.0 fusion.8
  265.4 3.0 %fusion.10 = f32[512,6,256]{0,2,1:T(8,128)S(1)} fusion(f32[256,512,1]{1,0,2:T(8,128)S(1)} %bitcast.193, f32[8,6,256,256]{3,2,1,0:T(8,128)} %param.4), kind=kOutput, calls=%fused_computation.12 | convolution fusion | flops 1207959552 | bytes 5242880 | tf_op jit(solution)/shard_map/jrc,cs->jrs/dot_general | solution.py:91
  268.4 2.9 fusion.12
  271.4 3.1 %fusion.14 = f32[512,6,256]{0,2,1:T(8,128)} fusion(f32[256,512,1]{1,0,2:T(8,128)S(1)} %bitcast.191, f32[8,6,256,256]{3,2,1,0:T(8,128)S(1)} %bitcast.180), kind=kOutput, calls=%fused_computation.16 | convolution fusion | flops 1207959552 | bytes 5242880 | tf_op jit(solution)/shard_map/jrc,cs->jrs/dot_general | solution.py:91
  274.5 3.1 %fusion.16 = f32[512,6,256]{0,2,1:T(8,128)} fusion(f32[256,512,1]{1,0,2:T(8,128)S(1)} %bitcast.190, f32[8,6,256,256]{3,2,1,0:T(8,128)S(1)} %bitcast.180), kind=kOutput, calls=%fused_computation.18 | convolution fusion | flops 1207959552 | bytes 5242880 | tf_op jit(solution)/shard_map/jrc,cs->jrs/dot_general | solution.py:91
  277.5 3.1 %fusion.18 = f32[512,6,256]{0,2,1:T(8,128)} fusion(f32[256,512,1]{1,0,2:T(8,128)S(1)} %bitcast.189, f32[8,6,256,256]{3,2,1,0:T(8,128)S(1)} %bitcast.180), kind=kOutput, calls=%fused_computation.20 | convolution fusion | flops 1207959552 | bytes 5242880 | tf_op jit(solution)/shard_map/jrc,cs->jrs/dot_general | solution.py:91
  280.6 3.1 %fusion.20 = f32[512,6,256]{0,2,1:T(8,128)} fusion(f32[256,512,1]{1,0,2:T(8,128)S(1)} %bitcast.188, f32[8,6,256,256]{3,2,1,0:T(8,128)S(1)} %bitcast.180), kind=kOutput, calls=%fused_computation.22 | convolution fusion | flops 1207959552 | bytes 5242880 | tf_op jit(solution)/shard_map/jrc,cs->jrs/dot_general | solution.py:91
  283.8 8.1 %fusion.6 = f32[6,256,512]{2,1,0:T(8,128)} fusion(f32[5,256,512]{2,1,0:T(8,128)} %bitcast.183, f32[1,256,512]{2,1,0:T(8,128)S(1)} %bitcast.185, f32[512,6,256]{0,2,1:T(8,128)S(1)} %fusion.8, f32[512,6,256]{0,2,1:T(8,128)S(1)} %fusion.10, f32[512,6,256]{0,2,1:T(8,128)S(1)} %fusion.12, f32[512,6,256]{0,2,1:T(8,128)} %fusion.14, f32[512,6,256]{0,2,1:T(8,128)} %fusion.16, ...), kind=kOutput, calls=%fused_computation.7 | convolution fusion | flops 1215037440 | bytes 30408704 | tf_op jit(solution)/shard_map/jrc,cs->jrs/dot_general | solution.py:91
  291.9 1.9 copy-done.2
  294.6 2.0 pad_maximum_fusion
  (119 shorter events, 21.1 us)
Async XLA Ops:
  6.5 32.3 %copy-start = (f32[8,256,256]{2,1,0:T(8,128)S(1)}, f32[8,256,256]{2,1,0:T(8,128)}, u32[]{:S(2)}) copy-start(f32[8,256,256]{2,1,0:T(8,128)} %param.5) | copy-start | bytes 6291460
  9.2 1.7 copy-start.3
  12.0 24.8 %all-to-all-start = ((f32[4,1,128,256]{3,0,1,2:T(4,128)}), f32[4,1,128,256]{3,0,1,2:T(4,128)S(1)}, u32[]{:S(2)}, u32[]{:S(2)}) async-start(f32[4,1,128,256]{3,0,1,2:T(4,128)} %copy.74), calls=%async_computation | async-start | bytes 1048576 | tf_op jit(solution)/shard_map/all_to_all | solution.py:16
  23.5 235.0 %all-gather.2.cloned.1.call-start = ((), (), s32[]{:S(2)}) async-start(), calls=%async_computation.3 | async-start | bytes 4227072 | tf_op jit(solution)/shard_map/all_gather | solution.py:82
  40.5 2.8 collective-permute-start
  43.4 0.7 copy-start.26
  46.7 6.2 %collective-permute-start.3 = (f32[256,512]{1,0:T(8,128)}, f32[256,512]{1,0:T(8,128)}, u32[]{:S(2)}, u32[]{:S(2)}) collective-permute-start(f32[256,512]{1,0:T(8,128)} %get-tuple-element.15), channel_id=1, source_target_pairs={{1,2}} | collective-permute-start | bytes 1572872 | tf_op jit(solution)/shard_map/ppermute | solution.py:59
  50.1 6.5 %collective-permute-start.1 = (f32[256,512]{1,0:T(8,128)}, f32[256,512]{1,0:T(8,128)}, u32[]{:S(2)}, u32[]{:S(2)}) collective-permute-start(f32[256,512]{1,0:T(8,128)} %add.58), channel_id=1, source_target_pairs={{0,2},{1,3}} | collective-permute-start | bytes 1572872 | tf_op jit(solution)/shard_map/ppermute | solution.py:59
  51.6 7.1 %copy-start.27 = (f32[256,256]{1,0:T(8,128)S(1)}, f32[256,256]{1,0:T(8,128)}, u32[]{:S(2)}) copy-start(f32[256,256]{1,0:T(8,128)} %copy-done.26) | copy-start | bytes 786436
  53.0 15.5 %copy-start.25 = (f32[256,256]{1,0:T(8,128)}, f32[256,256]{1,0:T(8,128)S(1)}, u32[]{:S(2)}) copy-start(f32[256,256]{1,0:T(8,128)S(1)} %fusion.65) | copy-start | bytes 786436
  55.2 12.0 %collective-permute-start.4 = (f32[256,512]{1,0:T(8,128)}, f32[256,512]{1,0:T(8,128)}, u32[]{:S(2)}, u32[]{:S(2)}) collective-permute-start(f32[256,512]{1,0:T(8,128)} %add.61), channel_id=1, source_target_pairs={{1,3},{2,4}} | collective-permute-start | bytes 1572872 | tf_op jit(solution)/shard_map/ppermute | solution.py:59
  57.9 0.8 copy-start.11
  59.4 0.8 copy-start.18
  62.8 7.1 %collective-permute-start.6 = (f32[256,512]{1,0:T(8,128)}, f32[256,512]{1,0:T(8,128)}, u32[]{:S(2)}, u32[]{:S(2)}) collective-permute-start(f32[256,512]{1,0:T(8,128)} %get-tuple-element.17), channel_id=1, source_target_pairs={{2,3}} | collective-permute-start | bytes 1572872 | tf_op jit(solution)/shard_map/ppermute | solution.py:59
  64.3 6.4 %copy-start.19 = (f32[256,512]{1,0:T(8,128)S(1)}, f32[256,512]{1,0:T(8,128)}, u32[]{:S(2)}) copy-start(f32[256,512]{1,0:T(8,128)} %copy-done.18) | copy-start | bytes 1572868
  65.7 7.7 %copy-start.22 = (f32[256,256]{1,0:T(8,128)}, f32[256,256]{1,0:T(8,128)S(1)}, u32[]{:S(2)}) copy-start(f32[256,256]{1,0:T(8,128)S(1)} %fusion.63) | copy-start | bytes 786436
  65.7 15.7 %collective-permute-start.2 = (f32[256,512]{1,0:T(8,128)}, f32[256,512]{1,0:T(8,128)}, u32[]{:S(2)}, u32[]{:S(2)}) collective-permute-start(f32[256,512]{1,0:T(8,128)} %copy-done.11), channel_id=1, source_target_pairs={{0,4},{1,5},{2,6},{3,7}} | collective-permute-start | bytes 1572872 | tf_op jit(solution)/shard_map/ppermute | solution.py:59
  68.5 0.8 copy-start.7
  69.9 0.8 copy-start.14
  73.4 9.9 %collective-permute-start.9 = (f32[256,512]{1,0:T(8,128)}, f32[256,512]{1,0:T(8,128)}, u32[]{:S(2)}, u32[]{:S(2)}) collective-permute-start(f32[256,512]{1,0:T(8,128)} %get-tuple-element.19), channel_id=1, source_target_pairs={{3,4}} | collective-permute-start | bytes 1572872 | tf_op jit(solution)/shard_map/ppermute | solution.py:59
  76.9 10.2 %collective-permute-start.7 = (f32[256,512]{1,0:T(8,128)}, f32[256,512]{1,0:T(8,128)}, u32[]{:S(2)}, u32[]{:S(2)}) collective-permute-start(f32[256,512]{1,0:T(8,128)} %add.64), channel_id=1, source_target_pairs={{2,4},{3,5}} | collective-permute-start | bytes 1572872 | tf_op jit(solution)/shard_map/ppermute | solution.py:59
  78.4 10.8 %copy-start.23 = (f32[256,256]{1,0:T(8,128)S(1)}, f32[256,256]{1,0:T(8,128)}, u32[]{:S(2)}) copy-start(f32[256,256]{1,0:T(8,128)} %copy-done.22) | copy-start | bytes 786436
  79.8 10.0 %copy-start.15 = (f32[256,512]{1,0:T(8,128)S(1)}, f32[256,512]{1,0:T(8,128)}, u32[]{:S(2)}) copy-start(f32[256,512]{1,0:T(8,128)} %copy-done.14) | copy-start | bytes 1572868
  79.8 18.6 %collective-permute-start.5 = (f32[256,512]{1,0:T(8,128)}, f32[256,512]{1,0:T(8,128)}, u32[]{:S(2)}, u32[]{:S(2)}) collective-permute-start(f32[256,512]{1,0:T(8,128)} %copy-done.7), channel_id=1, source_target_pairs={{1,5},{2,6},{3,7}} | collective-permute-start | bytes 1572872 | tf_op jit(solution)/shard_map/ppermute | solution.py:59
  83.3 9.4 %copy-start.20 = (f32[256,512]{1,0:T(8,128)}, f32[256,512]{1,0:T(8,128)S(1)}, u32[]{:S(2)}) copy-start(f32[256,512]{1,0:T(8,128)S(1)} %convolution_subtract_fusion.9) | copy-start | bytes 1572868
  85.6 16.9 %collective-permute-start.10 = (f32[256,512]{1,0:T(8,128)}, f32[256,512]{1,0:T(8,128)}, u32[]{:S(2)}, u32[]{:S(2)}) collective-permute-start(f32[256,512]{1,0:T(8,128)} %add.67), channel_id=1, source_target_pairs={{3,5},{4,6}} | collective-permute-start | bytes 1572872 | tf_op jit(solution)/shard_map/ppermute | solution.py:59
  88.4 0.8 copy-start.9
  89.2 9.2 %copy-start.8 = (f32[256,512]{1,0:T(8,128)S(1)}, f32[256,512]{1,0:T(8,128)}, u32[]{:S(2)}) copy-start(f32[256,512]{1,0:T(8,128)} %copy-done.7) | copy-start | bytes 1572868
  89.9 2.9 copy-start.16
  92.7 7.6 %collective-permute-start.12 = (f32[256,512]{1,0:T(8,128)}, f32[256,512]{1,0:T(8,128)}, u32[]{:S(2)}, u32[]{:S(2)}) collective-permute-start(f32[256,512]{1,0:T(8,128)} %get-tuple-element.21), channel_id=1, source_target_pairs={{4,5}} | collective-permute-start | bytes 1572872 | tf_op jit(solution)/shard_map/ppermute | solution.py:59
  97.6 11.4 %copy-start.28 = (f32[256,256]{1,0:T(8,128)}, f32[256,256]{1,0:T(8,128)S(1)}, u32[]{:S(2)}) copy-start(f32[256,256]{1,0:T(8,128)S(1)} %fusion.57) | copy-start | bytes 786436
  97.6 6.9 %copy-start.17 = (f32[256,512]{1,0:T(8,128)S(1)}, f32[256,512]{1,0:T(8,128)}, u32[]{:S(2)}) copy-start(f32[256,512]{1,0:T(8,128)} %copy-done.16) | copy-start | bytes 1572868
  97.6 6.9 %copy-start.29 = (f32[256,256]{1,0:T(8,128)S(1)}, f32[256,256]{1,0:T(8,128)}, u32[]{:S(2)}) copy-start(f32[256,256]{1,0:T(8,128)} %fusion.55) | copy-start | bytes 786436
  97.6 10.1 %collective-permute-start.8 = (f32[256,512]{1,0:T(8,128)}, f32[256,512]{1,0:T(8,128)S(1)}, u32[]{:S(2)}, u32[]{:S(2)}) collective-permute-start(f32[256,512]{1,0:T(8,128)} %copy-done.9), channel_id=1, source_target_pairs={{2,6},{3,7}} | collective-permute-start | bytes 1572872 | tf_op jit(solution)/shard_map/ppermute | solution.py:59
  101.7 6.0 %copy-start.10 = (f32[256,512]{1,0:T(8,128)S(1)}, f32[256,512]{1,0:T(8,128)}, u32[]{:S(2)}) copy-start(f32[256,512]{1,0:T(8,128)} %copy-done.9) | copy-start | bytes 1572868
  101.7 6.0 %copy-start.24 = (f32[256,256]{1,0:T(8,128)S(1)}, f32[256,256]{1,0:T(8,128)}, u32[]{:S(2)}) copy-start(f32[256,256]{1,0:T(8,128)} %copy-done.22) | copy-start | bytes 786436
  101.7 6.7 %collective-permute-start.14 = (f32[256,512]{1,0:T(8,128)S(1)}, f32[256,512]{1,0:T(8,128)S(1)}, u32[]{:S(2)}, u32[]{:S(2)}) collective-permute-start(f32[256,512]{1,0:T(8,128)S(1)} %add.70), channel_id=1, source_target_pairs={{4,6},{5,7}} | collective-permute-start | bytes 1572872 | tf_op jit(solution)/shard_map/ppermute | solution.py:59
  107.0 2.0 collective-permute-start.13
  108.3 5.4 %copy-start.12 = (f32[256,512]{1,0:T(8,128)}, f32[256,512]{1,0:T(8,128)S(1)}, u32[]{:S(2)}) copy-start(f32[256,512]{1,0:T(8,128)S(1)} %convolution_subtract_fusion.5) | copy-start | bytes 1572868
  109.0 0.8 copy-start.5
  111.4 6.1 %collective-permute-start.15 = (f32[256,512]{1,0:T(8,128)}, f32[256,512]{1,0:T(8,128)}, u32[]{:S(2)}, u32[]{:S(2)}) collective-permute-start(f32[256,512]{1,0:T(8,128)} %get-tuple-element.25), channel_id=1, source_target_pairs={{6,7}} | collective-permute-start | bytes 1572872 | tf_op jit(solution)/shard_map/ppermute | solution.py:59
  113.8 5.4 %collective-permute-start.16 = (f32[256,512]{1,0:T(8,128)}, f32[256,512]{1,0:T(8,128)}, u32[]{:S(2)}, u32[]{:S(2)}) collective-permute-start(f32[256,512]{1,0:T(8,128)} %add.72), channel_id=1, source_target_pairs={{5,7}} | collective-permute-start | bytes 1572872 | tf_op jit(solution)/shard_map/ppermute | solution.py:59
  115.2 5.8 %copy-start.6 = (f32[256,512]{1,0:T(8,128)S(1)}, f32[256,512]{1,0:T(8,128)}, u32[]{:S(2)}) copy-start(f32[256,512]{1,0:T(8,128)} %copy-done.5) | copy-start | bytes 1572868
  115.2 5.9 %copy-start.13 = (f32[256,512]{1,0:T(8,128)S(1)}, f32[256,512]{1,0:T(8,128)}, u32[]{:S(2)}) copy-start(f32[256,512]{1,0:T(8,128)} %copy-done.12) | copy-start | bytes 1572868
  115.2 5.9 %copy-start.30 = (f32[256,512]{1,0:T(8,128)S(1)}, f32[256,512]{1,0:T(8,128)}, u32[]{:S(2)}) copy-start(f32[256,512]{1,0:T(8,128)} %get-tuple-element.16) | copy-start | bytes 1572868
  115.3 5.9 %copy-start.31 = (f32[256,512]{1,0:T(8,128)S(1)}, f32[256,512]{1,0:T(8,128)}, u32[]{:S(2)}) copy-start(f32[256,512]{1,0:T(8,128)} %get-tuple-element.18) | copy-start | bytes 1572868
  115.3 5.9 %copy-start.32 = (f32[256,512]{1,0:T(8,128)S(1)}, f32[256,512]{1,0:T(8,128)}, u32[]{:S(2)}) copy-start(f32[256,512]{1,0:T(8,128)} %get-tuple-element.20) | copy-start | bytes 1572868
  115.3 5.9 %copy-start.33 = (f32[256,512]{1,0:T(8,128)S(1)}, f32[256,512]{1,0:T(8,128)}, u32[]{:S(2)}) copy-start(f32[256,512]{1,0:T(8,128)} %get-tuple-element.22) | copy-start | bytes 1572868
  115.3 5.9 %copy-start.34 = (f32[256,512]{1,0:T(8,128)S(1)}, f32[256,512]{1,0:T(8,128)}, u32[]{:S(2)}) copy-start(f32[256,512]{1,0:T(8,128)} %get-tuple-element.24) | copy-start | bytes 1572868
  116.8 4.3 %collective-permute-start.11 = (f32[256,512]{1,0:T(8,128)S(1)}, f32[256,512]{1,0:T(8,128)S(1)}, u32[]{:S(2)}, u32[]{:S(2)}) collective-permute-start(f32[256,512]{1,0:T(8,128)S(1)} %add.68), channel_id=1, source_target_pairs={{3,7}} | collective-permute-start | bytes 1572872 | tf_op jit(solution)/shard_map/ppermute | solution.py:59
  122.1 26.2 %copy-start.4 = (f32[256,512]{1,0:T(8,128)}, f32[256,512]{1,0:T(8,128)S(1)}, u32[]{:S(2)}) copy-start(f32[256,512]{1,0:T(8,128)S(1)} %fusion.39) | copy-start | bytes 1572868
  143.5 2.3 collective-permute-start.17
  151.5 73.5 %all-to-all-start.1 = ((f32[4,5,128,256]{3,0,1,2:T(4,128)}), f32[4,5,128,256]{3,0,1,2:T(4,128)}, u32[]{:S(2)}, u32[]{:S(2)}) async-start(f32[4,5,128,256]{3,0,1,2:T(4,128)} %copy.76), calls=%async_computation.1 | async-start | bytes 5242880 | tf_op jit(solution)/shard_map/all_to_all | solution.py:16
  258.6 12.8 %slice-start = ((s8[12582912]{0:T(1024)(128)(4,1)}), s8[4194304]{0:T(1024)(128)(4,1)S(1)}, s32[]{:S(2)}) async-start(s8[12582912]{0:T(1024)(128)(4,1)} %bitcast.179), calls=%async_computation.4 | async-start | bytes 8388608
  258.6 12.8 %slice-start.1 = ((s8[12582912]{0:T(1024)(128)(4,1)}), s8[4194304]{0:T(1024)(128)(4,1)S(1)}, s32[]{:S(2)}) async-start(s8[12582912]{0:T(1024)(128)(4,1)} %bitcast.179), calls=%async_computation.5 | async-start | bytes 8388608
  265.4 6.0 %slice-start.2 = ((s8[12582912]{0:T(1024)(128)(4,1)}), s8[4194304]{0:T(1024)(128)(4,1)S(1)}, s32[]{:S(2)}) async-start(s8[12582912]{0:T(1024)(128)(4,1)} %bitcast.179), calls=%async_computation.6 | async-start | bytes 8388608
  280.6 3.1 %copy-start.21 = (f32[512,1,256]{0,2,1:T(8,128)S(1)}, f32[512,1,256]{0,2,1:T(8,128)}, u32[]{:S(2)}) copy-start(f32[512,1,256]{0,2,1:T(8,128)} %copy.75) | copy-start | bytes 1572868
  280.6 3.1 %copy-start.35 = (f32[1,8,2,16,512]{4,3,0,2,1:T(8,128)S(1)}, f32[1,8,2,16,512]{4,3,0,2,1:T(8,128)}, u32[]{:S(2)}) copy-start(f32[1,8,2,16,512]{4,3,0,2,1:T(8,128)} %get-tuple-element.5) | copy-start | bytes 1572868
  291.9 1.9 copy-start.2
  291.9 2.7 slice-start.3
  293.8 2.8 copy-start.1
Sparse Core Ops, SparseCore 0:
  146.5 111.9 all-gather.1

commit v4 on v3

--- a/solution.py
+++ b/solution.py
@@ -37,6 +37,19 @@
     first_hop = [None] * sections
     own = jnp.zeros_like(lead)
     settled = mm(inverse, lead)
+
+    def tree_round(buf, root, level):
+        step = 2**level
+        pairs = [
+            (root + q, root + q + step)
+            for q in range(step)
+            if root + q + step < sections
+        ]
+        if not pairs:
+            return buf, None
+        got = lax.ppermute(buf, AXES, pairs)
+        return buf + got, got
+
     for section in range(sections):
         chain = settled
         if section >= 1:
@@ -48,19 +61,12 @@
         here = device == section
         own = jnp.where(here, solved, own)
         buf = jnp.where(here, solved, jnp.zeros_like(solved))
-        for level in range(3):
-            step = 2**level
-            pairs = [
-                (section + q, section + q + step)
-                for q in range(step)
-                if section + q + step < sections
-            ]
-            if pairs:
-                got = lax.ppermute(buf, AXES, pairs)
-                if level == 0:
-                    first_hop[section] = got
-                buf = buf + got
-            after[section][level] = buf
+        after[section][0], first_hop[section] = tree_round(buf, section, 0)
+        for level in (1, 2):
+            root = section - level
+            if root >= 0:
+                held, _ = lax.optimization_barrier((after[root][level - 1], solved))
+                after[root][level], _ = tree_round(held, root, level)
         if section - 3 >= 0:
             settled = settled - mm(low[section - 3], after[section - 3][2])
 

time: 305 us -> 316 us (1.036)
  starting transfers between devices: 73.1 us -> 83.9 us
    all_to_all x2, starting transfers between devices: 49.6 us -> 60.3 us  [transpose_in(): lax.all_to_all(pieces, AXES, split_axis=2, concat_axis=0, tiled=True)]
    unnamed x79 -> x87, local copies, waits for them, and re-layouts: 11.8 us -> 9.54 us
  transfers between devices with their start and end apart: 21 -> 21, of which waited for: 4 -> 4; matrix products, arithmetic and copies ran while one was open for 21% -> 18% of each run, Pallas kernels for 0% -> 0%
where the time goes in v4:
time: 316 us; the launch traced here: 315 us
  starting transfers between devices  83.9 us (27%)
  waiting for transfers between devices  72.3 us (23%)
  matrix products  69.6 us (22%)
  local copies, waits for them, and re-layouts  33.4 us (11%)
  blocking collectives  24 us (8%)
  other arithmetic  17.6 us (6%)
  between operations  14.2 us (4%)
    all_to_all x2, starting transfers between devices, transpose_in(): lax.all_to_all(pieces, AXES, split_axis=2, concat_axis=0, tiled=True)  60.3 us
    all_to_all x2, waiting for transfers between devices, transpose_in(): lax.all_to_all(pieces, AXES, split_axis=2, concat_axis=0, tiled=True)  48.6 us
    dot_general x25, matrix products, mm(): return jnp.dot(a, b, precision=HI, preferred_element_type=jnp.float32)  40.2 us
    dot_general x8, matrix products, per_device(): jnp.einsum('jrc,cs->jrs', panels[section], whole[section * width_block:(s...  29.4 us
    all_to_all x1, blocking collectives, per_device(): lax.all_to_all(own.reshape(rows, cut, -1), 'row', 0, 0, tiled=True)[0]  24 us
    all_gather x1, waiting for transfers between devices, per_device(): gathered = lax.all_gather(mine, AXES, tiled=True)  22.6 us
    ppermute x17, starting transfers between devices, tree_round(): got = lax.ppermute(buf, AXES, pairs)  22.3 us
    add x10, other arithmetic, tree_round(): return (buf + got, got)  14.9 us
  transfers between devices with their start and end apart: 21, of which 4 were waited for; matrix products, arithmetic and copies ran while one was open for 18% of the time, Pallas kernels for 0%

profile of v4, /device:TPU:1, one launch (start us, length us, event | category | flops | bytes accessed | tf_op | source)
XLA Modules:
  0.0 315.0 jit_solution(1020571771374842821)
XLA Ops:
  6.5 2.6 copy.119
  9.2 1.7 copy-done.3
  12.1 11.5 %all-to-all-start = ((f32[4,1,128,256]{3,0,1,2:T(4,128)}), f32[4,1,128,256]{3,0,1,2:T(4,128)S(1)}, u32[]{:S(2)}, u32[]{:S(2)}) async-start(f32[4,1,128,256]{3,0,1,2:T(4,128)} %copy.74), calls=%async_computation | async-start | bytes 1048576 | tf_op jit(solution)/shard_map/all_to_all | solution.py:16
  23.6 13.3 %all-to-all-done = f32[4,1,128,256]{3,0,1,2:T(4,128)S(1)} async-done(((f32[4,1,128,256]{3,0,1,2:T(4,128)}), f32[4,1,128,256]{3,0,1,2:T(4,128)S(1)}, u32[]{:S(2)}, u32[]{:S(2)}) %all-to-all-start) | async-done | bytes 524320 | tf_op jit(solution)/shard_map/all_to_all | solution.py:16
  37.5 1.4 copy.75
  38.9 1.7 broadcast_select_fusion.6
  40.6 1.5 collective-permute-start
  42.0 1.3 fusion.67
  43.4 2.0 add.58
  45.4 2.7 broadcast_select_fusion.5
  48.1 1.5 collective-permute-start.1
  49.5 1.5 collective-permute-start.2
  52.4 1.4 add.59
  54.5 1.6 fusion.102
  56.1 2.3 add.61
  58.4 2.7 broadcast_select_fusion.4
  61.1 1.5 collective-permute-start.4
  62.5 1.5 collective-permute-start.5
  64.0 1.4 fusion.63
  65.4 1.5 collective-permute-start.3
  69.6 2.3 add.64
  71.9 2.7 broadcast_select_fusion.3
  74.6 1.5 collective-permute-start.7
  76.0 1.4 fusion.61
  77.4 1.5 collective-permute-start.6
  79.8 1.9 convolution_subtract_fusion.7
  81.7 1.5 add.65
  85.5 1.6 broadcast_select_fusion.2
  87.2 1.5 collective-permute-start.10
  88.7 1.4 fusion.59
  90.1 1.5 collective-permute-start.9
  92.6 1.9 convolution_subtract_fusion.5
  94.5 1.5 add.68
  97.6 1.7 broadcast_select_fusion.1
  99.2 1.4 collective-permute-start.14
  100.7 1.4 fusion.55
  102.8 2.1 convolution_subtract_fusion.3
  104.9 2.0 fusion.49
  107.8 1.7 broadcast_select_fusion
  109.5 1.4 collective-permute-start.15
  111.8 1.5 collective-permute-start.16
  113.3 1.5 fusion.57
  115.5 1.7 fusion.106
  117.2 1.9 fusion.47
  120.2 24.0 %all_to_all.35 = f32[8,32,512]{2,1,0:T(8,128)S(1)} all-to-all(f32[8,32,512]{2,1,0:T(8,128)S(1)} %bitcast.184), channel_id=1, replica_groups=mesh['row'=8,'col'=16] {'row'}, dimensions={0} | all-to-all | bytes 1048576 | tf_op jit(solution)/shard_map/all_to_all | solution.py:76
  147.1 1.9 slice.154
  149.1 3.2 %copy.76 = f32[4,5,128,256]{3,0,1,2:T(4,128)} copy(f32[4,5,128,256]{3,2,1,0:T(8,128)S(1)} %slice.154) | data formatting | bytes 5242880 | tf_op jit(solution)/shard_map/slice | solution.py:27
  152.3 48.8 %all-to-all-start.1 = ((f32[4,5,128,256]{3,0,1,2:T(4,128)}), f32[4,5,128,256]{3,0,1,2:T(4,128)}, u32[]{:S(2)}, u32[]{:S(2)}) async-start(f32[4,5,128,256]{3,0,1,2:T(4,128)} %copy.76), calls=%async_computation.1 | async-start | bytes 5242880 | tf_op jit(solution)/shard_map/all_to_all | solution.py:16
  201.1 35.4 %all-to-all-done.1 = f32[4,5,128,256]{3,0,1,2:T(4,128)} async-done(((f32[4,5,128,256]{3,0,1,2:T(4,128)}), f32[4,5,128,256]{3,0,1,2:T(4,128)}, u32[]{:S(2)}, u32[]{:S(2)}) %all-to-all-start.1) | async-done | bytes 2621472 | tf_op jit(solution)/shard_map/all_to_all | solution.py:16
  236.5 3.7 %copy.77 = f32[128,4,5,1,256]{4,1,0,2,3:T(4,128)} copy(f32[128,4,5,1,256]{4,1,2,0,3:T(4,128)} %bitcast.13) | data formatting | bytes 5242880 | tf_op jit(solution)/shard_map/all_to_all | solution.py:16
  240.2 4.0 %reshape.32 = f32[512,5,256]{2,0,1:T(8,128)} reshape(f32[128,4,5,1,256]{4,1,0,2,3:T(4,128)} %copy.77) | data formatting | bytes 5242880 | tf_op jit(solution)/shard_map/reshape | solution.py:17
  244.2 3.3 %copy.78 = f32[512,5,256]{0,2,1:T(8,128)} copy(f32[512,5,256]{2,0,1:T(8,128)} %reshape.32) | data formatting | bytes 5242880 | tf_op jit(solution)/shard_map/reshape | solution.py:17
  247.5 22.6 %all-gather.2.cloned.1.call-done = f32[2048,512]{1,0:T(8,128)} async-done(((f32[16,512]{1,0:T(8,128)}), f32[2048,512]{1,0:T(8,128)}) %all-gather.2.cloned.1.call-update) | async-done | bytes 4194320 | tf_op jit(solution)/shard_map/all_gather | solution.py:88
  270.1 3.8 %fusion.101 = (f32[1,8,2,16,512]{4,3,0,2,1:T(8,128)}, f32[1,8,2,16,512]{4,3,0,2,1:T(8,128)S(1)}, f32[1,8,2,16,512]{4,3,0,2,1:T(8,128)S(1)}, f32[1,8,2,16,512]{4,...) fusion(f32[8,8,2,16,512]{4,3,0,2,1:T(8,128)} %bitcast.186), kind=kLoop, calls=%fused_computation.123 | loop fusion | bytes 8388608 | tf_op jit(solution)/shard_map/slice | solution.py:100
  273.9 3.0 fusion.8
  276.9 3.0 fusion.10
  279.9 2.9 fusion.12
  282.9 3.1 fusion.14
  286.0 3.1 fusion.16
  289.1 3.1 fusion.18
  292.2 3.1 fusion.20
  295.3 8.1 %fusion.6 = f32[6,256,512]{2,1,0:T(8,128)} fusion(f32[5,256,512]{2,1,0:T(8,128)} %bitcast.183, f32[1,256,512]{2,1,0:T(8,128)S(1)} %bitcast.185, f32[512,6,256]{0,2,1:T(8,128)S(1)} %fusion.8, f32[512,6,256]{0,2,1:T(8,128)S(1)} %fusion.10, f32[512,6,256]{0,2,1:T(8,128)S(1)} %fusion.12, f32[512,6,256]{0,2,1:T(8,128)} %fusion.14, f32[512,6,256]{0,2,1:T(8,128)} %fusion.16, ...), kind=kOutput, calls=%fused_computation.7 | convolution fusion | flops 1215037440 | bytes 30408704 | tf_op jit(solution)/shard_map/jrc,cs->jrs/dot_general | solution.py:97
  303.4 1.9 copy-done.2
  306.1 2.0 pad_maximum_fusion
  (127 shorter events, 20.3 us)
Async XLA Ops:
  6.5 32.4 %copy-start = (f32[8,256,256]{2,1,0:T(8,128)S(1)}, f32[8,256,256]{2,1,0:T(8,128)}, u32[]{:S(2)}) copy-start(f32[8,256,256]{2,1,0:T(8,128)} %param.5) | copy-start | bytes 6291460
  9.2 1.7 copy-start.3
  12.1 24.8 %all-to-all-start = ((f32[4,1,128,256]{3,0,1,2:T(4,128)}), f32[4,1,128,256]{3,0,1,2:T(4,128)S(1)}, u32[]{:S(2)}, u32[]{:S(2)}) async-start(f32[4,1,128,256]{3,0,1,2:T(4,128)} %copy.74), calls=%async_computation | async-start | bytes 1048576 | tf_op jit(solution)/shard_map/all_to_all | solution.py:16
  23.6 246.5 %all-gather.2.cloned.1.call-start = ((), (), s32[]{:S(2)}) async-start(), calls=%async_computation.3 | async-start | bytes 4227072 | tf_op jit(solution)/shard_map/all_gather | solution.py:88
  40.6 2.8 collective-permute-start
  43.4 2.1 copy-start.27
  48.1 4.3 %collective-permute-start.1 = (f32[256,512]{1,0:T(8,128)}, f32[256,512]{1,0:T(8,128)}, u32[]{:S(2)}, u32[]{:S(2)}) collective-permute-start(f32[256,512]{1,0:T(8,128)} %add.58), channel_id=1, source_target_pairs={{0,2},{1,3}} | collective-permute-start | bytes 1572872 | tf_op jit(solution)/shard_map/ppermute | solution.py:50
  49.5 6.6 %collective-permute-start.2 = (f32[256,512]{1,0:T(8,128)}, f32[256,512]{1,0:T(8,128)}, u32[]{:S(2)}, u32[]{:S(2)}) collective-permute-start(f32[256,512]{1,0:T(8,128)} %get-tuple-element.35), channel_id=1, source_target_pairs={{1,2}} | collective-permute-start | bytes 1572872 | tf_op jit(solution)/shard_map/ppermute | solution.py:50
  52.3 15.9 %copy-start.26 = (f32[256,256]{1,0:T(8,128)}, f32[256,256]{1,0:T(8,128)S(1)}, u32[]{:S(2)}) copy-start(f32[256,256]{1,0:T(8,128)S(1)} %fusion.65) | copy-start | bytes 786436
  53.7 0.8 copy-start.10
  56.1 2.3 copy-start.19
  61.1 5.8 %collective-permute-start.4 = (f32[256,512]{1,0:T(8,128)}, f32[256,512]{1,0:T(8,128)}, u32[]{:S(2)}, u32[]{:S(2)}) collective-permute-start(f32[256,512]{1,0:T(8,128)} %add.61), channel_id=1, source_target_pairs={{1,3},{2,4}} | collective-permute-start | bytes 1572872 | tf_op jit(solution)/shard_map/ppermute | solution.py:50
  62.5 7.1 %collective-permute-start.5 = (f32[256,512]{1,0:T(8,128)}, f32[256,512]{1,0:T(8,128)}, u32[]{:S(2)}, u32[]{:S(2)}) collective-permute-start(f32[256,512]{1,0:T(8,128)} %get-tuple-element.37), channel_id=1, source_target_pairs={{2,3}} | collective-permute-start | bytes 1572872 | tf_op jit(solution)/shard_map/ppermute | solution.py:50
  64.0 7.9 %copy-start.20 = (f32[256,512]{1,0:T(8,128)S(1)}, f32[256,512]{1,0:T(8,128)}, u32[]{:S(2)}) copy-start(f32[256,512]{1,0:T(8,128)} %copy-done.19) | copy-start | bytes 1572868
  65.4 9.2 %copy-start.24 = (f32[256,256]{1,0:T(8,128)}, f32[256,256]{1,0:T(8,128)S(1)}, u32[]{:S(2)}) copy-start(f32[256,256]{1,0:T(8,128)S(1)} %fusion.63) | copy-start | bytes 786436
  65.4 14.3 %collective-permute-start.3 = (f32[256,512]{1,0:T(8,128)}, f32[256,512]{1,0:T(8,128)}, u32[]{:S(2)}, u32[]{:S(2)}) collective-permute-start(f32[256,512]{1,0:T(8,128)} %copy-done.10), channel_id=1, source_target_pairs={{0,4},{1,5},{2,6},{3,7}} | collective-permute-start | bytes 1572872 | tf_op jit(solution)/shard_map/ppermute | solution.py:50
  69.6 2.3 copy-start.13
  74.6 7.1 %collective-permute-start.7 = (f32[256,512]{1,0:T(8,128)}, f32[256,512]{1,0:T(8,128)}, u32[]{:S(2)}, u32[]{:S(2)}) collective-permute-start(f32[256,512]{1,0:T(8,128)} %add.64), channel_id=1, source_target_pairs={{2,4},{3,5}} | collective-permute-start | bytes 1572872 | tf_op jit(solution)/shard_map/ppermute | solution.py:50
  76.0 8.0 %copy-start.25 = (f32[256,256]{1,0:T(8,128)S(1)}, f32[256,256]{1,0:T(8,128)}, u32[]{:S(2)}) copy-start(f32[256,256]{1,0:T(8,128)} %copy-done.24) | copy-start | bytes 786436
  76.0 8.6 %copy-start.37 = (f32[256,512]{1,0:T(8,128)S(1)}, f32[256,512]{1,0:T(8,128)}, u32[]{:S(2)}) copy-start(f32[256,512]{1,0:T(8,128)} %get-tuple-element.39) | copy-start | bytes 1572868
  77.4 15.1 %collective-permute-start.6 = (f32[256,512]{1,0:T(8,128)}, f32[256,512]{1,0:T(8,128)}, u32[]{:S(2)}, u32[]{:S(2)}) collective-permute-start(f32[256,512]{1,0:T(8,128)} %copy-done.7), channel_id=1, source_target_pairs={{1,5},{2,6},{3,7}} | collective-permute-start | bytes 1572872 | tf_op jit(solution)/shard_map/ppermute | solution.py:50
  78.9 6.6 %copy-start.14 = (f32[256,512]{1,0:T(8,128)S(1)}, f32[256,512]{1,0:T(8,128)}, u32[]{:S(2)}) copy-start(f32[256,512]{1,0:T(8,128)} %copy-done.13) | copy-start | bytes 1572868
  78.9 5.7 %collective-permute-start.8 = (f32[256,512]{1,0:T(8,128)}, f32[256,512]{1,0:T(8,128)S(1)}, u32[]{:S(2)}, u32[]{:S(2)}) collective-permute-start(f32[256,512]{1,0:T(8,128)} %get-tuple-element.39), channel_id=1, source_target_pairs={{3,4}} | collective-permute-start | bytes 1572872 | tf_op jit(solution)/shard_map/ppermute | solution.py:50
  81.7 5.5 %copy-start.21 = (f32[256,512]{1,0:T(8,128)}, f32[256,512]{1,0:T(8,128)S(1)}, u32[]{:S(2)}) copy-start(f32[256,512]{1,0:T(8,128)S(1)} %convolution_subtract_fusion.7) | copy-start | bytes 1572868
  83.2 0.8 copy-start.9
  84.6 2.6 copy-start.15
  84.6 7.9 %copy-start.8 = (f32[256,512]{1,0:T(8,128)S(1)}, f32[256,512]{1,0:T(8,128)}, u32[]{:S(2)}) copy-start(f32[256,512]{1,0:T(8,128)} %copy-done.7) | copy-start | bytes 1572868
  87.2 7.3 %collective-permute-start.10 = (f32[256,512]{1,0:T(8,128)}, f32[256,512]{1,0:T(8,128)}, u32[]{:S(2)}, u32[]{:S(2)}) collective-permute-start(f32[256,512]{1,0:T(8,128)} %add.67), channel_id=1, source_target_pairs={{3,5},{4,6}} | collective-permute-start | bytes 1572872 | tf_op jit(solution)/shard_map/ppermute | solution.py:50
  88.7 8.0 %copy-start.38 = (f32[256,512]{1,0:T(8,128)S(1)}, f32[256,512]{1,0:T(8,128)}, u32[]{:S(2)}) copy-start(f32[256,512]{1,0:T(8,128)} %get-tuple-element.41) | copy-start | bytes 1572868
  90.0 7.5 %copy-start.28 = (f32[256,256]{1,0:T(8,128)}, f32[256,256]{1,0:T(8,128)S(1)}, u32[]{:S(2)}) copy-start(f32[256,256]{1,0:T(8,128)S(1)} %fusion.59) | copy-start | bytes 786436
  90.1 12.8 %collective-permute-start.9 = (f32[256,512]{1,0:T(8,128)}, f32[256,512]{1,0:T(8,128)}, u32[]{:S(2)}, u32[]{:S(2)}) collective-permute-start(f32[256,512]{1,0:T(8,128)} %copy-done.9), channel_id=1, source_target_pairs={{2,6},{3,7}} | collective-permute-start | bytes 1572872 | tf_op jit(solution)/shard_map/ppermute | solution.py:50
  91.5 6.1 %copy-start.16 = (f32[256,512]{1,0:T(8,128)S(1)}, f32[256,512]{1,0:T(8,128)}, u32[]{:S(2)}) copy-start(f32[256,512]{1,0:T(8,128)} %copy-done.15) | copy-start | bytes 1572868
  91.5 5.1 %collective-permute-start.11 = (f32[256,512]{1,0:T(8,128)}, f32[256,512]{1,0:T(8,128)S(1)}, u32[]{:S(2)}, u32[]{:S(2)}) collective-permute-start(f32[256,512]{1,0:T(8,128)} %get-tuple-element.41), channel_id=1, source_target_pairs={{4,5}} | collective-permute-start | bytes 1572872 | tf_op jit(solution)/shard_map/ppermute | solution.py:50
  94.5 4.8 %copy-start.22 = (f32[256,512]{1,0:T(8,128)}, f32[256,512]{1,0:T(8,128)S(1)}, u32[]{:S(2)}) copy-start(f32[256,512]{1,0:T(8,128)S(1)} %convolution_subtract_fusion.5) | copy-start | bytes 1572868
  96.6 2.7 copy-start.17
  99.2 5.7 %collective-permute-start.14 = (f32[256,512]{1,0:T(8,128)}, f32[256,512]{1,0:T(8,128)}, u32[]{:S(2)}, u32[]{:S(2)}) collective-permute-start(f32[256,512]{1,0:T(8,128)} %add.70), channel_id=1, source_target_pairs={{4,6},{5,7}} | collective-permute-start | bytes 1572872 | tf_op jit(solution)/shard_map/ppermute | solution.py:50
  100.7 4.2 %copy-start.29 = (f32[256,256]{1,0:T(8,128)S(1)}, f32[256,256]{1,0:T(8,128)}, u32[]{:S(2)}) copy-start(f32[256,256]{1,0:T(8,128)} %copy-done.28) | copy-start | bytes 786436
  100.7 7.1 %copy-start.18 = (f32[256,512]{1,0:T(8,128)S(1)}, f32[256,512]{1,0:T(8,128)}, u32[]{:S(2)}) copy-start(f32[256,512]{1,0:T(8,128)} %copy-done.17) | copy-start | bytes 1572868
  102.1 7.4 %copy-start.30 = (f32[256,256]{1,0:T(8,128)}, f32[256,256]{1,0:T(8,128)S(1)}, u32[]{:S(2)}) copy-start(f32[256,256]{1,0:T(8,128)S(1)} %fusion.55) | copy-start | bytes 786436
  102.1 4.9 %collective-permute-start.13 = (f32[256,512]{1,0:T(8,128)}, f32[256,512]{1,0:T(8,128)S(1)}, u32[]{:S(2)}, u32[]{:S(2)}) collective-permute-start(f32[256,512]{1,0:T(8,128)} %get-tuple-element.43), channel_id=1, source_target_pairs={{5,6}} | collective-permute-start | bytes 1572872 | tf_op jit(solution)/shard_map/ppermute | solution.py:50
  104.9 6.9 %copy-start.11 = (f32[256,512]{1,0:T(8,128)}, f32[256,512]{1,0:T(8,128)S(1)}, u32[]{:S(2)}) copy-start(f32[256,512]{1,0:T(8,128)S(1)} %convolution_subtract_fusion.3) | copy-start | bytes 1572868
  104.9 6.0 %copy-start.36 = (f32[256,512]{1,0:T(8,128)S(1)}, f32[256,512]{1,0:T(8,128)}, u32[]{:S(2)}) copy-start(f32[256,512]{1,0:T(8,128)} %get-tuple-element.43) | copy-start | bytes 1572868
  107.0 0.8 copy-start.5
  109.5 6.0 %collective-permute-start.15 = (f32[256,512]{1,0:T(8,128)}, f32[256,512]{1,0:T(8,128)}, u32[]{:S(2)}, u32[]{:S(2)}) collective-permute-start(f32[256,512]{1,0:T(8,128)} %get-tuple-element.45), channel_id=1, source_target_pairs={{6,7}} | collective-permute-start | bytes 1572872 | tf_op jit(solution)/shard_map/ppermute | solution.py:50
  111.8 5.4 %collective-permute-start.16 = (f32[256,512]{1,0:T(8,128)}, f32[256,512]{1,0:T(8,128)}, u32[]{:S(2)}, u32[]{:S(2)}) collective-permute-start(f32[256,512]{1,0:T(8,128)} %add.72), channel_id=1, source_target_pairs={{5,7}} | collective-permute-start | bytes 1572872 | tf_op jit(solution)/shard_map/ppermute | solution.py:50
  113.3 5.8 %copy-start.6 = (f32[256,512]{1,0:T(8,128)S(1)}, f32[256,512]{1,0:T(8,128)}, u32[]{:S(2)}) copy-start(f32[256,512]{1,0:T(8,128)} %copy-done.5) | copy-start | bytes 1572868
  113.3 5.9 %copy-start.12 = (f32[256,512]{1,0:T(8,128)S(1)}, f32[256,512]{1,0:T(8,128)}, u32[]{:S(2)}) copy-start(f32[256,512]{1,0:T(8,128)} %copy-done.11) | copy-start | bytes 1572868
  113.3 5.9 %copy-start.31 = (f32[256,512]{1,0:T(8,128)S(1)}, f32[256,512]{1,0:T(8,128)}, u32[]{:S(2)}) copy-start(f32[256,512]{1,0:T(8,128)} %get-tuple-element.36) | copy-start | bytes 1572868
  113.3 5.9 %copy-start.32 = (f32[256,512]{1,0:T(8,128)S(1)}, f32[256,512]{1,0:T(8,128)}, u32[]{:S(2)}) copy-start(f32[256,512]{1,0:T(8,128)} %get-tuple-element.38) | copy-start | bytes 1572868
  113.3 5.9 %copy-start.33 = (f32[256,512]{1,0:T(8,128)S(1)}, f32[256,512]{1,0:T(8,128)}, u32[]{:S(2)}) copy-start(f32[256,512]{1,0:T(8,128)} %get-tuple-element.40) | copy-start | bytes 1572868
  113.3 5.9 %copy-start.34 = (f32[256,512]{1,0:T(8,128)S(1)}, f32[256,512]{1,0:T(8,128)}, u32[]{:S(2)}) copy-start(f32[256,512]{1,0:T(8,128)} %get-tuple-element.42) | copy-start | bytes 1572868
  113.3 5.9 %copy-start.35 = (f32[256,512]{1,0:T(8,128)S(1)}, f32[256,512]{1,0:T(8,128)}, u32[]{:S(2)}) copy-start(f32[256,512]{1,0:T(8,128)} %get-tuple-element.44) | copy-start | bytes 1572868
  114.8 4.3 %collective-permute-start.12 = (f32[256,512]{1,0:T(8,128)S(1)}, f32[256,512]{1,0:T(8,128)S(1)}, u32[]{:S(2)}, u32[]{:S(2)}) collective-permute-start(f32[256,512]{1,0:T(8,128)S(1)} %add.68), channel_id=1, source_target_pairs={{3,7}} | collective-permute-start | bytes 1572872 | tf_op jit(solution)/shard_map/ppermute | solution.py:50
  120.2 28.9 %copy-start.4 = (f32[256,512]{1,0:T(8,128)}, f32[256,512]{1,0:T(8,128)S(1)}, u32[]{:S(2)}) copy-start(f32[256,512]{1,0:T(8,128)S(1)} %fusion.35) | copy-start | bytes 1572868
  144.2 2.3 collective-permute-start.17
  152.3 84.2 %all-to-all-start.1 = ((f32[4,5,128,256]{3,0,1,2:T(4,128)}), f32[4,5,128,256]{3,0,1,2:T(4,128)}, u32[]{:S(2)}, u32[]{:S(2)}) async-start(f32[4,5,128,256]{3,0,1,2:T(4,128)} %copy.76), calls=%async_computation.1 | async-start | bytes 5242880 | tf_op jit(solution)/shard_map/all_to_all | solution.py:16
  270.1 12.8 %slice-start = ((s8[12582912]{0:T(1024)(128)(4,1)}), s8[4194304]{0:T(1024)(128)(4,1)S(1)}, s32[]{:S(2)}) async-start(s8[12582912]{0:T(1024)(128)(4,1)} %bitcast.179), calls=%async_computation.4 | async-start | bytes 8388608
  270.1 12.8 %slice-start.1 = ((s8[12582912]{0:T(1024)(128)(4,1)}), s8[4194304]{0:T(1024)(128)(4,1)S(1)}, s32[]{:S(2)}) async-start(s8[12582912]{0:T(1024)(128)(4,1)} %bitcast.179), calls=%async_computation.5 | async-start | bytes 8388608
  276.9 6.0 %slice-start.2 = ((s8[12582912]{0:T(1024)(128)(4,1)}), s8[4194304]{0:T(1024)(128)(4,1)S(1)}, s32[]{:S(2)}) async-start(s8[12582912]{0:T(1024)(128)(4,1)} %bitcast.179), calls=%async_computation.6 | async-start | bytes 8388608
  292.2 3.1 copy-start.23
  292.2 3.1 copy-start.39
  303.4 1.9 copy-start.2
  303.4 2.7 slice-start.3
  305.3 2.8 copy-start.1
  (1 other events, 0.8 us)
Sparse Core Ops, SparseCore 0:
  147.3 122.7 all-gather.1

commit v5 on v4

--- a/solution.py
+++ b/solution.py
@@ -7,8 +7,12 @@
 HI = lax.Precision.HIGHEST
 
 
-def mm(a, b):
-    return jnp.dot(a, b, precision=HI, preferred_element_type=jnp.float32)
+def mm(a, b, precision=HI):
+    return jnp.dot(a, b, precision=precision, preferred_element_type=jnp.float32)
+
+
+def mm3(a, b):
+    return mm(a, b, lax.Precision.HIGH)
 
 
 def transpose_in(pieces, devices):
@@ -31,12 +35,12 @@
     inverse = lax.dynamic_index_in_dim(
         diag_inverse, jnp.minimum(device, sections - 1), 0, keepdims=False
     )
-    low = jnp.stack([mm(inverse, panels[k, 0]) for k in range(sections - 1)])
+    low = jnp.stack([mm3(inverse, panels[k, 0]) for k in range(sections - 1)])
 
     after = [[None] * 3 for _ in range(sections)]
-    first_hop = [None] * sections
+    received = [[None] * 3 for _ in range(sections)]
     own = jnp.zeros_like(lead)
-    settled = mm(inverse, lead)
+    settled = mm3(inverse, lead)
 
     def tree_round(buf, root, level):
         step = 2**level
@@ -53,22 +57,22 @@
     for section in range(sections):
         chain = settled
         if section >= 1:
-            chain = chain - mm(low[section - 1], first_hop[section - 1])
+            chain = chain - mm3(low[section - 1], received[section - 1][0])
         for back in (2, 3):
             if section - back >= 0:
-                chain = chain - mm(low[section - back], after[section - back][1])
+                chain = chain - mm3(low[section - back], received[section - back][1])
         solved = chain
         here = device == section
         own = jnp.where(here, solved, own)
         buf = jnp.where(here, solved, jnp.zeros_like(solved))
-        after[section][0], first_hop[section] = tree_round(buf, section, 0)
+        after[section][0], received[section][0] = tree_round(buf, section, 0)
         for level in (1, 2):
             root = section - level
             if root >= 0:
                 held, _ = lax.optimization_barrier((after[root][level - 1], solved))
-                after[root][level], _ = tree_round(held, root, level)
-        if section - 3 >= 0:
-            settled = settled - mm(low[section - 3], after[section - 3][2])
+                after[root][level], received[root][level] = tree_round(held, root, level)
+        if section - 3 >= 0 and received[section - 3][2] is not None:
+            settled = settled - mm3(low[section - 3], received[section - 3][2])
 
     rows = lax.axis_size("row")
     halves = cols // sections

time: 316 us -> 313 us (level)
  starting transfers between devices: 83.9 us -> 80.3 us
  local copies, waits for them, and re-layouts: 33.4 us -> 30 us
    all_to_all x2, starting transfers between devices: 60.3 us -> 56.4 us  [transpose_in(): lax.all_to_all(pieces, AXES, split_axis=2, concat_axis=0, tiled=True)]
    unnamed x87 -> x57, local copies, waits for them, and re-layouts: 9.54 us -> 6.3 us
  transfers between devices with their start and end apart: 21 -> 21, of which waited for: 4 -> 4; matrix products, arithmetic and copies ran while one was open for 18% -> 19% of each run, Pallas kernels for 0% -> 0%
where the time goes in v5:
time: 313 us; the launch traced here: 311 us
  starting transfers between devices  80.3 us (26%)
  waiting for transfers between devices  72.3 us (23%)
  matrix products  69.3 us (22%)
  local copies, waits for them, and re-layouts  30 us (10%)
  blocking collectives  24.3 us (8%)
  other arithmetic  20.6 us (7%)
  between operations  14 us (4%)
    all_to_all x2, starting transfers between devices, transpose_in(): lax.all_to_all(pieces, AXES, split_axis=2, concat_axis=0, tiled=True)  56.4 us
    all_to_all x2, waiting for transfers between devices, transpose_in(): lax.all_to_all(pieces, AXES, split_axis=2, concat_axis=0, tiled=True)  48.6 us
    dot_general x25, matrix products, mm(): jnp.dot(a, b, precision=precision, preferred_element_type=jnp.float32)  39.9 us
    dot_general x8, matrix products, per_device(): jnp.einsum('jrc,cs->jrs', panels[section], whole[section * width_block:(s...  29.4 us
    all_to_all x1, blocking collectives, per_device(): lax.all_to_all(own.reshape(rows, cut, -1), 'row', 0, 0, tiled=True)[0]  24.3 us
    ppermute x17, starting transfers between devices, tree_round(): got = lax.ppermute(buf, AXES, pairs)  22.7 us
    all_gather x1, waiting for transfers between devices, per_device(): gathered = lax.all_gather(mine, AXES, tiled=True)  22.6 us
    add x10, other arithmetic, tree_round(): return (buf + got, got)  17.9 us
  transfers between devices with their start and end apart: 21, of which 4 were waited for; matrix products, arithmetic and copies ran while one was open for 19% of the time, Pallas kernels for 0%

profile of v5, /device:TPU:1, one launch (start us, length us, event | category | flops | bytes accessed | tf_op | source)
XLA Modules:
  0.0 310.9 jit_solution(7774161787154247455)
XLA Ops:
  6.5 2.6 copy.119
  9.2 1.7 copy-done.3
  12.0 11.5 %all-to-all-start = ((f32[4,1,128,256]{3,0,1,2:T(4,128)}), f32[4,1,128,256]{3,0,1,2:T(4,128)S(1)}, u32[]{:S(2)}, u32[]{:S(2)}) async-start(f32[4,1,128,256]{3,0,1,2:T(4,128)} %copy.74), calls=%async_computation | async-start | bytes 1048576 | tf_op jit(solution)/shard_map/all_to_all | solution.py:20
  23.6 13.3 %all-to-all-done = f32[4,1,128,256]{3,0,1,2:T(4,128)S(1)} async-done(((f32[4,1,128,256]{3,0,1,2:T(4,128)}), f32[4,1,128,256]{3,0,1,2:T(4,128)S(1)}, u32[]{:S(2)}, u32[]{:S(2)}) %all-to-all-start) | async-done | bytes 524320 | tf_op jit(solution)/shard_map/all_to_all | solution.py:20
  38.9 1.4 broadcast_select_fusion.6
  40.3 1.5 collective-permute-start
  43.0 2.0 add.40
  45.0 2.5 broadcast_select_fusion.5
  47.5 1.5 collective-permute-start.1
  49.0 1.4 collective-permute-start.2
  51.6 1.6 fusion.94
  53.3 2.3 add.42
  55.5 2.4 broadcast_select_fusion.4
  58.0 1.4 collective-permute-start.4
  59.4 1.5 collective-permute-start.5
  62.2 2.2 add.41
  64.4 1.5 collective-permute-start.3
  65.8 1.4 fusion.95
  67.3 2.3 add.44
  69.6 2.5 broadcast_select_fusion.3
  72.0 1.5 collective-permute-start.7
  74.8 2.1 add.43
  76.9 1.5 collective-permute-start.6
  79.1 1.5 convolution_subtract_fusion.7
  80.6 1.6 fusion.96
  83.2 1.4 broadcast_select_fusion.2
  84.6 1.5 collective-permute-start.10
  87.3 2.2 add.45
  89.5 1.5 collective-permute-start.9
  91.7 1.7 convolution_subtract_fusion.5
  93.3 1.6 fusion.97
  96.0 1.4 broadcast_select_fusion.1
  97.4 1.5 collective-permute-start.14
  101.1 1.7 convolution_subtract_fusion.3
  102.8 1.5 fusion.98
  105.3 1.4 broadcast_select_fusion
  106.7 1.4 collective-permute-start.16
  108.1 1.5 collective-permute-start.15
  109.6 2.1 add.47
  111.7 1.5 collective-permute-start.12
  113.1 1.9 fusion.49
  115.0 1.5 fusion.100
  116.6 1.5 fusion.99
  118.1 1.8 fusion.35
  119.9 24.3 %all_to_all.35 = f32[8,32,512]{2,1,0:T(8,128)S(1)} all-to-all(f32[8,32,512]{2,1,0:T(8,128)S(1)} %bitcast.190), channel_id=1, replica_groups=mesh['row'=8,'col'=16] {'row'}, dimensions={0} | all-to-all | bytes 1048576 | tf_op jit(solution)/shard_map/all_to_all | solution.py:80
  147.1 1.9 slice.154
  149.1 3.2 %copy.76 = f32[4,5,128,256]{3,0,1,2:T(4,128)} copy(f32[4,5,128,256]{3,2,1,0:T(8,128)S(1)} %slice.154) | data formatting | bytes 5242880 | tf_op jit(solution)/shard_map/slice | solution.py:31
  152.2 44.9 %all-to-all-start.1 = ((f32[4,5,128,256]{3,0,1,2:T(4,128)}), f32[4,5,128,256]{3,0,1,2:T(4,128)}, u32[]{:S(2)}, u32[]{:S(2)}) async-start(f32[4,5,128,256]{3,0,1,2:T(4,128)} %copy.76), calls=%async_computation.1 | async-start | bytes 5242880 | tf_op jit(solution)/shard_map/all_to_all | solution.py:20
  197.1 35.4 %all-to-all-done.1 = f32[4,5,128,256]{3,0,1,2:T(4,128)} async-done(((f32[4,5,128,256]{3,0,1,2:T(4,128)}), f32[4,5,128,256]{3,0,1,2:T(4,128)}, u32[]{:S(2)}, u32[]{:S(2)}) %all-to-all-start.1) | async-done | bytes 2621472 | tf_op jit(solution)/shard_map/all_to_all | solution.py:20
  232.5 3.7 %copy.77 = f32[128,4,5,1,256]{4,1,0,2,3:T(4,128)} copy(f32[128,4,5,1,256]{4,1,2,0,3:T(4,128)} %bitcast.13) | data formatting | bytes 5242880 | tf_op jit(solution)/shard_map/all_to_all | solution.py:20
  236.2 4.0 %reshape.32 = f32[512,5,256]{2,0,1:T(8,128)} reshape(f32[128,4,5,1,256]{4,1,0,2,3:T(4,128)} %copy.77) | data formatting | bytes 5242880 | tf_op jit(solution)/shard_map/reshape | solution.py:21
  240.2 3.2 %copy.78 = f32[512,5,256]{0,2,1:T(8,128)} copy(f32[512,5,256]{2,0,1:T(8,128)} %reshape.32) | data formatting | bytes 5242880 | tf_op jit(solution)/shard_map/reshape | solution.py:21
  243.4 22.6 %all-gather.2.cloned.1.call-done = f32[2048,512]{1,0:T(8,128)} async-done(((f32[16,512]{1,0:T(8,128)}), f32[2048,512]{1,0:T(8,128)}) %all-gather.2.cloned.1.call-update) | async-done | bytes 4194320 | tf_op jit(solution)/shard_map/all_gather | solution.py:92
  266.1 3.8 %fusion.93 = (f32[1,8,2,16,512]{4,3,0,2,1:T(8,128)}, f32[1,8,2,16,512]{4,3,0,2,1:T(8,128)S(1)}, f32[1,8,2,16,512]{4,3,0,2,1:T(8,128)S(1)}, f32[1,8,2,16,512]{4,3...) fusion(f32[8,8,2,16,512]{4,3,0,2,1:T(8,128)} %bitcast.192), kind=kLoop, calls=%fused_computation.115 | loop fusion | bytes 8388608 | tf_op jit(solution)/shard_map/slice | solution.py:104
  269.9 3.0 fusion.8
  272.9 3.0 fusion.10
  275.9 2.9 fusion.12
  278.9 3.1 fusion.14
  282.0 3.0 fusion.16
  285.0 3.1 fusion.18
  288.1 3.1 %fusion.20 = f32[512,6,256]{0,2,1:T(8,128)} fusion(f32[256,512,1]{1,0,2:T(8,128)S(1)} %bitcast.194, f32[8,6,256,256]{3,2,1,0:T(8,128)S(1)} %bitcast.186), kind=kOutput, calls=%fused_computation.22 | convolution fusion | flops 1207959552 | bytes 5242880 | tf_op jit(solution)/shard_map/jrc,cs->jrs/dot_general | solution.py:101
  291.3 8.1 %fusion.6 = f32[6,256,512]{2,1,0:T(8,128)} fusion(f32[5,256,512]{2,1,0:T(8,128)} %bitcast.189, f32[1,256,512]{2,1,0:T(8,128)S(1)} %bitcast.191, f32[512,6,256]{0,2,1:T(8,128)S(1)} %fusion.8, f32[512,6,256]{0,2,1:T(8,128)S(1)} %fusion.10, f32[512,6,256]{0,2,1:T(8,128)S(1)} %fusion.12, f32[512,6,256]{0,2,1:T(8,128)} %fusion.14, f32[512,6,256]{0,2,1:T(8,128)} %fusion.16, ...), kind=kOutput, calls=%fused_computation.7 | convolution fusion | flops 1215037440 | bytes 30408704 | tf_op jit(solution)/shard_map/jrc,cs->jrs/dot_general | solution.py:101
  299.4 1.9 copy-done.2
  302.1 2.0 pad_maximum_fusion
  (97 shorter events, 19.7 us)
Async XLA Ops:
  6.5 32.4 %copy-start = (f32[8,256,256]{2,1,0:T(8,128)S(1)}, f32[8,256,256]{2,1,0:T(8,128)}, u32[]{:S(2)}) copy-start(f32[8,256,256]{2,1,0:T(8,128)} %param.5) | copy-start | bytes 6291460
  9.2 1.7 copy-start.3
  12.0 24.8 %all-to-all-start = ((f32[4,1,128,256]{3,0,1,2:T(4,128)}), f32[4,1,128,256]{3,0,1,2:T(4,128)S(1)}, u32[]{:S(2)}, u32[]{:S(2)}) async-start(f32[4,1,128,256]{3,0,1,2:T(4,128)} %copy.74), calls=%async_computation | async-start | bytes 1048576 | tf_op jit(solution)/shard_map/all_to_all | solution.py:20
  23.5 242.5 %all-gather.2.cloned.1.call-start = ((), (), s32[]{:S(2)}) async-start(), calls=%async_computation.3 | async-start | bytes 4227072 | tf_op jit(solution)/shard_map/all_gather | solution.py:92
  40.3 2.7 collective-permute-start
  43.0 2.0 copy-start.18
  47.5 4.1 %collective-permute-start.1 = (f32[256,512]{1,0:T(8,128)}, f32[256,512]{1,0:T(8,128)}, u32[]{:S(2)}, u32[]{:S(2)}) collective-permute-start(f32[256,512]{1,0:T(8,128)} %add.40), channel_id=1, source_target_pairs={{0,2},{1,3}} | collective-permute-start | bytes 1572872 | tf_op jit(solution)/shard_map/ppermute | solution.py:54
  49.0 4.3 %collective-permute-start.2 = (f32[256,512]{1,0:T(8,128)}, f32[256,512]{1,0:T(8,128)}, u32[]{:S(2)}, u32[]{:S(2)}) collective-permute-start(f32[256,512]{1,0:T(8,128)} %get-tuple-element.35), channel_id=1, source_target_pairs={{1,2}} | collective-permute-start | bytes 1572872 | tf_op jit(solution)/shard_map/ppermute | solution.py:54
  51.6 14.2 %copy-start.17 = (f32[256,256]{1,0:T(8,128)}, f32[256,256]{1,0:T(8,128)S(1)}, u32[]{:S(2)}) copy-start(f32[256,256]{1,0:T(8,128)S(1)} %fusion.57) | copy-start | bytes 786436
  53.3 2.3 copy-start.12
  58.0 7.8 %collective-permute-start.4 = (f32[256,512]{1,0:T(8,128)}, f32[256,512]{1,0:T(8,128)}, u32[]{:S(2)}, u32[]{:S(2)}) collective-permute-start(f32[256,512]{1,0:T(8,128)} %add.42), channel_id=1, source_target_pairs={{1,3},{2,4}} | collective-permute-start | bytes 1572872 | tf_op jit(solution)/shard_map/ppermute | solution.py:54
  59.4 7.8 %collective-permute-start.5 = (f32[256,512]{1,0:T(8,128)}, f32[256,512]{1,0:T(8,128)}, u32[]{:S(2)}, u32[]{:S(2)}) collective-permute-start(f32[256,512]{1,0:T(8,128)} %get-tuple-element.37), channel_id=1, source_target_pairs={{2,3}} | collective-permute-start | bytes 1572872 | tf_op jit(solution)/shard_map/ppermute | solution.py:54
  60.9 8.7 %copy-start.13 = (f32[256,512]{1,0:T(8,128)S(1)}, f32[256,512]{1,0:T(8,128)}, u32[]{:S(2)}) copy-start(f32[256,512]{1,0:T(8,128)} %copy-done.12) | copy-start | bytes 1572868
  62.2 9.8 %copy-start.15 = (f32[256,256]{1,0:T(8,128)}, f32[256,256]{1,0:T(8,128)S(1)}, u32[]{:S(2)}) copy-start(f32[256,256]{1,0:T(8,128)S(1)} %fusion.55) | copy-start | bytes 786436
  64.4 14.7 %collective-permute-start.3 = (f32[256,512]{1,0:T(8,128)}, f32[256,512]{1,0:T(8,128)}, u32[]{:S(2)}, u32[]{:S(2)}) collective-permute-start(f32[256,512]{1,0:T(8,128)} %add.41), channel_id=1, source_target_pairs={{0,4},{1,5},{2,6},{3,7}} | collective-permute-start | bytes 1572872 | tf_op jit(solution)/shard_map/ppermute | solution.py:54
  67.3 2.3 copy-start.8
  72.0 8.6 %collective-permute-start.7 = (f32[256,512]{1,0:T(8,128)}, f32[256,512]{1,0:T(8,128)}, u32[]{:S(2)}, u32[]{:S(2)}) collective-permute-start(f32[256,512]{1,0:T(8,128)} %add.44), channel_id=1, source_target_pairs={{2,4},{3,5}} | collective-permute-start | bytes 1572872 | tf_op jit(solution)/shard_map/ppermute | solution.py:54
  73.5 7.1 %copy-start.16 = (f32[256,256]{1,0:T(8,128)S(1)}, f32[256,256]{1,0:T(8,128)}, u32[]{:S(2)}) copy-start(f32[256,256]{1,0:T(8,128)} %copy-done.15) | copy-start | bytes 786436
  73.5 8.8 %copy-start.21 = (f32[256,512]{1,0:T(8,128)S(1)}, f32[256,512]{1,0:T(8,128)}, u32[]{:S(2)}) copy-start(f32[256,512]{1,0:T(8,128)} %get-tuple-element.39) | copy-start | bytes 1572868
  74.8 8.4 %copy-start.9 = (f32[256,512]{1,0:T(8,128)S(1)}, f32[256,512]{1,0:T(8,128)}, u32[]{:S(2)}) copy-start(f32[256,512]{1,0:T(8,128)} %copy-done.8) | copy-start | bytes 1572868
  76.9 14.7 %collective-permute-start.6 = (f32[256,512]{1,0:T(8,128)}, f32[256,512]{1,0:T(8,128)}, u32[]{:S(2)}, u32[]{:S(2)}) collective-permute-start(f32[256,512]{1,0:T(8,128)} %add.43), channel_id=1, source_target_pairs={{1,5},{2,6},{3,7}} | collective-permute-start | bytes 1572872 | tf_op jit(solution)/shard_map/ppermute | solution.py:54
  78.4 3.9 %collective-permute-start.8 = (f32[256,512]{1,0:T(8,128)}, f32[256,512]{1,0:T(8,128)S(1)}, u32[]{:S(2)}, u32[]{:S(2)}) collective-permute-start(f32[256,512]{1,0:T(8,128)} %get-tuple-element.39), channel_id=1, source_target_pairs={{3,4}} | collective-permute-start | bytes 1572872 | tf_op jit(solution)/shard_map/ppermute | solution.py:54
  80.6 3.9 %copy-start.5 = (f32[256,512]{1,0:T(8,128)}, f32[256,512]{1,0:T(8,128)S(1)}, u32[]{:S(2)}) copy-start(f32[256,512]{1,0:T(8,128)S(1)} %convolution_subtract_fusion.7) | copy-start | bytes 1572868
  84.6 8.8 %collective-permute-start.10 = (f32[256,512]{1,0:T(8,128)}, f32[256,512]{1,0:T(8,128)}, u32[]{:S(2)}, u32[]{:S(2)}) collective-permute-start(f32[256,512]{1,0:T(8,128)} %add.46), channel_id=1, source_target_pairs={{3,5},{4,6}} | collective-permute-start | bytes 1572872 | tf_op jit(solution)/shard_map/ppermute | solution.py:54
  86.0 9.0 %copy-start.22 = (f32[256,512]{1,0:T(8,128)S(1)}, f32[256,512]{1,0:T(8,128)}, u32[]{:S(2)}) copy-start(f32[256,512]{1,0:T(8,128)} %get-tuple-element.41) | copy-start | bytes 1572868
  87.3 8.7 %copy-start.19 = (f32[256,256]{1,0:T(8,128)}, f32[256,256]{1,0:T(8,128)S(1)}, u32[]{:S(2)}) copy-start(f32[256,256]{1,0:T(8,128)S(1)} %fusion.51) | copy-start | bytes 786436
  89.5 11.6 %collective-permute-start.9 = (f32[256,512]{1,0:T(8,128)}, f32[256,512]{1,0:T(8,128)}, u32[]{:S(2)}, u32[]{:S(2)}) collective-permute-start(f32[256,512]{1,0:T(8,128)} %add.45), channel_id=1, source_target_pairs={{2,6},{3,7}} | collective-permute-start | bytes 1572872 | tf_op jit(solution)/shard_map/ppermute | solution.py:54
  91.0 4.0 %collective-permute-start.11 = (f32[256,512]{1,0:T(8,128)}, f32[256,512]{1,0:T(8,128)S(1)}, u32[]{:S(2)}, u32[]{:S(2)}) collective-permute-start(f32[256,512]{1,0:T(8,128)} %get-tuple-element.41), channel_id=1, source_target_pairs={{4,5}} | collective-permute-start | bytes 1572872 | tf_op jit(solution)/shard_map/ppermute | solution.py:54
  93.3 4.0 %copy-start.6 = (f32[256,512]{1,0:T(8,128)}, f32[256,512]{1,0:T(8,128)S(1)}, u32[]{:S(2)}) copy-start(f32[256,512]{1,0:T(8,128)S(1)} %convolution_subtract_fusion.5) | copy-start | bytes 1572868
  95.0 2.4 copy-start.10
  97.4 5.4 %collective-permute-start.14 = (f32[256,512]{1,0:T(8,128)}, f32[256,512]{1,0:T(8,128)}, u32[]{:S(2)}, u32[]{:S(2)}) collective-permute-start(f32[256,512]{1,0:T(8,128)} %add.48), channel_id=1, source_target_pairs={{4,6},{5,7}} | collective-permute-start | bytes 1572872 | tf_op jit(solution)/shard_map/ppermute | solution.py:54
  98.9 5.4 %copy-start.23 = (f32[256,512]{1,0:T(8,128)S(1)}, f32[256,512]{1,0:T(8,128)}, u32[]{:S(2)}) copy-start(f32[256,512]{1,0:T(8,128)} %get-tuple-element.43) | copy-start | bytes 1572868
  98.9 6.4 %copy-start.11 = (f32[256,512]{1,0:T(8,128)S(1)}, f32[256,512]{1,0:T(8,128)}, u32[]{:S(2)}) copy-start(f32[256,512]{1,0:T(8,128)} %copy-done.10) | copy-start | bytes 1572868
  100.2 6.5 %copy-start.20 = (f32[256,256]{1,0:T(8,128)}, f32[256,256]{1,0:T(8,128)S(1)}, u32[]{:S(2)}) copy-start(f32[256,256]{1,0:T(8,128)S(1)} %fusion.47) | copy-start | bytes 786436
  100.2 4.1 %collective-permute-start.13 = (f32[256,512]{1,0:T(8,128)}, f32[256,512]{1,0:T(8,128)S(1)}, u32[]{:S(2)}, u32[]{:S(2)}) collective-permute-start(f32[256,512]{1,0:T(8,128)} %get-tuple-element.43), channel_id=1, source_target_pairs={{5,6}} | collective-permute-start | bytes 1572872 | tf_op jit(solution)/shard_map/ppermute | solution.py:54
  104.3 7.4 %copy-start.7 = (f32[256,512]{1,0:T(8,128)}, f32[256,512]{1,0:T(8,128)S(1)}, u32[]{:S(2)}) copy-start(f32[256,512]{1,0:T(8,128)S(1)} %fusion.98) | copy-start | bytes 1572868
  106.7 8.4 %collective-permute-start.16 = (f32[256,512]{1,0:T(8,128)}, f32[256,512]{1,0:T(8,128)}, u32[]{:S(2)}, u32[]{:S(2)}) collective-permute-start(f32[256,512]{1,0:T(8,128)} %add.49), channel_id=1, source_target_pairs={{5,7}} | collective-permute-start | bytes 1572872 | tf_op jit(solution)/shard_map/ppermute | solution.py:54
  108.1 8.4 %collective-permute-start.15 = (f32[256,512]{1,0:T(8,128)}, f32[256,512]{1,0:T(8,128)}, u32[]{:S(2)}, u32[]{:S(2)}) collective-permute-start(f32[256,512]{1,0:T(8,128)} %get-tuple-element.45), channel_id=1, source_target_pairs={{6,7}} | collective-permute-start | bytes 1572872 | tf_op jit(solution)/shard_map/ppermute | solution.py:54
  111.7 6.4 %collective-permute-start.12 = (f32[256,512]{1,0:T(8,128)}, f32[256,512]{1,0:T(8,128)}, u32[]{:S(2)}, u32[]{:S(2)}) collective-permute-start(f32[256,512]{1,0:T(8,128)} %add.47), channel_id=1, source_target_pairs={{3,7}} | collective-permute-start | bytes 1572872 | tf_op jit(solution)/shard_map/ppermute | solution.py:54
  119.9 29.2 %copy-start.4 = (f32[256,512]{1,0:T(8,128)}, f32[256,512]{1,0:T(8,128)S(1)}, u32[]{:S(2)}) copy-start(f32[256,512]{1,0:T(8,128)S(1)} %fusion.35) | copy-start | bytes 1572868
  144.2 2.3 collective-permute-start.17
  152.2 80.2 %all-to-all-start.1 = ((f32[4,5,128,256]{3,0,1,2:T(4,128)}), f32[4,5,128,256]{3,0,1,2:T(4,128)}, u32[]{:S(2)}, u32[]{:S(2)}) async-start(f32[4,5,128,256]{3,0,1,2:T(4,128)} %copy.76), calls=%async_computation.1 | async-start | bytes 5242880 | tf_op jit(solution)/shard_map/all_to_all | solution.py:20
  266.1 12.8 %slice-start = ((s8[12582912]{0:T(1024)(128)(4,1)}), s8[4194304]{0:T(1024)(128)(4,1)S(1)}, s32[]{:S(2)}) async-start(s8[12582912]{0:T(1024)(128)(4,1)} %bitcast.185), calls=%async_computation.4 | async-start | bytes 8388608
  266.1 12.8 %slice-start.1 = ((s8[12582912]{0:T(1024)(128)(4,1)}), s8[4194304]{0:T(1024)(128)(4,1)S(1)}, s32[]{:S(2)}) async-start(s8[12582912]{0:T(1024)(128)(4,1)} %bitcast.185), calls=%async_computation.5 | async-start | bytes 8388608
  272.9 6.0 %slice-start.2 = ((s8[12582912]{0:T(1024)(128)(4,1)}), s8[4194304]{0:T(1024)(128)(4,1)S(1)}, s32[]{:S(2)}) async-start(s8[12582912]{0:T(1024)(128)(4,1)} %bitcast.185), calls=%async_computation.6 | async-start | bytes 8388608
  288.1 3.1 %copy-start.14 = (f32[512,1,256]{0,2,1:T(8,128)S(1)}, f32[512,1,256]{0,2,1:T(8,128)}, u32[]{:S(2)}) copy-start(f32[512,1,256]{0,2,1:T(8,128)} %copy.75) | copy-start | bytes 1572868
  288.1 3.1 %copy-start.24 = (f32[1,8,2,16,512]{4,3,0,2,1:T(8,128)S(1)}, f32[1,8,2,16,512]{4,3,0,2,1:T(8,128)}, u32[]{:S(2)}) copy-start(f32[1,8,2,16,512]{4,3,0,2,1:T(8,128)} %get-tuple-element.25) | copy-start | bytes 1572868
  299.4 1.9 copy-start.2
  299.4 2.7 slice-start.3
  301.3 2.8 copy-start.1
Sparse Core Ops, SparseCore 0:
  147.2 118.7 all-gather.1

commit v6 on v4

--- a/solution.py
+++ b/solution.py
@@ -71,26 +71,10 @@
             settled = settled - mm(low[section - 3], after[section - 3][2])
 
     rows = lax.axis_size("row")
-    halves = cols // sections
-    cut = width_block // rows
-    down = lax.all_to_all(own.reshape(rows, cut, -1), "row", 0, 0, tiled=True)[0]
-    part = cut // halves
-    pieces_out = down.reshape(halves, part, -1)
-    mine = pieces_out[0]
-    for h in range(1, halves):
-        pairs = [
-            (r * cols + k, r * cols + k + h * sections)
-            for r in range(rows)
-            for k in range(sections)
-        ]
-        got = lax.ppermute(pieces_out[h], AXES, pairs)
-        mine = jnp.where(col // sections == h, got, mine)
-    gathered = lax.all_gather(mine, AXES, tiled=True)
-    whole = (
-        gathered.reshape(rows, halves, sections, part, -1)
-        .transpose(2, 0, 1, 3, 4)
-        .reshape(sections * width_block, -1)
-    )
+    chunk = width_block // cols
+    across = lax.all_to_all(own.reshape(cols, chunk, -1), "col", 0, 0, tiled=True)
+    mine = lax.all_to_all(across[:rows], "row", 0, 0, tiled=True)[0]
+    whole = lax.all_gather(mine, AXES, tiled=True)
 
     update = jnp.concatenate([lead[None], rest], axis=0)
     for section in range(sections):

time: 316 us -> 343 us (1.085); the launches traced: 315 us -> 337 us
  blocking collectives: 24 us -> 77.9 us
  starting transfers between devices: 83.9 us -> 39.3 us
  local copies, waits for them, and re-layouts: 33.4 us -> 50.5 us
    all_to_all x1 -> x2, blocking collectives: 24 us -> 77.9 us  [the longest x1 65.9 us: per_device(): mine = lax.all_to_all(across[:rows], 'row', 0, 0, tiled=True)[0]]
    all_to_all x2, starting transfers between devices: 60.3 us -> 17 us  [transpose_in(): lax.all_to_all(pieces, AXES, split_axis=2, concat_axis=0, tiled=True)]
    unnamed x87 -> x93, local copies, waits for them, and re-layouts: 9.54 us -> 25.1 us
  transfers between devices with their start and end apart: 21 -> 20, of which waited for: 4 -> 3; matrix products, arithmetic and copies ran while one was open for 18% -> 17% of each run, Pallas kernels for 0% -> 0%
where the time goes in v6:
time: 343 us; the launch traced here: 337 us
  blocking collectives  77.9 us (23%)
  waiting for transfers between devices  69.8 us (20%)
  matrix products  68.2 us (20%)
  local copies, waits for them, and re-layouts  50.5 us (15%)
  starting transfers between devices  39.3 us (11%)
  other arithmetic  17 us (5%)
  between operations  14.4 us (4%)
    all_to_all x1, blocking collectives, per_device(): mine = lax.all_to_all(across[:rows], 'row', 0, 0, tiled=True)[0]  65.9 us
    all_to_all x2, waiting for transfers between devices, transpose_in(): lax.all_to_all(pieces, AXES, split_axis=2, concat_axis=0, tiled=True)  48.7 us
    dot_general x25, matrix products, mm(): return jnp.dot(a, b, precision=HI, preferred_element_type=jnp.float32)  40.3 us
    dot_general x8, matrix products, per_device(): jnp.einsum('jrc,cs->jrs', panels[section], whole[section * width_block:(s...  27.9 us
    unnamed x93, local copies, waits for them, and re-layouts  25.1 us
    ppermute x17, starting transfers between devices, tree_round(): got = lax.ppermute(buf, AXES, pairs)  22.3 us
    all_gather x1, waiting for transfers between devices, per_device(): whole = lax.all_gather(mine, AXES, tiled=True)  21 us
    all_to_all x2, starting transfers between devices, transpose_in(): lax.all_to_all(pieces, AXES, split_axis=2, concat_axis=0, tiled=True)  17 us
  transfers between devices with their start and end apart: 20, of which 3 were waited for; matrix products, arithmetic and copies ran while one was open for 17% of the time, Pallas kernels for 0%

profile of v6, /device:TPU:1, one launch (start us, length us, event | category | flops | bytes accessed | tf_op | source)
XLA Modules:
  0.0 337.2 jit_solution(5428357737092779941)
XLA Ops:
  6.5 2.6 copy.86
  9.2 1.7 copy-done.2
  12.1 11.5 %all-to-all-start = ((f32[4,1,128,256]{3,0,1,2:T(4,128)}), f32[4,1,128,256]{3,0,1,2:T(4,128)S(1)}, u32[]{:S(2)}, u32[]{:S(2)}) async-start(f32[4,1,128,256]{3,0,1,2:T(4,128)} %copy.48), calls=%async_computation | async-start | bytes 1048576 | tf_op jit(solution)/shard_map/all_to_all | solution.py:16
  23.6 13.3 %all-to-all-done = f32[4,1,128,256]{3,0,1,2:T(4,128)S(1)} async-done(((f32[4,1,128,256]{3,0,1,2:T(4,128)}), f32[4,1,128,256]{3,0,1,2:T(4,128)S(1)}, u32[]{:S(2)}, u32[]{:S(2)}) %all-to-all-start) | async-done | bytes 524320 | tf_op jit(solution)/shard_map/all_to_all | solution.py:16
  38.9 1.7 broadcast_select_fusion.6
  40.6 1.5 collective-permute-start
  43.4 2.0 add.57
  45.4 2.7 broadcast_select_fusion.5
  48.1 1.5 collective-permute-start.1
  49.6 1.5 collective-permute-start.2
  52.4 1.4 add.58
  54.5 1.6 fusion.109
  56.1 2.3 add.60
  58.4 2.7 broadcast_select_fusion.4
  61.1 1.5 collective-permute-start.4
  62.5 1.5 collective-permute-start.5
  64.0 1.4 fusion.71
  65.4 1.5 collective-permute-start.3
  69.6 2.3 add.63
  71.9 2.7 broadcast_select_fusion.3
  74.6 1.5 collective-permute-start.7
  76.0 1.4 fusion.69
  77.4 1.5 collective-permute-start.6
  79.8 1.9 convolution_subtract_fusion.7
  81.7 1.5 add.64
  85.5 1.7 broadcast_select_fusion.2
  87.2 1.4 collective-permute-start.10
  88.6 1.4 fusion.67
  90.0 1.5 collective-permute-start.9
  92.6 1.9 convolution_subtract_fusion.5
  94.6 1.5 add.67
  97.7 1.7 broadcast_select_fusion.1
  99.3 1.5 collective-permute-start.14
  100.8 1.4 fusion.63
  102.9 2.1 convolution_subtract_fusion.3
  105.1 2.0 fusion.57
  107.9 1.6 broadcast_select_fusion
  109.5 1.5 collective-permute-start.15
  111.9 1.5 collective-permute-start.16
  113.4 1.5 fusion.65
  115.6 1.7 fusion.113
  117.3 1.9 fusion.55
  120.3 12.0 %all_to_all.40 = f32[16,16,512]{2,1,0:T(8,128)S(1)} all-to-all(f32[16,16,512]{2,1,0:T(8,128)S(1)} %bitcast.173), channel_id=1, replica_groups=mesh['row'=8,'col'=16] {'col'}, dimensions={0} | all-to-all | bytes 1048576 | tf_op jit(solution)/shard_map/all_to_all | solution.py:75
  132.3 65.9 %all_to_all.41 = f32[8,16,512]{2,1,0:T(8,128)S(1)} all-to-all(f32[8,16,512]{2,1,0:T(8,128)S(1)} %slice.126), channel_id=1, replica_groups=mesh['row'=8,'col'=16] {'row'}, dimensions={0} | all-to-all | bytes 524288 | tf_op jit(solution)/shard_map/all_to_all | solution.py:76
  198.9 1.9 slice.125
  200.8 3.2 copy.50
  204.0 5.5 %all-to-all-start.1 = ((f32[4,5,128,256]{3,0,1,2:T(4,128)}), f32[4,5,128,256]{3,0,1,2:T(4,128)}, u32[]{:S(2)}, u32[]{:S(2)}) async-start(f32[4,5,128,256]{3,0,1,2:T(4,128)} %copy.50), calls=%async_computation.1 | async-start | bytes 5242880 | tf_op jit(solution)/shard_map/all_to_all | solution.py:16
  209.5 35.4 %all-to-all-done.1 = f32[4,5,128,256]{3,0,1,2:T(4,128)} async-done(((f32[4,5,128,256]{3,0,1,2:T(4,128)}), f32[4,5,128,256]{3,0,1,2:T(4,128)}, u32[]{:S(2)}, u32[]{:S(2)}) %all-to-all-start.1) | async-done | bytes 2621472 | tf_op jit(solution)/shard_map/all_to_all | solution.py:16
  244.9 3.7 %copy.51 = f32[128,4,5,1,256]{4,1,0,2,3:T(4,128)} copy(f32[128,4,5,1,256]{4,1,2,0,3:T(4,128)} %bitcast.13) | data formatting | bytes 5242880 | tf_op jit(solution)/shard_map/all_to_all | solution.py:16
  248.6 4.0 %reshape.16 = f32[512,5,256]{2,0,1:T(8,128)} reshape(f32[128,4,5,1,256]{4,1,0,2,3:T(4,128)} %copy.51) | data formatting | bytes 5242880 | tf_op jit(solution)/shard_map/reshape | solution.py:17
  252.6 3.2 copy.52
  255.8 21.0 %all-gather.3.cloned.1.call-done = f32[1,2048,512]{2,0,1:T(1,128)} async-done(((f32[1,16,512]{2,0,1:T(1,128)}), f32[1,2048,512]{2,0,1:T(1,128)}) %all-gather.3.cloned.1.call-update) | async-done | bytes 4194320 | tf_op jit(solution)/shard_map/all_gather | solution.py:77
  276.8 5.3 %fusion.108 = (f32[1,256,512]{2,0,1:T(1,128)S(1)}, f32[1,256,512]{2,0,1:T(1,128)S(1)}, f32[1,256,512]{2,0,1:T(1,128)S(1)}, f32[1,256,512]{2,0,1:T(1,128)}, f32[1...) fusion(f32[1,2048,512]{2,0,1:T(1,128)} %all-gather.3.cloned.1.call-done), kind=kLoop, calls=%fused_computation.128 | loop fusion | bytes 8388608 | tf_op jit(solution)/shard_map/slice | solution.py:84
  285.6 1.9 copy.81
  289.2 9.7 %copy.78 = f32[1,256,512]{1,2,0:T(8,128)S(1)} copy(f32[1,256,512]{2,0,1:T(1,128)S(1)} %get-tuple-element.32) | data formatting | bytes 1048576
  299.0 2.9 fusion.20
  301.9 2.9 fusion.18
  304.8 2.9 fusion.16
  307.8 2.9 fusion.14
  310.7 2.9 fusion.12
  313.6 2.9 fusion.10
  316.5 4.6 %fusion.8 = f32[512,6,256]{0,2,1:T(8,128)} fusion(f32[8,6,256,256]{3,2,1,0:T(8,128)} %param.4, f32[1,256,512]{1,2,0:T(8,128)S(1)} %copy.84), kind=kOutput, calls=%fused_computation.10 | convolution fusion | flops 1207959552 | bytes 5242880 | tf_op jit(solution)/shard_map/jrc,cs->jrs/dot_general | solution.py:81
  321.1 5.9 %fusion.6 = f32[6,256,512]{2,1,0:T(8,128)S(1)} fusion(f32[5,256,512]{2,1,0:T(8,128)} %bitcast.172, f32[1,256,512]{2,1,0:T(8,128)S(1)} %bitcast.174, f32[512,6,256]{0,2,1:T(8,128)} %fusion.8, f32[512,6,256]{0,2,1:T(8,128)S(1)} %fusion.10, f32[512,6,256]{0,2,1:T(8,128)S(1)} %fusion.12, f32[512,6,256]{0,2,1:T(8,128)S(1)} %fusion.14, ...), kind=kOutput, calls=%fused_computation.7 | convolution fusion | flops 1215037440 | bytes 30408704 | tf_op jit(solution)/shard_map/jrc,cs->jrs/dot_general | solution.py:81
  328.2 2.0 pad_maximum_fusion
  (131 shorter events, 26.2 us)
Async XLA Ops:
  6.5 32.4 %copy-start = (f32[8,256,256]{2,1,0:T(8,128)S(1)}, f32[8,256,256]{2,1,0:T(8,128)}, u32[]{:S(2)}) copy-start(f32[8,256,256]{2,1,0:T(8,128)} %param.5) | copy-start | bytes 6291460
  9.2 1.7 copy-start.2
  12.1 24.8 %all-to-all-start = ((f32[4,1,128,256]{3,0,1,2:T(4,128)}), f32[4,1,128,256]{3,0,1,2:T(4,128)S(1)}, u32[]{:S(2)}, u32[]{:S(2)}) async-start(f32[4,1,128,256]{3,0,1,2:T(4,128)} %copy.48), calls=%async_computation | async-start | bytes 1048576 | tf_op jit(solution)/shard_map/all_to_all | solution.py:16
  23.6 253.3 %all-gather.3.cloned.1.call-start = ((), (), s32[]{:S(2)}) async-start(), calls=%async_computation.4 | async-start | bytes 4227072 | tf_op jit(solution)/shard_map/all_gather | solution.py:77
  40.6 2.8 collective-permute-start
  43.4 2.0 copy-start.27
  48.1 4.3 %collective-permute-start.1 = (f32[256,512]{1,0:T(8,128)}, f32[256,512]{1,0:T(8,128)}, u32[]{:S(2)}, u32[]{:S(2)}) collective-permute-start(f32[256,512]{1,0:T(8,128)} %add.57), channel_id=1, source_target_pairs={{0,2},{1,3}} | collective-permute-start | bytes 1572872 | tf_op jit(solution)/shard_map/ppermute | solution.py:50
  49.6 6.6 %collective-permute-start.2 = (f32[256,512]{1,0:T(8,128)}, f32[256,512]{1,0:T(8,128)}, u32[]{:S(2)}, u32[]{:S(2)}) collective-permute-start(f32[256,512]{1,0:T(8,128)} %get-tuple-element.35), channel_id=1, source_target_pairs={{1,2}} | collective-permute-start | bytes 1572872 | tf_op jit(solution)/shard_map/ppermute | solution.py:50
  52.3 15.8 %copy-start.26 = (f32[256,256]{1,0:T(8,128)}, f32[256,256]{1,0:T(8,128)S(1)}, u32[]{:S(2)}) copy-start(f32[256,256]{1,0:T(8,128)S(1)} %fusion.73) | copy-start | bytes 786436
  53.7 0.8 copy-start.10
  56.1 2.3 copy-start.19
  61.1 5.8 %collective-permute-start.4 = (f32[256,512]{1,0:T(8,128)}, f32[256,512]{1,0:T(8,128)}, u32[]{:S(2)}, u32[]{:S(2)}) collective-permute-start(f32[256,512]{1,0:T(8,128)} %add.60), channel_id=1, source_target_pairs={{1,3},{2,4}} | collective-permute-start | bytes 1572872 | tf_op jit(solution)/shard_map/ppermute | solution.py:50
  62.5 7.1 %collective-permute-start.5 = (f32[256,512]{1,0:T(8,128)}, f32[256,512]{1,0:T(8,128)}, u32[]{:S(2)}, u32[]{:S(2)}) collective-permute-start(f32[256,512]{1,0:T(8,128)} %get-tuple-element.37), channel_id=1, source_target_pairs={{2,3}} | collective-permute-start | bytes 1572872 | tf_op jit(solution)/shard_map/ppermute | solution.py:50
  64.0 7.9 %copy-start.20 = (f32[256,512]{1,0:T(8,128)S(1)}, f32[256,512]{1,0:T(8,128)}, u32[]{:S(2)}) copy-start(f32[256,512]{1,0:T(8,128)} %copy-done.19) | copy-start | bytes 1572868
  65.4 9.2 %copy-start.24 = (f32[256,256]{1,0:T(8,128)}, f32[256,256]{1,0:T(8,128)S(1)}, u32[]{:S(2)}) copy-start(f32[256,256]{1,0:T(8,128)S(1)} %fusion.71) | copy-start | bytes 786436
  65.4 14.3 %collective-permute-start.3 = (f32[256,512]{1,0:T(8,128)}, f32[256,512]{1,0:T(8,128)}, u32[]{:S(2)}, u32[]{:S(2)}) collective-permute-start(f32[256,512]{1,0:T(8,128)} %copy-done.10), channel_id=1, source_target_pairs={{0,4},{1,5},{2,6},{3,7}} | collective-permute-start | bytes 1572872 | tf_op jit(solution)/shard_map/ppermute | solution.py:50
  68.2 0.8 copy-start.7
  69.6 2.3 copy-start.13
  74.6 7.1 %collective-permute-start.7 = (f32[256,512]{1,0:T(8,128)}, f32[256,512]{1,0:T(8,128)}, u32[]{:S(2)}, u32[]{:S(2)}) collective-permute-start(f32[256,512]{1,0:T(8,128)} %add.63), channel_id=1, source_target_pairs={{2,4},{3,5}} | collective-permute-start | bytes 1572872 | tf_op jit(solution)/shard_map/ppermute | solution.py:50
  76.0 7.9 %copy-start.25 = (f32[256,256]{1,0:T(8,128)S(1)}, f32[256,256]{1,0:T(8,128)}, u32[]{:S(2)}) copy-start(f32[256,256]{1,0:T(8,128)} %copy-done.24) | copy-start | bytes 786436
  76.0 8.6 %copy-start.39 = (f32[256,512]{1,0:T(8,128)S(1)}, f32[256,512]{1,0:T(8,128)}, u32[]{:S(2)}) copy-start(f32[256,512]{1,0:T(8,128)} %get-tuple-element.39) | copy-start | bytes 1572868
  77.4 15.2 %collective-permute-start.6 = (f32[256,512]{1,0:T(8,128)}, f32[256,512]{1,0:T(8,128)}, u32[]{:S(2)}, u32[]{:S(2)}) collective-permute-start(f32[256,512]{1,0:T(8,128)} %copy-done.7), channel_id=1, source_target_pairs={{1,5},{2,6},{3,7}} | collective-permute-start | bytes 1572872 | tf_op jit(solution)/shard_map/ppermute | solution.py:50
  78.9 6.6 %copy-start.14 = (f32[256,512]{1,0:T(8,128)S(1)}, f32[256,512]{1,0:T(8,128)}, u32[]{:S(2)}) copy-start(f32[256,512]{1,0:T(8,128)} %copy-done.13) | copy-start | bytes 1572868
  78.9 5.7 %collective-permute-start.8 = (f32[256,512]{1,0:T(8,128)}, f32[256,512]{1,0:T(8,128)S(1)}, u32[]{:S(2)}, u32[]{:S(2)}) collective-permute-start(f32[256,512]{1,0:T(8,128)} %get-tuple-element.39), channel_id=1, source_target_pairs={{3,4}} | collective-permute-start | bytes 1572872 | tf_op jit(solution)/shard_map/ppermute | solution.py:50
  81.7 5.5 %copy-start.21 = (f32[256,512]{1,0:T(8,128)}, f32[256,512]{1,0:T(8,128)S(1)}, u32[]{:S(2)}) copy-start(f32[256,512]{1,0:T(8,128)S(1)} %convolution_subtract_fusion.7) | copy-start | bytes 1572868
  83.2 0.8 copy-start.9
  84.6 2.6 copy-start.15
  84.6 8.0 %copy-start.8 = (f32[256,512]{1,0:T(8,128)S(1)}, f32[256,512]{1,0:T(8,128)}, u32[]{:S(2)}) copy-start(f32[256,512]{1,0:T(8,128)} %copy-done.7) | copy-start | bytes 1572868
  87.2 7.4 %collective-permute-start.10 = (f32[256,512]{1,0:T(8,128)}, f32[256,512]{1,0:T(8,128)}, u32[]{:S(2)}, u32[]{:S(2)}) collective-permute-start(f32[256,512]{1,0:T(8,128)} %add.66), channel_id=1, source_target_pairs={{3,5},{4,6}} | collective-permute-start | bytes 1572872 | tf_op jit(solution)/shard_map/ppermute | solution.py:50
  88.6 8.0 %copy-start.40 = (f32[256,512]{1,0:T(8,128)S(1)}, f32[256,512]{1,0:T(8,128)}, u32[]{:S(2)}) copy-start(f32[256,512]{1,0:T(8,128)} %get-tuple-element.41) | copy-start | bytes 1572868
  90.0 7.6 %copy-start.28 = (f32[256,256]{1,0:T(8,128)}, f32[256,256]{1,0:T(8,128)S(1)}, u32[]{:S(2)}) copy-start(f32[256,256]{1,0:T(8,128)S(1)} %fusion.67) | copy-start | bytes 786436
  90.0 12.9 %collective-permute-start.9 = (f32[256,512]{1,0:T(8,128)}, f32[256,512]{1,0:T(8,128)}, u32[]{:S(2)}, u32[]{:S(2)}) collective-permute-start(f32[256,512]{1,0:T(8,128)} %copy-done.9), channel_id=1, source_target_pairs={{2,6},{3,7}} | collective-permute-start | bytes 1572872 | tf_op jit(solution)/shard_map/ppermute | solution.py:50
  91.5 6.2 %copy-start.16 = (f32[256,512]{1,0:T(8,128)S(1)}, f32[256,512]{1,0:T(8,128)}, u32[]{:S(2)}) copy-start(f32[256,512]{1,0:T(8,128)} %copy-done.15) | copy-start | bytes 1572868
  91.5 5.1 %collective-permute-start.11 = (f32[256,512]{1,0:T(8,128)}, f32[256,512]{1,0:T(8,128)S(1)}, u32[]{:S(2)}, u32[]{:S(2)}) collective-permute-start(f32[256,512]{1,0:T(8,128)} %get-tuple-element.41), channel_id=1, source_target_pairs={{4,5}} | collective-permute-start | bytes 1572872 | tf_op jit(solution)/shard_map/ppermute | solution.py:50
  94.5 4.8 %copy-start.22 = (f32[256,512]{1,0:T(8,128)}, f32[256,512]{1,0:T(8,128)S(1)}, u32[]{:S(2)}) copy-start(f32[256,512]{1,0:T(8,128)S(1)} %convolution_subtract_fusion.5) | copy-start | bytes 1572868
  96.7 2.7 copy-start.17
  99.3 5.7 %collective-permute-start.14 = (f32[256,512]{1,0:T(8,128)}, f32[256,512]{1,0:T(8,128)}, u32[]{:S(2)}, u32[]{:S(2)}) collective-permute-start(f32[256,512]{1,0:T(8,128)} %add.69), channel_id=1, source_target_pairs={{4,6},{5,7}} | collective-permute-start | bytes 1572872 | tf_op jit(solution)/shard_map/ppermute | solution.py:50
  100.8 4.2 %copy-start.29 = (f32[256,256]{1,0:T(8,128)S(1)}, f32[256,256]{1,0:T(8,128)}, u32[]{:S(2)}) copy-start(f32[256,256]{1,0:T(8,128)} %copy-done.28) | copy-start | bytes 786436
  100.8 7.1 %copy-start.18 = (f32[256,512]{1,0:T(8,128)S(1)}, f32[256,512]{1,0:T(8,128)}, u32[]{:S(2)}) copy-start(f32[256,512]{1,0:T(8,128)} %copy-done.17) | copy-start | bytes 1572868
  102.2 7.3 %copy-start.30 = (f32[256,256]{1,0:T(8,128)}, f32[256,256]{1,0:T(8,128)S(1)}, u32[]{:S(2)}) copy-start(f32[256,256]{1,0:T(8,128)S(1)} %fusion.63) | copy-start | bytes 786436
  102.2 4.9 %collective-permute-start.13 = (f32[256,512]{1,0:T(8,128)}, f32[256,512]{1,0:T(8,128)S(1)}, u32[]{:S(2)}, u32[]{:S(2)}) collective-permute-start(f32[256,512]{1,0:T(8,128)} %get-tuple-element.43), channel_id=1, source_target_pairs={{5,6}} | collective-permute-start | bytes 1572872 | tf_op jit(solution)/shard_map/ppermute | solution.py:50
  105.0 6.9 %copy-start.11 = (f32[256,512]{1,0:T(8,128)}, f32[256,512]{1,0:T(8,128)S(1)}, u32[]{:S(2)}) copy-start(f32[256,512]{1,0:T(8,128)S(1)} %convolution_subtract_fusion.3) | copy-start | bytes 1572868
  105.0 6.0 %copy-start.38 = (f32[256,512]{1,0:T(8,128)S(1)}, f32[256,512]{1,0:T(8,128)}, u32[]{:S(2)}) copy-start(f32[256,512]{1,0:T(8,128)} %get-tuple-element.43) | copy-start | bytes 1572868
  107.1 0.8 copy-start.5
  109.5 6.0 %collective-permute-start.15 = (f32[256,512]{1,0:T(8,128)}, f32[256,512]{1,0:T(8,128)}, u32[]{:S(2)}, u32[]{:S(2)}) collective-permute-start(f32[256,512]{1,0:T(8,128)} %get-tuple-element.45), channel_id=1, source_target_pairs={{6,7}} | collective-permute-start | bytes 1572872 | tf_op jit(solution)/shard_map/ppermute | solution.py:50
  111.9 5.4 %collective-permute-start.16 = (f32[256,512]{1,0:T(8,128)}, f32[256,512]{1,0:T(8,128)}, u32[]{:S(2)}, u32[]{:S(2)}) collective-permute-start(f32[256,512]{1,0:T(8,128)} %add.71), channel_id=1, source_target_pairs={{5,7}} | collective-permute-start | bytes 1572872 | tf_op jit(solution)/shard_map/ppermute | solution.py:50
  113.4 5.8 %copy-start.6 = (f32[256,512]{1,0:T(8,128)S(1)}, f32[256,512]{1,0:T(8,128)}, u32[]{:S(2)}) copy-start(f32[256,512]{1,0:T(8,128)} %copy-done.5) | copy-start | bytes 1572868
  113.4 5.9 %copy-start.12 = (f32[256,512]{1,0:T(8,128)S(1)}, f32[256,512]{1,0:T(8,128)}, u32[]{:S(2)}) copy-start(f32[256,512]{1,0:T(8,128)} %copy-done.11) | copy-start | bytes 1572868
  113.4 5.9 %copy-start.31 = (f32[256,512]{1,0:T(8,128)S(1)}, f32[256,512]{1,0:T(8,128)}, u32[]{:S(2)}) copy-start(f32[256,512]{1,0:T(8,128)} %get-tuple-element.36) | copy-start | bytes 1572868
  113.4 5.9 %copy-start.34 = (f32[256,512]{1,0:T(8,128)S(1)}, f32[256,512]{1,0:T(8,128)}, u32[]{:S(2)}) copy-start(f32[256,512]{1,0:T(8,128)} %get-tuple-element.38) | copy-start | bytes 1572868
  113.4 5.9 %copy-start.35 = (f32[256,512]{1,0:T(8,128)S(1)}, f32[256,512]{1,0:T(8,128)}, u32[]{:S(2)}) copy-start(f32[256,512]{1,0:T(8,128)} %get-tuple-element.40) | copy-start | bytes 1572868
  113.4 5.9 %copy-start.36 = (f32[256,512]{1,0:T(8,128)S(1)}, f32[256,512]{1,0:T(8,128)}, u32[]{:S(2)}) copy-start(f32[256,512]{1,0:T(8,128)} %get-tuple-element.42) | copy-start | bytes 1572868
  113.4 5.9 %copy-start.37 = (f32[256,512]{1,0:T(8,128)S(1)}, f32[256,512]{1,0:T(8,128)}, u32[]{:S(2)}) copy-start(f32[256,512]{1,0:T(8,128)} %get-tuple-element.44) | copy-start | bytes 1572868
  114.9 4.3 %collective-permute-start.12 = (f32[256,512]{1,0:T(8,128)S(1)}, f32[256,512]{1,0:T(8,128)S(1)}, u32[]{:S(2)}, u32[]{:S(2)}) collective-permute-start(f32[256,512]{1,0:T(8,128)S(1)} %add.67), channel_id=1, source_target_pairs={{3,7}} | collective-permute-start | bytes 1572872 | tf_op jit(solution)/shard_map/ppermute | solution.py:50
  120.3 80.6 %copy-start.3 = (f32[256,512]{1,0:T(8,128)}, f32[256,512]{1,0:T(8,128)S(1)}, u32[]{:S(2)}) copy-start(f32[256,512]{1,0:T(8,128)S(1)} %fusion.35) | copy-start | bytes 1572868
  204.0 40.9 %all-to-all-start.1 = ((f32[4,5,128,256]{3,0,1,2:T(4,128)}), f32[4,5,128,256]{3,0,1,2:T(4,128)}, u32[]{:S(2)}, u32[]{:S(2)}) async-start(f32[4,5,128,256]{3,0,1,2:T(4,128)} %copy.50), calls=%async_computation.1 | async-start | bytes 5242880 | tf_op jit(solution)/shard_map/all_to_all | solution.py:16
  301.9 3.0 copy-start.33
  304.8 3.0 copy-start.32
  316.5 4.6 %copy-start.23 = (f32[512,1,256]{0,2,1:T(8,128)S(1)}, f32[512,1,256]{0,2,1:T(8,128)}, u32[]{:S(2)}) copy-start(f32[512,1,256]{0,2,1:T(8,128)} %copy.49) | copy-start | bytes 1572868
  316.5 4.6 %copy-start.41 = (f32[1,256,512]{1,2,0:T(8,128)S(1)}, f32[1,256,512]{1,2,0:T(8,128)}, u32[]{:S(2)}) copy-start(f32[1,256,512]{1,2,0:T(8,128)} %copy.85) | copy-start | bytes 1572868
  327.0 1.0 copy-start.4
  328.1 2.1 copy-start.1
Sparse Core Ops, SparseCore 0:
  199.0 77.8 all-gather.2

commit v7 on v3

--- a/solution.py
+++ b/solution.py
@@ -23,8 +23,8 @@
     devices = lax.axis_size(AXES)
     cols = lax.axis_size("col")
     pieces = snapshots.reshape(local_count, blocks, devices, width_block)
-    lead = transpose_in(pieces[:, :1], devices)[0]
-    rest = transpose_in(pieces[:, 1:], devices)
+    remaining = transpose_in(pieces, devices)
+    lead = remaining[0]
     device = lax.axis_index(AXES)
     row = lax.axis_index("row")
     col = lax.axis_index("col")
@@ -86,7 +86,7 @@
         .reshape(sections * width_block, -1)
     )
 
-    update = jnp.concatenate([lead[None], rest], axis=0)
+    update = remaining
     for section in range(sections):
         update = update - jnp.einsum(
             "jrc,cs->jrs",

time: 305 us -> 332 us (1.089)
  waiting for transfers between devices: 72.3 us -> 138 us
  starting transfers between devices: 73.1 us -> 35.6 us
  local copies, waits for them, and re-layouts: 35.6 us -> 30.8 us
  matrix products: 68.5 us -> 72.3 us
    all_gather x1, waiting for transfers between devices: 22.6 us -> 97 us  [per_device(): gathered = lax.all_gather(mine, AXES, tiled=True)]
    all_to_all x2 -> x1, starting transfers between devices: 49.6 us -> 11.9 us  [transpose_in(): lax.all_to_all(pieces, AXES, split_axis=2, concat_axis=0, tiled=True)]
    all_to_all x2 -> x1, waiting for transfers between devices: 48.6 us -> 40.7 us  [transpose_in(): lax.all_to_all(pieces, AXES, split_axis=2, concat_axis=0, tiled=True)]
    slice x4 -> x0, local copies, waits for them, and re-layouts: 6.29 us -> none  [the longest x2 5.1 us: per_device(): rest = transpose_in(pieces[:, 1:], devices)]
    dot_general x8, matrix products: 29.4 us -> 33.2 us  [per_device(): jnp.einsum('jrc,cs->jrs', panels[section], whole[section * width_block:(s...]
    reshape x0 -> x1, local copies, waits for them, and re-layouts: none -> 3.69 us  [per_device(): pieces = snapshots.reshape(local_count, blocks, devices, width_block)]
    unnamed x79 -> x77, local copies, waits for them, and re-layouts: 11.8 us -> 10.1 us
    reshape x4 -> x2, local copies, waits for them, and re-layouts: 9.26 us -> 8.47 us  [transpose_in(): arrived.reshape(devices * local_count, blocks, width_block)]
  transfers between devices with their start and end apart: 21 -> 20, of which waited for: 4 -> 3; matrix products, arithmetic and copies ran while one was open for 21% -> 14% of each run, Pallas kernels for 0% -> 0%
where the time goes in v7:
time: 332 us; the launch traced here: 331 us
  waiting for transfers between devices  138 us (42%)
  matrix products  72.3 us (22%)
  starting transfers between devices  35.6 us (11%)
  local copies, waits for them, and re-layouts  30.8 us (9%)
  blocking collectives  21 us (6%)
  other arithmetic  18.4 us (6%)
  between operations  14.1 us (4%)
    all_gather x1, waiting for transfers between devices, per_device(): gathered = lax.all_gather(mine, AXES, tiled=True)  97 us
    all_to_all x1, waiting for transfers between devices, transpose_in(): lax.all_to_all(pieces, AXES, split_axis=2, concat_axis=0, tiled=True)  40.7 us
    dot_general x25, matrix products, mm(): return jnp.dot(a, b, precision=HI, preferred_element_type=jnp.float32)  39.1 us
    dot_general x8, matrix products, per_device(): jnp.einsum('jrc,cs->jrs', panels[section], whole[section * width_block:(s...  33.2 us
    ppermute x17, starting transfers between devices, per_device(): got = lax.ppermute(buf, AXES, pairs)  22.2 us
    all_to_all x1, blocking collectives, per_device(): lax.all_to_all(own.reshape(rows, cut, -1), 'row', 0, 0, tiled=True)[0]  21 us
    add x10, other arithmetic, per_device(): buf = buf + got  15.7 us
    all_to_all x1, starting transfers between devices, transpose_in(): lax.all_to_all(pieces, AXES, split_axis=2, concat_axis=0, tiled=True)  11.9 us
  transfers between devices with their start and end apart: 20, of which 3 were waited for; matrix products, arithmetic and copies ran while one was open for 14% of the time, Pallas kernels for 0%

profile of v7, /device:TPU:1, one launch (start us, length us, event | category | flops | bytes accessed | tf_op | source)
XLA Modules:
  0.0 330.7 jit_solution(2027028809115052013)
XLA Ops:
  6.5 2.6 copy.111
  9.2 3.7 %copy.68 = f32[4,6,128,256]{3,0,1,2:T(4,128)} copy(f32[4,6,128,256]{3,2,1,0:T(8,128)S(1)} %bitcast.190) | data formatting | bytes 6291456 | tf_op jit(solution)/shard_map/reshape | solution.py:25
  12.9 11.9 %all-to-all-start = ((f32[4,6,128,256]{3,0,1,2:T(4,128)}), f32[4,6,128,256]{3,0,1,2:T(4,128)}, u32[]{:S(2)}, u32[]{:S(2)}) async-start(f32[4,6,128,256]{3,0,1,2:T(4,128)} %copy.68), calls=%async_computation | async-start | bytes 6291456 | tf_op jit(solution)/shard_map/all_to_all | solution.py:16
  24.8 40.7 %all-to-all-done = f32[4,6,128,256]{3,0,1,2:T(4,128)} async-done(((f32[4,6,128,256]{3,0,1,2:T(4,128)}), f32[4,6,128,256]{3,0,1,2:T(4,128)}, u32[]{:S(2)}, u32[]{:S(2)}) %all-to-all-start) | async-done | bytes 3145760 | tf_op jit(solution)/shard_map/all_to_all | solution.py:16
  65.5 4.1 %copy.69 = f32[128,4,6,1,256]{4,1,0,2,3:T(4,128)} copy(f32[128,4,6,1,256]{4,1,2,0,3:T(4,128)} %bitcast.2) | data formatting | bytes 6291456 | tf_op jit(solution)/shard_map/all_to_all | solution.py:16
  69.6 4.9 %reshape.27 = f32[512,6,256]{2,0,1:T(8,128)} reshape(f32[128,4,6,1,256]{4,1,0,2,3:T(4,128)} %copy.69) | data formatting | bytes 6291456 | tf_op jit(solution)/shard_map/reshape | solution.py:17
  74.5 3.5 %copy.70 = f32[512,6,256]{0,2,1:T(8,128)} copy(f32[512,6,256]{2,0,1:T(8,128)} %reshape.27) | data formatting | bytes 6291456 | tf_op jit(solution)/shard_map/reshape | solution.py:17
  78.1 1.7 broadcast_select_fusion.6
  79.8 1.5 collective-permute-start
  81.2 1.3 fusion.59
  83.3 2.7 broadcast_select_fusion.5
  85.9 1.5 collective-permute-start.3
  87.4 1.9 add.58
  89.3 1.4 collective-permute-start.1
  90.8 1.4 fusion.57
  92.2 2.2 add.61
  94.3 1.5 collective-permute-start.4
  95.8 1.3 add.59
  99.3 2.6 broadcast_select_fusion.4
  102.0 1.4 collective-permute-start.6
  103.4 1.4 fusion.55
  104.8 1.5 collective-permute-start.2
  106.3 1.3 add.62
  109.8 2.7 broadcast_select_fusion.3
  112.5 1.5 collective-permute-start.9
  113.9 2.1 add.64
  116.0 1.5 collective-permute-start.7
  117.5 1.4 fusion.53
  118.9 1.6 collective-permute-start.5
  120.5 1.9 convolution_subtract_fusion.9
  122.4 2.2 add.67
  124.7 1.5 collective-permute-start.10
  126.2 1.3 add.65
  128.9 2.9 broadcast_select_fusion.2
  131.8 1.5 collective-permute-start.12
  133.2 2.1 fusion.47
  135.3 1.3 fusion.49
  136.7 0.8 collective-permute-start.8
  137.5 1.9 convolution_subtract_fusion.7
  139.5 1.3 add.70
  141.6 1.3 add.68
  143.5 2.5 broadcast_select_fusion.1
  148.9 1.6 broadcast_select_fusion
  150.5 1.5 collective-permute-start.15
  152.0 0.9 add.72
  152.9 1.4 collective-permute-start.16
  154.3 1.5 fusion.51
  156.5 1.7 fusion.98
  158.2 1.9 fusion.39
  160.2 1.0 fusion.32
  161.2 21.0 %all_to_all.20 = f32[8,32,512]{2,1,0:T(8,128)S(1)} all-to-all(f32[8,32,512]{2,1,0:T(8,128)S(1)} %bitcast.191), channel_id=1, replica_groups=mesh['row'=8,'col'=16] {'row'}, dimensions={0} | all-to-all | bytes 1048576 | tf_op jit(solution)/shard_map/all_to_all | solution.py:70
  182.2 1.5 collective-permute-start.17
  185.1 97.0 %all-gather.2.cloned.1.call-done = f32[2048,512]{1,0:T(8,128)} async-done(((f32[16,512]{1,0:T(8,128)}), f32[2048,512]{1,0:T(8,128)}) %all-gather.2.cloned.1.call-update) | async-done | bytes 4194320 | tf_op jit(solution)/shard_map/all_gather | solution.py:82
  282.1 3.7 %fusion.93 = (f32[1,8,2,16,512]{4,3,0,2,1:T(8,128)}, f32[1,8,2,16,512]{4,3,0,2,1:T(8,128)S(1)}, f32[1,8,2,16,512]{4,3,0,2,1:T(8,128)S(1)}, f32[1,8,2,16,512]{4,3...) fusion(f32[8,8,2,16,512]{4,3,0,2,1:T(8,128)} %bitcast.192), kind=kLoop, calls=%fused_computation.123 | loop fusion | bytes 8388608 | tf_op jit(solution)/shard_map/slice | solution.py:94
  285.9 3.0 fusion.1
  288.9 3.0 fusion.3
  292.0 4.5 %fusion.5 = f32[512,6,256]{0,2,1:T(8,128)} fusion(f32[256,512,1]{1,0,2:T(8,128)S(1)} %bitcast.198, f32[8,6,256,256]{3,2,1,0:T(8,128)} %param.4), kind=kOutput, calls=%fused_computation.14 | convolution fusion | flops 1207959552 | bytes 5242880 | tf_op jit(solution)/shard_map/jrc,cs->jrs/dot_general | solution.py:91
  296.5 3.1 fusion.7
  299.6 3.1 fusion.9
  302.7 3.2 fusion.11
  305.9 3.0 fusion.13
  308.9 10.2 %bitcast_subtract_fusion = f32[6,256,512]{2,1,0:T(8,128)} fusion(f32[512,6,256]{0,2,1:T(8,128)S(1)} %fusion.1, f32[512,6,256]{0,2,1:T(8,128)S(1)} %fusion.3, f32[512,6,256]{0,2,1:T(8,128)} %fusion.5, f32[512,6,256]{0,2,1:T(8,128)} %fusion.7, f32[512,6,256]{0,2,1:T(8,128)} %fusion.9, f32[512,6,256]{0,2,1:T(8,128)} %fusion.11, f32[512,6,256]{0,2,1:T(8,128)} %fusion.13, ...), kind=kOutput, calls=%fused_computation.1 | convolution fusion | flops 1214251008 | bytes 30408704 | tf_op jit(solution)/shard_map/jrc,cs->jrs/dot_general | solution.py:91
  319.1 1.9 copy-done.3
  321.8 2.0 pad_maximum_fusion
  (110 shorter events, 13.8 us)
Async XLA Ops:
  6.5 71.6 %copy-start = (f32[8,256,256]{2,1,0:T(8,128)S(1)}, f32[8,256,256]{2,1,0:T(8,128)}, u32[]{:S(2)}) copy-start(f32[8,256,256]{2,1,0:T(8,128)} %param.5) | copy-start | bytes 6291460
  12.9 52.7 %all-to-all-start = ((f32[4,6,128,256]{3,0,1,2:T(4,128)}), f32[4,6,128,256]{3,0,1,2:T(4,128)}, u32[]{:S(2)}, u32[]{:S(2)}) async-start(f32[4,6,128,256]{3,0,1,2:T(4,128)} %copy.68), calls=%async_computation | async-start | bytes 6291456 | tf_op jit(solution)/shard_map/all_to_all | solution.py:16
  24.8 257.3 %all-gather.2.cloned.1.call-start = ((), (), s32[]{:S(2)}) async-start(), calls=%async_computation.2 | async-start | bytes 4227072 | tf_op jit(solution)/shard_map/all_gather | solution.py:82
  79.8 2.8 collective-permute-start
  82.5 0.7 copy-start.25
  85.9 6.2 %collective-permute-start.3 = (f32[256,512]{1,0:T(8,128)}, f32[256,512]{1,0:T(8,128)}, u32[]{:S(2)}, u32[]{:S(2)}) collective-permute-start(f32[256,512]{1,0:T(8,128)} %get-tuple-element.15), channel_id=1, source_target_pairs={{1,2}} | collective-permute-start | bytes 1572872 | tf_op jit(solution)/shard_map/ppermute | solution.py:59
  89.3 6.5 %collective-permute-start.1 = (f32[256,512]{1,0:T(8,128)}, f32[256,512]{1,0:T(8,128)}, u32[]{:S(2)}, u32[]{:S(2)}) collective-permute-start(f32[256,512]{1,0:T(8,128)} %add.58), channel_id=1, source_target_pairs={{0,2},{1,3}} | collective-permute-start | bytes 1572872 | tf_op jit(solution)/shard_map/ppermute | solution.py:59
  90.8 7.1 %copy-start.26 = (f32[256,256]{1,0:T(8,128)S(1)}, f32[256,256]{1,0:T(8,128)}, u32[]{:S(2)}) copy-start(f32[256,256]{1,0:T(8,128)} %copy-done.25) | copy-start | bytes 786436
  92.2 15.4 %copy-start.24 = (f32[256,256]{1,0:T(8,128)}, f32[256,256]{1,0:T(8,128)S(1)}, u32[]{:S(2)}) copy-start(f32[256,256]{1,0:T(8,128)S(1)} %fusion.57) | copy-start | bytes 786436
  94.3 11.9 %collective-permute-start.4 = (f32[256,512]{1,0:T(8,128)}, f32[256,512]{1,0:T(8,128)}, u32[]{:S(2)}, u32[]{:S(2)}) collective-permute-start(f32[256,512]{1,0:T(8,128)} %add.61), channel_id=1, source_target_pairs={{1,3},{2,4}} | collective-permute-start | bytes 1572872 | tf_op jit(solution)/shard_map/ppermute | solution.py:59
  97.1 0.8 copy-start.11
  98.5 0.8 copy-start.18
  102.0 7.1 %collective-permute-start.6 = (f32[256,512]{1,0:T(8,128)}, f32[256,512]{1,0:T(8,128)}, u32[]{:S(2)}, u32[]{:S(2)}) collective-permute-start(f32[256,512]{1,0:T(8,128)} %get-tuple-element.17), channel_id=1, source_target_pairs={{2,3}} | collective-permute-start | bytes 1572872 | tf_op jit(solution)/shard_map/ppermute | solution.py:59
  103.4 6.4 %copy-start.19 = (f32[256,512]{1,0:T(8,128)S(1)}, f32[256,512]{1,0:T(8,128)}, u32[]{:S(2)}) copy-start(f32[256,512]{1,0:T(8,128)} %copy-done.18) | copy-start | bytes 1572868
  104.8 7.7 %copy-start.21 = (f32[256,256]{1,0:T(8,128)}, f32[256,256]{1,0:T(8,128)S(1)}, u32[]{:S(2)}) copy-start(f32[256,256]{1,0:T(8,128)S(1)} %fusion.55) | copy-start | bytes 786436
  104.8 15.7 %collective-permute-start.2 = (f32[256,512]{1,0:T(8,128)}, f32[256,512]{1,0:T(8,128)}, u32[]{:S(2)}, u32[]{:S(2)}) collective-permute-start(f32[256,512]{1,0:T(8,128)} %copy-done.11), channel_id=1, source_target_pairs={{0,4},{1,5},{2,6},{3,7}} | collective-permute-start | bytes 1572872 | tf_op jit(solution)/shard_map/ppermute | solution.py:59
  107.6 0.8 copy-start.7
  109.0 0.8 copy-start.14
  112.5 9.9 %collective-permute-start.9 = (f32[256,512]{1,0:T(8,128)}, f32[256,512]{1,0:T(8,128)}, u32[]{:S(2)}, u32[]{:S(2)}) collective-permute-start(f32[256,512]{1,0:T(8,128)} %get-tuple-element.19), channel_id=1, source_target_pairs={{3,4}} | collective-permute-start | bytes 1572872 | tf_op jit(solution)/shard_map/ppermute | solution.py:59
  116.0 10.2 %collective-permute-start.7 = (f32[256,512]{1,0:T(8,128)}, f32[256,512]{1,0:T(8,128)}, u32[]{:S(2)}, u32[]{:S(2)}) collective-permute-start(f32[256,512]{1,0:T(8,128)} %add.64), channel_id=1, source_target_pairs={{2,4},{3,5}} | collective-permute-start | bytes 1572872 | tf_op jit(solution)/shard_map/ppermute | solution.py:59
  117.5 10.8 %copy-start.22 = (f32[256,256]{1,0:T(8,128)S(1)}, f32[256,256]{1,0:T(8,128)}, u32[]{:S(2)}) copy-start(f32[256,256]{1,0:T(8,128)} %copy-done.21) | copy-start | bytes 786436
  118.9 10.0 %copy-start.15 = (f32[256,512]{1,0:T(8,128)S(1)}, f32[256,512]{1,0:T(8,128)}, u32[]{:S(2)}) copy-start(f32[256,512]{1,0:T(8,128)} %copy-done.14) | copy-start | bytes 1572868
  118.9 18.6 %collective-permute-start.5 = (f32[256,512]{1,0:T(8,128)}, f32[256,512]{1,0:T(8,128)}, u32[]{:S(2)}, u32[]{:S(2)}) collective-permute-start(f32[256,512]{1,0:T(8,128)} %copy-done.7), channel_id=1, source_target_pairs={{1,5},{2,6},{3,7}} | collective-permute-start | bytes 1572872 | tf_op jit(solution)/shard_map/ppermute | solution.py:59
  122.4 9.4 %copy-start.20 = (f32[256,512]{1,0:T(8,128)}, f32[256,512]{1,0:T(8,128)S(1)}, u32[]{:S(2)}) copy-start(f32[256,512]{1,0:T(8,128)S(1)} %convolution_subtract_fusion.9) | copy-start | bytes 1572868
  124.7 16.9 %collective-permute-start.10 = (f32[256,512]{1,0:T(8,128)}, f32[256,512]{1,0:T(8,128)}, u32[]{:S(2)}, u32[]{:S(2)}) collective-permute-start(f32[256,512]{1,0:T(8,128)} %add.67), channel_id=1, source_target_pairs={{3,5},{4,6}} | collective-permute-start | bytes 1572872 | tf_op jit(solution)/shard_map/ppermute | solution.py:59
  127.4 0.8 copy-start.9
  128.3 9.3 %copy-start.8 = (f32[256,512]{1,0:T(8,128)S(1)}, f32[256,512]{1,0:T(8,128)}, u32[]{:S(2)}) copy-start(f32[256,512]{1,0:T(8,128)} %copy-done.7) | copy-start | bytes 1572868
  128.9 2.9 copy-start.16
  131.8 7.7 %collective-permute-start.12 = (f32[256,512]{1,0:T(8,128)}, f32[256,512]{1,0:T(8,128)}, u32[]{:S(2)}, u32[]{:S(2)}) collective-permute-start(f32[256,512]{1,0:T(8,128)} %get-tuple-element.21), channel_id=1, source_target_pairs={{4,5}} | collective-permute-start | bytes 1572872 | tf_op jit(solution)/shard_map/ppermute | solution.py:59
  136.6 11.4 %copy-start.27 = (f32[256,256]{1,0:T(8,128)}, f32[256,256]{1,0:T(8,128)S(1)}, u32[]{:S(2)}) copy-start(f32[256,256]{1,0:T(8,128)S(1)} %fusion.49) | copy-start | bytes 786436
  136.7 6.9 %copy-start.17 = (f32[256,512]{1,0:T(8,128)S(1)}, f32[256,512]{1,0:T(8,128)}, u32[]{:S(2)}) copy-start(f32[256,512]{1,0:T(8,128)} %copy-done.16) | copy-start | bytes 1572868
  136.7 6.9 %copy-start.28 = (f32[256,256]{1,0:T(8,128)S(1)}, f32[256,256]{1,0:T(8,128)}, u32[]{:S(2)}) copy-start(f32[256,256]{1,0:T(8,128)} %fusion.47) | copy-start | bytes 786436
  136.7 10.0 %collective-permute-start.8 = (f32[256,512]{1,0:T(8,128)}, f32[256,512]{1,0:T(8,128)S(1)}, u32[]{:S(2)}, u32[]{:S(2)}) collective-permute-start(f32[256,512]{1,0:T(8,128)} %copy-done.9), channel_id=1, source_target_pairs={{2,6},{3,7}} | collective-permute-start | bytes 1572872 | tf_op jit(solution)/shard_map/ppermute | solution.py:59
  140.7 6.0 %copy-start.10 = (f32[256,512]{1,0:T(8,128)S(1)}, f32[256,512]{1,0:T(8,128)}, u32[]{:S(2)}) copy-start(f32[256,512]{1,0:T(8,128)} %copy-done.9) | copy-start | bytes 1572868
  140.8 6.0 %copy-start.23 = (f32[256,256]{1,0:T(8,128)S(1)}, f32[256,256]{1,0:T(8,128)}, u32[]{:S(2)}) copy-start(f32[256,256]{1,0:T(8,128)} %copy-done.21) | copy-start | bytes 786436
  140.8 6.6 %collective-permute-start.14 = (f32[256,512]{1,0:T(8,128)S(1)}, f32[256,512]{1,0:T(8,128)S(1)}, u32[]{:S(2)}, u32[]{:S(2)}) collective-permute-start(f32[256,512]{1,0:T(8,128)S(1)} %add.70), channel_id=1, source_target_pairs={{4,6},{5,7}} | collective-permute-start | bytes 1572872 | tf_op jit(solution)/shard_map/ppermute | solution.py:59
  146.0 2.0 collective-permute-start.13
  147.4 5.5 %copy-start.12 = (f32[256,512]{1,0:T(8,128)}, f32[256,512]{1,0:T(8,128)S(1)}, u32[]{:S(2)}) copy-start(f32[256,512]{1,0:T(8,128)S(1)} %convolution_subtract_fusion.5) | copy-start | bytes 1572868
  148.1 0.8 copy-start.5
  150.5 6.0 %collective-permute-start.15 = (f32[256,512]{1,0:T(8,128)}, f32[256,512]{1,0:T(8,128)}, u32[]{:S(2)}, u32[]{:S(2)}) collective-permute-start(f32[256,512]{1,0:T(8,128)} %get-tuple-element.25), channel_id=1, source_target_pairs={{6,7}} | collective-permute-start | bytes 1572872 | tf_op jit(solution)/shard_map/ppermute | solution.py:59
  152.9 5.3 %collective-permute-start.16 = (f32[256,512]{1,0:T(8,128)}, f32[256,512]{1,0:T(8,128)}, u32[]{:S(2)}, u32[]{:S(2)}) collective-permute-start(f32[256,512]{1,0:T(8,128)} %add.72), channel_id=1, source_target_pairs={{5,7}} | collective-permute-start | bytes 1572872 | tf_op jit(solution)/shard_map/ppermute | solution.py:59
  154.3 5.9 %copy-start.6 = (f32[256,512]{1,0:T(8,128)S(1)}, f32[256,512]{1,0:T(8,128)}, u32[]{:S(2)}) copy-start(f32[256,512]{1,0:T(8,128)} %copy-done.5) | copy-start | bytes 1572868
  154.3 5.9 %copy-start.13 = (f32[256,512]{1,0:T(8,128)S(1)}, f32[256,512]{1,0:T(8,128)}, u32[]{:S(2)}) copy-start(f32[256,512]{1,0:T(8,128)} %copy-done.12) | copy-start | bytes 1572868
  154.3 5.9 %copy-start.29 = (f32[256,512]{1,0:T(8,128)S(1)}, f32[256,512]{1,0:T(8,128)}, u32[]{:S(2)}) copy-start(f32[256,512]{1,0:T(8,128)} %get-tuple-element.16) | copy-start | bytes 1572868
  154.3 5.9 %copy-start.30 = (f32[256,512]{1,0:T(8,128)S(1)}, f32[256,512]{1,0:T(8,128)}, u32[]{:S(2)}) copy-start(f32[256,512]{1,0:T(8,128)} %get-tuple-element.18) | copy-start | bytes 1572868
  154.3 5.9 %copy-start.31 = (f32[256,512]{1,0:T(8,128)S(1)}, f32[256,512]{1,0:T(8,128)}, u32[]{:S(2)}) copy-start(f32[256,512]{1,0:T(8,128)} %get-tuple-element.20) | copy-start | bytes 1572868
  154.3 5.9 %copy-start.32 = (f32[256,512]{1,0:T(8,128)S(1)}, f32[256,512]{1,0:T(8,128)}, u32[]{:S(2)}) copy-start(f32[256,512]{1,0:T(8,128)} %get-tuple-element.22) | copy-start | bytes 1572868
  154.3 5.9 %copy-start.33 = (f32[256,512]{1,0:T(8,128)S(1)}, f32[256,512]{1,0:T(8,128)}, u32[]{:S(2)}) copy-start(f32[256,512]{1,0:T(8,128)} %get-tuple-element.24) | copy-start | bytes 1572868
  155.8 4.3 %collective-permute-start.11 = (f32[256,512]{1,0:T(8,128)S(1)}, f32[256,512]{1,0:T(8,128)S(1)}, u32[]{:S(2)}, u32[]{:S(2)}) collective-permute-start(f32[256,512]{1,0:T(8,128)S(1)} %add.68), channel_id=1, source_target_pairs={{3,7}} | collective-permute-start | bytes 1572872 | tf_op jit(solution)/shard_map/ppermute | solution.py:59
  161.2 124.7 %copy-start.4 = (f32[256,512]{1,0:T(8,128)}, f32[256,512]{1,0:T(8,128)S(1)}, u32[]{:S(2)}) copy-start(f32[256,512]{1,0:T(8,128)S(1)} %fusion.32) | copy-start | bytes 1572868
  182.2 2.3 collective-permute-start.17
  282.1 14.3 %slice-start = ((s8[12582912]{0:T(1024)(128)(4,1)}), s8[4194304]{0:T(1024)(128)(4,1)S(1)}, s32[]{:S(2)}) async-start(s8[12582912]{0:T(1024)(128)(4,1)} %bitcast.187), calls=%async_computation.3 | async-start | bytes 8388608
  282.1 14.3 %slice-start.1 = ((s8[12582912]{0:T(1024)(128)(4,1)}), s8[4194304]{0:T(1024)(128)(4,1)S(1)}, s32[]{:S(2)}) async-start(s8[12582912]{0:T(1024)(128)(4,1)} %bitcast.187), calls=%async_computation.4 | async-start | bytes 8388608
  288.9 7.5 %slice-start.2 = ((s8[12582912]{0:T(1024)(128)(4,1)}), s8[4194304]{0:T(1024)(128)(4,1)S(1)}, s32[]{:S(2)}) async-start(s8[12582912]{0:T(1024)(128)(4,1)} %bitcast.187), calls=%async_computation.5 | async-start | bytes 8388608
  305.9 3.0 copy-start.2
  305.9 3.0 copy-start.34
  319.1 1.9 copy-start.3
  319.1 2.7 slice-start.3
  321.0 2.8 copy-start.1
Sparse Core Ops, SparseCore 0:
  185.3 96.8 all-gather.1

commit v8 on v3

--- a/solution.py
+++ b/solution.py
@@ -56,7 +56,7 @@
                 if section + q + step < sections
             ]
             if pairs:
-                got = lax.ppermute(buf, AXES, pairs)
+                got = lax.ppermute(buf, "col", pairs)
                 if level == 0:
                     first_hop[section] = got
                 buf = buf + got
@@ -72,12 +72,8 @@
     pieces_out = down.reshape(halves, part, -1)
     mine = pieces_out[0]
     for h in range(1, halves):
-        pairs = [
-            (r * cols + k, r * cols + k + h * sections)
-            for r in range(rows)
-            for k in range(sections)
-        ]
-        got = lax.ppermute(pieces_out[h], AXES, pairs)
+        pairs = [(k, k + h * sections) for k in range(sections)]
+        got = lax.ppermute(pieces_out[h], "col", pairs)
         mine = jnp.where(col // sections == h, got, mine)
     gathered = lax.all_gather(mine, AXES, tiled=True)
     whole = (

time: 305 us -> 346 us (1.13)
  starting transfers between devices: 73.1 us -> 109 us
  waiting for transfers between devices: 72.3 us -> 83.9 us
  blocking collectives: 21.3 us -> 14.7 us
    all_to_all x2, starting transfers between devices: 49.6 us -> 83 us  [transpose_in(): lax.all_to_all(pieces, AXES, split_axis=2, concat_axis=0, tiled=True)]
    ppermute x18, waiting for transfers between devices: 1.03 us -> 12.6 us  [the longest x17 11.6 us: per_device(): got = lax.ppermute(buf, 'col', pairs)]
    all_to_all x1, blocking collectives: 21.3 us -> 14.7 us  [per_device(): lax.all_to_all(own.reshape(rows, cut, -1), 'row', 0, 0, tiled=True)[0]]
  transfers between devices with their start and end apart: 21 -> 21, of which waited for: 4 -> 6; matrix products, arithmetic and copies ran while one was open for 21% -> 19% of each run, Pallas kernels for 0% -> 0%
where the time goes in v8:
time: 346 us; the launch traced here: 344 us
  starting transfers between devices  109 us (32%)
  waiting for transfers between devices  83.9 us (24%)
  matrix products  68.5 us (20%)
  local copies, waits for them, and re-layouts  34.9 us (10%)
  other arithmetic  18.5 us (5%)
  blocking collectives  14.7 us (4%)
  between operations  14.2 us (4%)
    all_to_all x2, starting transfers between devices, transpose_in(): lax.all_to_all(pieces, AXES, split_axis=2, concat_axis=0, tiled=True)  83 us
    all_to_all x2, waiting for transfers between devices, transpose_in(): lax.all_to_all(pieces, AXES, split_axis=2, concat_axis=0, tiled=True)  48.6 us
    dot_general x25, matrix products, mm(): return jnp.dot(a, b, precision=HI, preferred_element_type=jnp.float32)  39.1 us
    dot_general x8, matrix products, per_device(): jnp.einsum('jrc,cs->jrs', panels[section], whole[section * width_block:(s...  29.4 us
    ppermute x17, starting transfers between devices, per_device(): got = lax.ppermute(buf, 'col', pairs)  25.2 us
    all_gather x1, waiting for transfers between devices, per_device(): gathered = lax.all_gather(mine, AXES, tiled=True)  22.6 us
    add x10, other arithmetic, per_device(): buf = buf + got  15.8 us
    all_to_all x1, blocking collectives, per_device(): lax.all_to_all(own.reshape(rows, cut, -1), 'row', 0, 0, tiled=True)[0]  14.7 us
  transfers between devices with their start and end apart: 21, of which 6 were waited for; matrix products, arithmetic and copies ran while one was open for 19% of the time, Pallas kernels for 0%

profile of v8, /device:TPU:1, one launch (start us, length us, event | category | flops | bytes accessed | tf_op | source)
XLA Modules:
  0.0 344.2 jit_solution(16743388955326586950)
XLA Ops:
  6.5 2.6 copy.119
  9.2 1.7 copy-done.3
  12.0 11.5 %all-to-all-start = ((f32[4,1,128,256]{3,0,1,2:T(4,128)}), f32[4,1,128,256]{3,0,1,2:T(4,128)S(1)}, u32[]{:S(2)}, u32[]{:S(2)}) async-start(f32[4,1,128,256]{3,0,1,2:T(4,128)} %copy.74), calls=%async_computation | async-start | bytes 1048576 | tf_op jit(solution)/shard_map/all_to_all | solution.py:16
  23.6 13.3 %all-to-all-done = f32[4,1,128,256]{3,0,1,2:T(4,128)S(1)} async-done(((f32[4,1,128,256]{3,0,1,2:T(4,128)}), f32[4,1,128,256]{3,0,1,2:T(4,128)S(1)}, u32[]{:S(2)}, u32[]{:S(2)}) %all-to-all-start) | async-done | bytes 524320 | tf_op jit(solution)/shard_map/all_to_all | solution.py:16
  37.5 1.4 copy.75
  38.9 1.7 broadcast_select_fusion.6
  40.5 3.2 collective-permute-start
  43.7 1.3 fusion.67
  45.1 7.7 %collective-permute-done = f32[256,512]{1,0:T(8,128)} collective-permute-done((f32[256,512]{1,0:T(8,128)S(1)}, f32[256,512]{1,0:T(8,128)}, u32[]{:S(2)}, u32[]{:S(2)}) %collective-permute-start) | collective-permute-done | bytes 524320 | tf_op jit(solution)/shard_map/ppermute | solution.py:59
  52.8 2.7 broadcast_select_fusion.5
  55.5 1.5 collective-permute-start.3
  56.9 1.9 add.58
  58.9 2.1 collective-permute-start.1
  60.9 1.4 fusion.65
  62.3 2.2 add.61
  64.5 1.5 collective-permute-start.4
  66.0 3.8 %collective-permute-done.1 = f32[256,512]{1,0:T(8,128)} collective-permute-done((f32[256,512]{1,0:T(8,128)}, f32[256,512]{1,0:T(8,128)}, u32[]{:S(2)}, u32[]{:S(2)}) %collective-permute-start.1) | collective-permute-done | bytes 524320 | tf_op jit(solution)/shard_map/ppermute | solution.py:59
  73.3 2.7 broadcast_select_fusion.4
  76.0 1.5 collective-permute-start.6
  77.5 1.4 fusion.63
  78.9 2.1 collective-permute-start.2
  84.5 2.7 broadcast_select_fusion.3
  87.2 1.5 collective-permute-start.9
  88.7 2.1 add.64
  90.7 1.5 collective-permute-start.7
  92.3 1.4 fusion.61
  93.6 1.6 collective-permute-start.5
  95.2 1.9 convolution_subtract_fusion.9
  97.2 2.3 add.67
  99.4 1.5 collective-permute-start.10
  103.7 2.9 broadcast_select_fusion.2
  106.5 1.5 collective-permute-start.12
  108.0 2.1 fusion.55
  110.1 1.3 fusion.57
  112.3 1.9 convolution_subtract_fusion.7
  114.2 1.3 add.70
  116.3 1.3 add.68
  118.3 2.5 broadcast_select_fusion.1
  123.6 1.6 broadcast_select_fusion
  125.2 1.4 collective-permute-start.15
  127.6 1.5 collective-permute-start.16
  129.1 1.5 fusion.59
  131.3 1.7 fusion.106
  133.0 1.9 fusion.47
  136.0 14.7 %all_to_all.35 = f32[8,32,512]{2,1,0:T(8,128)S(1)} all-to-all(f32[8,32,512]{2,1,0:T(8,128)S(1)} %bitcast.184), channel_id=1, replica_groups=mesh['row'=8,'col'=16] {'row'}, dimensions={0} | all-to-all | bytes 1048576 | tf_op jit(solution)/shard_map/all_to_all | solution.py:70
  153.7 1.9 slice.154
  155.6 3.2 copy.76
  158.8 71.5 %all-to-all-start.1 = ((f32[4,5,128,256]{3,0,1,2:T(4,128)}), f32[4,5,128,256]{3,0,1,2:T(4,128)}, u32[]{:S(2)}, u32[]{:S(2)}) async-start(f32[4,5,128,256]{3,0,1,2:T(4,128)} %copy.76), calls=%async_computation.1 | async-start | bytes 5242880 | tf_op jit(solution)/shard_map/all_to_all | solution.py:16
  230.3 35.4 %all-to-all-done.1 = f32[4,5,128,256]{3,0,1,2:T(4,128)} async-done(((f32[4,5,128,256]{3,0,1,2:T(4,128)}), f32[4,5,128,256]{3,0,1,2:T(4,128)}, u32[]{:S(2)}, u32[]{:S(2)}) %all-to-all-start.1) | async-done | bytes 2621472 | tf_op jit(solution)/shard_map/all_to_all | solution.py:16
  265.7 3.7 %copy.77 = f32[128,4,5,1,256]{4,1,0,2,3:T(4,128)} copy(f32[128,4,5,1,256]{4,1,2,0,3:T(4,128)} %bitcast.13) | data formatting | bytes 5242880 | tf_op jit(solution)/shard_map/all_to_all | solution.py:16
  269.4 4.0 %reshape.32 = f32[512,5,256]{2,0,1:T(8,128)} reshape(f32[128,4,5,1,256]{4,1,0,2,3:T(4,128)} %copy.77) | data formatting | bytes 5242880 | tf_op jit(solution)/shard_map/reshape | solution.py:17
  273.4 3.3 copy.78
  276.7 22.6 %all-gather.2.cloned.1.call-done = f32[2048,512]{1,0:T(8,128)} async-done(((f32[16,512]{1,0:T(8,128)}), f32[2048,512]{1,0:T(8,128)}) %all-gather.2.cloned.1.call-update) | async-done | bytes 4194320 | tf_op jit(solution)/shard_map/all_gather | solution.py:78
  299.3 3.8 %fusion.101 = (f32[1,8,2,16,512]{4,3,0,2,1:T(8,128)}, f32[1,8,2,16,512]{4,3,0,2,1:T(8,128)S(1)}, f32[1,8,2,16,512]{4,3,0,2,1:T(8,128)S(1)}, f32[1,8,2,16,512]{4,...) fusion(f32[8,8,2,16,512]{4,3,0,2,1:T(8,128)} %bitcast.186), kind=kLoop, calls=%fused_computation.123 | loop fusion | bytes 8388608 | tf_op jit(solution)/shard_map/slice | solution.py:90
  303.1 3.0 fusion.8
  306.1 3.0 fusion.10
  309.1 2.9 fusion.12
  312.1 3.1 fusion.14
  315.2 3.1 fusion.16
  318.2 3.1 fusion.18
  321.3 3.1 fusion.20
  324.5 8.1 %fusion.6 = f32[6,256,512]{2,1,0:T(8,128)} fusion(f32[5,256,512]{2,1,0:T(8,128)} %bitcast.183, f32[1,256,512]{2,1,0:T(8,128)S(1)} %bitcast.185, f32[512,6,256]{0,2,1:T(8,128)S(1)} %fusion.8, f32[512,6,256]{0,2,1:T(8,128)S(1)} %fusion.10, f32[512,6,256]{0,2,1:T(8,128)S(1)} %fusion.12, f32[512,6,256]{0,2,1:T(8,128)} %fusion.14, f32[512,6,256]{0,2,1:T(8,128)} %fusion.16, ...), kind=kOutput, calls=%fused_computation.7 | convolution fusion | flops 1215037440 | bytes 30408704 | tf_op jit(solution)/shard_map/jrc,cs->jrs/dot_general | solution.py:87
  332.6 1.9 copy-done.2
  335.3 2.0 pad_maximum_fusion
  (119 shorter events, 23.0 us)
Async XLA Ops:
  6.5 32.3 %copy-start = (f32[8,256,256]{2,1,0:T(8,128)S(1)}, f32[8,256,256]{2,1,0:T(8,128)}, u32[]{:S(2)}) copy-start(f32[8,256,256]{2,1,0:T(8,128)} %param.5) | copy-start | bytes 6291460
  9.2 1.7 copy-start.3
  12.0 24.8 %all-to-all-start = ((f32[4,1,128,256]{3,0,1,2:T(4,128)}), f32[4,1,128,256]{3,0,1,2:T(4,128)S(1)}, u32[]{:S(2)}, u32[]{:S(2)}) async-start(f32[4,1,128,256]{3,0,1,2:T(4,128)} %copy.74), calls=%async_computation | async-start | bytes 1048576 | tf_op jit(solution)/shard_map/all_to_all | solution.py:16
  23.5 275.7 %all-gather.2.cloned.1.call-start = ((), (), s32[]{:S(2)}) async-start(), calls=%async_computation.3 | async-start | bytes 4227072 | tf_op jit(solution)/shard_map/all_gather | solution.py:78
  40.5 12.3 %collective-permute-start = (f32[256,512]{1,0:T(8,128)S(1)}, f32[256,512]{1,0:T(8,128)}, u32[]{:S(2)}, u32[]{:S(2)}) collective-permute-start(f32[256,512]{1,0:T(8,128)S(1)} %get-tuple-element.13), channel_id=1, source_target_pairs={{0,1},{16,17},{32,33},{48,49},{64,65},{80,81},{96,97},{112,113}} | collective-permute-start | bytes 1572872 | tf_op jit(solution)/shard_map/ppermute | solution.py:59
  45.0 7.8 %copy-start.26 = (f32[256,256]{1,0:T(8,128)}, f32[256,256]{1,0:T(8,128)S(1)}, u32[]{:S(2)}) copy-start(f32[256,256]{1,0:T(8,128)S(1)} %fusion.67) | copy-start | bytes 786436
  55.5 6.9 %collective-permute-start.3 = (f32[256,512]{1,0:T(8,128)}, f32[256,512]{1,0:T(8,128)}, u32[]{:S(2)}, u32[]{:S(2)}) collective-permute-start(f32[256,512]{1,0:T(8,128)} %get-tuple-element.15), channel_id=1, source_target_pairs={{1,2},{17,18},{33,34},{49,50},{65,66},{81,82},{97,98},{113,114}} | collective-permute-start | bytes 1572872 | tf_op jit(solution)/shard_map/ppermute | solution.py:59
  58.9 11.0 %collective-permute-start.1 = (f32[256,512]{1,0:T(8,128)}, f32[256,512]{1,0:T(8,128)}, u32[]{:S(2)}, u32[]{:S(2)}) collective-permute-start(f32[256,512]{1,0:T(8,128)} %add.58), channel_id=1, source_target_pairs={{0,2},{1,3},{16,18},{17,19},{32,34},{33,35},{48,50},{49,51},{64,66... | collective-permute-start | bytes 1572872 | tf_op jit(solution)/shard_map/ppermute | solution.py:59
  60.9 11.0 %copy-start.27 = (f32[256,256]{1,0:T(8,128)S(1)}, f32[256,256]{1,0:T(8,128)}, u32[]{:S(2)}) copy-start(f32[256,256]{1,0:T(8,128)} %copy-done.26) | copy-start | bytes 786436
  62.3 20.0 %copy-start.25 = (f32[256,256]{1,0:T(8,128)}, f32[256,256]{1,0:T(8,128)S(1)}, u32[]{:S(2)}) copy-start(f32[256,256]{1,0:T(8,128)S(1)} %fusion.65) | copy-start | bytes 786436
  64.5 16.5 %collective-permute-start.4 = (f32[256,512]{1,0:T(8,128)}, f32[256,512]{1,0:T(8,128)}, u32[]{:S(2)}, u32[]{:S(2)}) collective-permute-start(f32[256,512]{1,0:T(8,128)} %add.61), channel_id=1, source_target_pairs={{1,3},{2,4},{17,19},{18,20},{33,35},{34,36},{49,51},{50,52},{65,67... | collective-permute-start | bytes 1572872 | tf_op jit(solution)/shard_map/ppermute | solution.py:59
  71.1 0.8 copy-start.11
  72.5 0.8 copy-start.18
  76.0 7.7 %collective-permute-start.6 = (f32[256,512]{1,0:T(8,128)}, f32[256,512]{1,0:T(8,128)}, u32[]{:S(2)}, u32[]{:S(2)}) collective-permute-start(f32[256,512]{1,0:T(8,128)} %get-tuple-element.17), channel_id=1, source_target_pairs={{2,3},{18,19},{34,35},{50,51},{66,67},{82,83},{98,99},{114,115}} | collective-permute-start | bytes 1572872 | tf_op jit(solution)/shard_map/ppermute | solution.py:59
  77.5 7.1 %copy-start.19 = (f32[256,512]{1,0:T(8,128)S(1)}, f32[256,512]{1,0:T(8,128)}, u32[]{:S(2)}) copy-start(f32[256,512]{1,0:T(8,128)} %copy-done.18) | copy-start | bytes 1572868
  78.9 8.4 %copy-start.22 = (f32[256,256]{1,0:T(8,128)}, f32[256,256]{1,0:T(8,128)S(1)}, u32[]{:S(2)}) copy-start(f32[256,256]{1,0:T(8,128)S(1)} %fusion.63) | copy-start | bytes 786436
  78.9 16.4 %collective-permute-start.2 = (f32[256,512]{1,0:T(8,128)}, f32[256,512]{1,0:T(8,128)}, u32[]{:S(2)}, u32[]{:S(2)}) collective-permute-start(f32[256,512]{1,0:T(8,128)} %copy-done.11), channel_id=1, source_target_pairs={{0,4},{1,5},{2,6},{3,7},{16,20},{17,21},{18,22},{19,23},{32,36},{3... | collective-permute-start | bytes 1572872 | tf_op jit(solution)/shard_map/ppermute | solution.py:59
  82.3 0.8 copy-start.7
  83.7 0.8 copy-start.14
  87.2 9.9 %collective-permute-start.9 = (f32[256,512]{1,0:T(8,128)}, f32[256,512]{1,0:T(8,128)}, u32[]{:S(2)}, u32[]{:S(2)}) collective-permute-start(f32[256,512]{1,0:T(8,128)} %get-tuple-element.19), channel_id=1, source_target_pairs={{3,4},{19,20},{35,36},{51,52},{67,68},{83,84},{99,100},{115,116}} | collective-permute-start | bytes 1572872 | tf_op jit(solution)/shard_map/ppermute | solution.py:59
  90.7 10.2 %collective-permute-start.7 = (f32[256,512]{1,0:T(8,128)}, f32[256,512]{1,0:T(8,128)}, u32[]{:S(2)}, u32[]{:S(2)}) collective-permute-start(f32[256,512]{1,0:T(8,128)} %add.64), channel_id=1, source_target_pairs={{2,4},{3,5},{18,20},{19,21},{34,36},{35,37},{50,52},{51,53},{66,68... | collective-permute-start | bytes 1572872 | tf_op jit(solution)/shard_map/ppermute | solution.py:59
  92.2 10.8 %copy-start.23 = (f32[256,256]{1,0:T(8,128)S(1)}, f32[256,256]{1,0:T(8,128)}, u32[]{:S(2)}) copy-start(f32[256,256]{1,0:T(8,128)} %copy-done.22) | copy-start | bytes 786436
  93.6 10.0 %copy-start.15 = (f32[256,512]{1,0:T(8,128)S(1)}, f32[256,512]{1,0:T(8,128)}, u32[]{:S(2)}) copy-start(f32[256,512]{1,0:T(8,128)} %copy-done.14) | copy-start | bytes 1572868
  93.6 18.6 %collective-permute-start.5 = (f32[256,512]{1,0:T(8,128)}, f32[256,512]{1,0:T(8,128)}, u32[]{:S(2)}, u32[]{:S(2)}) collective-permute-start(f32[256,512]{1,0:T(8,128)} %copy-done.7), channel_id=1, source_target_pairs={{1,5},{2,6},{3,7},{17,21},{18,22},{19,23},{33,37},{34,38},{35,39},... | collective-permute-start | bytes 1572872 | tf_op jit(solution)/shard_map/ppermute | solution.py:59
  97.2 9.4 %copy-start.20 = (f32[256,512]{1,0:T(8,128)}, f32[256,512]{1,0:T(8,128)S(1)}, u32[]{:S(2)}) copy-start(f32[256,512]{1,0:T(8,128)S(1)} %convolution_subtract_fusion.9) | copy-start | bytes 1572868
  99.4 16.9 %collective-permute-start.10 = (f32[256,512]{1,0:T(8,128)}, f32[256,512]{1,0:T(8,128)}, u32[]{:S(2)}, u32[]{:S(2)}) collective-permute-start(f32[256,512]{1,0:T(8,128)} %add.67), channel_id=1, source_target_pairs={{3,5},{4,6},{19,21},{20,22},{35,37},{36,38},{51,53},{52,54},{67,69... | collective-permute-start | bytes 1572872 | tf_op jit(solution)/shard_map/ppermute | solution.py:59
  102.2 0.8 copy-start.9
  103.0 9.2 %copy-start.8 = (f32[256,512]{1,0:T(8,128)S(1)}, f32[256,512]{1,0:T(8,128)}, u32[]{:S(2)}) copy-start(f32[256,512]{1,0:T(8,128)} %copy-done.7) | copy-start | bytes 1572868
  103.7 2.9 copy-start.16
  106.5 7.6 %collective-permute-start.12 = (f32[256,512]{1,0:T(8,128)}, f32[256,512]{1,0:T(8,128)}, u32[]{:S(2)}, u32[]{:S(2)}) collective-permute-start(f32[256,512]{1,0:T(8,128)} %get-tuple-element.21), channel_id=1, source_target_pairs={{4,5},{20,21},{36,37},{52,53},{68,69},{84,85},{100,101},{116,117}} | collective-permute-start | bytes 1572872 | tf_op jit(solution)/shard_map/ppermute | solution.py:59
  111.4 11.5 %copy-start.28 = (f32[256,256]{1,0:T(8,128)}, f32[256,256]{1,0:T(8,128)S(1)}, u32[]{:S(2)}) copy-start(f32[256,256]{1,0:T(8,128)S(1)} %fusion.57) | copy-start | bytes 786436
  111.4 6.9 %copy-start.17 = (f32[256,512]{1,0:T(8,128)S(1)}, f32[256,512]{1,0:T(8,128)}, u32[]{:S(2)}) copy-start(f32[256,512]{1,0:T(8,128)} %copy-done.16) | copy-start | bytes 1572868
  111.4 6.9 %copy-start.29 = (f32[256,256]{1,0:T(8,128)S(1)}, f32[256,256]{1,0:T(8,128)}, u32[]{:S(2)}) copy-start(f32[256,256]{1,0:T(8,128)} %fusion.55) | copy-start | bytes 786436
  111.4 10.1 %collective-permute-start.8 = (f32[256,512]{1,0:T(8,128)}, f32[256,512]{1,0:T(8,128)S(1)}, u32[]{:S(2)}, u32[]{:S(2)}) collective-permute-start(f32[256,512]{1,0:T(8,128)} %copy-done.9), channel_id=1, source_target_pairs={{2,6},{3,7},{18,22},{19,23},{34,38},{35,39},{50,54},{51,55},{66,70... | collective-permute-start | bytes 1572872 | tf_op jit(solution)/shard_map/ppermute | solution.py:59
  115.5 6.0 %copy-start.10 = (f32[256,512]{1,0:T(8,128)S(1)}, f32[256,512]{1,0:T(8,128)}, u32[]{:S(2)}) copy-start(f32[256,512]{1,0:T(8,128)} %copy-done.9) | copy-start | bytes 1572868
  115.5 6.0 %copy-start.24 = (f32[256,256]{1,0:T(8,128)S(1)}, f32[256,256]{1,0:T(8,128)}, u32[]{:S(2)}) copy-start(f32[256,256]{1,0:T(8,128)} %copy-done.22) | copy-start | bytes 786436
  115.5 6.7 %collective-permute-start.14 = (f32[256,512]{1,0:T(8,128)S(1)}, f32[256,512]{1,0:T(8,128)S(1)}, u32[]{:S(2)}, u32[]{:S(2)}) collective-permute-start(f32[256,512]{1,0:T(8,128)S(1)} %add.70), channel_id=1, source_target_pairs={{4,6},{5,7},{20,22},{21,23},{36,38},{37,39},{52,54},{53,55},{68,70... | collective-permute-start | bytes 1572872 | tf_op jit(solution)/shard_map/ppermute | solution.py:59
  120.8 2.0 collective-permute-start.13
  122.2 5.5 %copy-start.12 = (f32[256,512]{1,0:T(8,128)}, f32[256,512]{1,0:T(8,128)S(1)}, u32[]{:S(2)}) copy-start(f32[256,512]{1,0:T(8,128)S(1)} %convolution_subtract_fusion.5) | copy-start | bytes 1572868
  122.8 0.8 copy-start.5
  125.2 6.1 %collective-permute-start.15 = (f32[256,512]{1,0:T(8,128)}, f32[256,512]{1,0:T(8,128)}, u32[]{:S(2)}, u32[]{:S(2)}) collective-permute-start(f32[256,512]{1,0:T(8,128)} %get-tuple-element.25), channel_id=1, source_target_pairs={{6,7},{22,23},{38,39},{54,55},{70,71},{86,87},{102,103},{118,119}} | collective-permute-start | bytes 1572872 | tf_op jit(solution)/shard_map/ppermute | solution.py:59
  127.6 5.4 %collective-permute-start.16 = (f32[256,512]{1,0:T(8,128)}, f32[256,512]{1,0:T(8,128)}, u32[]{:S(2)}, u32[]{:S(2)}) collective-permute-start(f32[256,512]{1,0:T(8,128)} %add.72), channel_id=1, source_target_pairs={{5,7},{21,23},{37,39},{53,55},{69,71},{85,87},{101,103},{117,119}} | collective-permute-start | bytes 1572872 | tf_op jit(solution)/shard_map/ppermute | solution.py:59
  129.1 5.9 %copy-start.6 = (f32[256,512]{1,0:T(8,128)S(1)}, f32[256,512]{1,0:T(8,128)}, u32[]{:S(2)}) copy-start(f32[256,512]{1,0:T(8,128)} %copy-done.5) | copy-start | bytes 1572868
  129.1 5.9 %copy-start.13 = (f32[256,512]{1,0:T(8,128)S(1)}, f32[256,512]{1,0:T(8,128)}, u32[]{:S(2)}) copy-start(f32[256,512]{1,0:T(8,128)} %copy-done.12) | copy-start | bytes 1572868
  129.1 5.9 %copy-start.30 = (f32[256,512]{1,0:T(8,128)S(1)}, f32[256,512]{1,0:T(8,128)}, u32[]{:S(2)}) copy-start(f32[256,512]{1,0:T(8,128)} %get-tuple-element.16) | copy-start | bytes 1572868
  129.1 5.9 %copy-start.31 = (f32[256,512]{1,0:T(8,128)S(1)}, f32[256,512]{1,0:T(8,128)}, u32[]{:S(2)}) copy-start(f32[256,512]{1,0:T(8,128)} %get-tuple-element.18) | copy-start | bytes 1572868
  129.1 5.9 %copy-start.32 = (f32[256,512]{1,0:T(8,128)S(1)}, f32[256,512]{1,0:T(8,128)}, u32[]{:S(2)}) copy-start(f32[256,512]{1,0:T(8,128)} %get-tuple-element.20) | copy-start | bytes 1572868
  129.1 5.9 %copy-start.33 = (f32[256,512]{1,0:T(8,128)S(1)}, f32[256,512]{1,0:T(8,128)}, u32[]{:S(2)}) copy-start(f32[256,512]{1,0:T(8,128)} %get-tuple-element.22) | copy-start | bytes 1572868
  129.1 5.9 %copy-start.34 = (f32[256,512]{1,0:T(8,128)S(1)}, f32[256,512]{1,0:T(8,128)}, u32[]{:S(2)}) copy-start(f32[256,512]{1,0:T(8,128)} %get-tuple-element.24) | copy-start | bytes 1572868
  130.6 4.3 %collective-permute-start.11 = (f32[256,512]{1,0:T(8,128)S(1)}, f32[256,512]{1,0:T(8,128)S(1)}, u32[]{:S(2)}, u32[]{:S(2)}) collective-permute-start(f32[256,512]{1,0:T(8,128)S(1)} %add.68), channel_id=1, source_target_pairs={{3,7},{19,23},{35,39},{51,55},{67,71},{83,87},{99,103},{115,119}} | collective-permute-start | bytes 1572872 | tf_op jit(solution)/shard_map/ppermute | solution.py:59
  136.0 19.6 %copy-start.4 = (f32[256,512]{1,0:T(8,128)}, f32[256,512]{1,0:T(8,128)S(1)}, u32[]{:S(2)}) copy-start(f32[256,512]{1,0:T(8,128)S(1)} %fusion.39) | copy-start | bytes 1572868
  150.7 2.3 collective-permute-start.17
  158.8 106.9 %all-to-all-start.1 = ((f32[4,5,128,256]{3,0,1,2:T(4,128)}), f32[4,5,128,256]{3,0,1,2:T(4,128)}, u32[]{:S(2)}, u32[]{:S(2)}) async-start(f32[4,5,128,256]{3,0,1,2:T(4,128)} %copy.76), calls=%async_computation.1 | async-start | bytes 5242880 | tf_op jit(solution)/shard_map/all_to_all | solution.py:16
  299.3 12.8 %slice-start = ((s8[12582912]{0:T(1024)(128)(4,1)}), s8[4194304]{0:T(1024)(128)(4,1)S(1)}, s32[]{:S(2)}) async-start(s8[12582912]{0:T(1024)(128)(4,1)} %bitcast.179), calls=%async_computation.4 | async-start | bytes 8388608
  299.3 12.8 %slice-start.1 = ((s8[12582912]{0:T(1024)(128)(4,1)}), s8[4194304]{0:T(1024)(128)(4,1)S(1)}, s32[]{:S(2)}) async-start(s8[12582912]{0:T(1024)(128)(4,1)} %bitcast.179), calls=%async_computation.5 | async-start | bytes 8388608
  306.1 6.0 %slice-start.2 = ((s8[12582912]{0:T(1024)(128)(4,1)}), s8[4194304]{0:T(1024)(128)(4,1)S(1)}, s32[]{:S(2)}) async-start(s8[12582912]{0:T(1024)(128)(4,1)} %bitcast.179), calls=%async_computation.6 | async-start | bytes 8388608
  321.3 3.1 copy-start.21
  321.3 3.1 copy-start.35
  332.6 1.9 copy-start.2
  332.6 2.7 slice-start.3
  334.5 2.8 copy-start.1
Sparse Core Ops, SparseCore 0:
  153.8 145.4 all-gather.1

commit v9 on v3

--- a/solution.py
+++ b/solution.py
@@ -87,14 +87,13 @@
     )
 
     update = jnp.concatenate([lead[None], rest], axis=0)
-    for section in range(sections):
-        update = update - jnp.einsum(
-            "jrc,cs->jrs",
-            panels[section],
-            whole[section * width_block:(section + 1) * width_block],
-            precision=lax.Precision.HIGH,
-            preferred_element_type=jnp.float32,
-        )
+    update = update - jnp.einsum(
+        "kjrc,kcs->jrs",
+        panels,
+        whole.reshape(sections, width_block, -1),
+        precision=lax.Precision.HIGH,
+        preferred_element_type=jnp.float32,
+    )
     first = jnp.where(device < sections, own, update[0])
     return jnp.concatenate([first[None], update[1:]], axis=0)
 

time: 305 us -> 287 us (0.941)
  matrix products: 68.5 us -> 53.8 us
  local copies, waits for them, and re-layouts: 35.6 us -> 25.1 us
  waiting for transfers between devices: 72.3 us -> 77.2 us
  starting transfers between devices: 73.1 us -> 76.4 us
    dot_general x8 -> x1, matrix products: 29.4 us -> 12.9 us  [per_device(): jnp.einsum('kjrc,kcs->jrs', panels, whole.reshape(sections, width_block,...]
    all_to_all x2, starting transfers between devices: 49.6 us -> 55.1 us  [transpose_in(): lax.all_to_all(pieces, AXES, split_axis=2, concat_axis=0, tiled=True)]
    all_gather x1, waiting for transfers between devices: 22.6 us -> 27.2 us  [per_device(): gathered = lax.all_gather(mine, AXES, tiled=True)]
    slice x1 -> x0, local copies, waits for them, and re-layouts: 3.8 us -> none  [per_device(): whole[section * width_block:(section + 1) * width_block]]
    unnamed x79 -> x69, local copies, waits for them, and re-layouts: 11.8 us -> 8.57 us
  transfers between devices with their start and end apart: 21 -> 21, of which waited for: 4 -> 4; matrix products, arithmetic and copies ran while one was open for 21% -> 19% of each run, Pallas kernels for 0% -> 0%
where the time goes in v9:
time: 287 us; the launch traced here: 286 us
  waiting for transfers between devices  77.2 us (27%)
  starting transfers between devices  76.4 us (27%)
  matrix products  53.8 us (19%)
  local copies, waits for them, and re-layouts  25.1 us (9%)
  blocking collectives  21.4 us (7%)
  other arithmetic  17.5 us (6%)
  between operations  14.2 us (5%)
    all_to_all x2, starting transfers between devices, transpose_in(): lax.all_to_all(pieces, AXES, split_axis=2, concat_axis=0, tiled=True)  55.1 us
    all_to_all x2, waiting for transfers between devices, transpose_in(): lax.all_to_all(pieces, AXES, split_axis=2, concat_axis=0, tiled=True)  48.9 us
    dot_general x25, matrix products, mm(): return jnp.dot(a, b, precision=HI, preferred_element_type=jnp.float32)  40.9 us
    all_gather x1, waiting for transfers between devices, per_device(): gathered = lax.all_gather(mine, AXES, tiled=True)  27.2 us
    all_to_all x1, blocking collectives, per_device(): lax.all_to_all(own.reshape(rows, cut, -1), 'row', 0, 0, tiled=True)[0]  21.4 us
    ppermute x17, starting transfers between devices, per_device(): got = lax.ppermute(buf, AXES, pairs)  19.9 us
    add x10, other arithmetic, per_device(): buf = buf + got  14.1 us
    dot_general x1, matrix products, per_device(): jnp.einsum('kjrc,kcs->jrs', panels, whole.reshape(sections, width_block,...  12.9 us
  transfers between devices with their start and end apart: 21, of which 4 were waited for; matrix products, arithmetic and copies ran while one was open for 19% of the time, Pallas kernels for 0%

profile of v9, /device:TPU:1, one launch (start us, length us, event | category | flops | bytes accessed | tf_op | source)
XLA Modules:
  0.0 285.6 jit_solution(2750439579004539818)
XLA Ops:
  6.5 2.6 copy.44
  9.2 1.7 copy-done.2
  10.9 1.1 copy.31
  12.0 11.5 %all-to-all-start = ((f32[4,1,128,256]{3,0,1,2:T(4,128)}), f32[4,1,128,256]{3,0,1,2:T(4,128)S(1)}, u32[]{:S(2)}, u32[]{:S(2)}) async-start(f32[4,1,128,256]{3,0,1,2:T(4,128)} %copy.31), calls=%async_computation | async-start | bytes 1048576 | tf_op jit(solution)/shard_map/all_to_all | solution.py:16
  23.6 13.3 %all-to-all-done = f32[4,1,128,256]{3,0,1,2:T(4,128)S(1)} async-done(((f32[4,1,128,256]{3,0,1,2:T(4,128)}), f32[4,1,128,256]{3,0,1,2:T(4,128)S(1)}, u32[]{:S(2)}, u32[]{:S(2)}) %all-to-all-start) | async-done | bytes 524320 | tf_op jit(solution)/shard_map/all_to_all | solution.py:16
  37.5 1.4 copy.32
  38.9 1.7 broadcast_select_fusion.6
  40.6 1.5 collective-permute-start
  42.0 1.3 fusion.37
  43.4 2.0 add.58
  45.4 1.4 collective-permute-start.1
  46.9 2.6 broadcast_select_fusion.5
  49.5 1.5 collective-permute-start.3
  51.0 1.3 fusion.35
  52.3 2.2 add.59
  54.5 1.7 fusion.71
  57.0 2.7 broadcast_select_fusion.4
  59.7 1.5 collective-permute-start.6
  61.1 2.1 add.61
  63.2 1.4 collective-permute-start.4
  64.7 1.4 fusion.33
  66.1 1.4 fusion.31
  68.2 1.3 add.64
  69.5 0.8 collective-permute-start.7
  70.4 2.1 add.62
  72.5 1.5 collective-permute-start.5
  73.9 1.7 fusion.72
  75.6 2.5 broadcast_select_fusion.3
  78.8 1.7 convolution_subtract_fusion.9
  81.3 1.6 broadcast_select_fusion.2
  82.9 1.5 collective-permute-start.12
  84.4 0.9 add.67
  85.2 1.4 collective-permute-start.10
  86.7 2.0 fusion.25
  88.7 1.3 fusion.27
  90.1 0.8 collective-permute-start.8
  90.9 2.1 convolution_subtract_fusion.7
  93.1 1.3 add.70
  94.4 0.8 collective-permute-start.14
  95.2 1.3 add.68
  97.2 2.5 broadcast_select_fusion.1
  102.5 1.7 broadcast_select_fusion
  104.2 1.6 collective-permute-start.15
  105.8 0.9 add.72
  106.7 1.4 collective-permute-start.16
  108.2 1.5 fusion.29
  110.4 1.7 fusion.75
  112.1 1.8 fusion.17
  114.0 2.2 fusion.9
  117.0 21.4 %all_to_all.35 = f32[8,32,512]{2,1,0:T(8,128)S(1)} all-to-all(f32[8,32,512]{2,1,0:T(8,128)S(1)} %bitcast.123), channel_id=1, replica_groups=mesh['row'=8,'col'=16] {'row'}, dimensions={0} | all-to-all | bytes 1048576 | tf_op jit(solution)/shard_map/all_to_all | solution.py:70
  138.4 0.8 copy-done.33
  139.2 1.3 collective-permute-start.17
  140.5 1.0 collective-permute-done.17
  141.5 1.4 fusion.62
  143.1 3.2 %copy.33 = f32[4,5,128,256]{3,0,1,2:T(4,128)} copy(f32[4,5,128,256]{3,2,1,0:T(8,128)S(1)} %slice.58) | data formatting | bytes 5242880 | tf_op jit(solution)/shard_map/slice | solution.py:27
  146.2 43.6 %all-to-all-start.1 = ((f32[4,5,128,256]{3,0,1,2:T(4,128)}), f32[4,5,128,256]{3,0,1,2:T(4,128)S(1)}, u32[]{:S(2)}, u32[]{:S(2)}) async-start(f32[4,5,128,256]{3,0,1,2:T(4,128)} %copy.33), calls=%async_computation.1 | async-start | bytes 5242880 | tf_op jit(solution)/shard_map/all_to_all | solution.py:16
  189.9 35.7 %all-to-all-done.1 = f32[4,5,128,256]{3,0,1,2:T(4,128)S(1)} async-done(((f32[4,5,128,256]{3,0,1,2:T(4,128)}), f32[4,5,128,256]{3,0,1,2:T(4,128)S(1)}, u32[]{:S(2)}, u32[]{:S(2)}) %all-to-all-start.1) | async-done | bytes 2621472 | tf_op jit(solution)/shard_map/all_to_all | solution.py:16
  225.5 1.9 copy.34
  227.5 2.8 reshape.23
  230.3 2.1 copy.35
  232.4 27.2 %all-gather.2.cloned.1.call-done = f32[2048,512]{1,0:T(8,128)} async-done(((f32[16,512]{1,0:T(8,128)}), f32[2048,512]{1,0:T(8,128)}) %all-gather.2.cloned.1.call-update) | async-done | bytes 4194320 | tf_op jit(solution)/shard_map/all_gather | solution.py:82
  259.7 2.9 %copy.36 = f32[8,8,2,16,512]{4,3,2,1,0:T(8,128)S(1)} copy(f32[8,8,2,16,512]{4,3,0,2,1:T(8,128)} %bitcast.124) | data formatting | bytes 8388608 | tf_op jit(solution)/shard_map/transpose | solution.py:85
  262.7 12.9 %bitcast_subtract_fusion = f32[6,256,512]{2,1,0:T(8,128)S(1)} fusion(f32[5,256,512]{2,1,0:T(8,128)S(1)} %bitcast.127, f32[1,256,512]{2,1,0:T(8,128)S(1)} %bitcast.128, f32[8,256,512,1]{2,1,3,0:T(8,128)S(1)} %bitcast.125, f32[8,6,256,256]{3,2,1,0:T(8,128)} %param.4), kind=kOutput, calls=%fused_computation | convolution fusion | flops 9665249280 | bytes 23068672 | tf_op jit(solution)/shard_map/kjrc,kcs->jrs/dot_general | solution.py:90
  276.8 2.0 pad_maximum_fusion
  (100 shorter events, 10.1 us)
Async XLA Ops:
  6.5 32.4 %copy-start = (f32[8,256,256]{2,1,0:T(8,128)S(1)}, f32[8,256,256]{2,1,0:T(8,128)}, u32[]{:S(2)}) copy-start(f32[8,256,256]{2,1,0:T(8,128)} %param.5) | copy-start | bytes 6291460
  9.2 1.7 copy-start.2
  12.0 24.8 %all-to-all-start = ((f32[4,1,128,256]{3,0,1,2:T(4,128)}), f32[4,1,128,256]{3,0,1,2:T(4,128)S(1)}, u32[]{:S(2)}, u32[]{:S(2)}) async-start(f32[4,1,128,256]{3,0,1,2:T(4,128)} %copy.31), calls=%async_computation | async-start | bytes 1048576 | tf_op jit(solution)/shard_map/all_to_all | solution.py:16
  23.5 236.1 %all-gather.2.cloned.1.call-start = ((), (), s32[]{:S(2)}) async-start(), calls=%async_computation.3 | async-start | bytes 4227072 | tf_op jit(solution)/shard_map/all_gather | solution.py:82
  40.6 35.0 %copy-start.4 = (f32[256,512]{1,0:T(8,128)}, f32[256,512]{1,0:T(8,128)S(1)}, u32[]{:S(2)}) copy-start(f32[256,512]{1,0:T(8,128)S(1)} %get-tuple-element.5) | copy-start | bytes 1572868
  40.6 2.8 collective-permute-start
  43.4 11.1 %copy-start.22 = (f32[256,256]{1,0:T(8,128)}, f32[256,256]{1,0:T(8,128)S(1)}, u32[]{:S(2)}) copy-start(f32[256,256]{1,0:T(8,128)S(1)} %fusion.37) | copy-start | bytes 786436
  45.4 6.9 %collective-permute-start.1 = (f32[256,512]{1,0:T(8,128)}, f32[256,512]{1,0:T(8,128)}, u32[]{:S(2)}, u32[]{:S(2)}) collective-permute-start(f32[256,512]{1,0:T(8,128)} %add.58), channel_id=1, source_target_pairs={{0,2},{1,3}} | collective-permute-start | bytes 1572872 | tf_op jit(solution)/shard_map/ppermute | solution.py:59
  49.5 6.7 %collective-permute-start.3 = (f32[256,512]{1,0:T(8,128)}, f32[256,512]{1,0:T(8,128)}, u32[]{:S(2)}, u32[]{:S(2)}) collective-permute-start(f32[256,512]{1,0:T(8,128)} %get-tuple-element.7), channel_id=1, source_target_pairs={{1,2}} | collective-permute-start | bytes 1572872 | tf_op jit(solution)/shard_map/ppermute | solution.py:59
  52.3 10.9 %copy-start.20 = (f32[256,256]{1,0:T(8,128)}, f32[256,256]{1,0:T(8,128)S(1)}, u32[]{:S(2)}) copy-start(f32[256,256]{1,0:T(8,128)S(1)} %fusion.35) | copy-start | bytes 786436
  56.2 0.8 copy-start.15
  59.7 8.6 %collective-permute-start.6 = (f32[256,512]{1,0:T(8,128)}, f32[256,512]{1,0:T(8,128)}, u32[]{:S(2)}, u32[]{:S(2)}) collective-permute-start(f32[256,512]{1,0:T(8,128)} %get-tuple-element.9), channel_id=1, source_target_pairs={{2,3}} | collective-permute-start | bytes 1572872 | tf_op jit(solution)/shard_map/ppermute | solution.py:59
  63.2 7.1 %collective-permute-start.4 = (f32[256,512]{1,0:T(8,128)}, f32[256,512]{1,0:T(8,128)}, u32[]{:S(2)}, u32[]{:S(2)}) collective-permute-start(f32[256,512]{1,0:T(8,128)} %add.61), channel_id=1, source_target_pairs={{1,3},{2,4}} | collective-permute-start | bytes 1572872 | tf_op jit(solution)/shard_map/ppermute | solution.py:59
  64.7 9.3 %copy-start.21 = (f32[256,256]{1,0:T(8,128)S(1)}, f32[256,256]{1,0:T(8,128)}, u32[]{:S(2)}) copy-start(f32[256,256]{1,0:T(8,128)} %copy-done.20) | copy-start | bytes 786436
  64.7 10.9 %copy-start.16 = (f32[256,512]{1,0:T(8,128)S(1)}, f32[256,512]{1,0:T(8,128)}, u32[]{:S(2)}) copy-start(f32[256,512]{1,0:T(8,128)} %copy-done.15) | copy-start | bytes 1572868
  66.1 14.5 %copy-start.18 = (f32[256,256]{1,0:T(8,128)}, f32[256,256]{1,0:T(8,128)S(1)}, u32[]{:S(2)}) copy-start(f32[256,256]{1,0:T(8,128)S(1)} %fusion.33) | copy-start | bytes 786436
  67.5 11.3 %collective-permute-start.2 = (f32[256,512]{1,0:T(8,128)}, f32[256,512]{1,0:T(8,128)S(1)}, u32[]{:S(2)}, u32[]{:S(2)}) collective-permute-start(f32[256,512]{1,0:T(8,128)} %add.59), channel_id=1, source_target_pairs={{0,4},{1,5},{2,6},{3,7}} | collective-permute-start | bytes 1572872 | tf_op jit(solution)/shard_map/ppermute | solution.py:59
  69.5 9.3 %copy-start.23 = (f32[256,256]{1,0:T(8,128)S(1)}, f32[256,256]{1,0:T(8,128)}, u32[]{:S(2)}) copy-start(f32[256,256]{1,0:T(8,128)} %copy-done.22) | copy-start | bytes 786436
  69.5 11.0 %collective-permute-start.7 = (f32[256,512]{1,0:T(8,128)S(1)}, f32[256,512]{1,0:T(8,128)S(1)}, u32[]{:S(2)}, u32[]{:S(2)}) collective-permute-start(f32[256,512]{1,0:T(8,128)S(1)} %add.64), channel_id=1, source_target_pairs={{2,4},{3,5}} | collective-permute-start | bytes 1572872 | tf_op jit(solution)/shard_map/ppermute | solution.py:59
  72.5 18.5 %collective-permute-start.5 = (f32[256,512]{1,0:T(8,128)}, f32[256,512]{1,0:T(8,128)}, u32[]{:S(2)}, u32[]{:S(2)}) collective-permute-start(f32[256,512]{1,0:T(8,128)} %add.62), channel_id=1, source_target_pairs={{1,5},{2,6},{3,7}} | collective-permute-start | bytes 1572872 | tf_op jit(solution)/shard_map/ppermute | solution.py:59
  78.1 3.1 %collective-permute-start.9 = (f32[256,512]{1,0:T(8,128)S(1)}, f32[256,512]{1,0:T(8,128)S(1)}, u32[]{:S(2)}, u32[]{:S(2)}) collective-permute-start(f32[256,512]{1,0:T(8,128)S(1)} %get-tuple-element.11), channel_id=1, source_target_pairs={{3,4}} | collective-permute-start | bytes 1572872 | tf_op jit(solution)/shard_map/ppermute | solution.py:59
  80.5 2.4 copy-start.17
  81.2 8.8 %copy-start.13 = (f32[256,512]{1,0:T(8,128)}, f32[256,512]{1,0:T(8,128)S(1)}, u32[]{:S(2)}) copy-start(f32[256,512]{1,0:T(8,128)S(1)} %fusion.73) | copy-start | bytes 1572868
  82.9 10.2 %collective-permute-start.12 = (f32[256,512]{1,0:T(8,128)}, f32[256,512]{1,0:T(8,128)}, u32[]{:S(2)}, u32[]{:S(2)}) collective-permute-start(f32[256,512]{1,0:T(8,128)} %get-tuple-element.13), channel_id=1, source_target_pairs={{4,5}} | collective-permute-start | bytes 1572872 | tf_op jit(solution)/shard_map/ppermute | solution.py:59
  85.2 10.0 %collective-permute-start.10 = (f32[256,512]{1,0:T(8,128)}, f32[256,512]{1,0:T(8,128)}, u32[]{:S(2)}, u32[]{:S(2)}) collective-permute-start(f32[256,512]{1,0:T(8,128)} %add.67), channel_id=1, source_target_pairs={{3,5},{4,6}} | collective-permute-start | bytes 1572872 | tf_op jit(solution)/shard_map/ppermute | solution.py:59
  90.1 11.6 %copy-start.25 = (f32[256,256]{1,0:T(8,128)}, f32[256,256]{1,0:T(8,128)S(1)}, u32[]{:S(2)}) copy-start(f32[256,256]{1,0:T(8,128)S(1)} %fusion.27) | copy-start | bytes 786436
  90.1 7.1 %copy-start.27 = (f32[256,256]{1,0:T(8,128)S(1)}, f32[256,256]{1,0:T(8,128)}, u32[]{:S(2)}) copy-start(f32[256,256]{1,0:T(8,128)} %fusion.25) | copy-start | bytes 786436
  90.1 10.3 %collective-permute-start.8 = (f32[256,512]{1,0:T(8,128)S(1)}, f32[256,512]{1,0:T(8,128)S(1)}, u32[]{:S(2)}, u32[]{:S(2)}) collective-permute-start(f32[256,512]{1,0:T(8,128)S(1)} %add.65), channel_id=1, source_target_pairs={{2,6},{3,7}} | collective-permute-start | bytes 1572872 | tf_op jit(solution)/shard_map/ppermute | solution.py:59
  90.9 6.2 %copy-start.14 = (f32[256,512]{1,0:T(8,128)S(1)}, f32[256,512]{1,0:T(8,128)}, u32[]{:S(2)}) copy-start(f32[256,512]{1,0:T(8,128)} %copy-done.13) | copy-start | bytes 1572868
  94.4 6.0 %copy-start.19 = (f32[256,256]{1,0:T(8,128)S(1)}, f32[256,256]{1,0:T(8,128)}, u32[]{:S(2)}) copy-start(f32[256,256]{1,0:T(8,128)} %copy-done.18) | copy-start | bytes 786436
  94.4 6.6 %collective-permute-start.14 = (f32[256,512]{1,0:T(8,128)S(1)}, f32[256,512]{1,0:T(8,128)S(1)}, u32[]{:S(2)}, u32[]{:S(2)}) collective-permute-start(f32[256,512]{1,0:T(8,128)S(1)} %add.70), channel_id=1, source_target_pairs={{4,6},{5,7}} | collective-permute-start | bytes 1572872 | tf_op jit(solution)/shard_map/ppermute | solution.py:59
  96.5 13.1 %copy-start.5 = (f32[256,512]{1,0:T(8,128)}, f32[256,512]{1,0:T(8,128)S(1)}, u32[]{:S(2)}) copy-start(f32[256,512]{1,0:T(8,128)S(1)} %add.68) | copy-start | bytes 1572868
  99.7 2.0 collective-permute-start.13
  101.0 5.7 %copy-start.11 = (f32[256,512]{1,0:T(8,128)}, f32[256,512]{1,0:T(8,128)S(1)}, u32[]{:S(2)}) copy-start(f32[256,512]{1,0:T(8,128)S(1)} %convolution_subtract_fusion.5) | copy-start | bytes 1572868
  101.7 0.8 copy-start.9
  104.2 7.9 %copy-start.26 = (f32[256,256]{1,0:T(8,128)S(1)}, f32[256,256]{1,0:T(8,128)}, u32[]{:S(2)}) copy-start(f32[256,256]{1,0:T(8,128)} %copy-done.25) | copy-start | bytes 786436
  104.2 6.2 %collective-permute-start.15 = (f32[256,512]{1,0:T(8,128)}, f32[256,512]{1,0:T(8,128)}, u32[]{:S(2)}, u32[]{:S(2)}) collective-permute-start(f32[256,512]{1,0:T(8,128)} %get-tuple-element.17), channel_id=1, source_target_pairs={{6,7}} | collective-permute-start | bytes 1572872 | tf_op jit(solution)/shard_map/ppermute | solution.py:59
  106.7 5.4 %collective-permute-start.16 = (f32[256,512]{1,0:T(8,128)}, f32[256,512]{1,0:T(8,128)}, u32[]{:S(2)}, u32[]{:S(2)}) collective-permute-start(f32[256,512]{1,0:T(8,128)} %add.72), channel_id=1, source_target_pairs={{5,7}} | collective-permute-start | bytes 1572872 | tf_op jit(solution)/shard_map/ppermute | solution.py:59
  108.1 5.8 %copy-start.10 = (f32[256,512]{1,0:T(8,128)S(1)}, f32[256,512]{1,0:T(8,128)}, u32[]{:S(2)}) copy-start(f32[256,512]{1,0:T(8,128)} %copy-done.9) | copy-start | bytes 1572868
  108.1 5.8 %copy-start.12 = (f32[256,512]{1,0:T(8,128)S(1)}, f32[256,512]{1,0:T(8,128)}, u32[]{:S(2)}) copy-start(f32[256,512]{1,0:T(8,128)} %copy-done.11) | copy-start | bytes 1572868
  108.1 5.9 %copy-start.28 = (f32[256,512]{1,0:T(8,128)S(1)}, f32[256,512]{1,0:T(8,128)}, u32[]{:S(2)}) copy-start(f32[256,512]{1,0:T(8,128)} %get-tuple-element.8) | copy-start | bytes 1572868
  108.1 5.9 %copy-start.30 = (f32[256,512]{1,0:T(8,128)S(1)}, f32[256,512]{1,0:T(8,128)}, u32[]{:S(2)}) copy-start(f32[256,512]{1,0:T(8,128)} %get-tuple-element.10) | copy-start | bytes 1572868
  108.1 5.9 %copy-start.31 = (f32[256,512]{1,0:T(8,128)S(1)}, f32[256,512]{1,0:T(8,128)}, u32[]{:S(2)}) copy-start(f32[256,512]{1,0:T(8,128)} %get-tuple-element.12) | copy-start | bytes 1572868
  108.1 5.9 %copy-start.32 = (f32[256,512]{1,0:T(8,128)S(1)}, f32[256,512]{1,0:T(8,128)}, u32[]{:S(2)}) copy-start(f32[256,512]{1,0:T(8,128)} %get-tuple-element.14) | copy-start | bytes 1572868
  109.7 4.3 %collective-permute-start.11 = (f32[256,512]{1,0:T(8,128)S(1)}, f32[256,512]{1,0:T(8,128)S(1)}, u32[]{:S(2)}, u32[]{:S(2)}) collective-permute-start(f32[256,512]{1,0:T(8,128)S(1)} %add.68), channel_id=1, source_target_pairs={{3,7}} | collective-permute-start | bytes 1572872 | tf_op jit(solution)/shard_map/ppermute | solution.py:59
  110.4 3.7 %copy-start.6 = (f32[256,512]{1,0:T(8,128)S(1)}, f32[256,512]{1,0:T(8,128)}, u32[]{:S(2)}) copy-start(f32[256,512]{1,0:T(8,128)} %copy-done.5) | copy-start | bytes 1572868
  114.0 28.8 %copy-start.3 = (f32[1,4,768,256]{3,2,1,0:T(8,128)S(1)}, f32[1,4,768,256]{3,2,1,0:T(8,128)}, u32[]{:S(2)}) copy-start(f32[1,4,768,256]{3,2,1,0:T(8,128)} %copy-done.2) | copy-start | bytes 9437188
  116.2 0.8 copy-start.7
  138.4 0.8 copy-start.33
  139.2 2.3 collective-permute-start.17
  146.2 79.3 %all-to-all-start.1 = ((f32[4,5,128,256]{3,0,1,2:T(4,128)}), f32[4,5,128,256]{3,0,1,2:T(4,128)S(1)}, u32[]{:S(2)}, u32[]{:S(2)}) async-start(f32[4,5,128,256]{3,0,1,2:T(4,128)} %copy.33), calls=%async_computation.1 | async-start | bytes 5242880 | tf_op jit(solution)/shard_map/all_to_all | solution.py:16
  259.7 3.0 %copy-start.24 = (f32[512,5,256]{0,2,1:T(8,128)S(1)}, f32[512,5,256]{0,2,1:T(8,128)}, u32[]{:S(2)}) copy-start(f32[512,5,256]{0,2,1:T(8,128)} %copy.35) | copy-start | bytes 7864324
  259.7 3.1 %copy-start.29 = (f32[512,1,256]{0,2,1:T(8,128)S(1)}, f32[512,1,256]{0,2,1:T(8,128)}, u32[]{:S(2)}) copy-start(f32[512,1,256]{0,2,1:T(8,128)} %copy.32) | copy-start | bytes 1572868
  275.6 1.0 copy-start.8
  276.7 2.1 copy-start.1
Sparse Core Ops, SparseCore 0:
  143.0 116.6 all-gather.1

commit v10 on v9

--- a/solution.py
+++ b/solution.py
@@ -80,17 +80,12 @@
         got = lax.ppermute(pieces_out[h], AXES, pairs)
         mine = jnp.where(col // sections == h, got, mine)
     gathered = lax.all_gather(mine, AXES, tiled=True)
-    whole = (
-        gathered.reshape(rows, halves, sections, part, -1)
-        .transpose(2, 0, 1, 3, 4)
-        .reshape(sections * width_block, -1)
-    )
 
     update = jnp.concatenate([lead[None], rest], axis=0)
     update = update - jnp.einsum(
-        "kjrc,kcs->jrs",
-        panels,
-        whole.reshape(sections, width_block, -1),
+        "kjwrht,rhkts->jws",
+        panels.reshape(sections, blocks, width_block, rows, halves, part),
+        gathered.reshape(rows, halves, sections, part, -1),
         precision=lax.Precision.HIGH,
         preferred_element_type=jnp.float32,
     )

time: 287 us -> 285 us (level)
  local copies, waits for them, and re-layouts: 25.1 us -> 42.8 us
  waiting for transfers between devices: 77.2 us -> 60.4 us
  starting transfers between devices: 76.4 us -> 73.2 us
    unnamed x69 -> x70, local copies, waits for them, and re-layouts: 8.57 us -> 23.3 us
    all_to_all x2, waiting for transfers between devices: 48.9 us -> 35.9 us  [transpose_in(): lax.all_to_all(pieces, AXES, split_axis=2, concat_axis=0, tiled=True)]
    all_to_all x2, starting transfers between devices: 55.1 us -> 49.7 us  [transpose_in(): lax.all_to_all(pieces, AXES, split_axis=2, concat_axis=0, tiled=True)]
    all_gather x1, waiting for transfers between devices: 27.2 us -> 23.4 us  [per_device(): gathered = lax.all_gather(mine, AXES, tiled=True)]
  transfers between devices with their start and end apart: 21 -> 21, of which waited for: 4 -> 4; matrix products, arithmetic and copies ran while one was open for 19% -> 27% of each run, Pallas kernels for 0% -> 0%
where the time goes in v10:
time: 285 us; the launch traced here: 284 us
  starting transfers between devices  73.2 us (26%)
  waiting for transfers between devices  60.4 us (21%)
  matrix products  53.4 us (19%)
  local copies, waits for them, and re-layouts  42.8 us (15%)
  blocking collectives  21.3 us (7%)
  other arithmetic  18.4 us (6%)
  between operations  14.1 us (5%)
    all_to_all x2, starting transfers between devices, transpose_in(): lax.all_to_all(pieces, AXES, split_axis=2, concat_axis=0, tiled=True)  49.7 us
    dot_general x25, matrix products, mm(): return jnp.dot(a, b, precision=HI, preferred_element_type=jnp.float32)  39.1 us
    all_to_all x2, waiting for transfers between devices, transpose_in(): lax.all_to_all(pieces, AXES, split_axis=2, concat_axis=0, tiled=True)  35.9 us
    all_gather x1, waiting for transfers between devices, per_device(): gathered = lax.all_gather(mine, AXES, tiled=True)  23.4 us
    unnamed x70, local copies, waits for them, and re-layouts  23.3 us
    ppermute x17, starting transfers between devices, per_device(): got = lax.ppermute(buf, AXES, pairs)  22.1 us
    all_to_all x1, blocking collectives, per_device(): lax.all_to_all(own.reshape(rows, cut, -1), 'row', 0, 0, tiled=True)[0]  21.3 us
    add x10, other arithmetic, per_device(): buf = buf + got  15.7 us
  transfers between devices with their start and end apart: 21, of which 4 were waited for; matrix products, arithmetic and copies ran while one was open for 27% of the time, Pallas kernels for 0%

profile of v10, /device:TPU:1, one launch (start us, length us, event | category | flops | bytes accessed | tf_op | source)
XLA Modules:
  0.0 283.6 jit_solution(12311470911592794237)
XLA Ops:
  6.5 2.6 copy.37
  9.2 1.7 copy-done.2
  10.9 1.1 copy.23
  12.0 11.5 %all-to-all-start = ((f32[4,1,128,256]{3,0,1,2:T(4,128)}), f32[4,1,128,256]{3,0,1,2:T(4,128)S(1)}, u32[]{:S(2)}, u32[]{:S(2)}) async-start(f32[4,1,128,256]{3,0,1,2:T(4,128)} %copy.23), calls=%async_computation | async-start | bytes 1048576 | tf_op jit(solution)/shard_map/all_to_all | solution.py:16
  23.6 13.3 %all-to-all-done = f32[4,1,128,256]{3,0,1,2:T(4,128)S(1)} async-done(((f32[4,1,128,256]{3,0,1,2:T(4,128)}), f32[4,1,128,256]{3,0,1,2:T(4,128)S(1)}, u32[]{:S(2)}, u32[]{:S(2)}) %all-to-all-start) | async-done | bytes 524320 | tf_op jit(solution)/shard_map/all_to_all | solution.py:16
  37.5 1.4 copy.24
  38.9 1.7 broadcast_select_fusion.6
  40.5 1.5 collective-permute-start
  42.0 1.3 fusion.44
  44.1 2.7 broadcast_select_fusion.5
  46.7 1.4 collective-permute-start.3
  48.2 1.9 add.58
  50.1 1.5 collective-permute-start.1
  51.6 1.4 fusion.42
  53.0 2.2 add.61
  55.1 1.5 collective-permute-start.4
  56.6 1.3 add.59
  60.1 2.7 broadcast_select_fusion.4
  62.8 1.5 collective-permute-start.6
  64.2 1.4 fusion.40
  65.6 1.5 collective-permute-start.2
  67.1 1.3 add.62
  70.6 2.7 broadcast_select_fusion.3
  73.3 1.5 collective-permute-start.9
  74.8 2.1 add.64
  76.8 1.5 collective-permute-start.7
  78.3 1.4 fusion.38
  79.7 1.6 collective-permute-start.5
  81.3 1.9 convolution_subtract_fusion.9
  83.2 2.3 add.67
  85.5 1.5 collective-permute-start.10
  87.0 1.3 add.65
  89.7 2.9 %broadcast_select_fusion.2 = (f32[256,512]{1,0:T(8,128)}, f32[256,512]{1,0:T(8,128)}) fusion(pred[]{:T(512)S(6)} %eq.34, f32[256,512]{1,0:T(8,128)S(1)} %copy-done.15, f32[256,512]{1,0:T(8,128)S(1)} %fusion.80, f32[256,512]{1,0:T(8,128)S(1)} %convolution_subtract_fusion.9, f32[256,256]{1,0:T(8,128)S(1)} %fusion.38, f32[256,512]{1,0:T(8,128)} %collective-permute-done.9), kind=kOutput, calls=%fused_computation.71 | convolution fusion | flops 403177472 | bytes 3407873 | tf_op jit(solution)/shard_map/dot_general | solution.py:11
  92.6 1.5 collective-permute-start.12
  94.0 2.1 fusion.34
  96.1 1.3 fusion.32
  97.4 0.8 collective-permute-start.8
  98.3 1.9 convolution_subtract_fusion.7
  100.2 1.3 add.70
  101.5 0.8 collective-permute-start.14
  102.3 1.3 add.68
  104.3 2.5 broadcast_select_fusion.1
  109.6 1.6 broadcast_select_fusion
  111.3 1.5 collective-permute-start.15
  112.7 0.9 add.72
  113.6 1.5 collective-permute-start.16
  115.1 1.5 fusion.36
  117.3 1.7 fusion.82
  119.0 1.9 fusion.24
  121.0 1.0 fusion.16
  122.0 21.3 %all_to_all.35 = f32[8,32,512]{2,1,0:T(8,128)S(1)} all-to-all(f32[8,32,512]{2,1,0:T(8,128)S(1)} %bitcast.115), channel_id=1, replica_groups=mesh['row'=8,'col'=16] {'row'}, dimensions={0} | all-to-all | bytes 1048576 | tf_op jit(solution)/shard_map/all_to_all | solution.py:70
  143.4 1.3 collective-permute-start.17
  144.7 1.0 collective-permute-done.17
  146.3 1.9 slice.58
  148.2 3.2 %copy.25 = f32[4,5,128,256]{3,0,1,2:T(4,128)} copy(f32[4,5,128,256]{3,2,1,0:T(8,128)S(1)} %slice.58) | data formatting | bytes 5242880 | tf_op jit(solution)/shard_map/slice | solution.py:27
  151.4 38.2 %all-to-all-start.1 = ((f32[4,5,128,256]{3,0,1,2:T(4,128)}), f32[4,5,128,256]{3,0,1,2:T(4,128)}, u32[]{:S(2)}, u32[]{:S(2)}) async-start(f32[4,5,128,256]{3,0,1,2:T(4,128)} %copy.25), calls=%async_computation.1 | async-start | bytes 5242880 | tf_op jit(solution)/shard_map/all_to_all | solution.py:16
  189.6 12.7 %copy.28 = f32[8,6,256,256]{2,3,1,0:T(8,128)} copy(f32[8,6,256,256]{3,2,1,0:T(8,128)} %param.4) | data formatting | bytes 25165824 | tf_op args[1]
  202.3 22.7 %all-to-all-done.1 = f32[4,5,128,256]{3,0,1,2:T(4,128)} async-done(((f32[4,5,128,256]{3,0,1,2:T(4,128)}), f32[4,5,128,256]{3,0,1,2:T(4,128)}, u32[]{:S(2)}, u32[]{:S(2)}) %all-to-all-start.1) | async-done | bytes 2621472 | tf_op jit(solution)/shard_map/all_to_all | solution.py:16
  225.0 3.7 %copy.26 = f32[128,4,5,1,256]{4,1,0,2,3:T(4,128)} copy(f32[128,4,5,1,256]{4,1,2,0,3:T(4,128)} %bitcast.13) | data formatting | bytes 5242880 | tf_op jit(solution)/shard_map/all_to_all | solution.py:16
  228.7 4.0 %reshape.26 = f32[512,5,256]{2,0,1:T(8,128)} reshape(f32[128,4,5,1,256]{4,1,0,2,3:T(4,128)} %copy.26) | data formatting | bytes 5242880 | tf_op jit(solution)/shard_map/reshape | solution.py:17
  232.7 3.3 %copy.27 = f32[512,5,256]{0,2,1:T(8,128)} copy(f32[512,5,256]{2,0,1:T(8,128)} %reshape.26) | data formatting | bytes 5242880 | tf_op jit(solution)/shard_map/reshape | solution.py:17
  235.9 23.4 %all-gather.2.cloned.1.call-done = f32[2048,512]{1,0:T(8,128)} async-done(((f32[16,512]{1,0:T(8,128)}), f32[2048,512]{1,0:T(8,128)}) %all-gather.2.cloned.1.call-update) | async-done | bytes 4194320 | tf_op jit(solution)/shard_map/all_gather | solution.py:82
  259.4 14.3 %maximum_subtract_fusion = f32[6,256,512]{2,1,0:T(8,128)S(1)} fusion(f32[5,256,512]{2,1,0:T(8,128)} %bitcast.117, f32[1,256,512]{2,1,0:T(8,128)S(1)} %bitcast.118, f32[8,6,256,8,2,16]{2,5,4,3,1,0:T(8,128)} %bitcast.112, f32[8,2,8,16,512,1]{4,3,2,1,0,5:T(8,128)} %bitcast.120), kind=kOutput, calls=%fused_computation.3 | convolution fusion | flops 9665249280 | bytes 23068672 | tf_op jit(solution)/shard_map/kjwrht,rhkts->jws/dot_general | solution.py:85
  274.8 2.0 pad_maximum_fusion
  (100 shorter events, 13.1 us)
Async XLA Ops:
  6.5 32.3 %copy-start = (f32[8,256,256]{2,1,0:T(8,128)S(1)}, f32[8,256,256]{2,1,0:T(8,128)}, u32[]{:S(2)}) copy-start(f32[8,256,256]{2,1,0:T(8,128)} %param.5) | copy-start | bytes 6291460
  9.2 1.7 copy-start.2
  12.0 24.8 %all-to-all-start = ((f32[4,1,128,256]{3,0,1,2:T(4,128)}), f32[4,1,128,256]{3,0,1,2:T(4,128)S(1)}, u32[]{:S(2)}, u32[]{:S(2)}) async-start(f32[4,1,128,256]{3,0,1,2:T(4,128)} %copy.23), calls=%async_computation | async-start | bytes 1048576 | tf_op jit(solution)/shard_map/all_to_all | solution.py:16
  23.5 235.8 %all-gather.2.cloned.1.call-start = ((), (), s32[]{:S(2)}) async-start(), calls=%async_computation.3 | async-start | bytes 4227072 | tf_op jit(solution)/shard_map/all_gather | solution.py:82
  40.5 2.8 collective-permute-start
  43.3 0.7 copy-start.25
  46.7 6.2 %collective-permute-start.3 = (f32[256,512]{1,0:T(8,128)}, f32[256,512]{1,0:T(8,128)}, u32[]{:S(2)}, u32[]{:S(2)}) collective-permute-start(f32[256,512]{1,0:T(8,128)} %get-tuple-element.7), channel_id=1, source_target_pairs={{1,2}} | collective-permute-start | bytes 1572872 | tf_op jit(solution)/shard_map/ppermute | solution.py:59
  50.1 6.5 %collective-permute-start.1 = (f32[256,512]{1,0:T(8,128)}, f32[256,512]{1,0:T(8,128)}, u32[]{:S(2)}, u32[]{:S(2)}) collective-permute-start(f32[256,512]{1,0:T(8,128)} %add.58), channel_id=1, source_target_pairs={{0,2},{1,3}} | collective-permute-start | bytes 1572872 | tf_op jit(solution)/shard_map/ppermute | solution.py:59
  51.6 7.1 %copy-start.26 = (f32[256,256]{1,0:T(8,128)S(1)}, f32[256,256]{1,0:T(8,128)}, u32[]{:S(2)}) copy-start(f32[256,256]{1,0:T(8,128)} %copy-done.25) | copy-start | bytes 786436
  52.9 15.5 %copy-start.24 = (f32[256,256]{1,0:T(8,128)}, f32[256,256]{1,0:T(8,128)S(1)}, u32[]{:S(2)}) copy-start(f32[256,256]{1,0:T(8,128)S(1)} %fusion.42) | copy-start | bytes 786436
  55.1 12.0 %collective-permute-start.4 = (f32[256,512]{1,0:T(8,128)}, f32[256,512]{1,0:T(8,128)}, u32[]{:S(2)}, u32[]{:S(2)}) collective-permute-start(f32[256,512]{1,0:T(8,128)} %add.61), channel_id=1, source_target_pairs={{1,3},{2,4}} | collective-permute-start | bytes 1572872 | tf_op jit(solution)/shard_map/ppermute | solution.py:59
  57.9 0.8 copy-start.11
  59.3 0.8 copy-start.18
  62.8 7.1 %collective-permute-start.6 = (f32[256,512]{1,0:T(8,128)}, f32[256,512]{1,0:T(8,128)}, u32[]{:S(2)}, u32[]{:S(2)}) collective-permute-start(f32[256,512]{1,0:T(8,128)} %get-tuple-element.9), channel_id=1, source_target_pairs={{2,3}} | collective-permute-start | bytes 1572872 | tf_op jit(solution)/shard_map/ppermute | solution.py:59
  64.2 6.4 %copy-start.19 = (f32[256,512]{1,0:T(8,128)S(1)}, f32[256,512]{1,0:T(8,128)}, u32[]{:S(2)}) copy-start(f32[256,512]{1,0:T(8,128)} %copy-done.18) | copy-start | bytes 1572868
  65.6 7.7 %copy-start.21 = (f32[256,256]{1,0:T(8,128)}, f32[256,256]{1,0:T(8,128)S(1)}, u32[]{:S(2)}) copy-start(f32[256,256]{1,0:T(8,128)S(1)} %fusion.40) | copy-start | bytes 786436
  65.6 15.6 %collective-permute-start.2 = (f32[256,512]{1,0:T(8,128)}, f32[256,512]{1,0:T(8,128)}, u32[]{:S(2)}, u32[]{:S(2)}) collective-permute-start(f32[256,512]{1,0:T(8,128)} %copy-done.11), channel_id=1, source_target_pairs={{0,4},{1,5},{2,6},{3,7}} | collective-permute-start | bytes 1572872 | tf_op jit(solution)/shard_map/ppermute | solution.py:59
  68.4 0.8 copy-start.7
  69.8 0.8 copy-start.14
  73.3 9.9 %collective-permute-start.9 = (f32[256,512]{1,0:T(8,128)}, f32[256,512]{1,0:T(8,128)}, u32[]{:S(2)}, u32[]{:S(2)}) collective-permute-start(f32[256,512]{1,0:T(8,128)} %get-tuple-element.11), channel_id=1, source_target_pairs={{3,4}} | collective-permute-start | bytes 1572872 | tf_op jit(solution)/shard_map/ppermute | solution.py:59
  76.8 10.1 %collective-permute-start.7 = (f32[256,512]{1,0:T(8,128)}, f32[256,512]{1,0:T(8,128)}, u32[]{:S(2)}, u32[]{:S(2)}) collective-permute-start(f32[256,512]{1,0:T(8,128)} %add.64), channel_id=1, source_target_pairs={{2,4},{3,5}} | collective-permute-start | bytes 1572872 | tf_op jit(solution)/shard_map/ppermute | solution.py:59
  78.3 10.8 %copy-start.22 = (f32[256,256]{1,0:T(8,128)S(1)}, f32[256,256]{1,0:T(8,128)}, u32[]{:S(2)}) copy-start(f32[256,256]{1,0:T(8,128)} %copy-done.21) | copy-start | bytes 786436
  79.7 10.0 %copy-start.15 = (f32[256,512]{1,0:T(8,128)S(1)}, f32[256,512]{1,0:T(8,128)}, u32[]{:S(2)}) copy-start(f32[256,512]{1,0:T(8,128)} %copy-done.14) | copy-start | bytes 1572868
  79.7 18.6 %collective-permute-start.5 = (f32[256,512]{1,0:T(8,128)}, f32[256,512]{1,0:T(8,128)}, u32[]{:S(2)}, u32[]{:S(2)}) collective-permute-start(f32[256,512]{1,0:T(8,128)} %copy-done.7), channel_id=1, source_target_pairs={{1,5},{2,6},{3,7}} | collective-permute-start | bytes 1572872 | tf_op jit(solution)/shard_map/ppermute | solution.py:59
  83.2 9.4 %copy-start.20 = (f32[256,512]{1,0:T(8,128)}, f32[256,512]{1,0:T(8,128)S(1)}, u32[]{:S(2)}) copy-start(f32[256,512]{1,0:T(8,128)S(1)} %convolution_subtract_fusion.9) | copy-start | bytes 1572868
  85.5 16.8 %collective-permute-start.10 = (f32[256,512]{1,0:T(8,128)}, f32[256,512]{1,0:T(8,128)}, u32[]{:S(2)}, u32[]{:S(2)}) collective-permute-start(f32[256,512]{1,0:T(8,128)} %add.67), channel_id=1, source_target_pairs={{3,5},{4,6}} | collective-permute-start | bytes 1572872 | tf_op jit(solution)/shard_map/ppermute | solution.py:59
  88.2 0.8 copy-start.9
  89.0 9.2 %copy-start.8 = (f32[256,512]{1,0:T(8,128)S(1)}, f32[256,512]{1,0:T(8,128)}, u32[]{:S(2)}) copy-start(f32[256,512]{1,0:T(8,128)} %copy-done.7) | copy-start | bytes 1572868
  89.7 2.9 %copy-start.16 = (f32[256,512]{1,0:T(8,128)}, f32[256,512]{1,0:T(8,128)S(1)}, u32[]{:S(2)}) copy-start(f32[256,512]{1,0:T(8,128)S(1)} %fusion.80) | copy-start | bytes 1572868
  92.6 7.6 %collective-permute-start.12 = (f32[256,512]{1,0:T(8,128)}, f32[256,512]{1,0:T(8,128)}, u32[]{:S(2)}, u32[]{:S(2)}) collective-permute-start(f32[256,512]{1,0:T(8,128)} %get-tuple-element.13), channel_id=1, source_target_pairs={{4,5}} | collective-permute-start | bytes 1572872 | tf_op jit(solution)/shard_map/ppermute | solution.py:59
  97.4 6.8 %copy-start.17 = (f32[256,512]{1,0:T(8,128)S(1)}, f32[256,512]{1,0:T(8,128)}, u32[]{:S(2)}) copy-start(f32[256,512]{1,0:T(8,128)} %copy-done.16) | copy-start | bytes 1572868
  97.4 10.1 %collective-permute-start.8 = (f32[256,512]{1,0:T(8,128)}, f32[256,512]{1,0:T(8,128)S(1)}, u32[]{:S(2)}, u32[]{:S(2)}) collective-permute-start(f32[256,512]{1,0:T(8,128)} %copy-done.9), channel_id=1, source_target_pairs={{2,6},{3,7}} | collective-permute-start | bytes 1572872 | tf_op jit(solution)/shard_map/ppermute | solution.py:59
  101.5 6.0 %copy-start.10 = (f32[256,512]{1,0:T(8,128)S(1)}, f32[256,512]{1,0:T(8,128)}, u32[]{:S(2)}) copy-start(f32[256,512]{1,0:T(8,128)} %copy-done.9) | copy-start | bytes 1572868
  101.5 6.0 %copy-start.23 = (f32[256,256]{1,0:T(8,128)S(1)}, f32[256,256]{1,0:T(8,128)}, u32[]{:S(2)}) copy-start(f32[256,256]{1,0:T(8,128)} %copy-done.21) | copy-start | bytes 786436
  101.5 6.7 %collective-permute-start.14 = (f32[256,512]{1,0:T(8,128)S(1)}, f32[256,512]{1,0:T(8,128)S(1)}, u32[]{:S(2)}, u32[]{:S(2)}) collective-permute-start(f32[256,512]{1,0:T(8,128)S(1)} %add.70), channel_id=1, source_target_pairs={{4,6},{5,7}} | collective-permute-start | bytes 1572872 | tf_op jit(solution)/shard_map/ppermute | solution.py:59
  104.3 5.4 %copy-start.27 = (f32[256,256]{1,0:T(8,128)S(1)}, f32[256,256]{1,0:T(8,128)}, u32[]{:S(2)}) copy-start(f32[256,256]{1,0:T(8,128)} %fusion.34) | copy-start | bytes 786436
  106.8 2.0 collective-permute-start.13
  108.2 5.5 %copy-start.12 = (f32[256,512]{1,0:T(8,128)}, f32[256,512]{1,0:T(8,128)S(1)}, u32[]{:S(2)}) copy-start(f32[256,512]{1,0:T(8,128)S(1)} %convolution_subtract_fusion.5) | copy-start | bytes 1572868
  108.8 0.8 copy-start.5
  111.3 6.0 %collective-permute-start.15 = (f32[256,512]{1,0:T(8,128)}, f32[256,512]{1,0:T(8,128)}, u32[]{:S(2)}, u32[]{:S(2)}) collective-permute-start(f32[256,512]{1,0:T(8,128)} %get-tuple-element.17), channel_id=1, source_target_pairs={{6,7}} | collective-permute-start | bytes 1572872 | tf_op jit(solution)/shard_map/ppermute | solution.py:59
  113.6 5.4 %collective-permute-start.16 = (f32[256,512]{1,0:T(8,128)}, f32[256,512]{1,0:T(8,128)}, u32[]{:S(2)}, u32[]{:S(2)}) collective-permute-start(f32[256,512]{1,0:T(8,128)} %add.72), channel_id=1, source_target_pairs={{5,7}} | collective-permute-start | bytes 1572872 | tf_op jit(solution)/shard_map/ppermute | solution.py:59
  115.1 5.8 %copy-start.6 = (f32[256,512]{1,0:T(8,128)S(1)}, f32[256,512]{1,0:T(8,128)}, u32[]{:S(2)}) copy-start(f32[256,512]{1,0:T(8,128)} %copy-done.5) | copy-start | bytes 1572868
  115.1 5.9 %copy-start.13 = (f32[256,512]{1,0:T(8,128)S(1)}, f32[256,512]{1,0:T(8,128)}, u32[]{:S(2)}) copy-start(f32[256,512]{1,0:T(8,128)} %copy-done.12) | copy-start | bytes 1572868
  115.1 5.9 %copy-start.28 = (f32[256,512]{1,0:T(8,128)S(1)}, f32[256,512]{1,0:T(8,128)}, u32[]{:S(2)}) copy-start(f32[256,512]{1,0:T(8,128)} %get-tuple-element.8) | copy-start | bytes 1572868
  115.1 5.9 %copy-start.30 = (f32[256,512]{1,0:T(8,128)S(1)}, f32[256,512]{1,0:T(8,128)}, u32[]{:S(2)}) copy-start(f32[256,512]{1,0:T(8,128)} %get-tuple-element.10) | copy-start | bytes 1572868
  115.1 5.9 %copy-start.31 = (f32[256,512]{1,0:T(8,128)S(1)}, f32[256,512]{1,0:T(8,128)}, u32[]{:S(2)}) copy-start(f32[256,512]{1,0:T(8,128)} %get-tuple-element.12) | copy-start | bytes 1572868
  115.1 5.9 %copy-start.32 = (f32[256,512]{1,0:T(8,128)S(1)}, f32[256,512]{1,0:T(8,128)}, u32[]{:S(2)}) copy-start(f32[256,512]{1,0:T(8,128)} %get-tuple-element.14) | copy-start | bytes 1572868
  115.1 5.9 %copy-start.33 = (f32[256,512]{1,0:T(8,128)S(1)}, f32[256,512]{1,0:T(8,128)}, u32[]{:S(2)}) copy-start(f32[256,512]{1,0:T(8,128)} %get-tuple-element.16) | copy-start | bytes 1572868
  116.6 4.3 %collective-permute-start.11 = (f32[256,512]{1,0:T(8,128)S(1)}, f32[256,512]{1,0:T(8,128)S(1)}, u32[]{:S(2)}, u32[]{:S(2)}) collective-permute-start(f32[256,512]{1,0:T(8,128)S(1)} %add.68), channel_id=1, source_target_pairs={{3,7}} | collective-permute-start | bytes 1572872 | tf_op jit(solution)/shard_map/ppermute | solution.py:59
  122.0 26.2 %copy-start.3 = (f32[256,512]{1,0:T(8,128)}, f32[256,512]{1,0:T(8,128)S(1)}, u32[]{:S(2)}) copy-start(f32[256,512]{1,0:T(8,128)S(1)} %fusion.16) | copy-start | bytes 1572868
  143.4 2.3 collective-permute-start.17
  151.4 73.6 %all-to-all-start.1 = ((f32[4,5,128,256]{3,0,1,2:T(4,128)}), f32[4,5,128,256]{3,0,1,2:T(4,128)}, u32[]{:S(2)}, u32[]{:S(2)}) async-start(f32[4,5,128,256]{3,0,1,2:T(4,128)} %copy.25), calls=%async_computation.1 | async-start | bytes 5242880 | tf_op jit(solution)/shard_map/all_to_all | solution.py:16
  232.7 26.7 %copy-start.29 = (f32[512,1,256]{0,2,1:T(8,128)S(1)}, f32[512,1,256]{0,2,1:T(8,128)}, u32[]{:S(2)}) copy-start(f32[512,1,256]{0,2,1:T(8,128)} %copy.24) | copy-start | bytes 1572868
  273.6 1.0 copy-start.4
  274.7 2.1 copy-start.1
Sparse Core Ops, SparseCore 0:
  146.4 112.9 all-gather.1

commit v11 on v10

--- a/solution.py
+++ b/solution.py
@@ -33,17 +33,16 @@
     )
     low = jnp.stack([mm(inverse, panels[k, 0]) for k in range(sections - 1)])
 
-    after = [[None] * 3 for _ in range(sections)]
-    first_hop = [None] * sections
+    received = [[None] * 3 for _ in range(sections)]
     own = jnp.zeros_like(lead)
     settled = mm(inverse, lead)
     for section in range(sections):
         chain = settled
         if section >= 1:
-            chain = chain - mm(low[section - 1], first_hop[section - 1])
+            chain = chain - mm(low[section - 1], received[section - 1][0])
         for back in (2, 3):
             if section - back >= 0:
-                chain = chain - mm(low[section - back], after[section - back][1])
+                chain = chain - mm(low[section - back], received[section - back][1])
         solved = chain
         here = device == section
         own = jnp.where(here, solved, own)
@@ -57,12 +56,11 @@
             ]
             if pairs:
                 got = lax.ppermute(buf, AXES, pairs)
-                if level == 0:
-                    first_hop[section] = got
-                buf = buf + got
-            after[section][level] = buf
-        if section - 3 >= 0:
-            settled = settled - mm(low[section - 3], after[section - 3][2])
+                received[section][level] = got
+                if level < 2:
+                    buf = buf + got
+        if section - 3 >= 0 and received[section - 3][2] is not None:
+            settled = settled - mm(low[section - 3], received[section - 3][2])
 
     rows = lax.axis_size("row")
     halves = cols // sections

time: 285 us -> 290 us (1.018)
  matrix products: 53.4 us -> 57.5 us
  local copies, waits for them, and re-layouts: 42.8 us -> 39.5 us
    dot_general x25, matrix products: 39.1 us -> 43.2 us  [mm(): return jnp.dot(a, b, precision=HI, preferred_element_type=jnp.float32)]
    unnamed x70 -> x50, local copies, waits for them, and re-layouts: 23.3 us -> 20.1 us
  transfers between devices with their start and end apart: 21 -> 21, of which waited for: 4 -> 4; matrix products, arithmetic and copies ran while one was open for 27% -> 29% of each run, Pallas kernels for 0% -> 0%
where the time goes in v11:
time: 290 us; the launch traced here: 288 us
  starting transfers between devices  75.4 us (26%)
  waiting for transfers between devices  60.4 us (21%)
  matrix products  57.5 us (20%)
  local copies, waits for them, and re-layouts  39.5 us (14%)
  blocking collectives  21.4 us (7%)
  other arithmetic  19.8 us (7%)
  between operations  14 us (5%)
    all_to_all x2, starting transfers between devices, transpose_in(): lax.all_to_all(pieces, AXES, split_axis=2, concat_axis=0, tiled=True)  51.2 us
    dot_general x25, matrix products, mm(): return jnp.dot(a, b, precision=HI, preferred_element_type=jnp.float32)  43.2 us
    all_to_all x2, waiting for transfers between devices, transpose_in(): lax.all_to_all(pieces, AXES, split_axis=2, concat_axis=0, tiled=True)  35.9 us
    all_gather x1, waiting for transfers between devices, per_device(): gathered = lax.all_gather(mine, AXES, tiled=True)  23.4 us
    ppermute x17, starting transfers between devices, per_device(): got = lax.ppermute(buf, AXES, pairs)  22.9 us
    all_to_all x1, blocking collectives, per_device(): lax.all_to_all(own.reshape(rows, cut, -1), 'row', 0, 0, tiled=True)[0]  21.4 us
    unnamed x50, local copies, waits for them, and re-layouts  20.1 us
    add x10, other arithmetic, per_device(): buf = buf + got  17.1 us
  transfers between devices with their start and end apart: 21, of which 4 were waited for; matrix products, arithmetic and copies ran while one was open for 29% of the time, Pallas kernels for 0%

profile of v11, /device:TPU:1, one launch (start us, length us, event | category | flops | bytes accessed | tf_op | source)
XLA Modules:
  0.0 288.1 jit_solution(13800442391007430843)
XLA Ops:
  6.5 2.6 copy.37
  9.2 1.7 copy-done.2
  10.9 1.1 copy.23
  12.0 11.5 %all-to-all-start = ((f32[4,1,128,256]{3,0,1,2:T(4,128)}), f32[4,1,128,256]{3,0,1,2:T(4,128)S(1)}, u32[]{:S(2)}, u32[]{:S(2)}) async-start(f32[4,1,128,256]{3,0,1,2:T(4,128)} %copy.23), calls=%async_computation | async-start | bytes 1048576 | tf_op jit(solution)/shard_map/all_to_all | solution.py:16
  23.6 13.3 %all-to-all-done = f32[4,1,128,256]{3,0,1,2:T(4,128)S(1)} async-done(((f32[4,1,128,256]{3,0,1,2:T(4,128)}), f32[4,1,128,256]{3,0,1,2:T(4,128)S(1)}, u32[]{:S(2)}, u32[]{:S(2)}) %all-to-all-start) | async-done | bytes 524320 | tf_op jit(solution)/shard_map/all_to_all | solution.py:16
  37.5 1.4 copy.24
  38.9 1.7 broadcast_select_fusion.6
  40.5 1.5 collective-permute-start
  42.0 1.3 fusion.36
  44.0 2.7 broadcast_select_fusion.5
  46.7 1.4 collective-permute-start.3
  48.1 1.9 add.40
  50.1 1.5 collective-permute-start.1
  51.5 1.3 fusion.34
  52.9 2.2 add.42
  55.0 1.4 collective-permute-start.4
  56.5 1.7 fusion.70
  59.0 2.7 broadcast_select_fusion.4
  61.7 1.5 collective-permute-start.6
  63.2 1.4 fusion.32
  64.6 2.2 add.41
  66.8 1.4 collective-permute-start.2
  68.2 1.7 fusion.71
  70.7 2.7 broadcast_select_fusion.3
  73.4 1.5 collective-permute-start.9
  74.8 2.1 add.44
  76.9 1.5 collective-permute-start.7
  78.4 1.3 fusion.30
  79.7 1.3 fusion.24
  81.1 1.4 add.43
  83.3 1.7 convolution_subtract_fusion.9
  85.1 1.3 add.46
  87.2 2.1 add.45
  89.3 1.5 collective-permute-start.8
  90.7 1.7 fusion.72
  92.4 2.5 broadcast_select_fusion.2
  97.8 1.7 broadcast_select_fusion.1
  99.5 1.5 collective-permute-start.13
  101.9 1.4 collective-permute-start.14
  103.4 1.4 fusion.26
  104.8 1.8 convolution_subtract_fusion.5
  106.7 2.3 add.49
  109.0 1.4 collective-permute-start.16
  110.4 1.7 fusion.74
  112.1 2.9 broadcast_select_fusion
  115.0 1.5 collective-permute-start.15
  117.4 1.4 collective-permute-start.11
  118.8 1.3 fusion.28
  120.2 1.7 fusion.76
  121.9 1.7 fusion.75
  123.6 2.2 fusion.16
  125.8 21.4 %all_to_all.35 = f32[8,32,512]{2,1,0:T(8,128)S(1)} all-to-all(f32[8,32,512]{2,1,0:T(8,128)S(1)} %bitcast.121), channel_id=1, replica_groups=mesh['row'=8,'col'=16] {'row'}, dimensions={0} | all-to-all | bytes 1048576 | tf_op jit(solution)/shard_map/all_to_all | solution.py:68
  147.2 1.3 collective-permute-start.17
  150.1 1.9 slice.58
  152.0 3.2 %copy.25 = f32[4,5,128,256]{3,0,1,2:T(4,128)} copy(f32[4,5,128,256]{3,2,1,0:T(8,128)S(1)} %slice.58) | data formatting | bytes 5242880 | tf_op jit(solution)/shard_map/slice | solution.py:27
  155.2 39.7 %all-to-all-start.1 = ((f32[4,5,128,256]{3,0,1,2:T(4,128)}), f32[4,5,128,256]{3,0,1,2:T(4,128)}, u32[]{:S(2)}, u32[]{:S(2)}) async-start(f32[4,5,128,256]{3,0,1,2:T(4,128)} %copy.25), calls=%async_computation.1 | async-start | bytes 5242880 | tf_op jit(solution)/shard_map/all_to_all | solution.py:16
  194.9 12.7 %copy.28 = f32[8,6,256,256]{2,3,1,0:T(8,128)} copy(f32[8,6,256,256]{3,2,1,0:T(8,128)} %param.4) | data formatting | bytes 25165824 | tf_op args[1]
  207.6 22.6 %all-to-all-done.1 = f32[4,5,128,256]{3,0,1,2:T(4,128)} async-done(((f32[4,5,128,256]{3,0,1,2:T(4,128)}), f32[4,5,128,256]{3,0,1,2:T(4,128)}, u32[]{:S(2)}, u32[]{:S(2)}) %all-to-all-start.1) | async-done | bytes 2621472 | tf_op jit(solution)/shard_map/all_to_all | solution.py:16
  230.2 3.7 %copy.26 = f32[128,4,5,1,256]{4,1,0,2,3:T(4,128)} copy(f32[128,4,5,1,256]{4,1,2,0,3:T(4,128)} %bitcast.13) | data formatting | bytes 5242880 | tf_op jit(solution)/shard_map/all_to_all | solution.py:16
  233.9 4.0 %reshape.26 = f32[512,5,256]{2,0,1:T(8,128)} reshape(f32[128,4,5,1,256]{4,1,0,2,3:T(4,128)} %copy.26) | data formatting | bytes 5242880 | tf_op jit(solution)/shard_map/reshape | solution.py:17
  237.9 3.3 %copy.27 = f32[512,5,256]{0,2,1:T(8,128)} copy(f32[512,5,256]{2,0,1:T(8,128)} %reshape.26) | data formatting | bytes 5242880 | tf_op jit(solution)/shard_map/reshape | solution.py:17
  241.2 23.4 %all-gather.2.cloned.1.call-done = f32[2048,512]{1,0:T(8,128)} async-done(((f32[16,512]{1,0:T(8,128)}), f32[2048,512]{1,0:T(8,128)}) %all-gather.2.cloned.1.call-update) | async-done | bytes 4194320 | tf_op jit(solution)/shard_map/all_gather | solution.py:80
  264.6 14.3 %maximum_subtract_fusion = f32[6,256,512]{2,1,0:T(8,128)S(1)} fusion(f32[5,256,512]{2,1,0:T(8,128)} %bitcast.123, f32[1,256,512]{2,1,0:T(8,128)S(1)} %bitcast.124, f32[8,6,256,8,2,16]{2,5,4,3,1,0:T(8,128)} %bitcast.118, f32[8,2,8,16,512,1]{4,3,2,1,0,5:T(8,128)} %bitcast.126), kind=kOutput, calls=%fused_computation.3 | convolution fusion | flops 9665249280 | bytes 23068672 | tf_op jit(solution)/shard_map/kjwrht,rhkts->jws/dot_general | solution.py:83
  279.2 2.0 pad_maximum_fusion
  (80 shorter events, 11.3 us)
Async XLA Ops:
  6.5 32.3 %copy-start = (f32[8,256,256]{2,1,0:T(8,128)S(1)}, f32[8,256,256]{2,1,0:T(8,128)}, u32[]{:S(2)}) copy-start(f32[8,256,256]{2,1,0:T(8,128)} %param.5) | copy-start | bytes 6291460
  9.2 1.7 copy-start.2
  12.0 24.8 %all-to-all-start = ((f32[4,1,128,256]{3,0,1,2:T(4,128)}), f32[4,1,128,256]{3,0,1,2:T(4,128)S(1)}, u32[]{:S(2)}, u32[]{:S(2)}) async-start(f32[4,1,128,256]{3,0,1,2:T(4,128)} %copy.23), calls=%async_computation | async-start | bytes 1048576 | tf_op jit(solution)/shard_map/all_to_all | solution.py:16
  23.5 241.1 %all-gather.2.cloned.1.call-start = ((), (), s32[]{:S(2)}) async-start(), calls=%async_computation.3 | async-start | bytes 4227072 | tf_op jit(solution)/shard_map/all_gather | solution.py:80
  40.5 2.8 collective-permute-start
  43.3 0.7 copy-start.15
  46.7 6.2 %collective-permute-start.3 = (f32[256,512]{1,0:T(8,128)}, f32[256,512]{1,0:T(8,128)}, u32[]{:S(2)}, u32[]{:S(2)}) collective-permute-start(f32[256,512]{1,0:T(8,128)} %get-tuple-element.7), channel_id=1, source_target_pairs={{1,2}} | collective-permute-start | bytes 1572872 | tf_op jit(solution)/shard_map/ppermute | solution.py:58
  50.1 6.4 %collective-permute-start.1 = (f32[256,512]{1,0:T(8,128)}, f32[256,512]{1,0:T(8,128)}, u32[]{:S(2)}, u32[]{:S(2)}) collective-permute-start(f32[256,512]{1,0:T(8,128)} %add.40), channel_id=1, source_target_pairs={{0,2},{1,3}} | collective-permute-start | bytes 1572872 | tf_op jit(solution)/shard_map/ppermute | solution.py:58
  52.9 15.3 %copy-start.13 = (f32[256,256]{1,0:T(8,128)}, f32[256,256]{1,0:T(8,128)S(1)}, u32[]{:S(2)}) copy-start(f32[256,256]{1,0:T(8,128)S(1)} %fusion.34) | copy-start | bytes 786436
  55.0 13.2 %collective-permute-start.4 = (f32[256,512]{1,0:T(8,128)}, f32[256,512]{1,0:T(8,128)}, u32[]{:S(2)}, u32[]{:S(2)}) collective-permute-start(f32[256,512]{1,0:T(8,128)} %add.42), channel_id=1, source_target_pairs={{1,3},{2,4}} | collective-permute-start | bytes 1572872 | tf_op jit(solution)/shard_map/ppermute | solution.py:58
  58.2 0.8 copy-start.9
  61.7 8.2 %collective-permute-start.6 = (f32[256,512]{1,0:T(8,128)}, f32[256,512]{1,0:T(8,128)}, u32[]{:S(2)}, u32[]{:S(2)}) collective-permute-start(f32[256,512]{1,0:T(8,128)} %get-tuple-element.9), channel_id=1, source_target_pairs={{2,3}} | collective-permute-start | bytes 1572872 | tf_op jit(solution)/shard_map/ppermute | solution.py:58
  63.2 7.5 %copy-start.10 = (f32[256,512]{1,0:T(8,128)S(1)}, f32[256,512]{1,0:T(8,128)}, u32[]{:S(2)}) copy-start(f32[256,512]{1,0:T(8,128)} %copy-done.9) | copy-start | bytes 1572868
  64.6 8.8 %copy-start.11 = (f32[256,256]{1,0:T(8,128)}, f32[256,256]{1,0:T(8,128)S(1)}, u32[]{:S(2)}) copy-start(f32[256,256]{1,0:T(8,128)S(1)} %fusion.32) | copy-start | bytes 786436
  66.8 16.6 %collective-permute-start.2 = (f32[256,512]{1,0:T(8,128)}, f32[256,512]{1,0:T(8,128)}, u32[]{:S(2)}, u32[]{:S(2)}) collective-permute-start(f32[256,512]{1,0:T(8,128)} %add.41), channel_id=1, source_target_pairs={{0,4},{1,5},{2,6},{3,7}} | collective-permute-start | bytes 1572872 | tf_op jit(solution)/shard_map/ppermute | solution.py:58
  69.9 0.8 copy-start.5
  73.4 11.7 %collective-permute-start.9 = (f32[256,512]{1,0:T(8,128)}, f32[256,512]{1,0:T(8,128)}, u32[]{:S(2)}, u32[]{:S(2)}) collective-permute-start(f32[256,512]{1,0:T(8,128)} %get-tuple-element.11), channel_id=1, source_target_pairs={{3,4}} | collective-permute-start | bytes 1572872 | tf_op jit(solution)/shard_map/ppermute | solution.py:58
  76.9 10.3 %collective-permute-start.7 = (f32[256,512]{1,0:T(8,128)}, f32[256,512]{1,0:T(8,128)}, u32[]{:S(2)}, u32[]{:S(2)}) collective-permute-start(f32[256,512]{1,0:T(8,128)} %add.44), channel_id=1, source_target_pairs={{2,4},{3,5}} | collective-permute-start | bytes 1572872 | tf_op jit(solution)/shard_map/ppermute | solution.py:58
  81.1 16.0 %copy-start.16 = (f32[256,256]{1,0:T(8,128)}, f32[256,256]{1,0:T(8,128)S(1)}, u32[]{:S(2)}) copy-start(f32[256,256]{1,0:T(8,128)S(1)} %fusion.24) | copy-start | bytes 786436
  81.1 9.7 %copy-start.12 = (f32[256,256]{1,0:T(8,128)S(1)}, f32[256,256]{1,0:T(8,128)}, u32[]{:S(2)}) copy-start(f32[256,256]{1,0:T(8,128)} %copy-done.11) | copy-start | bytes 786436
  82.5 9.9 %copy-start.6 = (f32[256,512]{1,0:T(8,128)S(1)}, f32[256,512]{1,0:T(8,128)}, u32[]{:S(2)}) copy-start(f32[256,512]{1,0:T(8,128)} %copy-done.5) | copy-start | bytes 1572868
  82.5 13.3 %collective-permute-start.5 = (f32[256,512]{1,0:T(8,128)S(1)}, f32[256,512]{1,0:T(8,128)S(1)}, u32[]{:S(2)}, u32[]{:S(2)}) collective-permute-start(f32[256,512]{1,0:T(8,128)S(1)} %add.43), channel_id=1, source_target_pairs={{1,5},{2,6},{3,7}} | collective-permute-start | bytes 1572872 | tf_op jit(solution)/shard_map/ppermute | solution.py:58
  86.3 8.6 %copy-start.19 = (f32[256,512]{1,0:T(8,128)}, f32[256,512]{1,0:T(8,128)S(1)}, u32[]{:S(2)}) copy-start(f32[256,512]{1,0:T(8,128)S(1)} %add.46) | copy-start | bytes 1572868
  86.4 9.4 %copy-start.14 = (f32[256,256]{1,0:T(8,128)S(1)}, f32[256,256]{1,0:T(8,128)}, u32[]{:S(2)}) copy-start(f32[256,256]{1,0:T(8,128)} %copy-done.13) | copy-start | bytes 786436
  86.4 10.1 %collective-permute-start.10 = (f32[256,512]{1,0:T(8,128)S(1)}, f32[256,512]{1,0:T(8,128)S(1)}, u32[]{:S(2)}, u32[]{:S(2)}) collective-permute-start(f32[256,512]{1,0:T(8,128)S(1)} %add.46), channel_id=1, source_target_pairs={{3,5},{4,6}} | collective-permute-start | bytes 1572872 | tf_op jit(solution)/shard_map/ppermute | solution.py:58
  89.3 15.5 %collective-permute-start.8 = (f32[256,512]{1,0:T(8,128)}, f32[256,512]{1,0:T(8,128)}, u32[]{:S(2)}, u32[]{:S(2)}) collective-permute-start(f32[256,512]{1,0:T(8,128)} %add.45), channel_id=1, source_target_pairs={{2,6},{3,7}} | collective-permute-start | bytes 1572872 | tf_op jit(solution)/shard_map/ppermute | solution.py:58
  94.9 2.2 collective-permute-start.12
  96.4 5.5 %copy-start.22 = (f32[256,512]{1,0:T(8,128)}, f32[256,512]{1,0:T(8,128)S(1)}, u32[]{:S(2)}) copy-start(f32[256,512]{1,0:T(8,128)S(1)} %collective-permute-done.10) | copy-start | bytes 1572868
  97.1 0.8 copy-start.7
  99.5 7.1 %collective-permute-start.13 = (f32[256,512]{1,0:T(8,128)}, f32[256,512]{1,0:T(8,128)}, u32[]{:S(2)}, u32[]{:S(2)}) collective-permute-start(f32[256,512]{1,0:T(8,128)} %get-tuple-element.15), channel_id=1, source_target_pairs={{5,6}} | collective-permute-start | bytes 1572872 | tf_op jit(solution)/shard_map/ppermute | solution.py:58
  101.9 8.5 %collective-permute-start.14 = (f32[256,512]{1,0:T(8,128)}, f32[256,512]{1,0:T(8,128)}, u32[]{:S(2)}, u32[]{:S(2)}) collective-permute-start(f32[256,512]{1,0:T(8,128)} %add.48), channel_id=1, source_target_pairs={{4,6},{5,7}} | collective-permute-start | bytes 1572872 | tf_op jit(solution)/shard_map/ppermute | solution.py:58
  103.4 7.0 %copy-start.17 = (f32[256,256]{1,0:T(8,128)S(1)}, f32[256,256]{1,0:T(8,128)}, u32[]{:S(2)}) copy-start(f32[256,256]{1,0:T(8,128)} %copy-done.16) | copy-start | bytes 786436
  103.4 8.7 %copy-start.8 = (f32[256,512]{1,0:T(8,128)S(1)}, f32[256,512]{1,0:T(8,128)}, u32[]{:S(2)}) copy-start(f32[256,512]{1,0:T(8,128)} %copy-done.7) | copy-start | bytes 1572868
  104.8 10.2 %copy-start.18 = (f32[256,256]{1,0:T(8,128)}, f32[256,256]{1,0:T(8,128)S(1)}, u32[]{:S(2)}) copy-start(f32[256,256]{1,0:T(8,128)S(1)} %fusion.26) | copy-start | bytes 786436
  106.7 8.3 %copy-start.3 = (f32[256,512]{1,0:T(8,128)}, f32[256,512]{1,0:T(8,128)S(1)}, u32[]{:S(2)}) copy-start(f32[256,512]{1,0:T(8,128)S(1)} %convolution_subtract_fusion.5) | copy-start | bytes 1572868
  106.7 9.8 %copy-start.20 = (f32[256,512]{1,0:T(8,128)S(1)}, f32[256,512]{1,0:T(8,128)}, u32[]{:S(2)}) copy-start(f32[256,512]{1,0:T(8,128)} %copy-done.19) | copy-start | bytes 1572868
  106.7 9.8 %copy-start.23 = (f32[256,512]{1,0:T(8,128)S(1)}, f32[256,512]{1,0:T(8,128)}, u32[]{:S(2)}) copy-start(f32[256,512]{1,0:T(8,128)} %copy-done.22) | copy-start | bytes 1572868
  109.0 11.2 %collective-permute-start.16 = (f32[256,512]{1,0:T(8,128)}, f32[256,512]{1,0:T(8,128)}, u32[]{:S(2)}, u32[]{:S(2)}) collective-permute-start(f32[256,512]{1,0:T(8,128)} %add.49), channel_id=1, source_target_pairs={{5,7}} | collective-permute-start | bytes 1572872 | tf_op jit(solution)/shard_map/ppermute | solution.py:58
  112.1 2.9 %copy-start.4 = (f32[256,512]{1,0:T(8,128)}, f32[256,512]{1,0:T(8,128)S(1)}, u32[]{:S(2)}) copy-start(f32[256,512]{1,0:T(8,128)S(1)} %fusion.74) | copy-start | bytes 1572868
  115.0 6.9 %collective-permute-start.15 = (f32[256,512]{1,0:T(8,128)}, f32[256,512]{1,0:T(8,128)}, u32[]{:S(2)}, u32[]{:S(2)}) collective-permute-start(f32[256,512]{1,0:T(8,128)} %get-tuple-element.17), channel_id=1, source_target_pairs={{6,7}} | collective-permute-start | bytes 1572872 | tf_op jit(solution)/shard_map/ppermute | solution.py:58
  117.4 6.2 %collective-permute-start.11 = (f32[256,512]{1,0:T(8,128)}, f32[256,512]{1,0:T(8,128)}, u32[]{:S(2)}, u32[]{:S(2)}) collective-permute-start(f32[256,512]{1,0:T(8,128)} %add.47), channel_id=1, source_target_pairs={{3,7}} | collective-permute-start | bytes 1572872 | tf_op jit(solution)/shard_map/ppermute | solution.py:58
  147.2 2.3 collective-permute-start.17
  155.2 75.0 %all-to-all-start.1 = ((f32[4,5,128,256]{3,0,1,2:T(4,128)}), f32[4,5,128,256]{3,0,1,2:T(4,128)}, u32[]{:S(2)}, u32[]{:S(2)}) async-start(f32[4,5,128,256]{3,0,1,2:T(4,128)} %copy.25), calls=%async_computation.1 | async-start | bytes 5242880 | tf_op jit(solution)/shard_map/all_to_all | solution.py:16
  237.9 26.7 %copy-start.21 = (f32[512,1,256]{0,2,1:T(8,128)S(1)}, f32[512,1,256]{0,2,1:T(8,128)}, u32[]{:S(2)}) copy-start(f32[512,1,256]{0,2,1:T(8,128)} %copy.24) | copy-start | bytes 1572868
  279.1 2.1 copy-start.1
Sparse Core Ops, SparseCore 0:
  150.2 114.3 all-gather.1

commit v12 on v10

--- a/solution.py
+++ b/solution.py
@@ -31,12 +31,12 @@
     inverse = lax.dynamic_index_in_dim(
         diag_inverse, jnp.minimum(device, sections - 1), 0, keepdims=False
     )
-    low = jnp.stack([mm(inverse, panels[k, 0]) for k in range(sections - 1)])
+    low = jnp.stack([jnp.dot(inverse, panels[k, 0], precision=lax.Precision.HIGH, preferred_element_type=jnp.float32) for k in range(sections - 1)])
 
     after = [[None] * 3 for _ in range(sections)]
     first_hop = [None] * sections
     own = jnp.zeros_like(lead)
-    settled = mm(inverse, lead)
+    settled = jnp.dot(inverse, lead, precision=lax.Precision.HIGH, preferred_element_type=jnp.float32)
     for section in range(sections):
         chain = settled
         if section >= 1:

time: 285 us -> 285 us (level)
    dot_general x25 -> x17, matrix products: 39.1 us -> 27.2 us  [mm(): return jnp.dot(a, b, precision=HI, preferred_element_type=jnp.float32)]
    dot_general x0 -> x8, matrix products: none -> 11 us  [the longest x7 9.55 us: per_device(): jnp.dot(inverse, panels[k, 0], precision=lax.Precision.HIGH, preferred_el...]
where the time goes in v12:
time: 285 us; the launch traced here: 284 us
  starting transfers between devices  74 us (26%)
  waiting for transfers between devices  60.4 us (21%)
  matrix products  52.4 us (18%)
  local copies, waits for them, and re-layouts  42.8 us (15%)
  blocking collectives  21.6 us (8%)
  other arithmetic  18.4 us (6%)
  between operations  14.1 us (5%)
    all_to_all x2, starting transfers between devices, transpose_in(): lax.all_to_all(pieces, AXES, split_axis=2, concat_axis=0, tiled=True)  50.4 us
    all_to_all x2, waiting for transfers between devices, transpose_in(): lax.all_to_all(pieces, AXES, split_axis=2, concat_axis=0, tiled=True)  35.9 us
    dot_general x17, matrix products, mm(): return jnp.dot(a, b, precision=HI, preferred_element_type=jnp.float32)  27.2 us
    all_gather x1, waiting for transfers between devices, per_device(): gathered = lax.all_gather(mine, AXES, tiled=True)  23.4 us
    unnamed x70, local copies, waits for them, and re-layouts  23.3 us
    ppermute x17, starting transfers between devices, per_device(): got = lax.ppermute(buf, AXES, pairs)  22.3 us
    all_to_all x1, blocking collectives, per_device(): lax.all_to_all(own.reshape(rows, cut, -1), 'row', 0, 0, tiled=True)[0]  21.6 us
    add x10, other arithmetic, per_device(): buf = buf + got  15.7 us
  transfers between devices with their start and end apart: 21, of which 4 were waited for; matrix products, arithmetic and copies ran while one was open for 27% of the time, Pallas kernels for 0%

profile of v12, /device:TPU:1, one launch (start us, length us, event | category | flops | bytes accessed | tf_op | source)
XLA Modules:
  0.0 283.7 jit_solution(3215422239597787365)
XLA Ops:
  6.5 2.6 copy.37
  9.2 1.7 copy-done.2
  10.9 1.1 copy.23
  12.0 11.5 %all-to-all-start = ((f32[4,1,128,256]{3,0,1,2:T(4,128)}), f32[4,1,128,256]{3,0,1,2:T(4,128)S(1)}, u32[]{:S(2)}, u32[]{:S(2)}) async-start(f32[4,1,128,256]{3,0,1,2:T(4,128)} %copy.23), calls=%async_computation | async-start | bytes 1048576 | tf_op jit(solution)/shard_map/all_to_all | solution.py:16
  23.6 13.3 %all-to-all-done = f32[4,1,128,256]{3,0,1,2:T(4,128)S(1)} async-done(((f32[4,1,128,256]{3,0,1,2:T(4,128)}), f32[4,1,128,256]{3,0,1,2:T(4,128)S(1)}, u32[]{:S(2)}, u32[]{:S(2)}) %all-to-all-start) | async-done | bytes 524320 | tf_op jit(solution)/shard_map/all_to_all | solution.py:16
  37.5 1.4 copy.24
  38.9 1.4 broadcast_select_fusion.6
  40.3 1.5 collective-permute-start
  41.8 1.2 fusion.44
  43.7 2.7 broadcast_select_fusion.5
  46.4 1.4 collective-permute-start.3
  47.9 1.9 add.58
  49.8 1.5 collective-permute-start.1
  51.2 1.3 fusion.42
  52.5 2.2 add.61
  54.7 1.5 collective-permute-start.4
  56.1 1.3 add.59
  59.7 2.7 broadcast_select_fusion.4
  62.3 1.5 collective-permute-start.6
  63.8 1.3 fusion.40
  65.1 1.5 collective-permute-start.2
  66.6 1.3 add.62
  70.1 2.7 broadcast_select_fusion.3
  72.8 1.5 collective-permute-start.9
  74.2 2.1 add.64
  76.3 1.5 collective-permute-start.7
  77.7 1.3 fusion.38
  79.0 1.6 collective-permute-start.5
  80.6 1.9 convolution_subtract_fusion.9
  82.6 2.3 add.67
  84.8 1.5 collective-permute-start.10
  86.3 1.3 add.65
  89.0 2.9 %broadcast_select_fusion.2 = (f32[256,512]{1,0:T(8,128)}, f32[256,512]{1,0:T(8,128)}) fusion(pred[]{:T(512)S(6)} %eq.34, f32[256,512]{1,0:T(8,128)S(1)} %copy-done.15, f32[256,512]{1,0:T(8,128)S(1)} %fusion.80, f32[256,512]{1,0:T(8,128)S(1)} %convolution_subtract_fusion.9, f32[256,256]{1,0:T(8,128)S(1)} %fusion.38, f32[256,512]{1,0:T(8,128)} %collective-permute-done.9), kind=kOutput, calls=%fused_computation.71 | convolution fusion | flops 403177472 | bytes 3407873 | tf_op jit(solution)/shard_map/dot_general | solution.py:11
  91.9 1.5 collective-permute-start.12
  93.4 1.9 fusion.34
  95.3 1.2 fusion.32
  96.5 0.8 collective-permute-start.8
  97.4 1.9 convolution_subtract_fusion.7
  99.3 1.3 add.70
  100.6 1.0 collective-permute-start.14
  101.7 1.3 add.68
  103.6 2.5 broadcast_select_fusion.1
  108.9 1.6 broadcast_select_fusion
  110.6 1.5 collective-permute-start.15
  112.0 0.9 add.72
  112.9 1.5 collective-permute-start.16
  114.4 1.4 fusion.36
  116.5 1.7 fusion.82
  118.2 1.9 fusion.24
  120.2 1.0 fusion.16
  121.2 21.6 %all_to_all.35 = f32[8,32,512]{2,1,0:T(8,128)S(1)} all-to-all(f32[8,32,512]{2,1,0:T(8,128)S(1)} %bitcast.115), channel_id=1, replica_groups=mesh['row'=8,'col'=16] {'row'}, dimensions={0} | all-to-all | bytes 1048576 | tf_op jit(solution)/shard_map/all_to_all | solution.py:70
  142.8 1.3 collective-permute-start.17
  144.1 1.0 collective-permute-done.17
  145.7 1.9 slice.58
  147.6 3.2 %copy.25 = f32[4,5,128,256]{3,0,1,2:T(4,128)} copy(f32[4,5,128,256]{3,2,1,0:T(8,128)S(1)} %slice.58) | data formatting | bytes 5242880 | tf_op jit(solution)/shard_map/slice | solution.py:27
  150.8 38.9 %all-to-all-start.1 = ((f32[4,5,128,256]{3,0,1,2:T(4,128)}), f32[4,5,128,256]{3,0,1,2:T(4,128)}, u32[]{:S(2)}, u32[]{:S(2)}) async-start(f32[4,5,128,256]{3,0,1,2:T(4,128)} %copy.25), calls=%async_computation.1 | async-start | bytes 5242880 | tf_op jit(solution)/shard_map/all_to_all | solution.py:16
  189.7 12.7 %copy.28 = f32[8,6,256,256]{2,3,1,0:T(8,128)} copy(f32[8,6,256,256]{3,2,1,0:T(8,128)} %param.4) | data formatting | bytes 25165824 | tf_op args[1]
  202.4 22.7 %all-to-all-done.1 = f32[4,5,128,256]{3,0,1,2:T(4,128)} async-done(((f32[4,5,128,256]{3,0,1,2:T(4,128)}), f32[4,5,128,256]{3,0,1,2:T(4,128)}, u32[]{:S(2)}, u32[]{:S(2)}) %all-to-all-start.1) | async-done | bytes 2621472 | tf_op jit(solution)/shard_map/all_to_all | solution.py:16
  225.0 3.7 %copy.26 = f32[128,4,5,1,256]{4,1,0,2,3:T(4,128)} copy(f32[128,4,5,1,256]{4,1,2,0,3:T(4,128)} %bitcast.13) | data formatting | bytes 5242880 | tf_op jit(solution)/shard_map/all_to_all | solution.py:16
  228.7 4.0 %reshape.26 = f32[512,5,256]{2,0,1:T(8,128)} reshape(f32[128,4,5,1,256]{4,1,0,2,3:T(4,128)} %copy.26) | data formatting | bytes 5242880 | tf_op jit(solution)/shard_map/reshape | solution.py:17
  232.7 3.3 %copy.27 = f32[512,5,256]{0,2,1:T(8,128)} copy(f32[512,5,256]{2,0,1:T(8,128)} %reshape.26) | data formatting | bytes 5242880 | tf_op jit(solution)/shard_map/reshape | solution.py:17
  236.0 23.4 %all-gather.2.cloned.1.call-done = f32[2048,512]{1,0:T(8,128)} async-done(((f32[16,512]{1,0:T(8,128)}), f32[2048,512]{1,0:T(8,128)}) %all-gather.2.cloned.1.call-update) | async-done | bytes 4194320 | tf_op jit(solution)/shard_map/all_gather | solution.py:82
  259.4 14.3 %maximum_subtract_fusion = f32[6,256,512]{2,1,0:T(8,128)S(1)} fusion(f32[5,256,512]{2,1,0:T(8,128)} %bitcast.117, f32[1,256,512]{2,1,0:T(8,128)S(1)} %bitcast.118, f32[8,6,256,8,2,16]{2,5,4,3,1,0:T(8,128)} %bitcast.112, f32[8,2,8,16,512,1]{4,3,2,1,0,5:T(8,128)} %bitcast.120), kind=kOutput, calls=%fused_computation.3 | convolution fusion | flops 9665249280 | bytes 23068672 | tf_op jit(solution)/shard_map/kjwrht,rhkts->jws/dot_general | solution.py:85
  274.8 2.0 pad_maximum_fusion
  (100 shorter events, 13.1 us)
Async XLA Ops:
  6.5 32.3 %copy-start = (f32[8,256,256]{2,1,0:T(8,128)S(1)}, f32[8,256,256]{2,1,0:T(8,128)}, u32[]{:S(2)}) copy-start(f32[8,256,256]{2,1,0:T(8,128)} %param.5) | copy-start | bytes 6291460
  9.2 1.7 copy-start.2
  12.0 24.8 %all-to-all-start = ((f32[4,1,128,256]{3,0,1,2:T(4,128)}), f32[4,1,128,256]{3,0,1,2:T(4,128)S(1)}, u32[]{:S(2)}, u32[]{:S(2)}) async-start(f32[4,1,128,256]{3,0,1,2:T(4,128)} %copy.23), calls=%async_computation | async-start | bytes 1048576 | tf_op jit(solution)/shard_map/all_to_all | solution.py:16
  23.5 235.8 %all-gather.2.cloned.1.call-start = ((), (), s32[]{:S(2)}) async-start(), calls=%async_computation.3 | async-start | bytes 4227072 | tf_op jit(solution)/shard_map/all_gather | solution.py:82
  40.3 2.7 collective-permute-start
  43.0 0.7 copy-start.25
  46.4 6.1 %collective-permute-start.3 = (f32[256,512]{1,0:T(8,128)}, f32[256,512]{1,0:T(8,128)}, u32[]{:S(2)}, u32[]{:S(2)}) collective-permute-start(f32[256,512]{1,0:T(8,128)} %get-tuple-element.7), channel_id=1, source_target_pairs={{1,2}} | collective-permute-start | bytes 1572872 | tf_op jit(solution)/shard_map/ppermute | solution.py:59
  49.8 6.4 %collective-permute-start.1 = (f32[256,512]{1,0:T(8,128)}, f32[256,512]{1,0:T(8,128)}, u32[]{:S(2)}, u32[]{:S(2)}) collective-permute-start(f32[256,512]{1,0:T(8,128)} %add.58), channel_id=1, source_target_pairs={{0,2},{1,3}} | collective-permute-start | bytes 1572872 | tf_op jit(solution)/shard_map/ppermute | solution.py:59
  51.2 7.0 %copy-start.26 = (f32[256,256]{1,0:T(8,128)S(1)}, f32[256,256]{1,0:T(8,128)}, u32[]{:S(2)}) copy-start(f32[256,256]{1,0:T(8,128)} %copy-done.25) | copy-start | bytes 786436
  52.5 15.4 %copy-start.24 = (f32[256,256]{1,0:T(8,128)}, f32[256,256]{1,0:T(8,128)S(1)}, u32[]{:S(2)}) copy-start(f32[256,256]{1,0:T(8,128)S(1)} %fusion.42) | copy-start | bytes 786436
  54.7 11.9 %collective-permute-start.4 = (f32[256,512]{1,0:T(8,128)}, f32[256,512]{1,0:T(8,128)}, u32[]{:S(2)}, u32[]{:S(2)}) collective-permute-start(f32[256,512]{1,0:T(8,128)} %add.61), channel_id=1, source_target_pairs={{1,3},{2,4}} | collective-permute-start | bytes 1572872 | tf_op jit(solution)/shard_map/ppermute | solution.py:59
  57.4 0.8 copy-start.11
  58.9 0.8 copy-start.18
  62.3 6.9 %collective-permute-start.6 = (f32[256,512]{1,0:T(8,128)}, f32[256,512]{1,0:T(8,128)}, u32[]{:S(2)}, u32[]{:S(2)}) collective-permute-start(f32[256,512]{1,0:T(8,128)} %get-tuple-element.9), channel_id=1, source_target_pairs={{2,3}} | collective-permute-start | bytes 1572872 | tf_op jit(solution)/shard_map/ppermute | solution.py:59
  63.8 6.3 %copy-start.19 = (f32[256,512]{1,0:T(8,128)S(1)}, f32[256,512]{1,0:T(8,128)}, u32[]{:S(2)}) copy-start(f32[256,512]{1,0:T(8,128)} %copy-done.18) | copy-start | bytes 1572868
  65.1 7.7 %copy-start.21 = (f32[256,256]{1,0:T(8,128)}, f32[256,256]{1,0:T(8,128)S(1)}, u32[]{:S(2)}) copy-start(f32[256,256]{1,0:T(8,128)S(1)} %fusion.40) | copy-start | bytes 786436
  65.1 15.5 %collective-permute-start.2 = (f32[256,512]{1,0:T(8,128)}, f32[256,512]{1,0:T(8,128)}, u32[]{:S(2)}, u32[]{:S(2)}) collective-permute-start(f32[256,512]{1,0:T(8,128)} %copy-done.11), channel_id=1, source_target_pairs={{0,4},{1,5},{2,6},{3,7}} | collective-permute-start | bytes 1572872 | tf_op jit(solution)/shard_map/ppermute | solution.py:59
  67.9 0.8 copy-start.7
  69.3 0.8 copy-start.14
  72.8 9.8 %collective-permute-start.9 = (f32[256,512]{1,0:T(8,128)}, f32[256,512]{1,0:T(8,128)}, u32[]{:S(2)}, u32[]{:S(2)}) collective-permute-start(f32[256,512]{1,0:T(8,128)} %get-tuple-element.11), channel_id=1, source_target_pairs={{3,4}} | collective-permute-start | bytes 1572872 | tf_op jit(solution)/shard_map/ppermute | solution.py:59
  76.3 10.0 %collective-permute-start.7 = (f32[256,512]{1,0:T(8,128)}, f32[256,512]{1,0:T(8,128)}, u32[]{:S(2)}, u32[]{:S(2)}) collective-permute-start(f32[256,512]{1,0:T(8,128)} %add.64), channel_id=1, source_target_pairs={{2,4},{3,5}} | collective-permute-start | bytes 1572872 | tf_op jit(solution)/shard_map/ppermute | solution.py:59
  77.7 10.7 %copy-start.22 = (f32[256,256]{1,0:T(8,128)S(1)}, f32[256,256]{1,0:T(8,128)}, u32[]{:S(2)}) copy-start(f32[256,256]{1,0:T(8,128)} %copy-done.21) | copy-start | bytes 786436
  79.0 10.0 %copy-start.15 = (f32[256,512]{1,0:T(8,128)S(1)}, f32[256,512]{1,0:T(8,128)}, u32[]{:S(2)}) copy-start(f32[256,512]{1,0:T(8,128)} %copy-done.14) | copy-start | bytes 1572868
  79.0 18.4 %collective-permute-start.5 = (f32[256,512]{1,0:T(8,128)}, f32[256,512]{1,0:T(8,128)}, u32[]{:S(2)}, u32[]{:S(2)}) collective-permute-start(f32[256,512]{1,0:T(8,128)} %copy-done.7), channel_id=1, source_target_pairs={{1,5},{2,6},{3,7}} | collective-permute-start | bytes 1572872 | tf_op jit(solution)/shard_map/ppermute | solution.py:59
  82.5 9.4 %copy-start.20 = (f32[256,512]{1,0:T(8,128)}, f32[256,512]{1,0:T(8,128)S(1)}, u32[]{:S(2)}) copy-start(f32[256,512]{1,0:T(8,128)S(1)} %convolution_subtract_fusion.9) | copy-start | bytes 1572868
  84.8 16.8 %collective-permute-start.10 = (f32[256,512]{1,0:T(8,128)}, f32[256,512]{1,0:T(8,128)}, u32[]{:S(2)}, u32[]{:S(2)}) collective-permute-start(f32[256,512]{1,0:T(8,128)} %add.67), channel_id=1, source_target_pairs={{3,5},{4,6}} | collective-permute-start | bytes 1572872 | tf_op jit(solution)/shard_map/ppermute | solution.py:59
  87.6 0.8 copy-start.9
  88.4 9.0 %copy-start.8 = (f32[256,512]{1,0:T(8,128)S(1)}, f32[256,512]{1,0:T(8,128)}, u32[]{:S(2)}) copy-start(f32[256,512]{1,0:T(8,128)} %copy-done.7) | copy-start | bytes 1572868
  89.0 2.9 %copy-start.16 = (f32[256,512]{1,0:T(8,128)}, f32[256,512]{1,0:T(8,128)S(1)}, u32[]{:S(2)}) copy-start(f32[256,512]{1,0:T(8,128)S(1)} %fusion.80) | copy-start | bytes 1572868
  91.9 7.4 %collective-permute-start.12 = (f32[256,512]{1,0:T(8,128)}, f32[256,512]{1,0:T(8,128)}, u32[]{:S(2)}, u32[]{:S(2)}) collective-permute-start(f32[256,512]{1,0:T(8,128)} %get-tuple-element.13), channel_id=1, source_target_pairs={{4,5}} | collective-permute-start | bytes 1572872 | tf_op jit(solution)/shard_map/ppermute | solution.py:59
  96.5 7.0 %copy-start.17 = (f32[256,512]{1,0:T(8,128)S(1)}, f32[256,512]{1,0:T(8,128)}, u32[]{:S(2)}) copy-start(f32[256,512]{1,0:T(8,128)} %copy-done.16) | copy-start | bytes 1572868
  96.5 10.3 %collective-permute-start.8 = (f32[256,512]{1,0:T(8,128)}, f32[256,512]{1,0:T(8,128)S(1)}, u32[]{:S(2)}, u32[]{:S(2)}) collective-permute-start(f32[256,512]{1,0:T(8,128)} %copy-done.9), channel_id=1, source_target_pairs={{2,6},{3,7}} | collective-permute-start | bytes 1572872 | tf_op jit(solution)/shard_map/ppermute | solution.py:59
  100.6 6.2 %copy-start.10 = (f32[256,512]{1,0:T(8,128)S(1)}, f32[256,512]{1,0:T(8,128)}, u32[]{:S(2)}) copy-start(f32[256,512]{1,0:T(8,128)} %copy-done.9) | copy-start | bytes 1572868
  100.6 6.2 %copy-start.23 = (f32[256,256]{1,0:T(8,128)S(1)}, f32[256,256]{1,0:T(8,128)}, u32[]{:S(2)}) copy-start(f32[256,256]{1,0:T(8,128)} %copy-done.21) | copy-start | bytes 786436
  100.6 6.9 %collective-permute-start.14 = (f32[256,512]{1,0:T(8,128)S(1)}, f32[256,512]{1,0:T(8,128)S(1)}, u32[]{:S(2)}, u32[]{:S(2)}) collective-permute-start(f32[256,512]{1,0:T(8,128)S(1)} %add.70), channel_id=1, source_target_pairs={{4,6},{5,7}} | collective-permute-start | bytes 1572872 | tf_op jit(solution)/shard_map/ppermute | solution.py:59
  103.6 5.4 %copy-start.27 = (f32[256,256]{1,0:T(8,128)S(1)}, f32[256,256]{1,0:T(8,128)}, u32[]{:S(2)}) copy-start(f32[256,256]{1,0:T(8,128)} %fusion.34) | copy-start | bytes 786436
  106.1 2.0 collective-permute-start.13
  107.5 5.5 %copy-start.12 = (f32[256,512]{1,0:T(8,128)}, f32[256,512]{1,0:T(8,128)S(1)}, u32[]{:S(2)}) copy-start(f32[256,512]{1,0:T(8,128)S(1)} %convolution_subtract_fusion.5) | copy-start | bytes 1572868
  108.1 0.8 copy-start.5
  110.6 5.9 %collective-permute-start.15 = (f32[256,512]{1,0:T(8,128)}, f32[256,512]{1,0:T(8,128)}, u32[]{:S(2)}, u32[]{:S(2)}) collective-permute-start(f32[256,512]{1,0:T(8,128)} %get-tuple-element.17), channel_id=1, source_target_pairs={{6,7}} | collective-permute-start | bytes 1572872 | tf_op jit(solution)/shard_map/ppermute | solution.py:59
  112.9 5.3 %collective-permute-start.16 = (f32[256,512]{1,0:T(8,128)}, f32[256,512]{1,0:T(8,128)}, u32[]{:S(2)}, u32[]{:S(2)}) collective-permute-start(f32[256,512]{1,0:T(8,128)} %add.72), channel_id=1, source_target_pairs={{5,7}} | collective-permute-start | bytes 1572872 | tf_op jit(solution)/shard_map/ppermute | solution.py:59
  114.4 5.7 %copy-start.6 = (f32[256,512]{1,0:T(8,128)S(1)}, f32[256,512]{1,0:T(8,128)}, u32[]{:S(2)}) copy-start(f32[256,512]{1,0:T(8,128)} %copy-done.5) | copy-start | bytes 1572868
  114.4 5.8 %copy-start.13 = (f32[256,512]{1,0:T(8,128)S(1)}, f32[256,512]{1,0:T(8,128)}, u32[]{:S(2)}) copy-start(f32[256,512]{1,0:T(8,128)} %copy-done.12) | copy-start | bytes 1572868
  114.4 5.8 %copy-start.28 = (f32[256,512]{1,0:T(8,128)S(1)}, f32[256,512]{1,0:T(8,128)}, u32[]{:S(2)}) copy-start(f32[256,512]{1,0:T(8,128)} %get-tuple-element.8) | copy-start | bytes 1572868
  114.4 5.8 %copy-start.30 = (f32[256,512]{1,0:T(8,128)S(1)}, f32[256,512]{1,0:T(8,128)}, u32[]{:S(2)}) copy-start(f32[256,512]{1,0:T(8,128)} %get-tuple-element.10) | copy-start | bytes 1572868
  114.4 5.8 %copy-start.31 = (f32[256,512]{1,0:T(8,128)S(1)}, f32[256,512]{1,0:T(8,128)}, u32[]{:S(2)}) copy-start(f32[256,512]{1,0:T(8,128)} %get-tuple-element.12) | copy-start | bytes 1572868
  114.4 5.8 %copy-start.32 = (f32[256,512]{1,0:T(8,128)S(1)}, f32[256,512]{1,0:T(8,128)}, u32[]{:S(2)}) copy-start(f32[256,512]{1,0:T(8,128)} %get-tuple-element.14) | copy-start | bytes 1572868
  114.4 5.8 %copy-start.33 = (f32[256,512]{1,0:T(8,128)S(1)}, f32[256,512]{1,0:T(8,128)}, u32[]{:S(2)}) copy-start(f32[256,512]{1,0:T(8,128)} %get-tuple-element.16) | copy-start | bytes 1572868
  115.8 4.3 %collective-permute-start.11 = (f32[256,512]{1,0:T(8,128)S(1)}, f32[256,512]{1,0:T(8,128)S(1)}, u32[]{:S(2)}, u32[]{:S(2)}) collective-permute-start(f32[256,512]{1,0:T(8,128)S(1)} %add.68), channel_id=1, source_target_pairs={{3,7}} | collective-permute-start | bytes 1572872 | tf_op jit(solution)/shard_map/ppermute | solution.py:59
  121.2 26.4 %copy-start.3 = (f32[256,512]{1,0:T(8,128)}, f32[256,512]{1,0:T(8,128)S(1)}, u32[]{:S(2)}) copy-start(f32[256,512]{1,0:T(8,128)S(1)} %fusion.16) | copy-start | bytes 1572868
  142.8 2.3 collective-permute-start.17
  150.8 74.2 %all-to-all-start.1 = ((f32[4,5,128,256]{3,0,1,2:T(4,128)}), f32[4,5,128,256]{3,0,1,2:T(4,128)}, u32[]{:S(2)}, u32[]{:S(2)}) async-start(f32[4,5,128,256]{3,0,1,2:T(4,128)} %copy.25), calls=%async_computation.1 | async-start | bytes 5242880 | tf_op jit(solution)/shard_map/all_to_all | solution.py:16
  232.7 26.7 %copy-start.29 = (f32[512,1,256]{0,2,1:T(8,128)S(1)}, f32[512,1,256]{0,2,1:T(8,128)}, u32[]{:S(2)}) copy-start(f32[512,1,256]{0,2,1:T(8,128)} %copy.24) | copy-start | bytes 1572868
  273.7 1.0 copy-start.4
  274.7 2.1 copy-start.1
Sparse Core Ops, SparseCore 0:
  145.8 113.5 all-gather.1

commit v13 on v10

--- a/solution.py
+++ b/solution.py
@@ -66,25 +66,20 @@
 
     rows = lax.axis_size("row")
     halves = cols // sections
-    cut = width_block // rows
-    down = lax.all_to_all(own.reshape(rows, cut, -1), "row", 0, 0, tiled=True)[0]
-    part = cut // halves
-    pieces_out = down.reshape(halves, part, -1)
-    mine = pieces_out[0]
+    half_rows = width_block // halves
+    part = half_rows // rows
+    split = own.reshape(halves, half_rows, -1)
+    held = split[0]
     for h in range(1, halves):
-        pairs = [
-            (r * cols + k, r * cols + k + h * sections)
-            for r in range(rows)
-            for k in range(sections)
-        ]
-        got = lax.ppermute(pieces_out[h], AXES, pairs)
-        mine = jnp.where(col // sections == h, got, mine)
+        got = lax.ppermute(split[h], AXES, [(k, k + h * sections) for k in range(sections)])
+        held = jnp.where(col // sections == h, got, held)
+    mine = lax.all_to_all(held.reshape(rows, part, -1), "row", 0, 0, tiled=True)[0]
     gathered = lax.all_gather(mine, AXES, tiled=True)
 
     update = jnp.concatenate([lead[None], rest], axis=0)
     update = update - jnp.einsum(
-        "kjwrht,rhkts->jws",
-        panels.reshape(sections, blocks, width_block, rows, halves, part),
+        "kjwhrt,rhkts->jws",
+        panels.reshape(sections, blocks, width_block, halves, rows, part),
         gathered.reshape(rows, halves, sections, part, -1),
         precision=lax.Precision.HIGH,
         preferred_element_type=jnp.float32,

time: 285 us -> 285 us (level)
  transfers between devices with their start and end apart: 21 -> 21, of which waited for: 4 -> 3; matrix products, arithmetic and copies ran while one was open for 27% -> 27% of each run, Pallas kernels for 0% -> 0%
where the time goes in v13:
time: 285 us; the launch traced here: 283 us
  starting transfers between devices  72.2 us (25%)
  waiting for transfers between devices  59.4 us (21%)
  matrix products  53.4 us (19%)
  local copies, waits for them, and re-layouts  43.4 us (15%)
  blocking collectives  22.9 us (8%)
  other arithmetic  17.9 us (6%)
  between operations  14.1 us (5%)
    all_to_all x2, starting transfers between devices, transpose_in(): lax.all_to_all(pieces, AXES, split_axis=2, concat_axis=0, tiled=True)  49.3 us
    dot_general x25, matrix products, mm(): return jnp.dot(a, b, precision=HI, preferred_element_type=jnp.float32)  39.1 us
    all_to_all x2, waiting for transfers between devices, transpose_in(): lax.all_to_all(pieces, AXES, split_axis=2, concat_axis=0, tiled=True)  35.9 us
    all_gather x1, waiting for transfers between devices, per_device(): gathered = lax.all_gather(mine, AXES, tiled=True)  23.4 us
    unnamed x70, local copies, waits for them, and re-layouts  23.3 us
    all_to_all x1, blocking collectives, per_device(): lax.all_to_all(held.reshape(rows, part, -1), 'row', 0, 0, tiled=True)[0]  22.9 us
    ppermute x17, starting transfers between devices, per_device(): got = lax.ppermute(buf, AXES, pairs)  22.1 us
    add x10, other arithmetic, per_device(): buf = buf + got  15.7 us
  transfers between devices with their start and end apart: 21, of which 3 were waited for; matrix products, arithmetic and copies ran while one was open for 27% of the time, Pallas kernels for 0%

profile of v13, /device:TPU:1, one launch (start us, length us, event | category | flops | bytes accessed | tf_op | source)
XLA Modules:
  0.0 283.3 jit_solution(4825339450131895748)
XLA Ops:
  6.5 2.6 copy.37
  9.2 1.7 copy-done.2
  10.9 1.1 copy.23
  12.0 11.5 %all-to-all-start = ((f32[4,1,128,256]{3,0,1,2:T(4,128)}), f32[4,1,128,256]{3,0,1,2:T(4,128)S(1)}, u32[]{:S(2)}, u32[]{:S(2)}) async-start(f32[4,1,128,256]{3,0,1,2:T(4,128)} %copy.23), calls=%async_computation | async-start | bytes 1048576 | tf_op jit(solution)/shard_map/all_to_all | solution.py:16
  23.6 13.3 %all-to-all-done = f32[4,1,128,256]{3,0,1,2:T(4,128)S(1)} async-done(((f32[4,1,128,256]{3,0,1,2:T(4,128)}), f32[4,1,128,256]{3,0,1,2:T(4,128)S(1)}, u32[]{:S(2)}, u32[]{:S(2)}) %all-to-all-start) | async-done | bytes 524320 | tf_op jit(solution)/shard_map/all_to_all | solution.py:16
  37.5 1.4 copy.24
  38.9 1.7 broadcast_select_fusion.6
  40.5 1.5 collective-permute-start
  42.0 1.3 fusion.44
  44.1 2.7 broadcast_select_fusion.5
  46.7 1.4 collective-permute-start.3
  48.2 1.9 add.58
  50.1 1.5 collective-permute-start.1
  51.6 1.4 fusion.42
  53.0 2.2 add.61
  55.1 1.5 collective-permute-start.4
  56.6 1.3 add.59
  57.9 0.8 copy-done.11
  60.1 2.7 broadcast_select_fusion.4
  62.8 1.5 collective-permute-start.6
  64.2 1.4 fusion.40
  65.6 1.5 collective-permute-start.2
  67.1 1.3 add.62
  70.6 2.7 broadcast_select_fusion.3
  73.3 1.5 collective-permute-start.9
  74.8 2.1 add.64
  76.8 1.5 collective-permute-start.7
  78.3 1.4 fusion.38
  79.7 1.6 collective-permute-start.5
  81.3 1.9 convolution_subtract_fusion.9
  83.2 2.3 add.67
  85.5 1.5 collective-permute-start.10
  87.0 1.3 add.65
  88.3 0.8 copy-done.9
  89.7 2.9 %broadcast_select_fusion.2 = (f32[256,512]{1,0:T(8,128)}, f32[256,512]{1,0:T(8,128)}) fusion(pred[]{:T(512)S(6)} %eq.34, f32[256,512]{1,0:T(8,128)S(1)} %copy-done.15, f32[256,512]{1,0:T(8,128)S(1)} %fusion.79, f32[256,512]{1,0:T(8,128)S(1)} %convolution_subtract_fusion.9, f32[256,256]{1,0:T(8,128)S(1)} %fusion.38, f32[256,512]{1,0:T(8,128)} %collective-permute-done.9), kind=kOutput, calls=%fused_computation.72 | convolution fusion | flops 403177472 | bytes 3407873 | tf_op jit(solution)/shard_map/dot_general | solution.py:11
  92.6 1.5 collective-permute-start.12
  94.0 2.1 fusion.34
  96.1 1.3 fusion.32
  97.4 0.8 collective-permute-start.8
  98.3 1.9 convolution_subtract_fusion.7
  100.2 1.3 add.70
  101.5 0.8 collective-permute-start.14
  102.3 1.3 add.68
  104.3 2.5 broadcast_select_fusion.1
  109.6 1.6 broadcast_select_fusion
  111.3 1.5 collective-permute-start.15
  112.7 0.9 add.72
  113.6 1.5 collective-permute-start.16
  115.1 1.5 fusion.36
  117.3 1.7 fusion.81
  119.0 1.9 fusion.24
  121.0 1.0 fusion.16
  122.8 22.9 %all_to_all.35 = f32[8,16,512]{2,1,0:T(8,128)S(1)} all-to-all(f32[8,16,512]{2,1,0:T(8,128)S(1)} %bitcast.113), channel_id=1, replica_groups=mesh['row'=8,'col'=16] {'row'}, dimensions={0} | all-to-all | bytes 524288 | tf_op jit(solution)/shard_map/all_to_all | solution.py:76
  146.4 1.9 slice.59
  148.3 3.2 %copy.25 = f32[4,5,128,256]{3,0,1,2:T(4,128)} copy(f32[4,5,128,256]{3,2,1,0:T(8,128)S(1)} %slice.59) | data formatting | bytes 5242880 | tf_op jit(solution)/shard_map/slice | solution.py:27
  151.5 37.8 %all-to-all-start.1 = ((f32[4,5,128,256]{3,0,1,2:T(4,128)}), f32[4,5,128,256]{3,0,1,2:T(4,128)}, u32[]{:S(2)}, u32[]{:S(2)}) async-start(f32[4,5,128,256]{3,0,1,2:T(4,128)} %copy.25), calls=%async_computation.1 | async-start | bytes 5242880 | tf_op jit(solution)/shard_map/all_to_all | solution.py:16
  189.3 12.7 %copy.28 = f32[8,6,256,256]{2,3,1,0:T(8,128)} copy(f32[8,6,256,256]{3,2,1,0:T(8,128)} %param.4) | data formatting | bytes 25165824 | tf_op args[1]
  202.0 22.7 %all-to-all-done.1 = f32[4,5,128,256]{3,0,1,2:T(4,128)} async-done(((f32[4,5,128,256]{3,0,1,2:T(4,128)}), f32[4,5,128,256]{3,0,1,2:T(4,128)}, u32[]{:S(2)}, u32[]{:S(2)}) %all-to-all-start.1) | async-done | bytes 2621472 | tf_op jit(solution)/shard_map/all_to_all | solution.py:16
  224.7 3.7 %copy.26 = f32[128,4,5,1,256]{4,1,0,2,3:T(4,128)} copy(f32[128,4,5,1,256]{4,1,2,0,3:T(4,128)} %bitcast.13) | data formatting | bytes 5242880 | tf_op jit(solution)/shard_map/all_to_all | solution.py:16
  228.3 4.0 %reshape.27 = f32[512,5,256]{2,0,1:T(8,128)} reshape(f32[128,4,5,1,256]{4,1,0,2,3:T(4,128)} %copy.26) | data formatting | bytes 5242880 | tf_op jit(solution)/shard_map/reshape | solution.py:17
  232.3 3.3 %copy.27 = f32[512,5,256]{0,2,1:T(8,128)} copy(f32[512,5,256]{2,0,1:T(8,128)} %reshape.27) | data formatting | bytes 5242880 | tf_op jit(solution)/shard_map/reshape | solution.py:17
  235.6 23.4 %all-gather.3.cloned.1.call-done = f32[1,2048,512]{2,1,0:T(8,128)} async-done(((f32[1,16,512]{2,1,0:T(8,128)}), f32[1,2048,512]{2,1,0:T(8,128)}) %all-gather.3.cloned.1.call-update) | async-done | bytes 4194320 | tf_op jit(solution)/shard_map/all_gather | solution.py:77
  259.0 14.3 %maximum_subtract_fusion = f32[6,256,512]{2,1,0:T(8,128)S(1)} fusion(f32[5,256,512]{2,1,0:T(8,128)} %bitcast.110, f32[1,256,512]{2,1,0:T(8,128)S(1)} %bitcast.111, f32[8,6,256,2,8,16]{2,5,4,3,1,0:T(8,128)} %bitcast.106, f32[8,2,8,16,512,1]{4,3,2,1,0,5:T(8,128)} %bitcast.114), kind=kOutput, calls=%fused_computation.3 | convolution fusion | flops 9665249280 | bytes 23068672 | tf_op jit(solution)/shard_map/kjwhrt,rhkts->jws/dot_general | solution.py:80
  274.4 2.0 pad_maximum_fusion
  (101 shorter events, 12.3 us)
Async XLA Ops:
  6.5 32.3 %copy-start = (f32[8,256,256]{2,1,0:T(8,128)S(1)}, f32[8,256,256]{2,1,0:T(8,128)}, u32[]{:S(2)}) copy-start(f32[8,256,256]{2,1,0:T(8,128)} %param.5) | copy-start | bytes 6291460
  9.2 1.7 copy-start.2
  12.0 24.8 %all-to-all-start = ((f32[4,1,128,256]{3,0,1,2:T(4,128)}), f32[4,1,128,256]{3,0,1,2:T(4,128)S(1)}, u32[]{:S(2)}, u32[]{:S(2)}) async-start(f32[4,1,128,256]{3,0,1,2:T(4,128)} %copy.23), calls=%async_computation | async-start | bytes 1048576 | tf_op jit(solution)/shard_map/all_to_all | solution.py:16
  23.5 235.5 %all-gather.3.cloned.1.call-start = ((), (), s32[]{:S(2)}) async-start(), calls=%async_computation.3 | async-start | bytes 4227072 | tf_op jit(solution)/shard_map/all_gather | solution.py:77
  40.5 2.8 collective-permute-start
  43.3 0.7 copy-start.25
  46.7 6.2 %collective-permute-start.3 = (f32[256,512]{1,0:T(8,128)}, f32[256,512]{1,0:T(8,128)}, u32[]{:S(2)}, u32[]{:S(2)}) collective-permute-start(f32[256,512]{1,0:T(8,128)} %get-tuple-element.7), channel_id=1, source_target_pairs={{1,2}} | collective-permute-start | bytes 1572872 | tf_op jit(solution)/shard_map/ppermute | solution.py:59
  50.1 6.5 %collective-permute-start.1 = (f32[256,512]{1,0:T(8,128)}, f32[256,512]{1,0:T(8,128)}, u32[]{:S(2)}, u32[]{:S(2)}) collective-permute-start(f32[256,512]{1,0:T(8,128)} %add.58), channel_id=1, source_target_pairs={{0,2},{1,3}} | collective-permute-start | bytes 1572872 | tf_op jit(solution)/shard_map/ppermute | solution.py:59
  51.6 7.1 %copy-start.26 = (f32[256,256]{1,0:T(8,128)S(1)}, f32[256,256]{1,0:T(8,128)}, u32[]{:S(2)}) copy-start(f32[256,256]{1,0:T(8,128)} %copy-done.25) | copy-start | bytes 786436
  52.9 15.5 %copy-start.24 = (f32[256,256]{1,0:T(8,128)}, f32[256,256]{1,0:T(8,128)S(1)}, u32[]{:S(2)}) copy-start(f32[256,256]{1,0:T(8,128)S(1)} %fusion.42) | copy-start | bytes 786436
  55.1 12.0 %collective-permute-start.4 = (f32[256,512]{1,0:T(8,128)}, f32[256,512]{1,0:T(8,128)}, u32[]{:S(2)}, u32[]{:S(2)}) collective-permute-start(f32[256,512]{1,0:T(8,128)} %add.61), channel_id=1, source_target_pairs={{1,3},{2,4}} | collective-permute-start | bytes 1572872 | tf_op jit(solution)/shard_map/ppermute | solution.py:59
  57.9 0.8 copy-start.11
  59.3 0.8 copy-start.18
  62.8 7.1 %collective-permute-start.6 = (f32[256,512]{1,0:T(8,128)}, f32[256,512]{1,0:T(8,128)}, u32[]{:S(2)}, u32[]{:S(2)}) collective-permute-start(f32[256,512]{1,0:T(8,128)} %get-tuple-element.9), channel_id=1, source_target_pairs={{2,3}} | collective-permute-start | bytes 1572872 | tf_op jit(solution)/shard_map/ppermute | solution.py:59
  64.2 6.4 %copy-start.19 = (f32[256,512]{1,0:T(8,128)S(1)}, f32[256,512]{1,0:T(8,128)}, u32[]{:S(2)}) copy-start(f32[256,512]{1,0:T(8,128)} %copy-done.18) | copy-start | bytes 1572868
  65.6 7.7 %copy-start.21 = (f32[256,256]{1,0:T(8,128)}, f32[256,256]{1,0:T(8,128)S(1)}, u32[]{:S(2)}) copy-start(f32[256,256]{1,0:T(8,128)S(1)} %fusion.40) | copy-start | bytes 786436
  65.6 15.6 %collective-permute-start.2 = (f32[256,512]{1,0:T(8,128)}, f32[256,512]{1,0:T(8,128)}, u32[]{:S(2)}, u32[]{:S(2)}) collective-permute-start(f32[256,512]{1,0:T(8,128)} %copy-done.11), channel_id=1, source_target_pairs={{0,4},{1,5},{2,6},{3,7}} | collective-permute-start | bytes 1572872 | tf_op jit(solution)/shard_map/ppermute | solution.py:59
  68.4 0.8 copy-start.7
  69.8 0.8 copy-start.14
  73.3 9.9 %collective-permute-start.9 = (f32[256,512]{1,0:T(8,128)}, f32[256,512]{1,0:T(8,128)}, u32[]{:S(2)}, u32[]{:S(2)}) collective-permute-start(f32[256,512]{1,0:T(8,128)} %get-tuple-element.11), channel_id=1, source_target_pairs={{3,4}} | collective-permute-start | bytes 1572872 | tf_op jit(solution)/shard_map/ppermute | solution.py:59
  76.8 10.1 %collective-permute-start.7 = (f32[256,512]{1,0:T(8,128)}, f32[256,512]{1,0:T(8,128)}, u32[]{:S(2)}, u32[]{:S(2)}) collective-permute-start(f32[256,512]{1,0:T(8,128)} %add.64), channel_id=1, source_target_pairs={{2,4},{3,5}} | collective-permute-start | bytes 1572872 | tf_op jit(solution)/shard_map/ppermute | solution.py:59
  78.3 10.8 %copy-start.22 = (f32[256,256]{1,0:T(8,128)S(1)}, f32[256,256]{1,0:T(8,128)}, u32[]{:S(2)}) copy-start(f32[256,256]{1,0:T(8,128)} %copy-done.21) | copy-start | bytes 786436
  79.7 10.0 %copy-start.15 = (f32[256,512]{1,0:T(8,128)S(1)}, f32[256,512]{1,0:T(8,128)}, u32[]{:S(2)}) copy-start(f32[256,512]{1,0:T(8,128)} %copy-done.14) | copy-start | bytes 1572868
  79.7 18.6 %collective-permute-start.5 = (f32[256,512]{1,0:T(8,128)}, f32[256,512]{1,0:T(8,128)}, u32[]{:S(2)}, u32[]{:S(2)}) collective-permute-start(f32[256,512]{1,0:T(8,128)} %copy-done.7), channel_id=1, source_target_pairs={{1,5},{2,6},{3,7}} | collective-permute-start | bytes 1572872 | tf_op jit(solution)/shard_map/ppermute | solution.py:59
  83.2 9.4 %copy-start.20 = (f32[256,512]{1,0:T(8,128)}, f32[256,512]{1,0:T(8,128)S(1)}, u32[]{:S(2)}) copy-start(f32[256,512]{1,0:T(8,128)S(1)} %convolution_subtract_fusion.9) | copy-start | bytes 1572868
  85.5 16.8 %collective-permute-start.10 = (f32[256,512]{1,0:T(8,128)}, f32[256,512]{1,0:T(8,128)}, u32[]{:S(2)}, u32[]{:S(2)}) collective-permute-start(f32[256,512]{1,0:T(8,128)} %add.67), channel_id=1, source_target_pairs={{3,5},{4,6}} | collective-permute-start | bytes 1572872 | tf_op jit(solution)/shard_map/ppermute | solution.py:59
  88.2 0.8 copy-start.9
  89.0 9.2 %copy-start.8 = (f32[256,512]{1,0:T(8,128)S(1)}, f32[256,512]{1,0:T(8,128)}, u32[]{:S(2)}) copy-start(f32[256,512]{1,0:T(8,128)} %copy-done.7) | copy-start | bytes 1572868
  89.7 2.9 %copy-start.16 = (f32[256,512]{1,0:T(8,128)}, f32[256,512]{1,0:T(8,128)S(1)}, u32[]{:S(2)}) copy-start(f32[256,512]{1,0:T(8,128)S(1)} %fusion.79) | copy-start | bytes 1572868
  92.6 7.6 %collective-permute-start.12 = (f32[256,512]{1,0:T(8,128)}, f32[256,512]{1,0:T(8,128)}, u32[]{:S(2)}, u32[]{:S(2)}) collective-permute-start(f32[256,512]{1,0:T(8,128)} %get-tuple-element.13), channel_id=1, source_target_pairs={{4,5}} | collective-permute-start | bytes 1572872 | tf_op jit(solution)/shard_map/ppermute | solution.py:59
  97.4 6.8 %copy-start.17 = (f32[256,512]{1,0:T(8,128)S(1)}, f32[256,512]{1,0:T(8,128)}, u32[]{:S(2)}) copy-start(f32[256,512]{1,0:T(8,128)} %copy-done.16) | copy-start | bytes 1572868
  97.4 10.1 %collective-permute-start.8 = (f32[256,512]{1,0:T(8,128)}, f32[256,512]{1,0:T(8,128)S(1)}, u32[]{:S(2)}, u32[]{:S(2)}) collective-permute-start(f32[256,512]{1,0:T(8,128)} %copy-done.9), channel_id=1, source_target_pairs={{2,6},{3,7}} | collective-permute-start | bytes 1572872 | tf_op jit(solution)/shard_map/ppermute | solution.py:59
  101.5 6.0 %copy-start.10 = (f32[256,512]{1,0:T(8,128)S(1)}, f32[256,512]{1,0:T(8,128)}, u32[]{:S(2)}) copy-start(f32[256,512]{1,0:T(8,128)} %copy-done.9) | copy-start | bytes 1572868
  101.5 6.0 %copy-start.23 = (f32[256,256]{1,0:T(8,128)S(1)}, f32[256,256]{1,0:T(8,128)}, u32[]{:S(2)}) copy-start(f32[256,256]{1,0:T(8,128)} %copy-done.21) | copy-start | bytes 786436
  101.5 6.7 %collective-permute-start.14 = (f32[256,512]{1,0:T(8,128)S(1)}, f32[256,512]{1,0:T(8,128)S(1)}, u32[]{:S(2)}, u32[]{:S(2)}) collective-permute-start(f32[256,512]{1,0:T(8,128)S(1)} %add.70), channel_id=1, source_target_pairs={{4,6},{5,7}} | collective-permute-start | bytes 1572872 | tf_op jit(solution)/shard_map/ppermute | solution.py:59
  104.3 5.4 %copy-start.27 = (f32[256,256]{1,0:T(8,128)S(1)}, f32[256,256]{1,0:T(8,128)}, u32[]{:S(2)}) copy-start(f32[256,256]{1,0:T(8,128)} %fusion.34) | copy-start | bytes 786436
  106.8 2.0 collective-permute-start.13
  108.2 5.5 %copy-start.12 = (f32[256,512]{1,0:T(8,128)}, f32[256,512]{1,0:T(8,128)S(1)}, u32[]{:S(2)}) copy-start(f32[256,512]{1,0:T(8,128)S(1)} %convolution_subtract_fusion.5) | copy-start | bytes 1572868
  108.8 0.8 copy-start.5
  111.3 6.0 %collective-permute-start.15 = (f32[256,512]{1,0:T(8,128)}, f32[256,512]{1,0:T(8,128)}, u32[]{:S(2)}, u32[]{:S(2)}) collective-permute-start(f32[256,512]{1,0:T(8,128)} %get-tuple-element.17), channel_id=1, source_target_pairs={{6,7}} | collective-permute-start | bytes 1572872 | tf_op jit(solution)/shard_map/ppermute | solution.py:59
  113.6 5.4 %collective-permute-start.16 = (f32[256,512]{1,0:T(8,128)}, f32[256,512]{1,0:T(8,128)}, u32[]{:S(2)}, u32[]{:S(2)}) collective-permute-start(f32[256,512]{1,0:T(8,128)} %add.72), channel_id=1, source_target_pairs={{5,7}} | collective-permute-start | bytes 1572872 | tf_op jit(solution)/shard_map/ppermute | solution.py:59
  115.1 5.8 %copy-start.6 = (f32[256,512]{1,0:T(8,128)S(1)}, f32[256,512]{1,0:T(8,128)}, u32[]{:S(2)}) copy-start(f32[256,512]{1,0:T(8,128)} %copy-done.5) | copy-start | bytes 1572868
  115.1 5.9 %copy-start.13 = (f32[256,512]{1,0:T(8,128)S(1)}, f32[256,512]{1,0:T(8,128)}, u32[]{:S(2)}) copy-start(f32[256,512]{1,0:T(8,128)} %copy-done.12) | copy-start | bytes 1572868
  115.1 5.9 %copy-start.28 = (f32[256,512]{1,0:T(8,128)S(1)}, f32[256,512]{1,0:T(8,128)}, u32[]{:S(2)}) copy-start(f32[256,512]{1,0:T(8,128)} %get-tuple-element.8) | copy-start | bytes 1572868
  115.1 5.9 %copy-start.30 = (f32[256,512]{1,0:T(8,128)S(1)}, f32[256,512]{1,0:T(8,128)}, u32[]{:S(2)}) copy-start(f32[256,512]{1,0:T(8,128)} %get-tuple-element.10) | copy-start | bytes 1572868
  115.1 5.9 %copy-start.31 = (f32[256,512]{1,0:T(8,128)S(1)}, f32[256,512]{1,0:T(8,128)}, u32[]{:S(2)}) copy-start(f32[256,512]{1,0:T(8,128)} %get-tuple-element.12) | copy-start | bytes 1572868
  115.1 5.9 %copy-start.32 = (f32[256,512]{1,0:T(8,128)S(1)}, f32[256,512]{1,0:T(8,128)}, u32[]{:S(2)}) copy-start(f32[256,512]{1,0:T(8,128)} %get-tuple-element.14) | copy-start | bytes 1572868
  115.1 5.9 %copy-start.33 = (f32[256,512]{1,0:T(8,128)S(1)}, f32[256,512]{1,0:T(8,128)}, u32[]{:S(2)}) copy-start(f32[256,512]{1,0:T(8,128)} %get-tuple-element.16) | copy-start | bytes 1572868
  116.6 4.3 %collective-permute-start.11 = (f32[256,512]{1,0:T(8,128)S(1)}, f32[256,512]{1,0:T(8,128)S(1)}, u32[]{:S(2)}, u32[]{:S(2)}) collective-permute-start(f32[256,512]{1,0:T(8,128)S(1)} %add.68), channel_id=1, source_target_pairs={{3,7}} | collective-permute-start | bytes 1572872 | tf_op jit(solution)/shard_map/ppermute | solution.py:59
  122.0 26.3 %copy-start.3 = (f32[256,512]{1,0:T(8,128)}, f32[256,512]{1,0:T(8,128)S(1)}, u32[]{:S(2)}) copy-start(f32[256,512]{1,0:T(8,128)S(1)} %fusion.16) | copy-start | bytes 1572868
  122.0 0.7 collective-permute-start.17
  151.5 73.2 %all-to-all-start.1 = ((f32[4,5,128,256]{3,0,1,2:T(4,128)}), f32[4,5,128,256]{3,0,1,2:T(4,128)}, u32[]{:S(2)}, u32[]{:S(2)}) async-start(f32[4,5,128,256]{3,0,1,2:T(4,128)} %copy.25), calls=%async_computation.1 | async-start | bytes 5242880 | tf_op jit(solution)/shard_map/all_to_all | solution.py:16
  232.3 26.7 %copy-start.29 = (f32[512,1,256]{0,2,1:T(8,128)S(1)}, f32[512,1,256]{0,2,1:T(8,128)}, u32[]{:S(2)}) copy-start(f32[512,1,256]{0,2,1:T(8,128)} %copy.24) | copy-start | bytes 1572868
  273.3 1.0 copy-start.4
  274.3 2.1 copy-start.1
Sparse Core Ops, SparseCore 0:
  146.5 112.5 all-gather.2

commit v14 on v13

--- a/solution.py
+++ b/solution.py
@@ -77,13 +77,20 @@
     gathered = lax.all_gather(mine, AXES, tiled=True)
 
     update = jnp.concatenate([lead[None], rest], axis=0)
-    update = update - jnp.einsum(
-        "kjwhrt,rhkts->jws",
-        panels.reshape(sections, blocks, width_block, halves, rows, part),
-        gathered.reshape(rows, halves, sections, part, -1),
-        precision=lax.Precision.HIGH,
-        preferred_element_type=jnp.float32,
-    )
+    flat = panels.reshape(sections, blocks, width_block, halves, rows, part)
+    solved_rows = gathered.reshape(rows, halves, sections, part, -1)
+
+    def parts(a):
+        high = lax.reduce_precision(a, exponent_bits=8, mantissa_bits=7)
+        return high.astype(jnp.bfloat16), (a - high).astype(jnp.bfloat16)
+
+    flat_hi, flat_lo = parts(flat)
+    rows_hi, rows_lo = parts(solved_rows)
+
+    def term(a, b):
+        return jnp.einsum("kjwhrt,rhkts->jws", a, b, preferred_element_type=jnp.float32)
+
+    update = update - (term(flat_hi, rows_hi) + (term(flat_hi, rows_lo) + term(flat_lo, rows_hi)))
     first = jnp.where(device < sections, own, update[0])
     return jnp.concatenate([first[None], update[1:]], axis=0)
 

time: 285 us -> 288 us (1.011)
  waiting for transfers between devices: 59.4 us -> 47.5 us
  other arithmetic: 17.9 us -> 28.2 us
  matrix products: 53.4 us -> 58.5 us
    convert_element_type x0 -> x1, other arithmetic: none -> 12 us  [parts(): return (high.astype(jnp.bfloat16), (a - high).astype(jnp.bfloat16))]
    all_to_all x2, waiting for transfers between devices: 35.9 us -> 24 us  [transpose_in(): lax.all_to_all(pieces, AXES, split_axis=2, concat_axis=0, tiled=True)]
    dot_general x1 -> x3, matrix products: 14.3 us -> 19 us  [term(): jnp.einsum('kjwhrt,rhkts->jws', a, b, preferred_element_type=jnp.float32)]
    all_to_all x2, starting transfers between devices: 49.3 us -> 52.7 us  [transpose_in(): lax.all_to_all(pieces, AXES, split_axis=2, concat_axis=0, tiled=True)]
    unnamed x70 -> x68, local copies, waits for them, and re-layouts: 23.3 us -> 21 us
  transfers between devices with their start and end apart: 21 -> 21, of which waited for: 3 -> 3; matrix products, arithmetic and copies ran while one was open for 27% -> 30% of each run, Pallas kernels for 0% -> 0%
where the time goes in v14:
time: 288 us; the launch traced here: 286 us
  starting transfers between devices  73.3 us (25%)
  matrix products  58.5 us (20%)
  waiting for transfers between devices  47.5 us (16%)
  local copies, waits for them, and re-layouts  41.1 us (14%)
  other arithmetic  28.2 us (10%)
  blocking collectives  23 us (8%)
  between operations  14.2 us (5%)
    all_to_all x2, starting transfers between devices, transpose_in(): lax.all_to_all(pieces, AXES, split_axis=2, concat_axis=0, tiled=True)  52.7 us
    dot_general x25, matrix products, mm(): return jnp.dot(a, b, precision=HI, preferred_element_type=jnp.float32)  39.5 us
    all_to_all x2, waiting for transfers between devices, transpose_in(): lax.all_to_all(pieces, AXES, split_axis=2, concat_axis=0, tiled=True)  24 us
    all_gather x1, waiting for transfers between devices, per_device(): gathered = lax.all_gather(mine, AXES, tiled=True)  23.5 us
    all_to_all x1, blocking collectives, per_device(): lax.all_to_all(held.reshape(rows, part, -1), 'row', 0, 0, tiled=True)[0]  23 us
    unnamed x68, local copies, waits for them, and re-layouts  21 us
    ppermute x17, starting transfers between devices, per_device(): got = lax.ppermute(buf, AXES, pairs)  19.9 us
    dot_general x3, matrix products, term(): jnp.einsum('kjwhrt,rhkts->jws', a, b, preferred_element_type=jnp.float32)  19 us
  transfers between devices with their start and end apart: 21, of which 3 were waited for; matrix products, arithmetic and copies ran while one was open for 30% of the time, Pallas kernels for 0%

profile of v14, /device:TPU:1, one launch (start us, length us, event | category | flops | bytes accessed | tf_op | source)
XLA Modules:
  0.0 285.8 jit_solution(14844873160855772551)
XLA Ops:
  6.5 2.6 copy.53
  9.2 1.7 copy-done.2
  10.9 1.1 copy.33
  12.0 11.5 %all-to-all-start = ((f32[4,1,128,256]{3,0,1,2:T(4,128)}), f32[4,1,128,256]{3,0,1,2:T(4,128)S(1)}, u32[]{:S(2)}, u32[]{:S(2)}) async-start(f32[4,1,128,256]{3,0,1,2:T(4,128)} %copy.33), calls=%async_computation | async-start | bytes 1048576 | tf_op jit(solution)/shard_map/all_to_all | solution.py:16
  23.6 13.3 %all-to-all-done = f32[4,1,128,256]{3,0,1,2:T(4,128)S(1)} async-done(((f32[4,1,128,256]{3,0,1,2:T(4,128)}), f32[4,1,128,256]{3,0,1,2:T(4,128)S(1)}, u32[]{:S(2)}, u32[]{:S(2)}) %all-to-all-start) | async-done | bytes 524320 | tf_op jit(solution)/shard_map/all_to_all | solution.py:16
  37.5 1.4 copy.34
  38.9 1.7 broadcast_select_fusion.6
  40.5 1.5 collective-permute-start
  42.0 1.3 fusion.53
  43.3 2.0 add.64
  45.4 1.5 collective-permute-start.1
  46.8 2.6 broadcast_select_fusion.5
  49.5 1.5 collective-permute-start.3
  50.9 1.3 fusion.51
  52.3 1.4 add.65
  55.9 2.7 broadcast_select_fusion.4
  58.6 1.5 collective-permute-start.6
  60.0 2.1 add.67
  62.1 1.4 collective-permute-start.4
  63.5 1.4 fusion.49
  64.9 1.4 fusion.47
  67.1 1.3 add.70
  68.4 0.8 collective-permute-start.7
  69.2 2.1 add.68
  71.3 1.4 collective-permute-start.5
  72.7 1.7 fusion.87
  74.4 2.5 broadcast_select_fusion.3
  78.3 1.0 add.71
  79.3 1.7 fusion.88
  81.7 1.7 broadcast_select_fusion.2
  83.4 1.6 collective-permute-start.12
  85.0 0.9 add.73
  85.9 1.5 collective-permute-start.10
  87.3 2.0 fusion.41
  89.4 1.3 fusion.43
  90.7 0.8 collective-permute-start.8
  91.6 1.9 convolution_subtract_fusion.7
  93.5 1.3 add.76
  95.7 1.3 add.74
  97.6 2.5 broadcast_select_fusion.1
  100.8 1.7 convolution_subtract_fusion.5
  103.9 1.6 broadcast_select_fusion
  105.6 1.5 collective-permute-start.15
  107.0 0.9 add.78
  107.9 1.5 collective-permute-start.16
  109.4 1.5 fusion.45
  111.6 1.7 fusion.90
  113.3 1.9 fusion.33
  115.3 1.0 fusion.23
  117.1 23.0 %all_to_all.35 = f32[8,16,512]{2,1,0:T(8,128)S(1)} all-to-all(f32[8,16,512]{2,1,0:T(8,128)S(1)} %bitcast.134), channel_id=1, replica_groups=mesh['row'=8,'col'=16] {'row'}, dimensions={0} | all-to-all | bytes 524288 | tf_op jit(solution)/shard_map/all_to_all | solution.py:76
  140.7 1.9 slice.59
  142.6 3.2 %copy.35 = f32[4,5,128,256]{3,0,1,2:T(4,128)} copy(f32[4,5,128,256]{3,2,1,0:T(8,128)S(1)} %slice.59) | data formatting | bytes 5242880 | tf_op jit(solution)/shard_map/slice | solution.py:27
  145.8 41.2 %all-to-all-start.1 = ((f32[4,5,128,256]{3,0,1,2:T(4,128)}), f32[4,5,128,256]{3,0,1,2:T(4,128)}, u32[]{:S(2)}, u32[]{:S(2)}) async-start(f32[4,5,128,256]{3,0,1,2:T(4,128)} %copy.35), calls=%async_computation.1 | async-start | bytes 5242880 | tf_op jit(solution)/shard_map/all_to_all | solution.py:16
  187.0 12.7 %copy.39 = f32[8,6,256,256]{2,3,1,0:T(8,128)} copy(f32[8,6,256,256]{3,2,1,0:T(8,128)} %param.4) | data formatting | bytes 25165824 | tf_op args[1]
  199.7 12.0 %fusion = (bf16[8,6,256,2,8,16]{2,5,4,3,1,0:T(8,128)(2,1)}, bf16[8,6,256,2,8,16]{2,5,4,3,1,0:T(8,128)(2,1)}) fusion(f32[8,6,256,2,8,16]{2,5,4,3,1,0:T(8,128)} %bitcast.127), kind=kLoop, calls=%fused_computation.2 | loop fusion | flops 12582912 | bytes 25165824 | tf_op jit(solution)/shard_map/convert_element_type | solution.py:85
  211.6 10.7 %all-to-all-done.1 = f32[4,5,128,256]{3,0,1,2:T(4,128)} async-done(((f32[4,5,128,256]{3,0,1,2:T(4,128)}), f32[4,5,128,256]{3,0,1,2:T(4,128)}, u32[]{:S(2)}, u32[]{:S(2)}) %all-to-all-start.1) | async-done | bytes 2621472 | tf_op jit(solution)/shard_map/all_to_all | solution.py:16
  222.3 3.7 %copy.36 = f32[128,4,5,1,256]{4,1,0,2,3:T(4,128)} copy(f32[128,4,5,1,256]{4,1,2,0,3:T(4,128)} %bitcast.13) | data formatting | bytes 5242880 | tf_op jit(solution)/shard_map/all_to_all | solution.py:16
  226.0 4.0 %reshape.27 = f32[512,5,256]{2,0,1:T(8,128)} reshape(f32[128,4,5,1,256]{4,1,0,2,3:T(4,128)} %copy.36) | data formatting | bytes 5242880 | tf_op jit(solution)/shard_map/reshape | solution.py:17
  230.0 3.2 %copy.37 = f32[512,5,256]{0,2,1:T(8,128)} copy(f32[512,5,256]{2,0,1:T(8,128)} %reshape.27) | data formatting | bytes 5242880 | tf_op jit(solution)/shard_map/reshape | solution.py:17
  233.2 23.5 %all-gather.3.cloned.1.call-done = f32[1,2048,512]{2,1,0:T(8,128)} async-done(((f32[1,16,512]{2,1,0:T(8,128)}), f32[1,2048,512]{2,1,0:T(8,128)}) %all-gather.3.cloned.1.call-update) | async-done | bytes 4194320 | tf_op jit(solution)/shard_map/all_gather | solution.py:77
  256.7 7.5 %fusion.3 = f32[512,6,256,1,1,1]{0,2,5,1,4,3:T(8,128)S(1)} fusion(bf16[8,6,256,2,8,16]{2,5,4,3,1,0:T(8,128)(2,1)} %get-tuple-element.6, f32[8,2,8,16,512]{4,3,2,1,0:T(8,128)} %bitcast.135), kind=kOutput, calls=%fused_computation.7 | convolution fusion | flops 3224371200 | bytes 13631488 | tf_op jit(solution)/shard_map/kjwhrt,rhkts->jws/dot_general | solution.py:91
  264.2 5.8 %fusion.5 = f32[512,6,256,1,1,1]{0,2,5,1,4,3:T(8,128)S(1)} fusion(bf16[8,6,256,2,8,16]{2,5,4,3,1,0:T(8,128)(2,1)} %get-tuple-element.6, f32[8,2,8,16,512]{4,3,2,1,0:T(8,128)S(1)} %bitcast.136), kind=kOutput, calls=%fused_computation.9 | convolution fusion | flops 3223322624 | bytes 13631488 | tf_op jit(solution)/shard_map/kjwhrt,rhkts->jws/dot_general | solution.py:91
  270.1 5.7 %maximum_subtract_fusion = f32[6,256,512]{2,1,0:T(8,128)S(1)} fusion(f32[5,256,512]{2,1,0:T(8,128)S(1)} %bitcast.131, f32[1,256,512]{2,1,0:T(8,128)S(1)} %bitcast.132, f32[512,6,256,1,1,1]{0,2,5,1,4,3:T(8,128)S(1)} %fusion.3, f32[512,6,256,1,1,1]{0,2,5,1,4,3:T(8,128)S(1)} %fusion.5, bf16[8,6,256,2,8,16]{2,5,4,3,1,0:T(8,128)(2,1)} %get-tuple-element.5, ...), kind=kOutput, calls=%fused_computation.12 | convolution fusion | flops 3226468352 | bytes 23068672 | tf_op jit(solution)/shard_map/kjwhrt,rhkts->jws/dot_general | solution.py:91
  276.9 2.0 pad_maximum_fusion
  (102 shorter events, 12.5 us)
Async XLA Ops:
  6.5 32.3 %copy-start = (f32[8,256,256]{2,1,0:T(8,128)S(1)}, f32[8,256,256]{2,1,0:T(8,128)}, u32[]{:S(2)}) copy-start(f32[8,256,256]{2,1,0:T(8,128)} %param.5) | copy-start | bytes 6291460
  9.2 1.7 copy-start.2
  12.0 24.8 %all-to-all-start = ((f32[4,1,128,256]{3,0,1,2:T(4,128)}), f32[4,1,128,256]{3,0,1,2:T(4,128)S(1)}, u32[]{:S(2)}, u32[]{:S(2)}) async-start(f32[4,1,128,256]{3,0,1,2:T(4,128)} %copy.33), calls=%async_computation | async-start | bytes 1048576 | tf_op jit(solution)/shard_map/all_to_all | solution.py:16
  23.5 233.1 %all-gather.3.cloned.1.call-start = ((), (), s32[]{:S(2)}) async-start(), calls=%async_computation.3 | async-start | bytes 4227072 | tf_op jit(solution)/shard_map/all_gather | solution.py:77
  40.5 2.8 collective-permute-start
  43.3 10.3 %copy-start.21 = (f32[256,256]{1,0:T(8,128)}, f32[256,256]{1,0:T(8,128)S(1)}, u32[]{:S(2)}) copy-start(f32[256,256]{1,0:T(8,128)S(1)} %fusion.53) | copy-start | bytes 786436
  45.4 6.9 %collective-permute-start.1 = (f32[256,512]{1,0:T(8,128)}, f32[256,512]{1,0:T(8,128)}, u32[]{:S(2)}, u32[]{:S(2)}) collective-permute-start(f32[256,512]{1,0:T(8,128)} %add.64), channel_id=1, source_target_pairs={{0,2},{1,3}} | collective-permute-start | bytes 1572872 | tf_op jit(solution)/shard_map/ppermute | solution.py:59
  49.5 5.6 %collective-permute-start.3 = (f32[256,512]{1,0:T(8,128)}, f32[256,512]{1,0:T(8,128)}, u32[]{:S(2)}, u32[]{:S(2)}) collective-permute-start(f32[256,512]{1,0:T(8,128)} %get-tuple-element.9), channel_id=1, source_target_pairs={{1,2}} | collective-permute-start | bytes 1572872 | tf_op jit(solution)/shard_map/ppermute | solution.py:59
  52.3 9.8 %copy-start.19 = (f32[256,256]{1,0:T(8,128)}, f32[256,256]{1,0:T(8,128)S(1)}, u32[]{:S(2)}) copy-start(f32[256,256]{1,0:T(8,128)S(1)} %fusion.51) | copy-start | bytes 786436
  53.7 0.8 copy-start.7
  55.1 0.8 copy-start.13
  58.6 8.5 %collective-permute-start.6 = (f32[256,512]{1,0:T(8,128)}, f32[256,512]{1,0:T(8,128)}, u32[]{:S(2)}, u32[]{:S(2)}) collective-permute-start(f32[256,512]{1,0:T(8,128)} %get-tuple-element.11), channel_id=1, source_target_pairs={{2,3}} | collective-permute-start | bytes 1572872 | tf_op jit(solution)/shard_map/ppermute | solution.py:59
  62.1 7.2 %collective-permute-start.4 = (f32[256,512]{1,0:T(8,128)}, f32[256,512]{1,0:T(8,128)}, u32[]{:S(2)}, u32[]{:S(2)}) collective-permute-start(f32[256,512]{1,0:T(8,128)} %add.67), channel_id=1, source_target_pairs={{1,3},{2,4}} | collective-permute-start | bytes 1572872 | tf_op jit(solution)/shard_map/ppermute | solution.py:59
  63.5 9.2 %copy-start.20 = (f32[256,256]{1,0:T(8,128)S(1)}, f32[256,256]{1,0:T(8,128)}, u32[]{:S(2)}) copy-start(f32[256,256]{1,0:T(8,128)} %copy-done.19) | copy-start | bytes 786436
  63.5 10.9 %copy-start.14 = (f32[256,512]{1,0:T(8,128)S(1)}, f32[256,512]{1,0:T(8,128)}, u32[]{:S(2)}) copy-start(f32[256,512]{1,0:T(8,128)} %copy-done.13) | copy-start | bytes 1572868
  64.9 14.3 %copy-start.17 = (f32[256,256]{1,0:T(8,128)}, f32[256,256]{1,0:T(8,128)S(1)}, u32[]{:S(2)}) copy-start(f32[256,256]{1,0:T(8,128)S(1)} %fusion.49) | copy-start | bytes 786436
  66.4 11.2 %collective-permute-start.2 = (f32[256,512]{1,0:T(8,128)}, f32[256,512]{1,0:T(8,128)S(1)}, u32[]{:S(2)}, u32[]{:S(2)}) collective-permute-start(f32[256,512]{1,0:T(8,128)} %copy-done.7), channel_id=1, source_target_pairs={{0,4},{1,5},{2,6},{3,7}} | collective-permute-start | bytes 1572872 | tf_op jit(solution)/shard_map/ppermute | solution.py:59
  68.4 9.2 %copy-start.8 = (f32[256,512]{1,0:T(8,128)S(1)}, f32[256,512]{1,0:T(8,128)}, u32[]{:S(2)}) copy-start(f32[256,512]{1,0:T(8,128)} %copy-done.7) | copy-start | bytes 1572868
  68.4 9.2 %copy-start.22 = (f32[256,256]{1,0:T(8,128)S(1)}, f32[256,256]{1,0:T(8,128)}, u32[]{:S(2)}) copy-start(f32[256,256]{1,0:T(8,128)} %copy-done.21) | copy-start | bytes 786436
  68.4 9.9 %collective-permute-start.7 = (f32[256,512]{1,0:T(8,128)S(1)}, f32[256,512]{1,0:T(8,128)S(1)}, u32[]{:S(2)}, u32[]{:S(2)}) collective-permute-start(f32[256,512]{1,0:T(8,128)S(1)} %add.70), channel_id=1, source_target_pairs={{2,4},{3,5}} | collective-permute-start | bytes 1572872 | tf_op jit(solution)/shard_map/ppermute | solution.py:59
  71.3 20.3 %collective-permute-start.5 = (f32[256,512]{1,0:T(8,128)}, f32[256,512]{1,0:T(8,128)}, u32[]{:S(2)}, u32[]{:S(2)}) collective-permute-start(f32[256,512]{1,0:T(8,128)} %add.68), channel_id=1, source_target_pairs={{1,5},{2,6},{3,7}} | collective-permute-start | bytes 1572872 | tf_op jit(solution)/shard_map/ppermute | solution.py:59
  76.9 4.0 %collective-permute-start.9 = (f32[256,512]{1,0:T(8,128)S(1)}, f32[256,512]{1,0:T(8,128)S(1)}, u32[]{:S(2)}, u32[]{:S(2)}) collective-permute-start(f32[256,512]{1,0:T(8,128)S(1)} %get-tuple-element.13), channel_id=1, source_target_pairs={{3,4}} | collective-permute-start | bytes 1572872 | tf_op jit(solution)/shard_map/ppermute | solution.py:59
  78.3 5.1 %copy-start.15 = (f32[256,512]{1,0:T(8,128)}, f32[256,512]{1,0:T(8,128)S(1)}, u32[]{:S(2)}) copy-start(f32[256,512]{1,0:T(8,128)S(1)} %convolution_subtract_fusion.9) | copy-start | bytes 1572868
  80.9 0.8 copy-start.11
  83.4 8.2 %copy-start.16 = (f32[256,512]{1,0:T(8,128)S(1)}, f32[256,512]{1,0:T(8,128)}, u32[]{:S(2)}) copy-start(f32[256,512]{1,0:T(8,128)} %copy-done.15) | copy-start | bytes 1572868
  83.4 10.1 %collective-permute-start.12 = (f32[256,512]{1,0:T(8,128)}, f32[256,512]{1,0:T(8,128)}, u32[]{:S(2)}, u32[]{:S(2)}) collective-permute-start(f32[256,512]{1,0:T(8,128)} %get-tuple-element.15), channel_id=1, source_target_pairs={{4,5}} | collective-permute-start | bytes 1572872 | tf_op jit(solution)/shard_map/ppermute | solution.py:59
  85.9 9.8 %collective-permute-start.10 = (f32[256,512]{1,0:T(8,128)}, f32[256,512]{1,0:T(8,128)}, u32[]{:S(2)}, u32[]{:S(2)}) collective-permute-start(f32[256,512]{1,0:T(8,128)} %add.73), channel_id=1, source_target_pairs={{3,5},{4,6}} | collective-permute-start | bytes 1572872 | tf_op jit(solution)/shard_map/ppermute | solution.py:59
  90.7 12.4 %copy-start.24 = (f32[256,256]{1,0:T(8,128)}, f32[256,256]{1,0:T(8,128)S(1)}, u32[]{:S(2)}) copy-start(f32[256,256]{1,0:T(8,128)S(1)} %fusion.43) | copy-start | bytes 786436
  90.7 6.8 %copy-start.12 = (f32[256,512]{1,0:T(8,128)S(1)}, f32[256,512]{1,0:T(8,128)}, u32[]{:S(2)}) copy-start(f32[256,512]{1,0:T(8,128)} %copy-done.11) | copy-start | bytes 1572868
  90.7 6.8 %copy-start.25 = (f32[256,256]{1,0:T(8,128)S(1)}, f32[256,256]{1,0:T(8,128)}, u32[]{:S(2)}) copy-start(f32[256,256]{1,0:T(8,128)} %fusion.41) | copy-start | bytes 786436
  90.7 10.0 %collective-permute-start.8 = (f32[256,512]{1,0:T(8,128)}, f32[256,512]{1,0:T(8,128)S(1)}, u32[]{:S(2)}, u32[]{:S(2)}) collective-permute-start(f32[256,512]{1,0:T(8,128)} %add.71), channel_id=1, source_target_pairs={{2,6},{3,7}} | collective-permute-start | bytes 1572872 | tf_op jit(solution)/shard_map/ppermute | solution.py:59
  94.8 6.0 %copy-start.18 = (f32[256,256]{1,0:T(8,128)S(1)}, f32[256,256]{1,0:T(8,128)}, u32[]{:S(2)}) copy-start(f32[256,256]{1,0:T(8,128)} %copy-done.17) | copy-start | bytes 786436
  94.8 7.7 %collective-permute-start.14 = (f32[256,512]{1,0:T(8,128)S(1)}, f32[256,512]{1,0:T(8,128)S(1)}, u32[]{:S(2)}, u32[]{:S(2)}) collective-permute-start(f32[256,512]{1,0:T(8,128)S(1)} %add.76), channel_id=1, source_target_pairs={{4,6},{5,7}} | collective-permute-start | bytes 1572872 | tf_op jit(solution)/shard_map/ppermute | solution.py:59
  100.1 3.1 %collective-permute-start.13 = (f32[256,512]{1,0:T(8,128)S(1)}, f32[256,512]{1,0:T(8,128)S(1)}, u32[]{:S(2)}, u32[]{:S(2)}) collective-permute-start(f32[256,512]{1,0:T(8,128)S(1)} %get-tuple-element.17), channel_id=1, source_target_pairs={{5,6}} | collective-permute-start | bytes 1572872 | tf_op jit(solution)/shard_map/ppermute | solution.py:59
  102.5 5.5 %copy-start.9 = (f32[256,512]{1,0:T(8,128)}, f32[256,512]{1,0:T(8,128)S(1)}, u32[]{:S(2)}) copy-start(f32[256,512]{1,0:T(8,128)S(1)} %convolution_subtract_fusion.5) | copy-start | bytes 1572868
  103.1 0.8 copy-start.5
  105.6 6.0 %collective-permute-start.15 = (f32[256,512]{1,0:T(8,128)}, f32[256,512]{1,0:T(8,128)}, u32[]{:S(2)}, u32[]{:S(2)}) collective-permute-start(f32[256,512]{1,0:T(8,128)} %get-tuple-element.19), channel_id=1, source_target_pairs={{6,7}} | collective-permute-start | bytes 1572872 | tf_op jit(solution)/shard_map/ppermute | solution.py:59
  107.9 5.4 %collective-permute-start.16 = (f32[256,512]{1,0:T(8,128)}, f32[256,512]{1,0:T(8,128)}, u32[]{:S(2)}, u32[]{:S(2)}) collective-permute-start(f32[256,512]{1,0:T(8,128)} %add.78), channel_id=1, source_target_pairs={{5,7}} | collective-permute-start | bytes 1572872 | tf_op jit(solution)/shard_map/ppermute | solution.py:59
  109.4 5.8 %copy-start.6 = (f32[256,512]{1,0:T(8,128)S(1)}, f32[256,512]{1,0:T(8,128)}, u32[]{:S(2)}) copy-start(f32[256,512]{1,0:T(8,128)} %copy-done.5) | copy-start | bytes 1572868
  109.4 5.9 %copy-start.10 = (f32[256,512]{1,0:T(8,128)S(1)}, f32[256,512]{1,0:T(8,128)}, u32[]{:S(2)}) copy-start(f32[256,512]{1,0:T(8,128)} %copy-done.9) | copy-start | bytes 1572868
  109.4 5.9 %copy-start.26 = (f32[256,512]{1,0:T(8,128)S(1)}, f32[256,512]{1,0:T(8,128)}, u32[]{:S(2)}) copy-start(f32[256,512]{1,0:T(8,128)} %get-tuple-element.10) | copy-start | bytes 1572868
  109.4 5.9 %copy-start.28 = (f32[256,512]{1,0:T(8,128)S(1)}, f32[256,512]{1,0:T(8,128)}, u32[]{:S(2)}) copy-start(f32[256,512]{1,0:T(8,128)} %get-tuple-element.12) | copy-start | bytes 1572868
  109.4 5.9 %copy-start.29 = (f32[256,512]{1,0:T(8,128)S(1)}, f32[256,512]{1,0:T(8,128)}, u32[]{:S(2)}) copy-start(f32[256,512]{1,0:T(8,128)} %get-tuple-element.14) | copy-start | bytes 1572868
  109.4 5.9 %copy-start.30 = (f32[256,512]{1,0:T(8,128)S(1)}, f32[256,512]{1,0:T(8,128)}, u32[]{:S(2)}) copy-start(f32[256,512]{1,0:T(8,128)} %get-tuple-element.16) | copy-start | bytes 1572868
  109.4 5.9 %copy-start.31 = (f32[256,512]{1,0:T(8,128)S(1)}, f32[256,512]{1,0:T(8,128)}, u32[]{:S(2)}) copy-start(f32[256,512]{1,0:T(8,128)} %get-tuple-element.18) | copy-start | bytes 1572868
  110.9 4.3 %collective-permute-start.11 = (f32[256,512]{1,0:T(8,128)S(1)}, f32[256,512]{1,0:T(8,128)S(1)}, u32[]{:S(2)}, u32[]{:S(2)}) collective-permute-start(f32[256,512]{1,0:T(8,128)S(1)} %add.74), channel_id=1, source_target_pairs={{3,7}} | collective-permute-start | bytes 1572872 | tf_op jit(solution)/shard_map/ppermute | solution.py:59
  116.3 26.3 %copy-start.3 = (f32[256,512]{1,0:T(8,128)}, f32[256,512]{1,0:T(8,128)S(1)}, u32[]{:S(2)}) copy-start(f32[256,512]{1,0:T(8,128)S(1)} %fusion.23) | copy-start | bytes 1572868
  116.3 0.7 collective-permute-start.17
  145.8 76.5 %all-to-all-start.1 = ((f32[4,5,128,256]{3,0,1,2:T(4,128)}), f32[4,5,128,256]{3,0,1,2:T(4,128)}, u32[]{:S(2)}, u32[]{:S(2)}) async-start(f32[4,5,128,256]{3,0,1,2:T(4,128)} %copy.35), calls=%async_computation.1 | async-start | bytes 5242880 | tf_op jit(solution)/shard_map/all_to_all | solution.py:16
  256.7 7.5 %copy-start.32 = (f32[1,2048,512]{2,1,0:T(8,128)S(1)}, f32[1,2048,512]{2,1,0:T(8,128)}, u32[]{:S(2)}) copy-start(f32[1,2048,512]{2,1,0:T(8,128)} %all-gather.3.cloned.1.call-done) | copy-start | bytes 12582916
  264.2 5.9 %copy-start.23 = (f32[512,5,256]{0,2,1:T(8,128)S(1)}, f32[512,5,256]{0,2,1:T(8,128)}, u32[]{:S(2)}) copy-start(f32[512,5,256]{0,2,1:T(8,128)} %copy.37) | copy-start | bytes 7864324
  264.2 5.9 %copy-start.27 = (f32[512,1,256]{0,2,1:T(8,128)S(1)}, f32[512,1,256]{0,2,1:T(8,128)}, u32[]{:S(2)}) copy-start(f32[512,1,256]{0,2,1:T(8,128)} %copy.34) | copy-start | bytes 1572868
  275.8 1.0 copy-start.4
  276.8 2.1 copy-start.1
Sparse Core Ops, SparseCore 0:
  140.8 115.8 all-gather.2
